TPU v7x, 32 devices: a whole 2x2x4 slice. The times are simulated.
32 devices in a mesh: panel: 2 (over y), lat: 4 (over z), lon: 4 (over x, core).
Axes of the slice: x: 2, y: 2, z: 4, core: 2. Of those that a mesh axis runs over, the one named last changes fastest.
Arguments:
- state: float32 [2, 7, 2, 256, 512], P('panel', None, None, 'lat', 'lon'), may hold values from -4 to 4
- source_slot: int32 [2, 4, 4, 768], P('panel', 'lat', 'lon'), may hold values from 0 to 3071, as said below
- donor_cell: int32 [2, 4, 4, 192], P('panel', 'lat', 'lon'), may hold values from 0 to 8000
- donor_frac: float32 [2, 4, 4, 2, 192], P('panel', 'lat', 'lon'), may hold values from 0 to 1
- donor_turn: float32 [2, 4, 4, 192], P('panel', 'lat', 'lon'), may hold values from -3.140625 to 3.140625
Outputs:
- new_state: float32 [2, 7, 2, 256, 512], P('panel', None, None, 'lat', 'lon')
Inputs may be any that keep to these rules, and one draw needn't show every extreme that they name: `source_slot`: entries name a partner panel donation (a * 4 + b) * 192 + s. For a device on an edge of its panel, the rim entries that lie on that edge name the donations that fill them; over a panel's whole border every donation of the partner panel is named exactly once. Other entries are unused.
All inputs are finite; a program needn't handle non-finite values.
Results may differ from a plain program's by a relative error of at most 0.00002.
Values sent between devices are 32-bit elements; how exact they have to be, the bound alone decides.
No kernel may reach another device: no remote copies, remote signals or barrier semaphores. Data moves between devices by JAX's collectives and lax.ppermute only.
A program may use at most 64 MiB of HBM per device.

v0:
```python
import jax
import jax.numpy as jnp
from jax import lax
from jax.sharding import PartitionSpec as P

viscosity = 0.05
resistivity = 0.05
diffusivity = 0.05
buoyancy = 0.5
time_step = 0.25


def partner_2(block, axis, apart):
    count = lax.axis_size(axis)
    route = []
    for low in range(count):
        high = low | 1 << apart
        if high != low and high < count:
            route += [(low, high), (high, low)]
    return lax.ppermute(block, axis, route)


def with_halo(value, sides, width):
    for axis, dim in sides:
        size, length = (lax.axis_size(axis), value.shape[dim])
        up = [(i, (i + 1) % size) for i in range(size - 1)]
        down = [(j, i) for i, j in up]
        last = lax.slice_in_dim(value, length - width, length, axis=dim)
        initial = lax.slice_in_dim(value, 0, width, axis=dim)
        before = lax.ppermute(last, axis, up)
        after = lax.ppermute(initial, axis, down)
        value = jnp.concatenate([before, value, after], axis=dim)
    return value


def rate(ext):
    height = ext.shape[2] - 4
    width = ext.shape[3] - 4

    def lat_at(k):
        return ext[:, :, 2 + k : 2 + k + height, 2 : 2 + width]

    def lon_at(k):
        return ext[:, :, 2 : 2 + height, 2 + k : 2 + k + width]

    middle = lat_at(0)
    d_lat = (8.0 * (lat_at(1) - lat_at(-1)) - (lat_at(2) - lat_at(-2))) / 12.0
    d_lon = (8.0 * (lon_at(1) - lon_at(-1)) - (lon_at(2) - lon_at(-2))) / 12.0
    padded = jnp.pad(middle, ((0, 0), (1, 1), (0, 0), (0, 0)))
    lap = lat_at(1) + lat_at(-1) + lon_at(1) + lon_at(-1) - 4.0 * middle
    lap = lap + padded[:, 2:] + padded[:, :-2] - 2.0 * middle
    adv_u = middle[1:2] * d_lat + middle[2:3] * d_lon
    adv_b = middle[4:5] * d_lat + middle[5:6] * d_lon
    moment = -adv_u[0:3] + adv_b[3:6] + viscosity * lap[0:3]
    induct = adv_b[0:3] - adv_u[3:6] + resistivity * lap[3:6]
    heat = -adv_u[6:7] + diffusivity * lap[6:7]
    first = moment[0:1] + buoyancy * middle[6:7]
    return jnp.concatenate([first, moment[1:3], induct, heat], axis=0)


def rotate(values, turn):
    cosine = jnp.cos(turn)
    sine = jnp.sin(turn)
    parts = [
        values[0],
        cosine * values[1] - sine * values[2],
        sine * values[1] + cosine * values[2],
        values[3],
        cosine * values[4] - sine * values[5],
        sine * values[4] + cosine * values[5],
        values[6],
    ]
    return jnp.stack(parts)


def per_device(state, source_slot, donor_cell, donor_frac, donor_turn):
    comps = state.shape[1]
    levels = state.shape[2]
    rows = state.shape[3]
    cols = state.shape[4]
    cells = donor_cell[0, 0, 0]
    frac_t = donor_frac[0, 0, 0, 0]
    frac_p = donor_frac[0, 0, 0, 1]
    turn = donor_turn[0, 0, 0]
    slots = source_slot[0, 0, 0]
    index = cells // (cols - 1) * cols + cells % (cols - 1)
    lat_pos = lax.axis_index("lat")
    lon_pos = lax.axis_index("lon")
    lat_count = lax.axis_size("lat")
    lon_count = lax.axis_size("lon")

    def donate(field):
        flat = field.reshape(comps, levels, rows * cols)
        lower = jnp.take(flat, index, axis=2)
        lower_next = jnp.take(flat, index + 1, axis=2)
        upper = jnp.take(flat, index + cols, axis=2)
        upper_next = jnp.take(flat, index + cols + 1, axis=2)
        value = (
            (1.0 - frac_t) * (1.0 - frac_p) * lower
            + (1.0 - frac_t) * frac_p * lower_next
            + frac_t * (1.0 - frac_p) * upper
            + frac_t * frac_p * upper_next
        )
        return rotate(value, turn).reshape(comps * levels, -1)

    def receive(given):
        whole = lax.all_gather(given, ("lat", "lon"), axis=1, tiled=True)
        partner = partner_2(whole, "panel", 0)
        return jnp.take(partner, slots, axis=1)

    def extended(field):
        ext = with_halo(field, (("lat", 2), ("lon", 3)), 2)
        rim_values = receive(donate(field)).reshape(comps, levels, -1)
        top = rim_values[:, :, 0 : 2 * cols].reshape(comps, levels, 2, cols)
        bottom = rim_values[:, :, 2 * cols : 4 * cols].reshape(comps, levels, 2, cols)
        left = rim_values[:, :, 4 * cols : 4 * cols + 2 * rows].reshape(comps, levels, 2, rows)
        left = jnp.transpose(left, (0, 1, 3, 2))
        right = rim_values[:, :, 4 * cols + 2 * rows :].reshape(comps, levels, 2, rows)
        right = jnp.transpose(right, (0, 1, 3, 2))
        ext = ext.at[:, :, 0:2, 2 : 2 + cols].set(
            jnp.where(lat_pos == 0, top, ext[:, :, 0:2, 2 : 2 + cols])
        )
        ext = ext.at[:, :, rows + 2 : rows + 4, 2 : 2 + cols].set(
            jnp.where(
                lat_pos == lat_count - 1, bottom, ext[:, :, rows + 2 : rows + 4, 2 : 2 + cols]
            )
        )
        ext = ext.at[:, :, 2 : 2 + rows, 0:2].set(
            jnp.where(lon_pos == 0, left, ext[:, :, 2 : 2 + rows, 0:2])
        )
        ext = ext.at[:, :, 2 : 2 + rows, cols + 2 : cols + 4].set(
            jnp.where(lon_pos == lon_count - 1, right, ext[:, :, 2 : 2 + rows, cols + 2 : cols + 4])
        )
        return ext

    field = state[0]
    section_one = field + time_step * rate(extended(field))
    second = rate(extended(section_one))
    new_field = 0.5 * field + 0.5 * (section_one + time_step * second)
    return new_field[None]


def solution(mesh):
    in_specs = (
        P("panel", None, None, "lat", "lon"),
        P("panel", "lat", "lon", None),
        P("panel", "lat", "lon", None),
        P("panel", "lat", "lon", None, None),
        P("panel", "lat", "lon", None),
    )
    out_specs = P("panel", None, None, "lat", "lon")
    return jax.shard_map(
        per_device, mesh=mesh, in_specs=in_specs, out_specs=out_specs, check_vma=False
    )
```

profile of v0, /device:TPU:1, one launch (start us, length us, event | category | flops | bytes accessed | tf_op | source)
XLA Modules:
  0.0 220.7 jit_solution(9015375217256349187)
XLA Ops:
  2.8 7.8 %copy.156 = f32[7,2,8192]{0,1,2:T(2,128)} copy(f32[7,2,8192]{2,1,0:T(2,128)S(1)} %reshape_squeeze.3) | data formatting | bytes 917504 | tf_op jit(solution)/shard_map/reshape;squeeze | solution.py:93
  10.7 4.3 %gather_fusion = f32[192,7,2]{1,2,0:T(2,128)S(1)} fusion(f32[7,2,8192]{0,1,2:T(2,128)} %copy.156, s32[1024]{0:T(1024)S(1)} %get-tuple-element.165), kind=kCustom, calls=%fused_computation.clone | custom fusion | bytes 22272 | tf_op jit(solution)/shard_map/jit(_take)/gather | solution.py:94
  15.0 4.3 %gather_fusion.1 = f32[192,7,2]{1,2,0:T(2,128)S(1)} fusion(f32[7,2,8192]{0,1,2:T(2,128)} %copy.156, s32[1024]{0:T(1024)S(1)} %get-tuple-element.164), kind=kCustom, calls=%fused_computation.2.clone | custom fusion | bytes 22272 | tf_op jit(solution)/shard_map/jit(_take)/gather | solution.py:95
  19.5 4.3 %gather_fusion.2 = f32[192,7,2]{1,2,0:T(2,128)S(1)} fusion(f32[7,2,8192]{0,1,2:T(2,128)} %copy.156, s32[1024]{0:T(1024)S(1)} %get-tuple-element.163), kind=kCustom, calls=%fused_computation.3.clone | custom fusion | bytes 22272 | tf_op jit(solution)/shard_map/jit(_take)/gather | solution.py:96
  23.8 4.3 %gather_fusion.3 = f32[192,7,2]{1,2,0:T(2,128)S(1)} fusion(f32[7,2,8192]{0,1,2:T(2,128)} %copy.156, s32[1024]{0:T(1024)S(1)} %get-tuple-element.162), kind=kCustom, calls=%fused_computation.4.clone | custom fusion | bytes 22272 | tf_op jit(solution)/shard_map/jit(_take)/gather | solution.py:97
  28.5 23.7 %all-gather = f32[16,192,14]{1,2,0:T(8,128)S(1)} all-gather(f32[1,192,14]{1,2,0:T(8,128)S(1)} %bitcast.137), channel_id=1, replica_groups=mesh['panel'=2,'lat'=4,'lon'=4] {'lat','lon'}, dimensions={0}, use_global_device_ids=true | all-gather | bytes 182784 | tf_op jit(solution)/shard_map/all_gather | solution.py:107
  65.4 3.0 %collective-permute-done.2 = f32[7,2,68,2]{3,2,1,0:T(8,128)S(1)} collective-permute-done((f32[7,2,68,2]{3,2,1,0:T(8,128)S(1)}, f32[7,2,68,2]{3,2,1,0:T(8,128)S(1)}, u32[]{:S(2)}, u32[]{:S(2)}) %collective-permute-start.2) | collective-permute-done | bytes 7648 | tf_op jit(solution)/shard_map/ppermute | solution.py:30
  68.4 4.4 %collective-permute-done.3 = f32[7,2,68,2]{3,2,1,0:T(8,128)S(1)} collective-permute-done((f32[7,2,68,2]{3,2,1,0:T(8,128)S(1)}, f32[7,2,68,2]{3,2,1,0:T(8,128)S(1)}, u32[]{:S(2)}, u32[]{:S(2)}) %collective-permute-start.3) | collective-permute-done | bytes 7648 | tf_op jit(solution)/shard_map/ppermute | solution.py:31
  80.4 5.8 %scatter.26 = f32[7,2,68,132]{3,2,1,0:T(8,128)S(1)} dynamic-update-slice(f32[7,2,68,132]{3,2,1,0:T(8,128)S(1)} %pad_maximum_fusion, f32[7,2,2,128]{3,2,1,0:T(2,128)S(1)} %dynamic-slice_select_fusion.1, s32[]{:T(128)} %constant.261.clone.1, s32[]{:T(128)} %constant.261.clone.1, s32[]{:T(128)} %bitcast.15, s32[]{:T(128)} %bitcast.16) | dynamic-update-slice | bytes 28676 | tf_op jit(solution)/shard_map/scatter | solution.py:120
  86.7 4.5 %scatter.29 = f32[7,2,68,132]{3,2,1,0:T(8,128)S(1)} dynamic-update-slice(f32[7,2,68,132]{3,2,1,0:T(8,128)S(1)} %scatter.26, f32[7,2,2,128]{3,2,1,0:T(2,128)S(1)} %slice_select_fusion.5, s32[]{:T(128)} %constant.261.clone.1, s32[]{:T(128)} %constant.261.clone.1, s32[]{:T(128)} %constant.275.clone.1, s32[]{:T(128)} %constant.263.clone.1) | dynamic-update-slice | bytes 28676 | tf_op jit(solution)/shard_map/scatter | solution.py:123
  91.2 9.3 %scatter.30 = f32[7,2,68,132]{3,2,1,0:T(8,128)S(1)} dynamic-update-slice(f32[7,2,68,132]{3,2,1,0:T(8,128)S(1)} %scatter.29, f32[7,2,64,2]{3,2,1,0:T(8,128)S(1)} %slice_select_fusion.3, s32[]{:T(128)} %constant.261.clone.1, s32[]{:T(128)} %constant.261.clone.1, s32[]{:T(128)} %constant.263.clone.1, s32[]{:T(128)} %constant.261.clone.1) | dynamic-update-slice | bytes 14340 | tf_op jit(solution)/shard_map/scatter | solution.py:128
  101.1 11.6 %scatter.31 = f32[7,2,68,132]{3,2,1,0:T(8,128)S(1)} dynamic-update-slice(f32[7,2,68,132]{3,2,1,0:T(8,128)S(1)} %scatter.30, f32[7,2,64,2]{3,2,1,0:T(8,128)S(1)} %slice_select_fusion.2, s32[]{:T(128)} %constant.261.clone.1, s32[]{:T(128)} %constant.261.clone.1, s32[]{:T(128)} %constant.263.clone.1, s32[]{:T(128)} %constant.276.clone.1) | dynamic-update-slice | bytes 14340 | tf_op jit(solution)/shard_map/scatter | solution.py:131
  114.9 7.8 %copy.171 = f32[7,2,8192]{0,1,2:T(2,128)} copy(f32[7,2,8192]{2,1,0:T(2,128)S(1)} %fusion.15) | data formatting | bytes 917504 | tf_op jit(solution)/shard_map/add | solution.py:137
  122.7 4.3 %gather_fusion.5 = f32[192,7,2]{1,2,0:T(2,128)S(1)} fusion(f32[7,2,8192]{0,1,2:T(2,128)} %copy.171, s32[1024]{0:T(1024)S(1)} %get-tuple-element.165), kind=kCustom, calls=%fused_computation.5.clone | custom fusion | bytes 22272 | tf_op jit(solution)/shard_map/jit(_take)/gather | solution.py:94
  127.0 4.3 %gather_fusion.6 = f32[192,7,2]{1,2,0:T(2,128)S(1)} fusion(f32[7,2,8192]{0,1,2:T(2,128)} %copy.171, s32[1024]{0:T(1024)S(1)} %get-tuple-element.164), kind=kCustom, calls=%fused_computation.6.clone | custom fusion | bytes 22272 | tf_op jit(solution)/shard_map/jit(_take)/gather | solution.py:95
  131.2 4.3 %gather_fusion.7 = f32[192,7,2]{1,2,0:T(2,128)S(1)} fusion(f32[7,2,8192]{0,1,2:T(2,128)} %copy.171, s32[1024]{0:T(1024)S(1)} %get-tuple-element.163), kind=kCustom, calls=%fused_computation.7.clone | custom fusion | bytes 22272 | tf_op jit(solution)/shard_map/jit(_take)/gather | solution.py:96
  135.5 4.3 %gather_fusion.8 = f32[192,7,2]{1,2,0:T(2,128)S(1)} fusion(f32[7,2,8192]{0,1,2:T(2,128)} %copy.171, s32[1024]{0:T(1024)S(1)} %get-tuple-element.162), kind=kCustom, calls=%fused_computation.8.clone | custom fusion | bytes 22272 | tf_op jit(solution)/shard_map/jit(_take)/gather | solution.py:97
  144.2 21.1 %all-gather.1 = f32[16,192,14]{1,2,0:T(8,128)S(1)} all-gather(f32[1,192,14]{1,2,0:T(8,128)S(1)} %bitcast.136), channel_id=1, replica_groups=mesh['panel'=2,'lat'=4,'lon'=4] {'lat','lon'}, dimensions={0}, use_global_device_ids=true | all-gather | bytes 182784 | tf_op jit(solution)/shard_map/all_gather | solution.py:107
  170.7 3.4 %collective-permute-done.7 = f32[7,2,68,2]{3,2,1,0:T(8,128)S(1)} collective-permute-done((f32[7,2,68,2]{3,2,1,0:T(8,128)S(1)}, f32[7,2,68,2]{3,2,1,0:T(8,128)S(1)}, u32[]{:S(2)}, u32[]{:S(2)}) %collective-permute-start.7) | collective-permute-done | bytes 7648 | tf_op jit(solution)/shard_map/ppermute | solution.py:30
  174.0 4.4 %collective-permute-done.8 = f32[7,2,68,2]{3,2,1,0:T(8,128)S(1)} collective-permute-done((f32[7,2,68,2]{3,2,1,0:T(8,128)S(1)}, f32[7,2,68,2]{3,2,1,0:T(8,128)S(1)}, u32[]{:S(2)}, u32[]{:S(2)}) %collective-permute-start.8) | collective-permute-done | bytes 7648 | tf_op jit(solution)/shard_map/ppermute | solution.py:31
  186.0 5.8 %scatter.34 = f32[7,2,68,132]{3,2,1,0:T(8,128)S(1)} dynamic-update-slice(f32[7,2,68,132]{3,2,1,0:T(8,128)S(1)} %pad_maximum_fusion.1, f32[7,2,2,128]{3,2,1,0:T(2,128)S(1)} %dynamic-slice_select_fusion, s32[]{:T(128)} %constant.261.clone.1, s32[]{:T(128)} %constant.261.clone.1, s32[]{:T(128)} %bitcast.15, s32[]{:T(128)} %bitcast.16) | dynamic-update-slice | bytes 28676 | tf_op jit(solution)/shard_map/scatter | solution.py:120
  192.0 4.5 %scatter.35 = f32[7,2,68,132]{3,2,1,0:T(8,128)S(1)} dynamic-update-slice(f32[7,2,68,132]{3,2,1,0:T(8,128)S(1)} %scatter.34, f32[7,2,2,128]{3,2,1,0:T(2,128)S(1)} %slice_select_fusion.4, s32[]{:T(128)} %constant.261.clone.1, s32[]{:T(128)} %constant.261.clone.1, s32[]{:T(128)} %constant.275.clone.1, s32[]{:T(128)} %constant.263.clone.1) | dynamic-update-slice | bytes 28676 | tf_op jit(solution)/shard_map/scatter | solution.py:123
  196.8 9.3 %scatter.36 = f32[7,2,68,132]{3,2,1,0:T(8,128)S(1)} dynamic-update-slice(f32[7,2,68,132]{3,2,1,0:T(8,128)S(1)} %scatter.35, f32[7,2,64,2]{3,2,1,0:T(8,128)S(1)} %slice_select_fusion.1, s32[]{:T(128)} %constant.261.clone.1, s32[]{:T(128)} %constant.261.clone.1, s32[]{:T(128)} %constant.263.clone.1, s32[]{:T(128)} %constant.261.clone.1) | dynamic-update-slice | bytes 14340 | tf_op jit(solution)/shard_map/scatter | solution.py:128
  206.7 11.6 %scatter.39 = f32[7,2,68,132]{3,2,1,0:T(8,128)S(1)} dynamic-update-slice(f32[7,2,68,132]{3,2,1,0:T(8,128)S(1)} %scatter.36, f32[7,2,64,2]{3,2,1,0:T(8,128)S(1)} %slice_select_fusion, s32[]{:T(128)} %constant.261.clone.1, s32[]{:T(128)} %constant.261.clone.1, s32[]{:T(128)} %constant.263.clone.1, s32[]{:T(128)} %constant.276.clone.1) | dynamic-update-slice | bytes 14340 | tf_op jit(solution)/shard_map/scatter | solution.py:131
  (139 shorter events, 47.9 us)
Async XLA Ops:
  0.0 57.0 %copy-start.4 = (s32[4]{0:T(128)S(1)}, s32[4]{0:T(128)}, u32[]{:S(2)}) copy-start(s32[4]{0:T(128)} %constant.264.clone.1) | copy-start | bytes 52
  0.0 54.3 %copy-start = (f32[1,7,2,64,128]{4,3,2,1,0:T(8,128)S(1)}, f32[1,7,2,64,128]{4,3,2,1,0:T(8,128)}, u32[]{:S(2)}) copy-start(f32[1,7,2,64,128]{4,3,2,1,0:T(8,128)} %param.25) | copy-start | bytes 1376260
  0.0 28.2 %copy-start.2 = (f32[1,1,1,2,192]{4,3,2,1,0:T(2,128)S(1)}, f32[1,1,1,2,192]{4,3,2,1,0:T(2,128)}, u32[]{:S(2)}) copy-start(f32[1,1,1,2,192]{4,3,2,1,0:T(2,128)} %param.28) | copy-start | bytes 4612
  0.0 28.3 %copy-start.3 = (f32[1,1,1,192]{3,2,1,0:T(1,128)S(1)}, f32[1,1,1,192]{3,2,1,0:T(1,128)}, u32[]{:S(2)}) copy-start(f32[1,1,1,192]{3,2,1,0:T(1,128)} %param.29) | copy-start | bytes 2308
  0.0 56.9 %copy-start.1 = (s32[1,1,1,768]{3,2,1,0:T(1,128)S(1)}, s32[1,1,1,768]{3,2,1,0:T(1,128)}, u32[]{:S(2)}) copy-start(s32[1,1,1,768]{3,2,1,0:T(1,128)} %param.26) | copy-start | bytes 9220
  53.1 20.3 %collective-permute-start.4 = (f32[14,3072]{1,0:T(8,128)}, f32[14,3072]{1,0:T(8,128)S(1)}, u32[]{:S(2)}, u32[]{:S(2)}) collective-permute-start(f32[14,3072]{1,0:T(8,128)} %bitcast.13), channel_id=1, source_target_pairs={{0,16},{16,0},{1,17},{17,1},{2,18},{18,2},{3,19},{19,3},{4,20},{20... | collective-permute-start | bytes 516104 | tf_op jit(solution)/shard_map/ppermute | solution.py:20
  54.3 4.0 %collective-permute-start = (f32[7,2,2,128]{3,2,1,0:T(2,128)S(1)}, f32[7,2,2,128]{3,2,1,0:T(2,128)S(1)}, u32[]{:S(2)}, u32[]{:S(2)}) collective-permute-start(f32[7,2,2,128]{3,2,1,0:T(2,128)S(1)} %get-tuple-element.131), channel_id=1, source_target_pairs={{0,4},{4,8},{8,12},{1,5},{5,9},{9,13},{2,6},{6,10},{10,14},{3,7},{... | collective-permute-start | bytes 43016 | tf_op jit(solution)/shard_map/ppermute | solution.py:30
  55.6 4.6 %collective-permute-start.1 = (f32[7,2,2,128]{3,2,1,0:T(2,128)S(1)}, f32[7,2,2,128]{3,2,1,0:T(2,128)S(1)}, u32[]{:S(2)}, u32[]{:S(2)}) collective-permute-start(f32[7,2,2,128]{3,2,1,0:T(2,128)S(1)} %get-tuple-element.132), channel_id=1, source_target_pairs={{4,0},{8,4},{12,8},{5,1},{9,5},{13,9},{6,2},{10,6},{14,10},{7,3},{... | collective-permute-start | bytes 43016 | tf_op jit(solution)/shard_map/ppermute | solution.py:31
  60.5 7.9 %collective-permute-start.2 = (f32[7,2,68,2]{3,2,1,0:T(8,128)S(1)}, f32[7,2,68,2]{3,2,1,0:T(8,128)S(1)}, u32[]{:S(2)}, u32[]{:S(2)}) collective-permute-start(f32[7,2,68,2]{3,2,1,0:T(8,128)S(1)} %get-tuple-element.127), channel_id=1, source_target_pairs={{0,1},{1,2},{2,3},{4,5},{5,6},{6,7},{8,9},{9,10},{10,11},{12,13},{... | collective-permute-start | bytes 22856 | tf_op jit(solution)/shard_map/ppermute | solution.py:30
  62.4 10.4 %collective-permute-start.3 = (f32[7,2,68,2]{3,2,1,0:T(8,128)S(1)}, f32[7,2,68,2]{3,2,1,0:T(8,128)S(1)}, u32[]{:S(2)}, u32[]{:S(2)}) collective-permute-start(f32[7,2,68,2]{3,2,1,0:T(8,128)S(1)} %get-tuple-element.128), channel_id=1, source_target_pairs={{1,0},{2,1},{3,2},{5,4},{6,5},{7,6},{9,8},{10,9},{11,10},{13,12},{... | collective-permute-start | bytes 22856 | tf_op jit(solution)/shard_map/ppermute | solution.py:31
  140.5 25.3 %collective-permute-start.5 = (f32[7,2,2,128]{3,2,1,0:T(2,128)S(1)}, f32[7,2,2,128]{3,2,1,0:T(2,128)S(1)}, u32[]{:S(2)}, u32[]{:S(2)}) collective-permute-start(f32[7,2,2,128]{3,2,1,0:T(2,128)S(1)} %get-tuple-element.129), channel_id=1, source_target_pairs={{0,4},{4,8},{8,12},{1,5},{5,9},{9,13},{2,6},{6,10},{10,14},{3,7},{... | collective-permute-start | bytes 43016 | tf_op jit(solution)/shard_map/ppermute | solution.py:30
  142.9 23.0 %collective-permute-start.6 = (f32[7,2,2,128]{3,2,1,0:T(2,128)S(1)}, f32[7,2,2,128]{3,2,1,0:T(2,128)S(1)}, u32[]{:S(2)}, u32[]{:S(2)}) collective-permute-start(f32[7,2,2,128]{3,2,1,0:T(2,128)S(1)} %get-tuple-element.130), channel_id=1, source_target_pairs={{4,0},{8,4},{12,8},{5,1},{9,5},{13,9},{6,2},{10,6},{14,10},{7,3},{... | collective-permute-start | bytes 43016 | tf_op jit(solution)/shard_map/ppermute | solution.py:31
  165.6 13.4 %collective-permute-start.9 = (f32[14,3072]{1,0:T(8,128)S(1)}, f32[14,3072]{1,0:T(8,128)S(1)}, u32[]{:S(2)}, u32[]{:S(2)}) collective-permute-start(f32[14,3072]{1,0:T(8,128)S(1)} %bitcast.119), channel_id=1, source_target_pairs={{0,16},{16,0},{1,17},{17,1},{2,18},{18,2},{3,19},{19,3},{4,20},{20... | collective-permute-start | bytes 516104 | tf_op jit(solution)/shard_map/ppermute | solution.py:20
  166.1 7.9 %collective-permute-start.7 = (f32[7,2,68,2]{3,2,1,0:T(8,128)S(1)}, f32[7,2,68,2]{3,2,1,0:T(8,128)S(1)}, u32[]{:S(2)}, u32[]{:S(2)}) collective-permute-start(f32[7,2,68,2]{3,2,1,0:T(8,128)S(1)} %get-tuple-element.125), channel_id=1, source_target_pairs={{0,1},{1,2},{2,3},{4,5},{5,6},{6,7},{8,9},{9,10},{10,11},{12,13},{... | collective-permute-start | bytes 22856 | tf_op jit(solution)/shard_map/ppermute | solution.py:30
  168.0 10.4 %collective-permute-start.8 = (f32[7,2,68,2]{3,2,1,0:T(8,128)S(1)}, f32[7,2,68,2]{3,2,1,0:T(8,128)S(1)}, u32[]{:S(2)}, u32[]{:S(2)}) collective-permute-start(f32[7,2,68,2]{3,2,1,0:T(8,128)S(1)} %get-tuple-element.126), channel_id=1, source_target_pairs={{1,0},{2,1},{3,2},{5,4},{6,5},{7,6},{9,8},{10,9},{11,10},{13,12},{... | collective-permute-start | bytes 22856 | tf_op jit(solution)/shard_map/ppermute | solution.py:31
where the time goes:
time: 221 us
  local copies, waits for them, and re-layouts  128 us (58%)
  blocking collectives  44.8 us (20%)
  starting transfers between devices  17.2 us (8%)
  waiting for transfers between devices  17 us (8%)
  other arithmetic  12.4 us (6%)
    all_gather x2, blocking collectives, receive(): whole = lax.all_gather(given, ('lat', 'lon'), axis=1, tiled=True)  44.8 us
    scatter x2, local copies, waits for them, and re-layouts, extended(): ext.at[:, :, 2:2 + rows, cols + 2:cols + 4]  23.1 us
    scatter x2, local copies, waits for them, and re-layouts, extended(): ext.at[:, :, 2:2 + rows, 0:2]  18.7 us
    scatter x2, local copies, waits for them, and re-layouts, extended(): ext.at[:, :, 0:2, 2:2 + cols]  11.6 us
    ppermute x4, waiting for transfers between devices, with_halo(): after = lax.ppermute(initial, axis, down)  10.7 us
    another operation x2, local copies, waits for them, and re-layouts, donate(): flat = field.reshape(comps, levels, rows * cols)  9.12 us
    scatter x2, local copies, waits for them, and re-layouts, extended(): ext.at[:, :, rows + 2:rows + 4, 2:2 + cols]  8.9 us
    gather x4, local copies, waits for them, and re-layouts, donate(): lower_next = jnp.take(flat, index + 1, axis=2)  8.77 us
  transfers between devices with their start and end apart: 10, of which 5 were waited for; matrix products, arithmetic and copies ran while one was open for 1% of the time, Pallas kernels for 0%

commit v1 on v0

v1 whole, which is shorter than its diff:
```python
import jax
import jax.numpy as jnp
from jax import lax
from jax.sharding import PartitionSpec as P

viscosity = 0.05
resistivity = 0.05
diffusivity = 0.05
buoyancy = 0.5
time_step = 0.25

HIGHEST = lax.Precision.HIGHEST


def partner_2(block, axis, apart):
    count = lax.axis_size(axis)
    route = []
    for low in range(count):
        high = low | 1 << apart
        if high != low and high < count:
            route += [(low, high), (high, low)]
    return lax.ppermute(block, axis, route)


def shift(value, axis, step):
    size = lax.axis_size(axis)
    if step > 0:
        route = [(i, i + 1) for i in range(size - 1)]
    else:
        route = [(i + 1, i) for i in range(size - 1)]
    return lax.ppermute(value, axis, route)


def rate(up, mid, down, left, right):
    vert = jnp.concatenate([up, mid, down], axis=2)
    horz = jnp.concatenate([left, mid, right], axis=3)
    height = mid.shape[2]
    width = mid.shape[3]

    def lat_at(k):
        return vert[:, :, 2 + k : 2 + k + height, :]

    def lon_at(k):
        return horz[:, :, :, 2 + k : 2 + k + width]

    middle = mid
    d_lat = (8.0 * (lat_at(1) - lat_at(-1)) - (lat_at(2) - lat_at(-2))) / 12.0
    d_lon = (8.0 * (lon_at(1) - lon_at(-1)) - (lon_at(2) - lon_at(-2))) / 12.0
    padded = jnp.pad(middle, ((0, 0), (1, 1), (0, 0), (0, 0)))
    lap = lat_at(1) + lat_at(-1) + lon_at(1) + lon_at(-1) - 4.0 * middle
    lap = lap + padded[:, 2:] + padded[:, :-2] - 2.0 * middle
    adv_u = middle[1:2] * d_lat + middle[2:3] * d_lon
    adv_b = middle[4:5] * d_lat + middle[5:6] * d_lon
    moment = -adv_u[0:3] + adv_b[3:6] + viscosity * lap[0:3]
    induct = adv_b[0:3] - adv_u[3:6] + resistivity * lap[3:6]
    heat = -adv_u[6:7] + diffusivity * lap[6:7]
    first = moment[0:1] + buoyancy * middle[6:7]
    return jnp.concatenate([first, moment[1:3], induct, heat], axis=0)


def rotate(values, turn):
    cosine = jnp.cos(turn)
    sine = jnp.sin(turn)
    parts = [
        values[0],
        cosine * values[1] - sine * values[2],
        sine * values[1] + cosine * values[2],
        values[3],
        cosine * values[4] - sine * values[5],
        sine * values[4] + cosine * values[5],
        values[6],
    ]
    return jnp.stack(parts)


def per_device(state, source_slot, donor_cell, donor_frac, donor_turn):
    comps = state.shape[1]
    levels = state.shape[2]
    rows = state.shape[3]
    cols = state.shape[4]
    cells = donor_cell[0, 0, 0]
    frac_t = donor_frac[0, 0, 0, 0]
    frac_p = donor_frac[0, 0, 0, 1]
    turn = donor_turn[0, 0, 0]
    slots = source_slot[0, 0, 0]
    lat_pos = lax.axis_index("lat")
    lon_pos = lax.axis_index("lon")
    lat_count = lax.axis_size("lat")
    lon_count = lax.axis_size("lon")
    on_top = lat_pos == 0
    on_bottom = lat_pos == lat_count - 1
    on_left = lon_pos == 0
    on_right = lon_pos == lon_count - 1

    row = cells // (cols - 1)
    col = cells % (cols - 1)
    col_ids = jnp.arange(cols, dtype=jnp.int32)[None, :]
    row_ids = jnp.arange(rows, dtype=jnp.int32)[None, :]
    weight_lon = jnp.where(col_ids == col[:, None], (1.0 - frac_p)[:, None], 0.0) + jnp.where(
        col_ids == col[:, None] + 1, frac_p[:, None], 0.0
    )
    weight_lat = jnp.where(row_ids == row[:, None], (1.0 - frac_t)[:, None], 0.0) + jnp.where(
        row_ids == row[:, None] + 1, frac_t[:, None], 0.0
    )

    band = 2 * cols
    side = 2 * rows
    lat_slots = jnp.where(on_top, slots[0:band], slots[band : 2 * band])
    lon_slots = jnp.where(on_left, slots[2 * band : 2 * band + side], slots[2 * band + side :])
    wanted = jnp.concatenate([lat_slots, lon_slots])
    total = lax.axis_size("lat") * lax.axis_size("lon") * cells.shape[0]
    pick = (jnp.arange(total, dtype=jnp.int32)[:, None] == wanted[None, :]).astype(jnp.float32)

    def donate(field):
        flat = field.reshape(comps * levels, rows, cols)
        along = jnp.einsum("kij,sj->kis", flat, weight_lon, precision=HIGHEST)
        value = jnp.sum(along * weight_lat.T[None], axis=1)
        return rotate(value.reshape(comps, levels, -1), turn).reshape(comps * levels, -1)

    def receive(given):
        whole = lax.all_gather(given, ("lat", "lon"), axis=1, tiled=True)
        partner = partner_2(whole, "panel", 0)
        return jnp.dot(partner, pick, precision=HIGHEST)

    def section(field):
        up = shift(field[:, :, rows - 2 :, :], "lat", 1)
        down = shift(field[:, :, :2, :], "lat", -1)
        left = shift(field[:, :, :, cols - 2 :], "lon", 1)
        right = shift(field[:, :, :, :2], "lon", -1)
        rim = receive(donate(field)).reshape(comps, levels, -1)
        rim_lat = rim[:, :, :band].reshape(comps, levels, 2, cols)
        rim_lon = jnp.transpose(rim[:, :, band:].reshape(comps, levels, 2, rows), (0, 1, 3, 2))
        up = jnp.where(on_top, rim_lat, up)
        down = jnp.where(on_bottom, rim_lat, down)
        left = jnp.where(on_left, rim_lon, left)
        right = jnp.where(on_right, rim_lon, right)
        return rate(up, field, down, left, right)

    field = state[0]
    section_one = field + time_step * section(field)
    second = section(section_one)
    new_field = 0.5 * field + 0.5 * (section_one + time_step * second)
    return new_field[None]


def solution(mesh):
    in_specs = (
        P("panel", None, None, "lat", "lon"),
        P("panel", "lat", "lon", None),
        P("panel", "lat", "lon", None),
        P("panel", "lat", "lon", None, None),
        P("panel", "lat", "lon", None),
    )
    out_specs = P("panel", None, None, "lat", "lon")
    return jax.shard_map(
        per_device, mesh=mesh, in_specs=in_specs, out_specs=out_specs, check_vma=False
    )
```

time: 221 us -> 84.2 us (0.38)
  the two profiles are of different devices: /device:TPU:1 before, /device:TPU:0 now
where the time goes in v1:
time: 84.2 us; the launch traced here: 83.1 us
  blocking collectives  42.9 us (51%)
  starting transfers between devices  24.2 us (29%)
  other arithmetic  6.12 us (7%)
  matrix products  6.05 us (7%)
  local copies, waits for them, and re-layouts  3.29 us (4%)
    all_gather x2, blocking collectives, receive(): whole = lax.all_gather(given, ('lat', 'lon'), axis=1, tiled=True)  42.9 us
    ppermute x8, starting transfers between devices, shift(): return lax.ppermute(value, axis, route)  21.7 us
    dot_general x2, matrix products, donate(): along = jnp.einsum('kij,sj->kis', flat, weight_lon, precision=HIGHEST)  3.09 us
    dot_general x2, matrix products, receive(): return jnp.dot(partner, pick, precision=HIGHEST)  2.97 us
    ppermute x2, starting transfers between devices, partner_2(): return lax.ppermute(block, axis, route)  2.5 us
    add x2, other arithmetic, rate(): adv_b = middle[4:5] * d_lat + middle[5:6] * d_lon  1.8 us
  transfers between devices with their start and end apart: 10, of which 0 were waited for; matrix products, arithmetic and copies ran while one was open for 5% of the time, Pallas kernels for 0%

profile of v1, /device:TPU:0, one launch (start us, length us, event | category | flops | bytes accessed | tf_op | source)
XLA Modules:
  0.0 83.1 jit_solution(6090372736300227283)
XLA Ops:
  0.0 0.7 broadcast_remainder_fusion
  0.7 0.7 compare_reduce_fusion
  1.4 0.8 fusion.71
  2.2 2.1 %fusion.6 = f32[14,192]{1,0:T(8,128)S(1)} fusion(f32[14,64,128]{2,1,0:T(8,128)} %bitcast.119, f32[64,192]{1,0:T(8,128)S(1)} %select_add_fusion.3, f32[192]{0:T(256)S(1)} %bitcast.153, s32[192]{0:T(256)S(1)} %get-tuple-element.50, f32[192]{0:T(256)S(1)} %broadcast_subtract_fusion.1, s32[192]{0:T(256)S(1)} %get-tuple-element.49), kind=kOutput, calls=%fused_computation.9 | convolution fusion | flops 264705408 | bytes 521728 | tf_op jit(solution)/shard_map/kij,sj->kis/dot_general | solution.py:116
  4.5 23.8 %all-gather = f32[16,192,14]{1,2,0:T(8,128)S(1)} all-gather(f32[1,192,14]{1,2,0:T(8,128)S(1)} %bitcast.145), channel_id=1, replica_groups=mesh['panel'=2,'lat'=4,'lon'=4] {'lat','lon'}, dimensions={0}, use_global_device_ids=true | all-gather | bytes 182784 | tf_op jit(solution)/shard_map/all_gather | solution.py:121
  28.5 1.6 %collective-permute-start = (f32[14,3072]{1,0:T(8,128)S(1)}, f32[14,3072]{1,0:T(8,128)S(1)}, u32[]{:S(2)}, u32[]{:S(2)}) collective-permute-start(f32[14,3072]{1,0:T(8,128)S(1)} %bitcast.127), channel_id=1, source_target_pairs={{0,16},{16,0},{1,17},{17,1},{2,18},{18,2},{3,19},{19,3},{4,20},{20... | collective-permute-start | bytes 516104 | tf_op jit(solution)/shard_map/ppermute | solution.py:22
  30.3 1.3 %collective-permute-start.3 = (f32[7,2,64,2]{3,2,1,0:T(8,128)S(1)}, f32[7,2,64,2]{3,2,1,0:T(8,128)S(1)}, u32[]{:S(2)}, u32[]{:S(2)}) collective-permute-start(f32[7,2,64,2]{3,2,1,0:T(8,128)S(1)} %get-tuple-element.36), channel_id=1, source_target_pairs={{1,0},{2,1},{3,2},{5,4},{6,5},{7,6},{9,8},{10,9},{11,10},{13,12},{... | collective-permute-start | bytes 21512 | tf_op jit(solution)/shard_map/ppermute | solution.py:31
  31.6 3.1 %collective-permute-start.4 = (f32[7,2,64,2]{3,2,1,0:T(8,128)S(1)}, f32[7,2,64,2]{3,2,1,0:T(8,128)S(1)}, u32[]{:S(2)}, u32[]{:S(2)}) collective-permute-start(f32[7,2,64,2]{3,2,1,0:T(8,128)S(1)} %get-tuple-element.35), channel_id=1, source_target_pairs={{0,1},{1,2},{2,3},{4,5},{5,6},{6,7},{8,9},{9,10},{10,11},{12,13},{... | collective-permute-start | bytes 21512 | tf_op jit(solution)/shard_map/ppermute | solution.py:31
  34.7 1.3 %collective-permute-start.1 = (f32[7,2,2,128]{3,2,1,0:T(2,128)S(1)}, f32[7,2,2,128]{3,2,1,0:T(2,128)S(1)}, u32[]{:S(2)}, u32[]{:S(2)}) collective-permute-start(f32[7,2,2,128]{3,2,1,0:T(2,128)S(1)} %get-tuple-element.38), channel_id=1, source_target_pairs={{4,0},{8,4},{12,8},{5,1},{9,5},{13,9},{6,2},{10,6},{14,10},{7,3},{... | collective-permute-start | bytes 43016 | tf_op jit(solution)/shard_map/ppermute | solution.py:31
  36.0 4.5 %collective-permute-start.2 = (f32[7,2,2,128]{3,2,1,0:T(2,128)S(1)}, f32[7,2,2,128]{3,2,1,0:T(2,128)S(1)}, u32[]{:S(2)}, u32[]{:S(2)}) collective-permute-start(f32[7,2,2,128]{3,2,1,0:T(2,128)S(1)} %get-tuple-element.37), channel_id=1, source_target_pairs={{0,4},{4,8},{8,12},{1,5},{5,9},{9,13},{2,6},{6,10},{10,14},{3,7},{... | collective-permute-start | bytes 43016 | tf_op jit(solution)/shard_map/ppermute | solution.py:31
  40.6 1.5 %fusion.1 = f32[14,384]{1,0:T(8,128)S(1)} fusion(f32[14,3072]{1,0:T(8,128)S(1)} %collective-permute-done, s32[384]{0:T(512)S(1)} %pad_add_fusion), kind=kOutput, calls=%fused_computation.2 | convolution fusion | flops 199360512 | bytes 195072 | tf_op jit(solution)/shard_map/dot_general | solution.py:123
  42.7 0.9 %multiply_add_fusion.2 = (f32[7,2,64,128]{3,2,1,0:T(8,128)S(1)}, f32[7,2,64,128]{3,2,1,0:T(8,128)S(1)}, f32[7,2,64,128]{3,2,1,0:T(8,128)S(1)}) fusion(f32[2,64,128]{2,1,0:T(8,128)S(1)} %get-tuple-element.30, f32[2,64,128]{2,1,0:T(8,128)S(1)} %get-tuple-element.31, f32[7,2,64,128]{3,2,1,0:T(8,128)S(1)} %bitcast.122, ...), kind=kLoop, calls=%fused_computation.74 | loop fusion | flops 2179072 | bytes 2009088 | tf_op jit(solution)/shard_map/add | solution.py:53
  43.6 0.6 fusion.17
  44.5 0.9 %fusion.66 = (f32[7,2,64,2]{3,2,1,0:T(8,128)S(1)}, f32[7,2,64,2]{3,2,1,0:T(8,128)}) fusion(f32[7,2,64,128]{3,2,1,0:T(8,128)S(1)} %get-tuple-element.28), kind=kLoop, calls=%fused_computation.175 | loop fusion | bytes 28672 | tf_op jit(solution)/shard_map/slice | solution.py:128
  45.4 1.0 %fusion.5 = f32[14,192]{1,0:T(8,128)S(1)} fusion(f32[14,64,128]{2,1,0:T(8,128)S(1)} %bitcast_add_fusion, f32[64,192]{1,0:T(8,128)S(1)} %select_add_fusion.3, f32[192]{0:T(256)S(1)} %bitcast.154, s32[192]{0:T(256)S(1)} %get-tuple-element.50, f32[192]{0:T(256)S(1)} %broadcast_subtract_fusion.1, s32[192]{0:T(256)S(1)} %get-tuple-element.49), kind=kOutput, calls=%fused_computation.8 | convolution fusion | flops 264705408 | bytes 521728 | tf_op jit(solution)/shard_map/kij,sj->kis/dot_general | solution.py:116
  46.6 19.1 %all-gather.1 = f32[16,192,14]{1,2,0:T(8,128)S(1)} all-gather(f32[1,192,14]{1,2,0:T(8,128)S(1)} %bitcast.146), channel_id=1, replica_groups=mesh['panel'=2,'lat'=4,'lon'=4] {'lat','lon'}, dimensions={0}, use_global_device_ids=true | all-gather | bytes 182784 | tf_op jit(solution)/shard_map/all_gather | solution.py:121
  66.0 0.9 %collective-permute-start.5 = (f32[14,3072]{1,0:T(8,128)S(1)}, f32[14,3072]{1,0:T(8,128)S(1)}, u32[]{:S(2)}, u32[]{:S(2)}) collective-permute-start(f32[14,3072]{1,0:T(8,128)S(1)} %bitcast.128), channel_id=1, source_target_pairs={{0,16},{16,0},{1,17},{17,1},{2,18},{18,2},{3,19},{19,3},{4,20},{20... | collective-permute-start | bytes 516104 | tf_op jit(solution)/shard_map/ppermute | solution.py:22
  66.9 1.3 %collective-permute-start.8 = (f32[7,2,64,2]{3,2,1,0:T(8,128)}, f32[7,2,64,2]{3,2,1,0:T(8,128)S(1)}, u32[]{:S(2)}, u32[]{:S(2)}) collective-permute-start(f32[7,2,64,2]{3,2,1,0:T(8,128)} %get-tuple-element.24), channel_id=1, source_target_pairs={{1,0},{2,1},{3,2},{5,4},{6,5},{7,6},{9,8},{10,9},{11,10},{13,12},{... | collective-permute-start | bytes 21512 | tf_op jit(solution)/shard_map/ppermute | solution.py:31
  68.2 3.8 %collective-permute-start.9 = (f32[7,2,64,2]{3,2,1,0:T(8,128)S(1)}, f32[7,2,64,2]{3,2,1,0:T(8,128)}, u32[]{:S(2)}, u32[]{:S(2)}) collective-permute-start(f32[7,2,64,2]{3,2,1,0:T(8,128)S(1)} %get-tuple-element.23), channel_id=1, source_target_pairs={{0,1},{1,2},{2,3},{4,5},{5,6},{6,7},{8,9},{9,10},{10,11},{12,13},{... | collective-permute-start | bytes 21512 | tf_op jit(solution)/shard_map/ppermute | solution.py:31
  72.0 1.3 %collective-permute-start.6 = (f32[7,2,2,128]{3,2,1,0:T(2,128)S(1)}, f32[7,2,2,128]{3,2,1,0:T(2,128)S(1)}, u32[]{:S(2)}, u32[]{:S(2)}) collective-permute-start(f32[7,2,2,128]{3,2,1,0:T(2,128)S(1)} %get-tuple-element.26), channel_id=1, source_target_pairs={{4,0},{8,4},{12,8},{5,1},{9,5},{13,9},{6,2},{10,6},{14,10},{7,3},{... | collective-permute-start | bytes 43016 | tf_op jit(solution)/shard_map/ppermute | solution.py:31
  73.3 5.1 %collective-permute-start.7 = (f32[7,2,2,128]{3,2,1,0:T(2,128)S(1)}, f32[7,2,2,128]{3,2,1,0:T(2,128)}, u32[]{:S(2)}, u32[]{:S(2)}) collective-permute-start(f32[7,2,2,128]{3,2,1,0:T(2,128)S(1)} %get-tuple-element.25), channel_id=1, source_target_pairs={{0,4},{4,8},{8,12},{1,5},{5,9},{9,13},{2,6},{6,10},{10,14},{3,7},{... | collective-permute-start | bytes 43016 | tf_op jit(solution)/shard_map/ppermute | solution.py:31
  78.4 1.5 %fusion = f32[14,384]{1,0:T(8,128)S(1)} fusion(f32[14,3072]{1,0:T(8,128)S(1)} %collective-permute-done.5, s32[384]{0:T(512)S(1)} %pad_add_fusion), kind=kOutput, calls=%fused_computation.1 | convolution fusion | flops 199360512 | bytes 195072 | tf_op jit(solution)/shard_map/dot_general | solution.py:123
  81.1 0.9 %multiply_add_fusion = (f32[7,2,64,128]{3,2,1,0:T(8,128)S(1)}, f32[7,2,64,128]{3,2,1,0:T(8,128)S(1)}, f32[7,2,64,128]{3,2,1,0:T(8,128)S(1)}) fusion(f32[2,64,128]{2,1,0:T(8,128)S(1)} %get-tuple-element.20, f32[2,64,128]{2,1,0:T(8,128)S(1)} %get-tuple-element.18, f32[7,2,64,128]{3,2,1,0:T(8,128)S(1)} %get-tuple-element.28, ...), kind=kLoop, calls=%fused_computation.72 | loop fusion | flops 2179072 | bytes 2009088 | tf_op jit(solution)/shard_map/add | solution.py:53
  82.2 0.9 %fusion.32 = f32[1,7,2,64,128]{4,3,2,1,0:T(8,128)} fusion(f32[1,7,2,64,128]{4,3,2,1,0:T(8,128)S(1)} %copy-done, f32[1,1,2,64,128]{4,3,2,1,0:T(8,128)S(1)} %bitcast.126, f32[1,3,2,64,128]{4,3,2,1,0:T(8,128)S(1)} %bitcast.124, f32[1,2,2,64,128]{4,3,2,1,0:T(8,128)S(1)} %get-tuple-element.40, f32[1,1,2,64,128]{4,3,2,1,0:T(8,128)S(1)} %bitcast.125, ...), kind=kLoop, calls=%fused_computation.64 | loop fusion | flops 1376256 | bytes 1835008 | tf_op jit(solution)/shard_map/add | solution.py:142
  (77 shorter events, 3.1 us)
Async XLA Ops:
  0.0 4.3 %copy-start.2 = (f32[1,1,1,192]{3,2,1,0:T(1,128)S(1)}, f32[1,1,1,192]{3,2,1,0:T(1,128)}, u32[]{:S(2)}) copy-start(f32[1,1,1,192]{3,2,1,0:T(1,128)} %param.9) | copy-start | bytes 2308
  28.2 1.9 %copy-start = (f32[1,7,2,64,128]{4,3,2,1,0:T(8,128)S(1)}, f32[1,7,2,64,128]{4,3,2,1,0:T(8,128)}, u32[]{:S(2)}) copy-start(f32[1,7,2,64,128]{4,3,2,1,0:T(8,128)} %param.5) | copy-start | bytes 1376260
  28.5 12.1 %collective-permute-start = (f32[14,3072]{1,0:T(8,128)S(1)}, f32[14,3072]{1,0:T(8,128)S(1)}, u32[]{:S(2)}, u32[]{:S(2)}) collective-permute-start(f32[14,3072]{1,0:T(8,128)S(1)} %bitcast.127), channel_id=1, source_target_pairs={{0,16},{16,0},{1,17},{17,1},{2,18},{18,2},{3,19},{19,3},{4,20},{20... | collective-permute-start | bytes 516104 | tf_op jit(solution)/shard_map/ppermute | solution.py:22
  30.3 10.3 %copy-start.1 = (s32[1,1,1,768]{3,2,1,0:T(1,128)S(1)}, s32[1,1,1,768]{3,2,1,0:T(1,128)}, u32[]{:S(2)}) copy-start(s32[1,1,1,768]{3,2,1,0:T(1,128)} %param.6) | copy-start | bytes 9220
  30.3 12.2 %collective-permute-start.3 = (f32[7,2,64,2]{3,2,1,0:T(8,128)S(1)}, f32[7,2,64,2]{3,2,1,0:T(8,128)S(1)}, u32[]{:S(2)}, u32[]{:S(2)}) collective-permute-start(f32[7,2,64,2]{3,2,1,0:T(8,128)S(1)} %get-tuple-element.36), channel_id=1, source_target_pairs={{1,0},{2,1},{3,2},{5,4},{6,5},{7,6},{9,8},{10,9},{11,10},{13,12},{... | collective-permute-start | bytes 21512 | tf_op jit(solution)/shard_map/ppermute | solution.py:31
  31.6 10.9 %collective-permute-start.4 = (f32[7,2,64,2]{3,2,1,0:T(8,128)S(1)}, f32[7,2,64,2]{3,2,1,0:T(8,128)S(1)}, u32[]{:S(2)}, u32[]{:S(2)}) collective-permute-start(f32[7,2,64,2]{3,2,1,0:T(8,128)S(1)} %get-tuple-element.35), channel_id=1, source_target_pairs={{0,1},{1,2},{2,3},{4,5},{5,6},{6,7},{8,9},{9,10},{10,11},{12,13},{... | collective-permute-start | bytes 21512 | tf_op jit(solution)/shard_map/ppermute | solution.py:31
  34.7 8.0 %collective-permute-start.1 = (f32[7,2,2,128]{3,2,1,0:T(2,128)S(1)}, f32[7,2,2,128]{3,2,1,0:T(2,128)S(1)}, u32[]{:S(2)}, u32[]{:S(2)}) collective-permute-start(f32[7,2,2,128]{3,2,1,0:T(2,128)S(1)} %get-tuple-element.38), channel_id=1, source_target_pairs={{4,0},{8,4},{12,8},{5,1},{9,5},{13,9},{6,2},{10,6},{14,10},{7,3},{... | collective-permute-start | bytes 43016 | tf_op jit(solution)/shard_map/ppermute | solution.py:31
  36.0 6.7 %collective-permute-start.2 = (f32[7,2,2,128]{3,2,1,0:T(2,128)S(1)}, f32[7,2,2,128]{3,2,1,0:T(2,128)S(1)}, u32[]{:S(2)}, u32[]{:S(2)}) collective-permute-start(f32[7,2,2,128]{3,2,1,0:T(2,128)S(1)} %get-tuple-element.37), channel_id=1, source_target_pairs={{0,4},{4,8},{8,12},{1,5},{5,9},{9,13},{2,6},{6,10},{10,14},{3,7},{... | collective-permute-start | bytes 43016 | tf_op jit(solution)/shard_map/ppermute | solution.py:31
  66.0 12.5 %collective-permute-start.5 = (f32[14,3072]{1,0:T(8,128)S(1)}, f32[14,3072]{1,0:T(8,128)S(1)}, u32[]{:S(2)}, u32[]{:S(2)}) collective-permute-start(f32[14,3072]{1,0:T(8,128)S(1)} %bitcast.128), channel_id=1, source_target_pairs={{0,16},{16,0},{1,17},{17,1},{2,18},{18,2},{3,19},{19,3},{4,20},{20... | collective-permute-start | bytes 516104 | tf_op jit(solution)/shard_map/ppermute | solution.py:22
  66.9 13.4 %collective-permute-start.8 = (f32[7,2,64,2]{3,2,1,0:T(8,128)}, f32[7,2,64,2]{3,2,1,0:T(8,128)S(1)}, u32[]{:S(2)}, u32[]{:S(2)}) collective-permute-start(f32[7,2,64,2]{3,2,1,0:T(8,128)} %get-tuple-element.24), channel_id=1, source_target_pairs={{1,0},{2,1},{3,2},{5,4},{6,5},{7,6},{9,8},{10,9},{11,10},{13,12},{... | collective-permute-start | bytes 21512 | tf_op jit(solution)/shard_map/ppermute | solution.py:31
  68.2 12.1 %collective-permute-start.9 = (f32[7,2,64,2]{3,2,1,0:T(8,128)S(1)}, f32[7,2,64,2]{3,2,1,0:T(8,128)}, u32[]{:S(2)}, u32[]{:S(2)}) collective-permute-start(f32[7,2,64,2]{3,2,1,0:T(8,128)S(1)} %get-tuple-element.23), channel_id=1, source_target_pairs={{0,1},{1,2},{2,3},{4,5},{5,6},{6,7},{8,9},{9,10},{10,11},{12,13},{... | collective-permute-start | bytes 21512 | tf_op jit(solution)/shard_map/ppermute | solution.py:31
  72.0 8.5 %collective-permute-start.6 = (f32[7,2,2,128]{3,2,1,0:T(2,128)S(1)}, f32[7,2,2,128]{3,2,1,0:T(2,128)S(1)}, u32[]{:S(2)}, u32[]{:S(2)}) collective-permute-start(f32[7,2,2,128]{3,2,1,0:T(2,128)S(1)} %get-tuple-element.26), channel_id=1, source_target_pairs={{4,0},{8,4},{12,8},{5,1},{9,5},{13,9},{6,2},{10,6},{14,10},{7,3},{... | collective-permute-start | bytes 43016 | tf_op jit(solution)/shard_map/ppermute | solution.py:31
  73.3 7.2 %collective-permute-start.7 = (f32[7,2,2,128]{3,2,1,0:T(2,128)S(1)}, f32[7,2,2,128]{3,2,1,0:T(2,128)}, u32[]{:S(2)}, u32[]{:S(2)}) collective-permute-start(f32[7,2,2,128]{3,2,1,0:T(2,128)S(1)} %get-tuple-element.25), channel_id=1, source_target_pairs={{0,4},{4,8},{8,12},{1,5},{5,9},{9,13},{2,6},{6,10},{10,14},{3,7},{... | collective-permute-start | bytes 43016 | tf_op jit(solution)/shard_map/ppermute | solution.py:31

commit v2 on v1

--- a/solution.py
+++ b/solution.py
@@ -10,25 +10,6 @@
 time_step = 0.25
 
 HIGHEST = lax.Precision.HIGHEST
-
-
-def partner_2(block, axis, apart):
-    count = lax.axis_size(axis)
-    route = []
-    for low in range(count):
-        high = low | 1 << apart
-        if high != low and high < count:
-            route += [(low, high), (high, low)]
-    return lax.ppermute(block, axis, route)
-
-
-def shift(value, axis, step):
-    size = lax.axis_size(axis)
-    if step > 0:
-        route = [(i, i + 1) for i in range(size - 1)]
-    else:
-        route = [(i + 1, i) for i in range(size - 1)]
-    return lax.ppermute(value, axis, route)
 
 
 def rate(up, mid, down, left, right):
@@ -117,17 +98,38 @@
         value = jnp.sum(along * weight_lat.T[None], axis=1)
         return rotate(value.reshape(comps, levels, -1), turn).reshape(comps * levels, -1)
 
-    def receive(given):
-        whole = lax.all_gather(given, ("lat", "lon"), axis=1, tiled=True)
-        partner = partner_2(whole, "panel", 0)
-        return jnp.dot(partner, pick, precision=HIGHEST)
+    def gather(packet, axis):
+        size = lax.axis_size(axis)
+        pos = lax.axis_index(axis)
+        held = packet[None]
+        k = 1
+        while k < size:
+            other = lax.ppermute(held, axis, [(i, i ^ k) for i in range(size)])
+            low = (pos // k) % 2 == 0
+            held = jnp.where(low, jnp.concatenate([held, other]), jnp.concatenate([other, held]))
+            k *= 2
+        return held
 
     def section(field):
-        up = shift(field[:, :, rows - 2 :, :], "lat", 1)
-        down = shift(field[:, :, :2, :], "lat", -1)
-        left = shift(field[:, :, :, cols - 2 :], "lon", 1)
-        right = shift(field[:, :, :, :2], "lon", -1)
-        rim = receive(donate(field)).reshape(comps, levels, -1)
+        flat = field.reshape(comps * levels, rows, cols)
+        given = lax.ppermute(donate(field), "panel", [(0, 1), (1, 0)])
+        dons = given.shape[1]
+        side_cols = jnp.concatenate([flat[:, :, :2], flat[:, :, cols - 2 :]], axis=2)
+        lon_packet = jnp.concatenate([given, side_cols.reshape(comps * levels, -1)], axis=1)
+        lon_all = gather(lon_packet, "lon")
+        row_given = jnp.transpose(lon_all[:, :, :dons], (1, 0, 2)).reshape(comps * levels, -1)
+        side_cols = lon_all[:, :, dons:].reshape(lon_count, comps, levels, rows, 4)
+        side_rows = jnp.concatenate([flat[:, :2, :], flat[:, rows - 2 :, :]], axis=1)
+        lat_packet = jnp.concatenate([row_given, side_rows.reshape(comps * levels, -1)], axis=1)
+        lat_all = gather(lat_packet, "lat")
+        width = row_given.shape[1]
+        partner = jnp.transpose(lat_all[:, :, :width], (1, 0, 2)).reshape(comps * levels, -1)
+        side_rows = lat_all[:, :, width:].reshape(lat_count, comps, levels, 4, cols)
+        up = lax.dynamic_index_in_dim(side_rows, jnp.maximum(lat_pos - 1, 0), keepdims=False)[:, :, 2:]
+        down = lax.dynamic_index_in_dim(side_rows, jnp.minimum(lat_pos + 1, lat_count - 1), keepdims=False)[:, :, :2]
+        left = lax.dynamic_index_in_dim(side_cols, jnp.maximum(lon_pos - 1, 0), keepdims=False)[..., 2:]
+        right = lax.dynamic_index_in_dim(side_cols, jnp.minimum(lon_pos + 1, lon_count - 1), keepdims=False)[..., :2]
+        rim = jnp.dot(partner, pick, precision=HIGHEST).reshape(comps, levels, -1)
         rim_lat = rim[:, :, :band].reshape(comps, levels, 2, cols)
         rim_lon = jnp.transpose(rim[:, :, band:].reshape(comps, levels, 2, rows), (0, 1, 3, 2))
         up = jnp.where(on_top, rim_lat, up)

time: 84.2 us -> 76.3 us (0.906)
  blocking collectives: 42.9 us -> 0 us
  waiting for transfers between devices: 0.03 us -> 19.6 us
  local copies, waits for them, and re-layouts: 3.29 us -> 21.2 us
  starting transfers between devices: 24.2 us -> 13.6 us
  other arithmetic: 6.12 us -> 13.1 us
  matrix products: 6.05 us -> 7.22 us
    all_gather x2 -> x0, blocking collectives: 42.9 us -> none  [receive(): whole = lax.all_gather(given, ('lat', 'lon'), axis=1, tiled=True)]
    ppermute x10, waiting for transfers between devices: 0.03 us -> 19.6 us  [the longest x8 16.6 us: gather(): other = lax.ppermute(held, axis, [(i, i ^ k) for i in range(size)])]
    ppermute x10, starting transfers between devices: 24.2 us -> 13.6 us  [the longest x8 10.1 us: gather(): other = lax.ppermute(held, axis, [(i, i ^ k) for i in range(size)])]
    dynamic_slice x0 -> x6, local copies, waits for them, and re-layouts: none -> 4.53 us  [the longest x4 4.12 us: section(): lax.dynamic_index_in_dim(side_cols, jnp.maximum(lon_pos - 1, 0), keepdims...]
    reshape x2 -> x8, local copies, waits for them, and re-layouts: 0.05 us -> 4.26 us  [the longest x2 3.83 us: section(): side_cols = lon_all[:, :, dons:].reshape(lon_count, comps, levels, rows, 4)]
    select_n x0 -> x8, other arithmetic: none -> 3.28 us  [gather(): jnp.where(low, jnp.concatenate([held, other]), jnp.concatenate([other, he...]
    slice x4 -> x12, local copies, waits for them, and re-layouts: 1.1 us -> 4.15 us  [the longest x6 3.94 us: section(): side_rows = jnp.concatenate([flat[:, :2, :], flat[:, rows - 2:, :]], axis=1)]
    unnamed x12 -> x43, local copies, waits for them, and re-layouts: 0.29 us -> 2.73 us
  transfers between devices with their start and end apart: 10 -> 10, of which waited for: 0 -> 8; matrix products, arithmetic and copies ran while one was open for 5% -> 22% of each run, Pallas kernels for 0% -> 0%
where the time goes in v2:
time: 76.3 us; the launch traced here: 75.8 us
  local copies, waits for them, and re-layouts  21.2 us (28%)
  waiting for transfers between devices  19.6 us (26%)
  starting transfers between devices  13.6 us (18%)
  other arithmetic  13.1 us (17%)
  matrix products  7.22 us (9%)
  between operations  0.98 us (1%)
    ppermute x8, waiting for transfers between devices, gather(): other = lax.ppermute(held, axis, [(i, i ^ k) for i in range(size)])  16.6 us
    ppermute x8, starting transfers between devices, gather(): other = lax.ppermute(held, axis, [(i, i ^ k) for i in range(size)])  10.1 us
    dynamic_slice x4, local copies, waits for them, and re-layouts, section(): lax.dynamic_index_in_dim(side_cols, jnp.maximum(lon_pos - 1, 0), keepdims...  4.12 us
    slice x6, local copies, waits for them, and re-layouts, section(): side_rows = jnp.concatenate([flat[:, :2, :], flat[:, rows - 2:, :]], axis=1)  3.94 us
    reshape x2, local copies, waits for them, and re-layouts, section(): side_cols = lon_all[:, :, dons:].reshape(lon_count, comps, levels, rows, 4)  3.83 us
    dot_general x2, matrix products, donate(): along = jnp.einsum('kij,sj->kis', flat, weight_lon, precision=HIGHEST)  3.78 us
    ppermute x2, starting transfers between devices, section(): given = lax.ppermute(donate(field), 'panel', [(0, 1), (1, 0)])  3.55 us
    dot_general x2, matrix products, section(): rim = jnp.dot(partner, pick, precision=HIGHEST).reshape(comps, levels, -1)  3.44 us
  transfers between devices with their start and end apart: 10, of which 8 were waited for; matrix products, arithmetic and copies ran while one was open for 22% of the time, Pallas kernels for 0%

profile of v2, /device:TPU:0, one launch (start us, length us, event | category | flops | bytes accessed | tf_op | source)
XLA Modules:
  0.0 75.8 jit_solution(15081215024517773370)
XLA Ops:
  3.6 2.1 %fusion.8 = f32[14,192]{1,0:T(8,128)S(1)} fusion(f32[14,64,128]{2,1,0:T(8,128)} %bitcast.162, f32[64,192]{1,0:T(8,128)S(1)} %select_add_fusion.3, f32[192]{0:T(256)S(1)} %bitcast.199, s32[192]{0:T(256)S(1)} %get-tuple-element.58, f32[192]{0:T(256)S(1)} %broadcast_subtract_fusion.1, s32[192]{0:T(256)S(1)} %get-tuple-element.57), kind=kOutput, calls=%fused_computation.9 | convolution fusion | flops 264705408 | bytes 521728 | tf_op jit(solution)/shard_map/kij,sj->kis/dot_general | solution.py:97
  5.8 3.0 %collective-permute-start = (f32[14,192]{1,0:T(8,128)S(1)}, f32[14,192]{1,0:T(8,128)S(1)}, u32[]{:S(2)}, u32[]{:S(2)}) collective-permute-start(f32[14,192]{1,0:T(8,128)S(1)} %reshape.388), channel_id=1, source_target_pairs={{0,16},{16,0},{1,17},{17,1},{2,18},{18,2},{3,19},{19,3},{4,20},{20... | collective-permute-start | bytes 32264 | tf_op jit(solution)/shard_map/ppermute | solution.py:115
  8.8 1.6 %multiply_bitcast_fusion.3 = (f32[2,64,128]{2,1,0:T(8,128)S(1)}, f32[2,64,128]{2,1,0:T(8,128)}, f32[2,64,128]{2,1,0:T(8,128)}, f32[2,64,128]{2,1,0:T(8,128)S(1)}) fusion(f32[1,7,2,64,128]{4,3,2,1,0:T(8,128)} %param.5), kind=kLoop, calls=%fused_computation.128 | loop fusion | flops 65536 | bytes 524288 | tf_op jit(solution)/shard_map/mul | solution.py:33
  10.4 1.3 %copy.114 = f32[1,7,2,64,128]{3,4,2,1,0:T(8,128)S(1)} copy(f32[1,7,2,64,128]{4,3,2,1,0:T(8,128)} %param.5) | data formatting | bytes 917504 | tf_op args[0]
  13.8 1.6 %collective-permute-start.2 = (f32[2,14,448]{2,0,1:T(2,128)S(1)}, f32[2,14,448]{2,0,1:T(2,128)S(1)}, u32[]{:S(2)}, u32[]{:S(2)}) collective-permute-start(f32[2,14,448]{2,0,1:T(2,128)S(1)} %maximum_select_fusion.6), channel_id=1, source_target_pairs={{0,2},{1,3},{2,0},{3,1},{4,6},{5,7},{6,4},{7,5},{8,10},{9,11},{10,... | collective-permute-start | bytes 150536 | tf_op jit(solution)/shard_map/ppermute | solution.py:107
  15.4 2.6 %collective-permute-done.2 = f32[2,14,448]{2,0,1:T(2,128)S(1)} collective-permute-done((f32[2,14,448]{2,0,1:T(2,128)S(1)}, f32[2,14,448]{2,0,1:T(2,128)S(1)}, u32[]{:S(2)}, u32[]{:S(2)}) %collective-permute-start.2) | collective-permute-done | bytes 50208 | tf_op jit(solution)/shard_map/ppermute | solution.py:107
  18.3 1.6 %collective-permute-start.3 = (f32[1,14,1280]{2,1,0:T(8,128)S(1)}, f32[1,14,1280]{2,1,0:T(8,128)S(1)}, u32[]{:S(2)}, u32[]{:S(2)}) collective-permute-start(f32[1,14,1280]{2,1,0:T(8,128)S(1)} %maximum_bitcast_fusion), channel_id=1, source_target_pairs={{0,4},{4,0},{8,12},{12,8},{1,5},{5,1},{9,13},{13,9},{2,6},{6,2},{1... | collective-permute-start | bytes 215048 | tf_op jit(solution)/shard_map/ppermute | solution.py:107
  19.9 2.9 %collective-permute-done.3 = f32[1,14,1280]{2,1,0:T(8,128)S(1)} collective-permute-done((f32[1,14,1280]{2,1,0:T(8,128)S(1)}, f32[1,14,1280]{2,1,0:T(8,128)S(1)}, u32[]{:S(2)}, u32[]{:S(2)}) %collective-permute-start.3) | collective-permute-done | bytes 71712 | tf_op jit(solution)/shard_map/ppermute | solution.py:107
  22.8 2.6 %collective-permute-start.4 = (f32[2,14,1280]{2,1,0:T(8,128)S(1)}, f32[2,14,1280]{2,1,0:T(8,128)}, u32[]{:S(2)}, u32[]{:S(2)}) collective-permute-start(f32[2,14,1280]{2,1,0:T(8,128)S(1)} %maximum_select_fusion.2), channel_id=1, source_target_pairs={{0,8},{4,12},{8,0},{12,4},{1,9},{5,13},{9,1},{13,5},{2,10},{6,14},... | collective-permute-start | bytes 430088 | tf_op jit(solution)/shard_map/ppermute | solution.py:107
  25.6 1.9 %reshape.395 = f32[4,7,2,64,4]{4,3,0,2,1:T(8,128)S(1)} reshape(f32[4,14,256]{2,0,1:T(4,128)S(1)} %slice.487) | data formatting | bytes 114688 | tf_op jit(solution)/shard_map/reshape | solution.py:121
  29.8 1.6 %collective-permute-done.4 = f32[2,14,1280]{2,1,0:T(8,128)} collective-permute-done((f32[2,14,1280]{2,1,0:T(8,128)S(1)}, f32[2,14,1280]{2,1,0:T(8,128)}, u32[]{:S(2)}, u32[]{:S(2)}) %collective-permute-start.4) | collective-permute-done | bytes 143392 | tf_op jit(solution)/shard_map/ppermute | solution.py:107
  32.7 1.7 %fusion.3 = f32[7,2,384]{2,0,1:T(8,128)S(1)} fusion(s32[384]{0:T(512)S(1)} %pad_add_fusion, f32[7,2,3072]{2,1,0:T(2,128)S(1)} %dot_general.20), kind=kOutput, calls=%fused_computation.3 | convolution fusion | flops 199360512 | bytes 195072 | tf_op jit(solution)/shard_map/dot_general | solution.py:132
  37.6 1.2 %copy.133 = f32[7,2,64,128]{2,3,1,0:T(8,128)} copy(f32[7,2,64,128]{3,2,1,0:T(8,128)S(1)} %get-tuple-element.33) | data formatting | bytes 917504 | tf_op jit(solution)/shard_map/mul | solution.py:142
  38.9 1.3 %bitcast_add_fusion = f32[14,64,128]{1,2,0:T(8,128)S(1)} fusion(f32[7,2,64,128]{2,3,1,0:T(8,128)} %copy.133, f32[1,7,2,64,128]{3,4,2,1,0:T(8,128)S(1)} %copy.114), kind=kLoop, calls=%fused_computation.23 | loop fusion | flops 114688 | bytes 1376256 | tf_op jit(solution)/shard_map/add | solution.py:142
  40.2 1.7 %fusion.9 = f32[14,192]{1,0:T(8,128)S(1)} fusion(f32[14,64,128]{1,2,0:T(8,128)S(1)} %bitcast_add_fusion, f32[64,192]{1,0:T(8,128)S(1)} %copy-done.9, f32[192]{0:T(256)S(1)} %bitcast.200, s32[192]{0:T(256)S(1)} %copy-done.13, f32[192]{0:T(256)S(1)} %broadcast_subtract_fusion.1, s32[192]{0:T(256)S(1)} %copy-done.11), kind=kOutput, calls=%fused_computation.10 | convolution fusion | flops 264705408 | bytes 521728 | tf_op jit(solution)/shard_map/kij,sj->kis/dot_general | solution.py:97
  42.8 3.1 %collective-permute-done.5 = f32[14,192]{1,0:T(8,128)S(1)} collective-permute-done((f32[14,192]{1,0:T(8,128)S(1)}, f32[14,192]{1,0:T(8,128)S(1)}, u32[]{:S(2)}, u32[]{:S(2)}) %collective-permute-start.5) | collective-permute-done | bytes 10784 | tf_op jit(solution)/shard_map/ppermute | solution.py:115
  47.2 1.5 %copy.141 = f32[14,2,128]{2,1,0:T(2,128)S(1)} copy(f32[14,2,128]{1,2,0:T(8,128)} %get-tuple-element.23) | data formatting | bytes 28672 | tf_op jit(solution)/shard_map/slice | solution.py:122
  49.1 1.6 %collective-permute-start.7 = (f32[2,14,448]{2,0,1:T(2,128)S(1)}, f32[2,14,448]{2,0,1:T(2,128)S(1)}, u32[]{:S(2)}, u32[]{:S(2)}) collective-permute-start(f32[2,14,448]{2,0,1:T(2,128)S(1)} %maximum_select_fusion.7), channel_id=1, source_target_pairs={{0,2},{1,3},{2,0},{3,1},{4,6},{5,7},{6,4},{7,5},{8,10},{9,11},{10,... | collective-permute-start | bytes 150536 | tf_op jit(solution)/shard_map/ppermute | solution.py:107
  50.8 2.8 %collective-permute-done.7 = f32[2,14,448]{2,0,1:T(2,128)S(1)} collective-permute-done((f32[2,14,448]{2,0,1:T(2,128)S(1)}, f32[2,14,448]{2,0,1:T(2,128)S(1)}, u32[]{:S(2)}, u32[]{:S(2)}) %collective-permute-start.7) | collective-permute-done | bytes 50208 | tf_op jit(solution)/shard_map/ppermute | solution.py:107
  54.6 3.9 %collective-permute-done.8 = f32[1,14,1280]{2,1,0:T(8,128)S(1)} collective-permute-done((f32[1,14,1280]{2,1,0:T(8,128)S(1)}, f32[1,14,1280]{2,1,0:T(8,128)S(1)}, u32[]{:S(2)}, u32[]{:S(2)}) %collective-permute-start.8) | collective-permute-done | bytes 71712 | tf_op jit(solution)/shard_map/ppermute | solution.py:107
  59.1 2.0 %collective-permute-start.9 = (f32[2,14,1280]{2,1,0:T(8,128)}, f32[2,14,1280]{2,1,0:T(8,128)}, u32[]{:S(2)}, u32[]{:S(2)}) collective-permute-start(f32[2,14,1280]{2,1,0:T(8,128)} %maximum_select_fusion.3), channel_id=1, source_target_pairs={{0,8},{4,12},{8,0},{12,4},{1,9},{5,13},{9,1},{13,5},{2,10},{6,14},... | collective-permute-start | bytes 430088 | tf_op jit(solution)/shard_map/ppermute | solution.py:107
  61.9 1.9 %reshape.403 = f32[4,7,2,64,4]{4,3,0,2,1:T(8,128)S(1)} reshape(f32[4,14,256]{2,0,1:T(4,128)S(1)} %slice.527) | data formatting | bytes 114688 | tf_op jit(solution)/shard_map/reshape | solution.py:121
  66.1 2.4 %collective-permute-done.9 = f32[2,14,1280]{2,1,0:T(8,128)} collective-permute-done((f32[2,14,1280]{2,1,0:T(8,128)}, f32[2,14,1280]{2,1,0:T(8,128)}, u32[]{:S(2)}, u32[]{:S(2)}) %collective-permute-start.9) | collective-permute-done | bytes 143392 | tf_op jit(solution)/shard_map/ppermute | solution.py:107
  70.0 1.7 %fusion.1 = f32[7,2,384]{2,0,1:T(8,128)S(1)} fusion(s32[384]{0:T(512)S(1)} %copy-done.16, f32[7,2,3072]{2,1,0:T(2,128)S(1)} %dot_general.23), kind=kOutput, calls=%fused_computation.2 | convolution fusion | flops 199360512 | bytes 195072 | tf_op jit(solution)/shard_map/dot_general | solution.py:132
  (161 shorter events, 25.3 us)
Async XLA Ops:
  2.9 2.8 %copy-start.10 = (s32[192]{0:T(256)}, s32[192]{0:T(256)S(1)}, u32[]{:S(2)}) copy-start(s32[192]{0:T(256)S(1)} %get-tuple-element.57) | copy-start | bytes 2308
  2.9 2.8 %copy-start.12 = (s32[192]{0:T(256)}, s32[192]{0:T(256)S(1)}, u32[]{:S(2)}) copy-start(s32[192]{0:T(256)S(1)} %get-tuple-element.58) | copy-start | bytes 2308
  5.8 6.6 %collective-permute-start = (f32[14,192]{1,0:T(8,128)S(1)}, f32[14,192]{1,0:T(8,128)S(1)}, u32[]{:S(2)}, u32[]{:S(2)}) collective-permute-start(f32[14,192]{1,0:T(8,128)S(1)} %reshape.388), channel_id=1, source_target_pairs={{0,16},{16,0},{1,17},{17,1},{2,18},{18,2},{3,19},{19,3},{4,20},{20... | collective-permute-start | bytes 32264 | tf_op jit(solution)/shard_map/ppermute | solution.py:115
  12.4 1.2 %collective-permute-start.1 = (f32[1,14,448]{2,1,0:T(8,128)S(1)}, f32[1,14,448]{2,1,0:T(8,128)S(1)}, u32[]{:S(2)}, u32[]{:S(2)}) collective-permute-start(f32[1,14,448]{2,1,0:T(8,128)S(1)} %maximum_bitcast_fusion.2), channel_id=1, source_target_pairs={{0,1},{1,0},{2,3},{3,2},{4,5},{5,4},{6,7},{7,6},{8,9},{9,8},{10,11... | collective-permute-start | bytes 75272 | tf_op jit(solution)/shard_map/ppermute | solution.py:107
  13.8 4.2 %collective-permute-start.2 = (f32[2,14,448]{2,0,1:T(2,128)S(1)}, f32[2,14,448]{2,0,1:T(2,128)S(1)}, u32[]{:S(2)}, u32[]{:S(2)}) collective-permute-start(f32[2,14,448]{2,0,1:T(2,128)S(1)} %maximum_select_fusion.6), channel_id=1, source_target_pairs={{0,2},{1,3},{2,0},{3,1},{4,6},{5,7},{6,4},{7,5},{8,10},{9,11},{10,... | collective-permute-start | bytes 150536 | tf_op jit(solution)/shard_map/ppermute | solution.py:107
  18.3 4.5 %collective-permute-start.3 = (f32[1,14,1280]{2,1,0:T(8,128)S(1)}, f32[1,14,1280]{2,1,0:T(8,128)S(1)}, u32[]{:S(2)}, u32[]{:S(2)}) collective-permute-start(f32[1,14,1280]{2,1,0:T(8,128)S(1)} %maximum_bitcast_fusion), channel_id=1, source_target_pairs={{0,4},{4,0},{8,12},{12,8},{1,5},{5,1},{9,13},{13,9},{2,6},{6,2},{1... | collective-permute-start | bytes 215048 | tf_op jit(solution)/shard_map/ppermute | solution.py:107
  22.8 8.5 %collective-permute-start.4 = (f32[2,14,1280]{2,1,0:T(8,128)S(1)}, f32[2,14,1280]{2,1,0:T(8,128)}, u32[]{:S(2)}, u32[]{:S(2)}) collective-permute-start(f32[2,14,1280]{2,1,0:T(8,128)S(1)} %maximum_select_fusion.2), channel_id=1, source_target_pairs={{0,8},{4,12},{8,0},{12,4},{1,9},{5,13},{9,1},{13,5},{2,10},{6,14},... | collective-permute-start | bytes 430088 | tf_op jit(solution)/shard_map/ppermute | solution.py:107
  25.4 7.3 %copy-start.15 = (s32[384]{0:T(512)}, s32[384]{0:T(512)S(1)}, u32[]{:S(2)}) copy-start(s32[384]{0:T(512)S(1)} %pad_add_fusion) | copy-start | bytes 4612
  32.4 2.8 %copy-start = (f32[1,7,2,64,128]{4,3,2,1,0:T(8,128)S(1)}, f32[1,7,2,64,128]{4,3,2,1,0:T(8,128)}, u32[]{:S(2)}) copy-start(f32[1,7,2,64,128]{4,3,2,1,0:T(8,128)} %param.5) | copy-start | bytes 1376260
  32.4 2.8 %copy-start.2 = (f32[2,64,128]{2,1,0:T(8,128)S(1)}, f32[2,64,128]{2,1,0:T(8,128)}, u32[]{:S(2)}) copy-start(f32[2,64,128]{2,1,0:T(8,128)} %get-tuple-element.36) | copy-start | bytes 196612
  32.4 2.8 %copy-start.3 = (f32[2,64,128]{2,1,0:T(8,128)S(1)}, f32[2,64,128]{2,1,0:T(8,128)}, u32[]{:S(2)}) copy-start(f32[2,64,128]{2,1,0:T(8,128)} %get-tuple-element.37) | copy-start | bytes 196612
  37.6 2.6 %copy-start.9 = (f32[64,192]{1,0:T(8,128)S(1)}, f32[64,192]{1,0:T(8,128)}, u32[]{:S(2)}) copy-start(f32[64,192]{1,0:T(8,128)} %copy-done.8) | copy-start | bytes 147460
  37.6 2.6 %copy-start.11 = (s32[192]{0:T(256)S(1)}, s32[192]{0:T(256)}, u32[]{:S(2)}) copy-start(s32[192]{0:T(256)} %copy-done.10) | copy-start | bytes 2308
  37.6 2.6 %copy-start.13 = (s32[192]{0:T(256)S(1)}, s32[192]{0:T(256)}, u32[]{:S(2)}) copy-start(s32[192]{0:T(256)} %copy-done.12) | copy-start | bytes 2308
  42.0 3.8 %collective-permute-start.5 = (f32[14,192]{1,0:T(8,128)S(1)}, f32[14,192]{1,0:T(8,128)S(1)}, u32[]{:S(2)}, u32[]{:S(2)}) collective-permute-start(f32[14,192]{1,0:T(8,128)S(1)} %reshape.396), channel_id=1, source_target_pairs={{0,16},{16,0},{1,17},{17,1},{2,18},{18,2},{3,19},{19,3},{4,20},{20... | collective-permute-start | bytes 32264 | tf_op jit(solution)/shard_map/ppermute | solution.py:115
  45.9 3.1 %collective-permute-start.6 = (f32[1,14,448]{2,1,0:T(8,128)S(1)}, f32[1,14,448]{2,1,0:T(8,128)S(1)}, u32[]{:S(2)}, u32[]{:S(2)}) collective-permute-start(f32[1,14,448]{2,1,0:T(8,128)S(1)} %maximum_bitcast_fusion.3), channel_id=1, source_target_pairs={{0,1},{1,0},{2,3},{3,2},{4,5},{5,4},{6,7},{7,6},{8,9},{9,8},{10,11... | collective-permute-start | bytes 75272 | tf_op jit(solution)/shard_map/ppermute | solution.py:107
  49.1 4.4 %collective-permute-start.7 = (f32[2,14,448]{2,0,1:T(2,128)S(1)}, f32[2,14,448]{2,0,1:T(2,128)S(1)}, u32[]{:S(2)}, u32[]{:S(2)}) collective-permute-start(f32[2,14,448]{2,0,1:T(2,128)S(1)} %maximum_select_fusion.7), channel_id=1, source_target_pairs={{0,2},{1,3},{2,0},{3,1},{4,6},{5,7},{6,4},{7,5},{8,10},{9,11},{10,... | collective-permute-start | bytes 150536 | tf_op jit(solution)/shard_map/ppermute | solution.py:107
  53.9 4.5 %collective-permute-start.8 = (f32[1,14,1280]{2,1,0:T(8,128)S(1)}, f32[1,14,1280]{2,1,0:T(8,128)S(1)}, u32[]{:S(2)}, u32[]{:S(2)}) collective-permute-start(f32[1,14,1280]{2,1,0:T(8,128)S(1)} %maximum_bitcast_fusion.1), channel_id=1, source_target_pairs={{0,4},{4,0},{8,12},{12,8},{1,5},{5,1},{9,13},{13,9},{2,6},{6,2},{1... | collective-permute-start | bytes 215048 | tf_op jit(solution)/shard_map/ppermute | solution.py:107
  59.1 9.4 %collective-permute-start.9 = (f32[2,14,1280]{2,1,0:T(8,128)}, f32[2,14,1280]{2,1,0:T(8,128)}, u32[]{:S(2)}, u32[]{:S(2)}) collective-permute-start(f32[2,14,1280]{2,1,0:T(8,128)} %maximum_select_fusion.3), channel_id=1, source_target_pairs={{0,8},{4,12},{8,0},{12,4},{1,9},{5,13},{9,1},{13,5},{2,10},{6,14},... | collective-permute-start | bytes 430088 | tf_op jit(solution)/shard_map/ppermute | solution.py:107
  64.7 5.3 %copy-start.16 = (s32[384]{0:T(512)S(1)}, s32[384]{0:T(512)}, u32[]{:S(2)}) copy-start(s32[384]{0:T(512)} %copy-done.15) | copy-start | bytes 4612
  71.7 1.3 %copy-start.6 = (f32[2,64,128]{2,1,0:T(8,128)S(1)}, f32[2,64,128]{2,1,0:T(8,128)}, u32[]{:S(2)}) copy-start(f32[2,64,128]{2,1,0:T(8,128)} %get-tuple-element.30) | copy-start | bytes 196612
  71.8 1.3 %copy-start.7 = (f32[2,64,128]{2,1,0:T(8,128)S(1)}, f32[2,64,128]{2,1,0:T(8,128)}, u32[]{:S(2)}) copy-start(f32[2,64,128]{2,1,0:T(8,128)} %get-tuple-element.32) | copy-start | bytes 196612
  73.0 0.9 %copy-start.4 = (f32[2,64,128]{2,1,0:T(8,128)S(1)}, f32[2,64,128]{2,1,0:T(8,128)}, u32[]{:S(2)}) copy-start(f32[2,64,128]{2,1,0:T(8,128)} %get-tuple-element.29) | copy-start | bytes 196612
  73.0 0.9 %copy-start.5 = (f32[2,64,128]{2,1,0:T(8,128)S(1)}, f32[2,64,128]{2,1,0:T(8,128)}, u32[]{:S(2)}) copy-start(f32[2,64,128]{2,1,0:T(8,128)} %get-tuple-element.31) | copy-start | bytes 196612
  (3 other events, 2.2 us)

commit v3 on v2

--- a/solution.py
+++ b/solution.py
@@ -89,8 +89,23 @@
     lat_slots = jnp.where(on_top, slots[0:band], slots[band : 2 * band])
     lon_slots = jnp.where(on_left, slots[2 * band : 2 * band + side], slots[2 * band + side :])
     wanted = jnp.concatenate([lat_slots, lon_slots])
-    total = lax.axis_size("lat") * lax.axis_size("lon") * cells.shape[0]
-    pick = (jnp.arange(total, dtype=jnp.int32)[:, None] == wanted[None, :]).astype(jnp.float32)
+    dons = cells.shape[0]
+    lane = 256
+    donor = wanted // dons
+    held_lat = donor // lon_count ^ lat_pos
+    held_lon = donor % lon_count ^ lon_pos
+    place = (held_lat * lon_count + held_lon) * lane + wanted % dons
+    total = lat_count * lon_count * lane
+    pick = (jnp.arange(total, dtype=jnp.int32)[:, None] == place[None, :]).astype(jnp.bfloat16)
+
+    def select(values):
+        high = lax.reduce_precision(values, exponent_bits=8, mantissa_bits=7)
+        rest = values - high
+        middle = lax.reduce_precision(rest, exponent_bits=8, mantissa_bits=7)
+        low = rest - middle
+        parts = [part.astype(jnp.bfloat16) for part in (high, middle, low)]
+        out = [jnp.dot(part, pick, preferred_element_type=jnp.float32) for part in parts]
+        return out[0] + (out[1] + out[2])
 
     def donate(field):
         flat = field.reshape(comps * levels, rows, cols)
@@ -100,36 +115,35 @@
 
     def gather(packet, axis):
         size = lax.axis_size(axis)
-        pos = lax.axis_index(axis)
-        held = packet[None]
+        held = packet
         k = 1
         while k < size:
             other = lax.ppermute(held, axis, [(i, i ^ k) for i in range(size)])
-            low = (pos // k) % 2 == 0
-            held = jnp.where(low, jnp.concatenate([held, other]), jnp.concatenate([other, held]))
+            held = jnp.concatenate([held, other])
             k *= 2
         return held
 
     def section(field):
         flat = field.reshape(comps * levels, rows, cols)
         given = lax.ppermute(donate(field), "panel", [(0, 1), (1, 0)])
-        dons = given.shape[1]
+        given = jnp.pad(given, ((0, 0), (0, lane - dons)))
         side_cols = jnp.concatenate([flat[:, :, :2], flat[:, :, cols - 2 :]], axis=2)
-        lon_packet = jnp.concatenate([given, side_cols.reshape(comps * levels, -1)], axis=1)
-        lon_all = gather(lon_packet, "lon")
-        row_given = jnp.transpose(lon_all[:, :, :dons], (1, 0, 2)).reshape(comps * levels, -1)
-        side_cols = lon_all[:, :, dons:].reshape(lon_count, comps, levels, rows, 4)
+        side_cols = jnp.transpose(side_cols, (0, 2, 1)).reshape(comps * levels, -1)
+        lon_all = gather(jnp.stack([given, side_cols]), "lon").reshape(lon_count, 2, comps * levels, lane)
         side_rows = jnp.concatenate([flat[:, :2, :], flat[:, rows - 2 :, :]], axis=1)
-        lat_packet = jnp.concatenate([row_given, side_rows.reshape(comps * levels, -1)], axis=1)
-        lat_all = gather(lat_packet, "lat")
-        width = row_given.shape[1]
-        partner = jnp.transpose(lat_all[:, :, :width], (1, 0, 2)).reshape(comps * levels, -1)
-        side_rows = lat_all[:, :, width:].reshape(lat_count, comps, levels, 4, cols)
-        up = lax.dynamic_index_in_dim(side_rows, jnp.maximum(lat_pos - 1, 0), keepdims=False)[:, :, 2:]
-        down = lax.dynamic_index_in_dim(side_rows, jnp.minimum(lat_pos + 1, lat_count - 1), keepdims=False)[:, :, :2]
-        left = lax.dynamic_index_in_dim(side_cols, jnp.maximum(lon_pos - 1, 0), keepdims=False)[..., 2:]
-        right = lax.dynamic_index_in_dim(side_cols, jnp.minimum(lon_pos + 1, lon_count - 1), keepdims=False)[..., :2]
-        rim = jnp.dot(partner, pick, precision=HIGHEST).reshape(comps, levels, -1)
+        side_rows = side_rows.reshape(comps * levels, 2, lane).transpose(1, 0, 2)
+        lat_packet = jnp.concatenate([lon_all[:, 0], side_rows])
+        lat_all = gather(lat_packet, "lat").reshape(lat_count, lon_count + 2, comps * levels, lane)
+        partner = jnp.transpose(lat_all[:, :lon_count], (2, 0, 1, 3)).reshape(comps * levels, -1)
+        side_rows = lat_all[:, lon_count:].transpose(0, 2, 1, 3).reshape(lat_count, comps, levels, 4, cols)
+        side_cols = lon_all[:, 1].reshape(lon_count, comps, levels, 4, rows)
+        up = lax.dynamic_index_in_dim(side_rows, lat_pos ^ jnp.maximum(lat_pos - 1, 0), keepdims=False)[:, :, 2:]
+        down = lax.dynamic_index_in_dim(side_rows, lat_pos ^ jnp.minimum(lat_pos + 1, lat_count - 1), keepdims=False)[:, :, :2]
+        left = lax.dynamic_index_in_dim(side_cols, lon_pos ^ jnp.maximum(lon_pos - 1, 0), keepdims=False)[:, :, 2:]
+        right = lax.dynamic_index_in_dim(side_cols, lon_pos ^ jnp.minimum(lon_pos + 1, lon_count - 1), keepdims=False)[:, :, :2]
+        left = jnp.transpose(left, (0, 1, 3, 2))
+        right = jnp.transpose(right, (0, 1, 3, 2))
+        rim = select(partner).reshape(comps, levels, -1)
         rim_lat = rim[:, :, :band].reshape(comps, levels, 2, cols)
         rim_lon = jnp.transpose(rim[:, :, band:].reshape(comps, levels, 2, rows), (0, 1, 3, 2))
         up = jnp.where(on_top, rim_lat, up)

time: 76.3 us -> 80.7 us (1.058)
  waiting for transfers between devices: 19.6 us -> 30.5 us
  local copies, waits for them, and re-layouts: 21.2 us -> 12.7 us
  other arithmetic: 13.1 us -> 9.49 us
  matrix products: 7.22 us -> 10.8 us
  starting transfers between devices: 13.6 us -> 16.1 us
    ppermute x8, waiting for transfers between devices: 16.6 us -> 27.2 us  [gather(): other = lax.ppermute(held, axis, [(i, i ^ k) for i in range(size)])]
    dynamic_slice x6 -> x0, local copies, waits for them, and re-layouts: 4.53 us -> none  [the longest x4 4.12 us: section(): lax.dynamic_index_in_dim(side_cols, jnp.maximum(lon_pos - 1, 0), keepdims...]
    reshape x8, local copies, waits for them, and re-layouts: 4.26 us -> 0.56 us  [the longest x2 0.24 us: section(): jnp.transpose(lat_all[:, :lon_count], (2, 0, 1, 3))]
    dot_general x2 -> x6, matrix products: 3.44 us -> 7.05 us  [select(): jnp.dot(part, pick, preferred_element_type=jnp.float32)]
    select_n x8 -> x0, other arithmetic: 3.28 us -> none  [gather(): jnp.where(low, jnp.concatenate([held, other]), jnp.concatenate([other, he...]
    mul x2, other arithmetic: 2.34 us -> 0.05 us  [rate(): adv_u = middle[1:2] * d_lat + middle[2:3] * d_lon]
    unnamed x43 -> x27, local copies, waits for them, and re-layouts: 2.73 us -> 1.07 us
    ppermute x8, starting transfers between devices: 10.1 us -> 11.5 us  [gather(): other = lax.ppermute(held, axis, [(i, i ^ k) for i in range(size)])]
  transfers between devices with their start and end apart: 10 -> 10, of which waited for: 8 -> 8; matrix products, arithmetic and copies ran while one was open for 22% -> 9% of each run, Pallas kernels for 0% -> 0%
where the time goes in v3:
time: 80.7 us; the launch traced here: 80.3 us
  waiting for transfers between devices  30.5 us (38%)
  starting transfers between devices  16.1 us (20%)
  local copies, waits for them, and re-layouts  12.7 us (16%)
  matrix products  10.8 us (13%)
  other arithmetic  9.49 us (12%)
    ppermute x8, waiting for transfers between devices, gather(): other = lax.ppermute(held, axis, [(i, i ^ k) for i in range(size)])  27.2 us
    ppermute x8, starting transfers between devices, gather(): other = lax.ppermute(held, axis, [(i, i ^ k) for i in range(size)])  11.5 us
    dot_general x6, matrix products, select(): jnp.dot(part, pick, preferred_element_type=jnp.float32)  7.05 us
    ppermute x2, starting transfers between devices, section(): given = lax.ppermute(donate(field), 'panel', [(0, 1), (1, 0)])  4.6 us
    slice x6, local copies, waits for them, and re-layouts, section(): side_rows = jnp.concatenate([flat[:, :2, :], flat[:, rows - 2:, :]], axis=1)  4.51 us
    dot_general x2, matrix products, donate(): along = jnp.einsum('kij,sj->kis', flat, weight_lon, precision=HIGHEST)  3.78 us
    ppermute x2, waiting for transfers between devices, section(): given = lax.ppermute(donate(field), 'panel', [(0, 1), (1, 0)])  3.29 us
    add x2, other arithmetic, rate(): adv_b = middle[4:5] * d_lat + middle[5:6] * d_lon  1.8 us
  transfers between devices with their start and end apart: 10, of which 8 were waited for; matrix products, arithmetic and copies ran while one was open for 9% of the time, Pallas kernels for 0%

profile of v3, /device:TPU:0, one launch (start us, length us, event | category | flops | bytes accessed | tf_op | source)
XLA Modules:
  0.0 80.3 jit_solution(7630939729589440637)
XLA Ops:
  3.6 2.1 %fusion.13 = f32[14,192]{1,0:T(8,128)S(1)} fusion(f32[14,64,128]{2,1,0:T(8,128)} %bitcast.158, f32[64,192]{1,0:T(8,128)S(1)} %select_add_fusion.3, f32[192]{0:T(256)S(1)} %bitcast.193, s32[192]{0:T(256)S(1)} %get-tuple-element.62, f32[192]{0:T(256)S(1)} %broadcast_subtract_fusion.1, s32[192]{0:T(256)S(1)} %get-tuple-element.61), kind=kOutput, calls=%fused_computation.16 | convolution fusion | flops 264705408 | bytes 521728 | tf_op jit(solution)/shard_map/kij,sj->kis/dot_general | solution.py:112
  6.4 3.0 %collective-permute-start = (f32[14,192]{1,0:T(8,128)}, f32[14,192]{1,0:T(8,128)}, u32[]{:S(2)}, u32[]{:S(2)}) collective-permute-start(f32[14,192]{1,0:T(8,128)} %reshape.471), channel_id=1, source_target_pairs={{0,16},{16,0},{1,17},{17,1},{2,18},{18,2},{3,19},{19,3},{4,20},{20... | collective-permute-start | bytes 32264 | tf_op jit(solution)/shard_map/ppermute | solution.py:128
  10.2 1.2 %collective-permute-done = f32[14,192]{1,0:T(8,128)} collective-permute-done((f32[14,192]{1,0:T(8,128)}, f32[14,192]{1,0:T(8,128)}, u32[]{:S(2)}, u32[]{:S(2)}) %collective-permute-start) | collective-permute-done | bytes 10784 | tf_op jit(solution)/shard_map/ppermute | solution.py:128
  14.7 2.1 %collective-permute-start.2 = (f32[4,14,256]{2,1,0:T(8,128)S(1)}, f32[4,14,256]{2,1,0:T(8,128)S(1)}, u32[]{:S(2)}, u32[]{:S(2)}) collective-permute-start(f32[4,14,256]{2,1,0:T(8,128)S(1)} %pad_maximum_fusion.16), channel_id=1, source_target_pairs={{0,2},{1,3},{2,0},{3,1},{4,6},{5,7},{6,4},{7,5},{8,10},{9,11},{10,... | collective-permute-start | bytes 172040 | tf_op jit(solution)/shard_map/ppermute | solution.py:121
  16.8 2.7 %collective-permute-done.2 = f32[4,14,256]{2,1,0:T(8,128)S(1)} collective-permute-done((f32[4,14,256]{2,1,0:T(8,128)S(1)}, f32[4,14,256]{2,1,0:T(8,128)S(1)}, u32[]{:S(2)}, u32[]{:S(2)}) %collective-permute-start.2) | collective-permute-done | bytes 57376 | tf_op jit(solution)/shard_map/ppermute | solution.py:121
  19.6 1.9 %collective-permute-start.3 = (f32[6,14,256]{2,1,0:T(8,128)S(1)}, f32[6,14,256]{2,1,0:T(8,128)S(1)}, u32[]{:S(2)}, u32[]{:S(2)}) collective-permute-start(f32[6,14,256]{2,1,0:T(8,128)S(1)} %pad_maximum_fusion.14), channel_id=1, source_target_pairs={{0,4},{4,0},{8,12},{12,8},{1,5},{5,1},{9,13},{13,9},{2,6},{6,2},{1... | collective-permute-start | bytes 258056 | tf_op jit(solution)/shard_map/ppermute | solution.py:121
  22.1 2.1 %collective-permute-done.3 = f32[6,14,256]{2,1,0:T(8,128)S(1)} collective-permute-done((f32[6,14,256]{2,1,0:T(8,128)S(1)}, f32[6,14,256]{2,1,0:T(8,128)S(1)}, u32[]{:S(2)}, u32[]{:S(2)}) %collective-permute-start.3) | collective-permute-done | bytes 86048 | tf_op jit(solution)/shard_map/ppermute | solution.py:121
  24.3 2.9 %collective-permute-start.4 = (f32[12,14,256]{2,1,0:T(8,128)S(1)}, f32[12,14,256]{2,1,0:T(8,128)S(1)}, u32[]{:S(2)}, u32[]{:S(2)}) collective-permute-start(f32[12,14,256]{2,1,0:T(8,128)S(1)} %pad_maximum_fusion.10), channel_id=1, source_target_pairs={{0,8},{4,12},{8,0},{12,4},{1,9},{5,13},{9,1},{13,5},{2,10},{6,14},... | collective-permute-start | bytes 516104 | tf_op jit(solution)/shard_map/ppermute | solution.py:121
  27.4 7.6 %collective-permute-done.4 = f32[12,14,256]{2,1,0:T(8,128)S(1)} collective-permute-done((f32[12,14,256]{2,1,0:T(8,128)S(1)}, f32[12,14,256]{2,1,0:T(8,128)S(1)}, u32[]{:S(2)}, u32[]{:S(2)}) %collective-permute-start.4) | collective-permute-done | bytes 172064 | tf_op jit(solution)/shard_map/ppermute | solution.py:121
  35.4 1.2 %fusion.3 = f32[14,384]{1,0:T(8,128)S(1)} fusion(s32[384]{0:T(512)S(1)} %fusion.83, f32[14,4096]{1,0:T(8,128)S(1)} %reshape.475), kind=kOutput, calls=%fused_computation.4 | convolution fusion | flops 45899776 | bytes 252416 | tf_op jit(solution)/shard_map/dot_general | solution.py:107
  36.6 1.2 %fusion.16 = f32[14,384]{1,0:T(8,128)S(1)} fusion(f32[14,384]{1,0:T(8,128)S(1)} %fusion.3, s32[384]{0:T(512)S(1)} %fusion.83, f32[14,4096]{1,0:T(8,128)S(1)} %reshape.475), kind=kOutput, calls=%fused_computation.19 | convolution fusion | flops 45847808 | bytes 273920 | tf_op jit(solution)/shard_map/dot_general | solution.py:107
  41.6 1.2 %copy.84 = f32[7,2,64,128]{2,3,1,0:T(8,128)} copy(f32[7,2,64,128]{3,2,1,0:T(8,128)S(1)} %get-tuple-element.29) | data formatting | bytes 917504 | tf_op jit(solution)/shard_map/mul | solution.py:156
  42.8 1.3 %bitcast_add_fusion = f32[14,64,128]{1,2,0:T(8,128)S(1)} fusion(f32[7,2,64,128]{2,3,1,0:T(8,128)} %copy.84, f32[1,7,2,64,128]{3,4,2,1,0:T(8,128)S(1)} %copy.71), kind=kLoop, calls=%fused_computation.34 | loop fusion | flops 114688 | bytes 1376256 | tf_op jit(solution)/shard_map/add | solution.py:156
  44.2 1.7 %fusion.14 = f32[14,192]{1,0:T(8,128)S(1)} fusion(f32[14,64,128]{1,2,0:T(8,128)S(1)} %bitcast_add_fusion, f32[64,192]{1,0:T(8,128)S(1)} %copy-done.2, f32[192]{0:T(256)S(1)} %bitcast.194, s32[192]{0:T(256)S(1)} %copy-done.9, f32[192]{0:T(256)S(1)} %copy-done.5, s32[192]{0:T(256)S(1)} %copy-done.7), kind=kOutput, calls=%fused_computation.17 | convolution fusion | flops 264705408 | bytes 521728 | tf_op jit(solution)/shard_map/kij,sj->kis/dot_general | solution.py:112
  46.1 1.6 %collective-permute-start.5 = (f32[14,192]{1,0:T(8,128)S(1)}, f32[14,192]{1,0:T(8,128)S(1)}, u32[]{:S(2)}, u32[]{:S(2)}) collective-permute-start(f32[14,192]{1,0:T(8,128)S(1)} %reshape.480), channel_id=1, source_target_pairs={{0,16},{16,0},{1,17},{17,1},{2,18},{18,2},{3,19},{19,3},{4,20},{20... | collective-permute-start | bytes 32264 | tf_op jit(solution)/shard_map/ppermute | solution.py:128
  47.8 2.1 %collective-permute-done.5 = f32[14,192]{1,0:T(8,128)S(1)} collective-permute-done((f32[14,192]{1,0:T(8,128)S(1)}, f32[14,192]{1,0:T(8,128)S(1)}, u32[]{:S(2)}, u32[]{:S(2)}) %collective-permute-start.5) | collective-permute-done | bytes 10784 | tf_op jit(solution)/shard_map/ppermute | solution.py:128
  50.0 1.2 %fusion.96 = (f32[14,2,128]{1,2,0:T(8,128)}, f32[14,2,128]{1,2,0:T(8,128)S(1)}) fusion(f32[14,64,128]{1,2,0:T(8,128)S(1)} %bitcast_add_fusion), kind=kLoop, calls=%fused_computation.252 | loop fusion | bytes 57344 | tf_op jit(solution)/shard_map/slice | solution.py:133
  51.2 1.5 %copy.87 = f32[14,2,128]{2,1,0:T(2,128)S(1)} copy(f32[14,2,128]{1,2,0:T(8,128)} %get-tuple-element.19) | data formatting | bytes 28672 | tf_op jit(solution)/shard_map/slice | solution.py:133
  53.0 1.6 %collective-permute-start.7 = (f32[4,14,256]{2,1,0:T(8,128)S(1)}, f32[4,14,256]{2,1,0:T(8,128)S(1)}, u32[]{:S(2)}, u32[]{:S(2)}) collective-permute-start(f32[4,14,256]{2,1,0:T(8,128)S(1)} %pad_maximum_fusion.17), channel_id=1, source_target_pairs={{0,2},{1,3},{2,0},{3,1},{4,6},{5,7},{6,4},{7,5},{8,10},{9,11},{10,... | collective-permute-start | bytes 172040 | tf_op jit(solution)/shard_map/ppermute | solution.py:121
  54.8 2.7 %collective-permute-done.7 = f32[4,14,256]{2,1,0:T(8,128)S(1)} collective-permute-done((f32[4,14,256]{2,1,0:T(8,128)S(1)}, f32[4,14,256]{2,1,0:T(8,128)S(1)}, u32[]{:S(2)}, u32[]{:S(2)}) %collective-permute-start.7) | collective-permute-done | bytes 57376 | tf_op jit(solution)/shard_map/ppermute | solution.py:121
  58.4 3.9 %collective-permute-done.8 = f32[6,14,256]{2,1,0:T(8,128)S(1)} collective-permute-done((f32[6,14,256]{2,1,0:T(8,128)S(1)}, f32[6,14,256]{2,1,0:T(8,128)S(1)}, u32[]{:S(2)}, u32[]{:S(2)}) %collective-permute-start.8) | collective-permute-done | bytes 86048 | tf_op jit(solution)/shard_map/ppermute | solution.py:121
  62.3 2.2 %collective-permute-start.9 = (f32[12,14,256]{2,1,0:T(8,128)S(1)}, f32[12,14,256]{2,1,0:T(8,128)S(1)}, u32[]{:S(2)}, u32[]{:S(2)}) collective-permute-start(f32[12,14,256]{2,1,0:T(8,128)S(1)} %pad_maximum_fusion.11), channel_id=1, source_target_pairs={{0,8},{4,12},{8,0},{12,4},{1,9},{5,13},{9,1},{13,5},{2,10},{6,14},... | collective-permute-start | bytes 516104 | tf_op jit(solution)/shard_map/ppermute | solution.py:121
  64.8 8.2 %collective-permute-done.9 = f32[12,14,256]{2,1,0:T(8,128)S(1)} collective-permute-done((f32[12,14,256]{2,1,0:T(8,128)S(1)}, f32[12,14,256]{2,1,0:T(8,128)S(1)}, u32[]{:S(2)}, u32[]{:S(2)}) %collective-permute-start.9) | collective-permute-done | bytes 172064 | tf_op jit(solution)/shard_map/ppermute | solution.py:121
  73.3 1.2 %fusion = f32[14,384]{1,0:T(8,128)S(1)} fusion(s32[384]{0:T(512)S(1)} %fusion.83, f32[14,4096]{1,0:T(8,128)S(1)} %reshape.484), kind=kOutput, calls=%fused_computation.1 | convolution fusion | flops 45899776 | bytes 252416 | tf_op jit(solution)/shard_map/dot_general | solution.py:107
  (143 shorter events, 21.3 us)
Async XLA Ops:
  0.0 9.4 %copy-start = (f32[1,7,2,64,128]{4,3,2,1,0:T(8,128)S(1)}, f32[1,7,2,64,128]{4,3,2,1,0:T(8,128)}, u32[]{:S(2)}) copy-start(f32[1,7,2,64,128]{4,3,2,1,0:T(8,128)} %param.5) | copy-start | bytes 1376260
  2.2 3.6 %copy-start.4 = (f32[192]{0:T(256)}, f32[192]{0:T(256)S(1)}, u32[]{:S(2)}) copy-start(f32[192]{0:T(256)S(1)} %broadcast_subtract_fusion.1) | copy-start | bytes 2308
  3.0 2.8 %copy-start.6 = (s32[192]{0:T(256)}, s32[192]{0:T(256)S(1)}, u32[]{:S(2)}) copy-start(s32[192]{0:T(256)S(1)} %get-tuple-element.61) | copy-start | bytes 2308
  3.0 2.8 %copy-start.8 = (s32[192]{0:T(256)}, s32[192]{0:T(256)S(1)}, u32[]{:S(2)}) copy-start(s32[192]{0:T(256)S(1)} %get-tuple-element.62) | copy-start | bytes 2308
  3.0 0.6 copy-start.1
  6.4 5.0 %collective-permute-start = (f32[14,192]{1,0:T(8,128)}, f32[14,192]{1,0:T(8,128)}, u32[]{:S(2)}, u32[]{:S(2)}) collective-permute-start(f32[14,192]{1,0:T(8,128)} %reshape.471), channel_id=1, source_target_pairs={{0,16},{16,0},{1,17},{17,1},{2,18},{18,2},{3,19},{19,3},{4,20},{20... | collective-permute-start | bytes 32264 | tf_op jit(solution)/shard_map/ppermute | solution.py:128
  12.8 1.9 %collective-permute-start.1 = (f32[2,14,256]{2,1,0:T(8,128)}, f32[2,14,256]{2,1,0:T(8,128)S(1)}, u32[]{:S(2)}, u32[]{:S(2)}) collective-permute-start(f32[2,14,256]{2,1,0:T(8,128)} %pad_maximum_fusion.18), channel_id=1, source_target_pairs={{0,1},{1,0},{2,3},{3,2},{4,5},{5,4},{6,7},{7,6},{8,9},{9,8},{10,11... | collective-permute-start | bytes 86024 | tf_op jit(solution)/shard_map/ppermute | solution.py:121
  14.4 2.4 %copy-start.3 = (f32[14,2,128]{2,1,0:T(2,128)S(1)}, f32[14,2,128]{2,1,0:T(2,128)}, u32[]{:S(2)}) copy-start(f32[14,2,128]{2,1,0:T(2,128)} %copy.74) | copy-start | bytes 43012
  14.7 4.8 %collective-permute-start.2 = (f32[4,14,256]{2,1,0:T(8,128)S(1)}, f32[4,14,256]{2,1,0:T(8,128)S(1)}, u32[]{:S(2)}, u32[]{:S(2)}) collective-permute-start(f32[4,14,256]{2,1,0:T(8,128)S(1)} %pad_maximum_fusion.16), channel_id=1, source_target_pairs={{0,2},{1,3},{2,0},{3,1},{4,6},{5,7},{6,4},{7,5},{8,10},{9,11},{10,... | collective-permute-start | bytes 172040 | tf_op jit(solution)/shard_map/ppermute | solution.py:121
  19.6 4.7 %collective-permute-start.3 = (f32[6,14,256]{2,1,0:T(8,128)S(1)}, f32[6,14,256]{2,1,0:T(8,128)S(1)}, u32[]{:S(2)}, u32[]{:S(2)}) collective-permute-start(f32[6,14,256]{2,1,0:T(8,128)S(1)} %pad_maximum_fusion.14), channel_id=1, source_target_pairs={{0,4},{4,0},{8,12},{12,8},{1,5},{5,1},{9,13},{13,9},{2,6},{6,2},{1... | collective-permute-start | bytes 258056 | tf_op jit(solution)/shard_map/ppermute | solution.py:121
  24.3 10.8 %collective-permute-start.4 = (f32[12,14,256]{2,1,0:T(8,128)S(1)}, f32[12,14,256]{2,1,0:T(8,128)S(1)}, u32[]{:S(2)}, u32[]{:S(2)}) collective-permute-start(f32[12,14,256]{2,1,0:T(8,128)S(1)} %pad_maximum_fusion.10), channel_id=1, source_target_pairs={{0,8},{4,12},{8,0},{12,4},{1,9},{5,13},{9,1},{13,5},{2,10},{6,14},... | collective-permute-start | bytes 516104 | tf_op jit(solution)/shard_map/ppermute | solution.py:121
  42.8 1.3 %copy-start.2 = (f32[64,192]{1,0:T(8,128)S(1)}, f32[64,192]{1,0:T(8,128)}, u32[]{:S(2)}) copy-start(f32[64,192]{1,0:T(8,128)} %copy-done.1) | copy-start | bytes 147460
  42.8 1.3 %copy-start.5 = (f32[192]{0:T(256)S(1)}, f32[192]{0:T(256)}, u32[]{:S(2)}) copy-start(f32[192]{0:T(256)} %copy-done.4) | copy-start | bytes 2308
  42.8 1.3 %copy-start.7 = (s32[192]{0:T(256)S(1)}, s32[192]{0:T(256)}, u32[]{:S(2)}) copy-start(s32[192]{0:T(256)} %copy-done.6) | copy-start | bytes 2308
  42.8 1.3 %copy-start.9 = (s32[192]{0:T(256)S(1)}, s32[192]{0:T(256)}, u32[]{:S(2)}) copy-start(s32[192]{0:T(256)} %copy-done.8) | copy-start | bytes 2308
  46.1 3.8 %collective-permute-start.5 = (f32[14,192]{1,0:T(8,128)S(1)}, f32[14,192]{1,0:T(8,128)S(1)}, u32[]{:S(2)}, u32[]{:S(2)}) collective-permute-start(f32[14,192]{1,0:T(8,128)S(1)} %reshape.480), channel_id=1, source_target_pairs={{0,16},{16,0},{1,17},{17,1},{2,18},{18,2},{3,19},{19,3},{4,20},{20... | collective-permute-start | bytes 32264 | tf_op jit(solution)/shard_map/ppermute | solution.py:128
  49.9 3.1 %collective-permute-start.6 = (f32[2,14,256]{2,1,0:T(8,128)S(1)}, f32[2,14,256]{2,1,0:T(8,128)S(1)}, u32[]{:S(2)}, u32[]{:S(2)}) collective-permute-start(f32[2,14,256]{2,1,0:T(8,128)S(1)} %pad_maximum_fusion.19), channel_id=1, source_target_pairs={{0,1},{1,0},{2,3},{3,2},{4,5},{5,4},{6,7},{7,6},{8,9},{9,8},{10,11... | collective-permute-start | bytes 86024 | tf_op jit(solution)/shard_map/ppermute | solution.py:121
  53.0 4.6 %collective-permute-start.7 = (f32[4,14,256]{2,1,0:T(8,128)S(1)}, f32[4,14,256]{2,1,0:T(8,128)S(1)}, u32[]{:S(2)}, u32[]{:S(2)}) collective-permute-start(f32[4,14,256]{2,1,0:T(8,128)S(1)} %pad_maximum_fusion.17), channel_id=1, source_target_pairs={{0,2},{1,3},{2,0},{3,1},{4,6},{5,7},{6,4},{7,5},{8,10},{9,11},{10,... | collective-permute-start | bytes 172040 | tf_op jit(solution)/shard_map/ppermute | solution.py:121
  57.6 4.7 %collective-permute-start.8 = (f32[6,14,256]{2,1,0:T(8,128)S(1)}, f32[6,14,256]{2,1,0:T(8,128)S(1)}, u32[]{:S(2)}, u32[]{:S(2)}) collective-permute-start(f32[6,14,256]{2,1,0:T(8,128)S(1)} %pad_maximum_fusion.15), channel_id=1, source_target_pairs={{0,4},{4,0},{8,12},{12,8},{1,5},{5,1},{9,13},{13,9},{2,6},{6,2},{1... | collective-permute-start | bytes 258056 | tf_op jit(solution)/shard_map/ppermute | solution.py:121
  62.3 10.7 %collective-permute-start.9 = (f32[12,14,256]{2,1,0:T(8,128)S(1)}, f32[12,14,256]{2,1,0:T(8,128)S(1)}, u32[]{:S(2)}, u32[]{:S(2)}) collective-permute-start(f32[12,14,256]{2,1,0:T(8,128)S(1)} %pad_maximum_fusion.11), channel_id=1, source_target_pairs={{0,8},{4,12},{8,0},{12,4},{1,9},{5,13},{9,1},{13,5},{2,10},{6,14},... | collective-permute-start | bytes 516104 | tf_op jit(solution)/shard_map/ppermute | solution.py:121

commit v4 on v2

--- a/solution.py
+++ b/solution.py
@@ -2,6 +2,11 @@
 import jax.numpy as jnp
 from jax import lax
 from jax.sharding import PartitionSpec as P
+from jax.experimental import pallas as pl
+from jax.experimental.pallas import tpu as pltpu
+import functools
+
+INTERPRET = False
 
 viscosity = 0.05
 resistivity = 0.05
@@ -12,31 +17,79 @@
 HIGHEST = lax.Precision.HIGHEST
 
 
-def rate(up, mid, down, left, right):
-    vert = jnp.concatenate([up, mid, down], axis=2)
-    horz = jnp.concatenate([left, mid, right], axis=3)
-    height = mid.shape[2]
-    width = mid.shape[3]
-
-    def lat_at(k):
-        return vert[:, :, 2 + k : 2 + k + height, :]
-
-    def lon_at(k):
-        return horz[:, :, :, 2 + k : 2 + k + width]
-
-    middle = mid
-    d_lat = (8.0 * (lat_at(1) - lat_at(-1)) - (lat_at(2) - lat_at(-2))) / 12.0
-    d_lon = (8.0 * (lon_at(1) - lon_at(-1)) - (lon_at(2) - lon_at(-2))) / 12.0
-    padded = jnp.pad(middle, ((0, 0), (1, 1), (0, 0), (0, 0)))
-    lap = lat_at(1) + lat_at(-1) + lon_at(1) + lon_at(-1) - 4.0 * middle
-    lap = lap + padded[:, 2:] + padded[:, :-2] - 2.0 * middle
-    adv_u = middle[1:2] * d_lat + middle[2:3] * d_lon
-    adv_b = middle[4:5] * d_lat + middle[5:6] * d_lon
-    moment = -adv_u[0:3] + adv_b[3:6] + viscosity * lap[0:3]
-    induct = adv_b[0:3] - adv_u[3:6] + resistivity * lap[3:6]
-    heat = -adv_u[6:7] + diffusivity * lap[6:7]
-    first = moment[0:1] + buoyancy * middle[6:7]
-    return jnp.concatenate([first, moment[1:3], induct, heat], axis=0)
+def stencil_kernel(f_ref, up_ref, down_ref, left_ref, right_ref, base_ref, o_ref, *, first):
+    planes, height, width = f_ref.shape
+    comps = planes // 2
+    row = lax.broadcasted_iota(jnp.int32, (height, width), 0)
+    col = lax.broadcasted_iota(jnp.int32, (height, width), 1)
+
+    def terms(k):
+        x = f_ref[k]
+        up = up_ref[k]
+        down = down_ref[k]
+        left = left_ref[k]
+        right = right_ref[k]
+        lat_m1 = jnp.where(row == 0, up[1:2, :], pltpu.roll(x, 1, 0))
+        lat_m2 = jnp.where(row == 0, up[0:1, :], jnp.where(row == 1, up[1:2, :], pltpu.roll(x, 2, 0)))
+        lat_p1 = jnp.where(row == height - 1, down[0:1, :], pltpu.roll(x, height - 1, 0))
+        lat_p2 = jnp.where(
+            row == height - 1, down[1:2, :], jnp.where(row == height - 2, down[0:1, :], pltpu.roll(x, height - 2, 0))
+        )
+        lon_m1 = jnp.where(col == 0, left[:, 1:2], pltpu.roll(x, 1, 1))
+        lon_m2 = jnp.where(col == 0, left[:, 0:1], jnp.where(col == 1, left[:, 1:2], pltpu.roll(x, 2, 1)))
+        lon_p1 = jnp.where(col == width - 1, right[:, 0:1], pltpu.roll(x, width - 1, 1))
+        lon_p2 = jnp.where(
+            col == width - 1, right[:, 1:2], jnp.where(col == width - 2, right[:, 0:1], pltpu.roll(x, width - 2, 1))
+        )
+        d_lat = (8.0 * (lat_p1 - lat_m1) - (lat_p2 - lat_m2)) / 12.0
+        d_lon = (8.0 * (lon_p1 - lon_m1) - (lon_p2 - lon_m2)) / 12.0
+        lap = lat_p1 + lat_m1 + lon_p1 + lon_m1 - 4.0 * x
+        return x, d_lat, d_lon, lap
+
+    for level in range(2):
+        def plane(c):
+            return c * 2 + level
+
+        def value(c):
+            return f_ref[plane(c)]
+
+        def lap_of(c, x, lap):
+            above = f_ref[c * 2 + 1] if level == 0 else 0.0
+            below = f_ref[c * 2] if level == 1 else 0.0
+            return lap + above + below - 2.0 * x
+
+        def store(c, x, rate):
+            section = x + time_step * rate
+            if first:
+                o_ref[plane(c)] = section
+            else:
+                o_ref[plane(c)] = 0.5 * base_ref[plane(c)] + 0.5 * section
+
+        u1, u2, u4, u5, u6 = value(1), value(2), value(4), value(5), value(6)
+        for c in range(3):
+            xa, lat_a, lon_a, lap_a = terms(plane(c))
+            xb, lat_b, lon_b, lap_b = terms(plane(c + 3))
+            adv_u_a = u1 * lat_a + u2 * lon_a
+            adv_b_a = u4 * lat_a + u5 * lon_a
+            adv_u_b = u1 * lat_b + u2 * lon_b
+            adv_b_b = u4 * lat_b + u5 * lon_b
+            rate_a = -adv_u_a + adv_b_b + viscosity * lap_of(c, xa, lap_a)
+            if c == 0:
+                rate_a = rate_a + buoyancy * u6
+            rate_b = adv_b_a - adv_u_b + resistivity * lap_of(c + 3, xb, lap_b)
+            store(c, xa, rate_a)
+            store(c + 3, xb, rate_b)
+        x6, lat_6, lon_6, lap_6 = terms(plane(6))
+        adv_u_6 = u1 * lat_6 + u2 * lon_6
+        store(6, x6, -adv_u_6 + diffusivity * lap_of(6, x6, lap_6))
+
+
+def advance(field, up, down, left, right, base, first):
+    return pl.pallas_call(
+        functools.partial(stencil_kernel, first=first),
+        out_shape=jax.ShapeDtypeStruct(field.shape, field.dtype),
+        interpret=INTERPRET,
+    )(field, up, down, left, right, base)
 
 
 def rotate(values, turn):
@@ -132,17 +185,16 @@
         rim = jnp.dot(partner, pick, precision=HIGHEST).reshape(comps, levels, -1)
         rim_lat = rim[:, :, :band].reshape(comps, levels, 2, cols)
         rim_lon = jnp.transpose(rim[:, :, band:].reshape(comps, levels, 2, rows), (0, 1, 3, 2))
-        up = jnp.where(on_top, rim_lat, up)
-        down = jnp.where(on_bottom, rim_lat, down)
-        left = jnp.where(on_left, rim_lon, left)
-        right = jnp.where(on_right, rim_lon, right)
-        return rate(up, field, down, left, right)
-
-    field = state[0]
-    section_one = field + time_step * section(field)
-    second = section(section_one)
-    new_field = 0.5 * field + 0.5 * (section_one + time_step * second)
-    return new_field[None]
+        up = jnp.where(on_top, rim_lat, up).reshape(comps * levels, 2, cols)
+        down = jnp.where(on_bottom, rim_lat, down).reshape(comps * levels, 2, cols)
+        left = jnp.where(on_left, rim_lon, left).reshape(comps * levels, rows, 2)
+        right = jnp.where(on_right, rim_lon, right).reshape(comps * levels, rows, 2)
+        return up, down, left, right
+
+    field = state[0].reshape(comps * levels, rows, cols)
+    section_one = advance(field, *section(field), field, True)
+    new_field = advance(section_one, *section(section_one), field, False)
+    return new_field.reshape(1, comps, levels, rows, cols)
 
 
 def solution(mesh):

time: 76.3 us -> 73.7 us (0.966)
  other arithmetic: 13.1 us -> 3.9 us
  Pallas kernels: 0 us -> 6.88 us
  local copies, waits for them, and re-layouts: 21.2 us -> 17.6 us
  waiting for transfers between devices: 19.6 us -> 22.7 us
    pallas_call x0 -> x2, Pallas kernels: none -> 6.88 us  [advance(): pl.pallas_call(functools.partial(stencil_kernel, first=first), out_shape=...]
    add x9 -> x0, other arithmetic: 4.2 us -> none  [the longest x2 1.8 us: rate(): adv_b = middle[4:5] * d_lat + middle[5:6] * d_lon]
    ppermute x8, waiting for transfers between devices: 16.6 us -> 20.4 us  [gather(): other = lax.ppermute(held, axis, [(i, i ^ k) for i in range(size)])]
    dynamic_slice x4 -> x2, local copies, waits for them, and re-layouts: 4.12 us -> 0.41 us  [section(): lax.dynamic_index_in_dim(side_cols, jnp.maximum(lon_pos - 1, 0), keepdims...]
    select_n x4, local copies, waits for them, and re-layouts: 0.88 us -> 3.97 us  [the longest x2 2 us: section(): right = jnp.where(on_right, rim_lon, right).reshape(comps * levels, rows, 2)]
    select_n x8, other arithmetic: 3.28 us -> 0.46 us  [gather(): jnp.where(low, jnp.concatenate([held, other]), jnp.concatenate([other, he...]
    slice x2, local copies, waits for them, and re-layouts: 0.03 us -> 2.7 us  [section(): side_cols = jnp.concatenate([flat[:, :, :2], flat[:, :, cols - 2:]], axis=2)]
    unnamed x43 -> x10, local copies, waits for them, and re-layouts: 2.73 us -> 0.06 us
  transfers between devices with their start and end apart: 10 -> 10, of which waited for: 8 -> 9; matrix products, arithmetic and copies ran while one was open for 22% -> 13% of each run, Pallas kernels for 0% -> 0%
where the time goes in v4:
time: 73.7 us; the launch traced here: 73.2 us
  waiting for transfers between devices  22.7 us (31%)
  local copies, waits for them, and re-layouts  17.6 us (24%)
  starting transfers between devices  14 us (19%)
  matrix products  7.57 us (10%)
  Pallas kernels  6.88 us (9%)
  other arithmetic  3.9 us (5%)
    ppermute x8, waiting for transfers between devices, gather(): other = lax.ppermute(held, axis, [(i, i ^ k) for i in range(size)])  20.4 us
    ppermute x8, starting transfers between devices, gather(): other = lax.ppermute(held, axis, [(i, i ^ k) for i in range(size)])  10.3 us
    pallas_call x2, Pallas kernels, advance(): pl.pallas_call(functools.partial(stencil_kernel, first=first), out_shape=...  6.88 us
    dot_general x2, matrix products, donate(): along = jnp.einsum('kij,sj->kis', flat, weight_lon, precision=HIGHEST)  4.12 us
    reshape x2, local copies, waits for them, and re-layouts, section(): side_cols = lon_all[:, :, dons:].reshape(lon_count, comps, levels, rows, 4)  3.83 us
    ppermute x2, starting transfers between devices, section(): given = lax.ppermute(donate(field), 'panel', [(0, 1), (1, 0)])  3.79 us
    dot_general x2, matrix products, section(): rim = jnp.dot(partner, pick, precision=HIGHEST).reshape(comps, levels, -1)  3.45 us
    slice x2, local copies, waits for them, and re-layouts, section(): side_cols = jnp.concatenate([flat[:, :, :2], flat[:, :, cols - 2:]], axis=2)  2.7 us
  transfers between devices with their start and end apart: 10, of which 9 were waited for; matrix products, arithmetic and copies ran while one was open for 13% of the time, Pallas kernels for 0%

profile of v4, /device:TPU:0, one launch (start us, length us, event | category | flops | bytes accessed | tf_op | source)
XLA Modules:
  0.0 73.2 jit_solution(10834385379020158311)
XLA Ops:
  2.9 2.1 %fusion.9 = f32[14,192]{1,0:T(8,128)S(1)} fusion(f32[14,64,128]{2,1,0:T(8,128)} %bitcast.134, f32[64,192]{1,0:T(8,128)S(1)} %select_add_fusion.3, f32[192]{0:T(256)S(1)} %bitcast.180, s32[192]{0:T(256)S(1)} %get-tuple-element.36, f32[192]{0:T(256)S(1)} %broadcast_subtract_fusion.1, s32[192]{0:T(256)S(1)} %get-tuple-element.35), kind=kOutput, calls=%fused_computation.10 | convolution fusion | flops 264705408 | bytes 521728 | tf_op jit(solution)/shard_map/kij,sj->kis/dot_general | solution.py:150
  5.1 3.0 %collective-permute-start = (f32[14,192]{1,0:T(8,128)S(1)}, f32[14,192]{1,0:T(8,128)S(1)}, u32[]{:S(2)}, u32[]{:S(2)}) collective-permute-start(f32[14,192]{1,0:T(8,128)S(1)} %reshape.260), channel_id=1, source_target_pairs={{0,16},{16,0},{1,17},{17,1},{2,18},{18,2},{3,19},{19,3},{4,20},{20... | collective-permute-start | bytes 32264 | tf_op jit(solution)/shard_map/ppermute | solution.py:168
  9.0 1.4 %fusion.29 = (f32[14,64,2]{2,1,0:T(8,128)S(1)}, f32[14,64,2]{2,1,0:T(8,128)S(1)}) fusion(f32[14,64,128]{2,1,0:T(8,128)} %bitcast.136), kind=kLoop, calls=%fused_computation.105 | loop fusion | bytes 28672 | tf_op jit(solution)/shard_map/slice | solution.py:170
  11.4 1.1 %collective-permute-done.1 = f32[1,14,448]{2,1,0:T(8,128)S(1)} collective-permute-done((f32[1,14,448]{2,1,0:T(8,128)S(1)}, f32[1,14,448]{2,1,0:T(8,128)S(1)}, u32[]{:S(2)}, u32[]{:S(2)}) %collective-permute-start.1) | collective-permute-done | bytes 25120 | tf_op jit(solution)/shard_map/ppermute | solution.py:160
  12.6 1.6 %collective-permute-start.2 = (f32[2,14,448]{2,0,1:T(2,128)S(1)}, f32[2,14,448]{2,0,1:T(2,128)S(1)}, u32[]{:S(2)}, u32[]{:S(2)}) collective-permute-start(f32[2,14,448]{2,0,1:T(2,128)S(1)} %maximum_select_fusion.6), channel_id=1, source_target_pairs={{0,2},{1,3},{2,0},{3,1},{4,6},{5,7},{6,4},{7,5},{8,10},{9,11},{10,... | collective-permute-start | bytes 150536 | tf_op jit(solution)/shard_map/ppermute | solution.py:160
  14.3 2.6 %collective-permute-done.2 = f32[2,14,448]{2,0,1:T(2,128)S(1)} collective-permute-done((f32[2,14,448]{2,0,1:T(2,128)S(1)}, f32[2,14,448]{2,0,1:T(2,128)S(1)}, u32[]{:S(2)}, u32[]{:S(2)}) %collective-permute-start.2) | collective-permute-done | bytes 50208 | tf_op jit(solution)/shard_map/ppermute | solution.py:160
  17.1 1.6 %collective-permute-start.3 = (f32[1,14,1280]{2,1,0:T(8,128)S(1)}, f32[1,14,1280]{2,1,0:T(8,128)S(1)}, u32[]{:S(2)}, u32[]{:S(2)}) collective-permute-start(f32[1,14,1280]{2,1,0:T(8,128)S(1)} %maximum_bitcast_fusion), channel_id=1, source_target_pairs={{0,4},{4,0},{8,12},{12,8},{1,5},{5,1},{9,13},{13,9},{2,6},{6,2},{1... | collective-permute-start | bytes 215048 | tf_op jit(solution)/shard_map/ppermute | solution.py:160
  18.7 2.9 %collective-permute-done.3 = f32[1,14,1280]{2,1,0:T(8,128)S(1)} collective-permute-done((f32[1,14,1280]{2,1,0:T(8,128)S(1)}, f32[1,14,1280]{2,1,0:T(8,128)S(1)}, u32[]{:S(2)}, u32[]{:S(2)}) %collective-permute-start.3) | collective-permute-done | bytes 71712 | tf_op jit(solution)/shard_map/ppermute | solution.py:160
  21.6 2.7 %collective-permute-start.4 = (f32[2,14,1280]{2,1,0:T(8,128)S(1)}, f32[2,14,1280]{2,1,0:T(8,128)S(1)}, u32[]{:S(2)}, u32[]{:S(2)}) collective-permute-start(f32[2,14,1280]{2,1,0:T(8,128)S(1)} %maximum_select_fusion.2), channel_id=1, source_target_pairs={{0,8},{4,12},{8,0},{12,4},{1,9},{5,13},{9,1},{13,5},{2,10},{6,14},... | collective-permute-start | bytes 430088 | tf_op jit(solution)/shard_map/ppermute | solution.py:160
  24.4 1.9 %reshape.269 = f32[4,7,2,64,4]{4,3,0,2,1:T(8,128)S(1)} reshape(f32[4,14,256]{2,0,1:T(4,128)S(1)} %slice.254) | data formatting | bytes 114688 | tf_op jit(solution)/shard_map/reshape | solution.py:174
  26.8 3.3 %collective-permute-done.4 = f32[2,14,1280]{2,1,0:T(8,128)S(1)} collective-permute-done((f32[2,14,1280]{2,1,0:T(8,128)S(1)}, f32[2,14,1280]{2,1,0:T(8,128)S(1)}, u32[]{:S(2)}, u32[]{:S(2)}) %collective-permute-start.4) | collective-permute-done | bytes 143392 | tf_op jit(solution)/shard_map/ppermute | solution.py:160
  30.4 1.7 %fusion.3 = f32[7,2,384]{2,0,1:T(8,128)S(1)} fusion(s32[384]{0:T(512)S(1)} %pad_add_fusion, f32[7,2,3072]{2,1,0:T(2,128)S(1)} %dot_general.20), kind=kOutput, calls=%fused_computation.3 | convolution fusion | flops 199360512 | bytes 195072 | tf_op jit(solution)/shard_map/dot_general | solution.py:185
  35.0 3.4 %shard_map.55.f_ref = f32[14,64,128]{2,1,0:T(8,128)} custom-call(f32[14,64,128]{2,1,0:T(8,128)} %bitcast.137, f32[14,2,128]{2,1,0:T(2,128)} %bitcast.173, f32[14,2,128]{2,1,0:T(2,128)} %bitcast.172, f32[14,64,2]{2,1,0:T(8,128)} %bitcast.142, f32[14,64,2]{2,1,0:T(8,128)} %bitcast.140, f32[14,64,128]{2,1,0:T(8,128)} %bitcast.138), custom_call_target="tpu_custom_call" | custom-call | tf_op jit(solution)/shard_map/pallas_call | solution.py:88
  38.4 2.1 %fusion.8 = f32[14,192]{1,0:T(8,128)S(1)} fusion(f32[14,64,128]{2,1,0:T(8,128)} %shard_map.55.f_ref, f32[64,192]{1,0:T(8,128)S(1)} %select_add_fusion.3, f32[192]{0:T(256)S(1)} %bitcast.181, s32[192]{0:T(256)S(1)} %get-tuple-element.36, f32[192]{0:T(256)S(1)} %broadcast_subtract_fusion.1, s32[192]{0:T(256)S(1)} %get-tuple-element.35), kind=kOutput, calls=%fused_computation.9 | convolution fusion | flops 264705408 | bytes 521728 | tf_op jit(solution)/shard_map/kij,sj->kis/dot_general | solution.py:150
  40.5 1.3 %fusion.27 = (f32[14,64,2]{2,1,0:T(8,128)S(1)}, f32[14,64,2]{2,1,0:T(8,128)S(1)}) fusion(f32[14,64,128]{2,1,0:T(8,128)} %shard_map.55.f_ref), kind=kLoop, calls=%fused_computation.103 | loop fusion | bytes 28672 | tf_op jit(solution)/shard_map/slice | solution.py:170
  43.5 2.3 %collective-permute-done.5 = f32[14,192]{1,0:T(8,128)S(1)} collective-permute-done((f32[14,192]{1,0:T(8,128)S(1)}, f32[14,192]{1,0:T(8,128)S(1)}, u32[]{:S(2)}, u32[]{:S(2)}) %collective-permute-start.5) | collective-permute-done | bytes 10784 | tf_op jit(solution)/shard_map/ppermute | solution.py:168
  47.2 1.6 %collective-permute-start.7 = (f32[2,14,448]{2,0,1:T(2,128)S(1)}, f32[2,14,448]{2,0,1:T(2,128)S(1)}, u32[]{:S(2)}, u32[]{:S(2)}) collective-permute-start(f32[2,14,448]{2,0,1:T(2,128)S(1)} %maximum_select_fusion.7), channel_id=1, source_target_pairs={{0,2},{1,3},{2,0},{3,1},{4,6},{5,7},{6,4},{7,5},{8,10},{9,11},{10,... | collective-permute-start | bytes 150536 | tf_op jit(solution)/shard_map/ppermute | solution.py:160
  48.8 2.6 %collective-permute-done.7 = f32[2,14,448]{2,0,1:T(2,128)S(1)} collective-permute-done((f32[2,14,448]{2,0,1:T(2,128)S(1)}, f32[2,14,448]{2,0,1:T(2,128)S(1)}, u32[]{:S(2)}, u32[]{:S(2)}) %collective-permute-start.7) | collective-permute-done | bytes 50208 | tf_op jit(solution)/shard_map/ppermute | solution.py:160
  52.4 3.8 %collective-permute-done.8 = f32[1,14,1280]{2,1,0:T(8,128)S(1)} collective-permute-done((f32[1,14,1280]{2,1,0:T(8,128)S(1)}, f32[1,14,1280]{2,1,0:T(8,128)S(1)}, u32[]{:S(2)}, u32[]{:S(2)}) %collective-permute-start.8) | collective-permute-done | bytes 71712 | tf_op jit(solution)/shard_map/ppermute | solution.py:160
  56.2 2.1 %collective-permute-start.9 = (f32[2,14,1280]{2,1,0:T(8,128)S(1)}, f32[2,14,1280]{2,1,0:T(8,128)S(1)}, u32[]{:S(2)}, u32[]{:S(2)}) collective-permute-start(f32[2,14,1280]{2,1,0:T(8,128)S(1)} %maximum_select_fusion.3), channel_id=1, source_target_pairs={{0,8},{4,12},{8,0},{12,4},{1,9},{5,13},{9,1},{13,5},{2,10},{6,14},... | collective-permute-start | bytes 430088 | tf_op jit(solution)/shard_map/ppermute | solution.py:160
  58.3 1.9 %reshape.281 = f32[4,7,2,64,4]{4,3,0,2,1:T(8,128)S(1)} reshape(f32[4,14,256]{2,0,1:T(4,128)S(1)} %slice.275) | data formatting | bytes 114688 | tf_op jit(solution)/shard_map/reshape | solution.py:174
  60.8 3.9 %collective-permute-done.9 = f32[2,14,1280]{2,1,0:T(8,128)S(1)} collective-permute-done((f32[2,14,1280]{2,1,0:T(8,128)S(1)}, f32[2,14,1280]{2,1,0:T(8,128)S(1)}, u32[]{:S(2)}, u32[]{:S(2)}) %collective-permute-start.9) | collective-permute-done | bytes 143392 | tf_op jit(solution)/shard_map/ppermute | solution.py:160
  65.2 1.7 %fusion.1 = f32[7,2,384]{2,0,1:T(8,128)S(1)} fusion(s32[384]{0:T(512)S(1)} %pad_add_fusion, f32[7,2,3072]{2,1,0:T(2,128)S(1)} %dot_general.23), kind=kOutput, calls=%fused_computation.2 | convolution fusion | flops 199360512 | bytes 195072 | tf_op jit(solution)/shard_map/dot_general | solution.py:185
  69.8 3.4 %shard_map.56 = f32[14,64,128]{2,1,0:T(8,128)} custom-call(f32[14,64,128]{2,1,0:T(8,128)} %shard_map.55.f_ref, f32[14,2,128]{2,1,0:T(2,128)} %bitcast.171, f32[14,2,128]{2,1,0:T(2,128)} %bitcast.170, f32[14,64,2]{2,1,0:T(8,128)} %bitcast.143, f32[14,64,2]{2,1,0:T(8,128)} %bitcast.141, f32[14,64,128]{2,1,0:T(8,128)} %bitcast.139), custom_call_target="tpu_custom_call" | custom-call | tf_op jit(solution)/shard_map/pallas_call | solution.py:88
  (107 shorter events, 16.8 us)
Async XLA Ops:
  5.1 6.1 %collective-permute-start = (f32[14,192]{1,0:T(8,128)S(1)}, f32[14,192]{1,0:T(8,128)S(1)}, u32[]{:S(2)}, u32[]{:S(2)}) collective-permute-start(f32[14,192]{1,0:T(8,128)S(1)} %reshape.260), channel_id=1, source_target_pairs={{0,16},{16,0},{1,17},{17,1},{2,18},{18,2},{3,19},{19,3},{4,20},{20... | collective-permute-start | bytes 32264 | tf_op jit(solution)/shard_map/ppermute | solution.py:168
  9.0 2.3 %copy-start = (s32[1,1,1,768]{3,2,1,0:T(1,128)S(1)}, s32[1,1,1,768]{3,2,1,0:T(1,128)}, u32[]{:S(2)}) copy-start(s32[1,1,1,768]{3,2,1,0:T(1,128)} %param.6) | copy-start | bytes 9220
  11.3 1.2 %collective-permute-start.1 = (f32[1,14,448]{2,1,0:T(8,128)S(1)}, f32[1,14,448]{2,1,0:T(8,128)S(1)}, u32[]{:S(2)}, u32[]{:S(2)}) collective-permute-start(f32[1,14,448]{2,1,0:T(8,128)S(1)} %maximum_bitcast_fusion.2), channel_id=1, source_target_pairs={{0,1},{1,0},{2,3},{3,2},{4,5},{5,4},{6,7},{7,6},{8,9},{9,8},{10,11... | collective-permute-start | bytes 75272 | tf_op jit(solution)/shard_map/ppermute | solution.py:160
  12.6 4.2 %collective-permute-start.2 = (f32[2,14,448]{2,0,1:T(2,128)S(1)}, f32[2,14,448]{2,0,1:T(2,128)S(1)}, u32[]{:S(2)}, u32[]{:S(2)}) collective-permute-start(f32[2,14,448]{2,0,1:T(2,128)S(1)} %maximum_select_fusion.6), channel_id=1, source_target_pairs={{0,2},{1,3},{2,0},{3,1},{4,6},{5,7},{6,4},{7,5},{8,10},{9,11},{10,... | collective-permute-start | bytes 150536 | tf_op jit(solution)/shard_map/ppermute | solution.py:160
  17.1 4.5 %collective-permute-start.3 = (f32[1,14,1280]{2,1,0:T(8,128)S(1)}, f32[1,14,1280]{2,1,0:T(8,128)S(1)}, u32[]{:S(2)}, u32[]{:S(2)}) collective-permute-start(f32[1,14,1280]{2,1,0:T(8,128)S(1)} %maximum_bitcast_fusion), channel_id=1, source_target_pairs={{0,4},{4,0},{8,12},{12,8},{1,5},{5,1},{9,13},{13,9},{2,6},{6,2},{1... | collective-permute-start | bytes 215048 | tf_op jit(solution)/shard_map/ppermute | solution.py:160
  21.6 8.4 %collective-permute-start.4 = (f32[2,14,1280]{2,1,0:T(8,128)S(1)}, f32[2,14,1280]{2,1,0:T(8,128)S(1)}, u32[]{:S(2)}, u32[]{:S(2)}) collective-permute-start(f32[2,14,1280]{2,1,0:T(8,128)S(1)} %maximum_select_fusion.2), channel_id=1, source_target_pairs={{0,8},{4,12},{8,0},{12,4},{1,9},{5,13},{9,1},{13,5},{2,10},{6,14},... | collective-permute-start | bytes 430088 | tf_op jit(solution)/shard_map/ppermute | solution.py:160
  41.9 3.8 %collective-permute-start.5 = (f32[14,192]{1,0:T(8,128)S(1)}, f32[14,192]{1,0:T(8,128)S(1)}, u32[]{:S(2)}, u32[]{:S(2)}) collective-permute-start(f32[14,192]{1,0:T(8,128)S(1)} %reshape.272), channel_id=1, source_target_pairs={{0,16},{16,0},{1,17},{17,1},{2,18},{18,2},{3,19},{19,3},{4,20},{20... | collective-permute-start | bytes 32264 | tf_op jit(solution)/shard_map/ppermute | solution.py:168
  45.8 1.2 %collective-permute-start.6 = (f32[1,14,448]{2,1,0:T(8,128)S(1)}, f32[1,14,448]{2,1,0:T(8,128)S(1)}, u32[]{:S(2)}, u32[]{:S(2)}) collective-permute-start(f32[1,14,448]{2,1,0:T(8,128)S(1)} %maximum_bitcast_fusion.3), channel_id=1, source_target_pairs={{0,1},{1,0},{2,3},{3,2},{4,5},{5,4},{6,7},{7,6},{8,9},{9,8},{10,11... | collective-permute-start | bytes 75272 | tf_op jit(solution)/shard_map/ppermute | solution.py:160
  47.2 4.2 %collective-permute-start.7 = (f32[2,14,448]{2,0,1:T(2,128)S(1)}, f32[2,14,448]{2,0,1:T(2,128)S(1)}, u32[]{:S(2)}, u32[]{:S(2)}) collective-permute-start(f32[2,14,448]{2,0,1:T(2,128)S(1)} %maximum_select_fusion.7), channel_id=1, source_target_pairs={{0,2},{1,3},{2,0},{3,1},{4,6},{5,7},{6,4},{7,5},{8,10},{9,11},{10,... | collective-permute-start | bytes 150536 | tf_op jit(solution)/shard_map/ppermute | solution.py:160
  51.6 4.5 %collective-permute-start.8 = (f32[1,14,1280]{2,1,0:T(8,128)S(1)}, f32[1,14,1280]{2,1,0:T(8,128)S(1)}, u32[]{:S(2)}, u32[]{:S(2)}) collective-permute-start(f32[1,14,1280]{2,1,0:T(8,128)S(1)} %maximum_bitcast_fusion.1), channel_id=1, source_target_pairs={{0,4},{4,0},{8,12},{12,8},{1,5},{5,1},{9,13},{13,9},{2,6},{6,2},{1... | collective-permute-start | bytes 215048 | tf_op jit(solution)/shard_map/ppermute | solution.py:160
  56.2 8.5 %collective-permute-start.9 = (f32[2,14,1280]{2,1,0:T(8,128)S(1)}, f32[2,14,1280]{2,1,0:T(8,128)S(1)}, u32[]{:S(2)}, u32[]{:S(2)}) collective-permute-start(f32[2,14,1280]{2,1,0:T(8,128)S(1)} %maximum_select_fusion.3), channel_id=1, source_target_pairs={{0,8},{4,12},{8,0},{12,4},{1,9},{5,13},{9,1},{13,5},{2,10},{6,14},... | collective-permute-start | bytes 430088 | tf_op jit(solution)/shard_map/ppermute | solution.py:160

commit v5 on v4

--- a/solution.py
+++ b/solution.py
@@ -17,7 +17,7 @@
 HIGHEST = lax.Precision.HIGHEST
 
 
-def stencil_kernel(f_ref, up_ref, down_ref, left_ref, right_ref, base_ref, o_ref, *, first):
+def stencil_kernel(f_ref, up_ref, down_ref, left_ref, right_ref, base_ref, lon_ref, lat_ref, turn_ref, o_ref, *rest, first):
     planes, height, width = f_ref.shape
     comps = planes // 2
     row = lax.broadcasted_iota(jnp.int32, (height, width), 0)
@@ -83,13 +83,75 @@
         adv_u_6 = u1 * lat_6 + u2 * lon_6
         store(6, x6, -adv_u_6 + diffusivity * lap_of(6, x6, lap_6))
 
-
-def advance(field, up, down, left, right, base, first):
+    if first:
+        donate_planes(lambda k: o_ref[k], planes, lon_ref[...], lat_ref[...], turn_ref, rest[0])
+
+
+def advance(field, up, down, left, right, base, lon, lat, turn, first):
+    shape = jax.ShapeDtypeStruct(field.shape, field.dtype)
+    if first:
+        shape = (shape, jax.ShapeDtypeStruct((field.shape[0], lon.shape[1]), jnp.float32))
     return pl.pallas_call(
         functools.partial(stencil_kernel, first=first),
-        out_shape=jax.ShapeDtypeStruct(field.shape, field.dtype),
+        out_shape=shape,
         interpret=INTERPRET,
-    )(field, up, down, left, right, base)
+    )(field, up, down, left, right, base, lon, lat, turn)
+
+
+def donation_weights(cells_ref, frac_ref, rows, cols):
+    dons = cells_ref.shape[1]
+    cell = cells_ref[...].astype(jnp.float32)
+    row = jnp.floor((cell + 0.5) * (1.0 / (cols - 1)))
+    col = cell - row * (cols - 1)
+    row = row.astype(jnp.int32)
+    col = col.astype(jnp.int32)
+    frac_t = frac_ref[0:1, :]
+    frac_p = frac_ref[1:2, :]
+    col_ids = lax.broadcasted_iota(jnp.int32, (cols, dons), 0)
+    row_ids = lax.broadcasted_iota(jnp.int32, (rows, dons), 0)
+    weight_lon = jnp.where(col_ids == col, 1.0 - frac_p, 0.0) + jnp.where(col_ids == col + 1, frac_p, 0.0)
+    weight_lat = jnp.where(row_ids == row, 1.0 - frac_t, 0.0) + jnp.where(row_ids == row + 1, frac_t, 0.0)
+    return weight_lon, weight_lat
+
+
+def donate_planes(plane_of, planes, weight_lon, weight_lat, turn_ref, out_ref):
+    cosine = turn_ref[0:1, :]
+    sine = turn_ref[1:2, :]
+    values = []
+    for k in range(planes):
+        along = jnp.dot(plane_of(k), weight_lon, precision=HIGHEST, preferred_element_type=jnp.float32)
+        values.append(jnp.sum(along * weight_lat, axis=0, keepdims=True))
+    for k in range(planes):
+        comp, level = divmod(k, 2)
+        if comp in (1, 4):
+            value = cosine * values[k] - sine * values[k + 2]
+        elif comp in (2, 5):
+            value = sine * values[k - 2] + cosine * values[k]
+        else:
+            value = values[k]
+        out_ref[k : k + 1, :] = value
+
+
+def donation_kernel(f_ref, cells_ref, frac_ref, turn_ref, out_ref, lon_ref, lat_ref):
+    planes, rows, cols = f_ref.shape
+    weight_lon, weight_lat = donation_weights(cells_ref, frac_ref, rows, cols)
+    lon_ref[...] = weight_lon
+    lat_ref[...] = weight_lat
+    donate_planes(lambda k: f_ref[k], planes, weight_lon, weight_lat, turn_ref, out_ref)
+
+
+def first_donation(field, cells, frac, turn):
+    planes, rows, cols = field.shape
+    dons = cells.shape[1]
+    return pl.pallas_call(
+        donation_kernel,
+        out_shape=(
+            jax.ShapeDtypeStruct((planes, dons), jnp.float32),
+            jax.ShapeDtypeStruct((cols, dons), jnp.float32),
+            jax.ShapeDtypeStruct((rows, dons), jnp.float32),
+        ),
+        interpret=INTERPRET,
+    )(field, cells, frac, turn)
 
 
 def rotate(values, turn):
@@ -126,30 +188,13 @@
     on_left = lon_pos == 0
     on_right = lon_pos == lon_count - 1
 
-    row = cells // (cols - 1)
-    col = cells % (cols - 1)
-    col_ids = jnp.arange(cols, dtype=jnp.int32)[None, :]
-    row_ids = jnp.arange(rows, dtype=jnp.int32)[None, :]
-    weight_lon = jnp.where(col_ids == col[:, None], (1.0 - frac_p)[:, None], 0.0) + jnp.where(
-        col_ids == col[:, None] + 1, frac_p[:, None], 0.0
-    )
-    weight_lat = jnp.where(row_ids == row[:, None], (1.0 - frac_t)[:, None], 0.0) + jnp.where(
-        row_ids == row[:, None] + 1, frac_t[:, None], 0.0
-    )
-
     band = 2 * cols
     side = 2 * rows
     lat_slots = jnp.where(on_top, slots[0:band], slots[band : 2 * band])
     lon_slots = jnp.where(on_left, slots[2 * band : 2 * band + side], slots[2 * band + side :])
     wanted = jnp.concatenate([lat_slots, lon_slots])
-    total = lax.axis_size("lat") * lax.axis_size("lon") * cells.shape[0]
+    total = lat_count * lon_count * cells.shape[0]
     pick = (jnp.arange(total, dtype=jnp.int32)[:, None] == wanted[None, :]).astype(jnp.float32)
-
-    def donate(field):
-        flat = field.reshape(comps * levels, rows, cols)
-        along = jnp.einsum("kij,sj->kis", flat, weight_lon, precision=HIGHEST)
-        value = jnp.sum(along * weight_lat.T[None], axis=1)
-        return rotate(value.reshape(comps, levels, -1), turn).reshape(comps * levels, -1)
 
     def gather(packet, axis):
         size = lax.axis_size(axis)
@@ -163,9 +208,9 @@
             k *= 2
         return held
 
-    def section(field):
-        flat = field.reshape(comps * levels, rows, cols)
-        given = lax.ppermute(donate(field), "panel", [(0, 1), (1, 0)])
+    def section(field, donation):
+        flat = field
+        given = lax.ppermute(donation, "panel", [(0, 1), (1, 0)])
         dons = given.shape[1]
         side_cols = jnp.concatenate([flat[:, :, :2], flat[:, :, cols - 2 :]], axis=2)
         lon_packet = jnp.concatenate([given, side_cols.reshape(comps * levels, -1)], axis=1)
@@ -192,8 +237,10 @@
         return up, down, left, right
 
     field = state[0].reshape(comps * levels, rows, cols)
-    section_one = advance(field, *section(field), field, True)
-    new_field = advance(section_one, *section(section_one), field, False)
+    turn_parts = jnp.concatenate([jnp.cos(donor_turn[0, 0]), jnp.sin(donor_turn[0, 0])])
+    donation, lon_w, lat_w = first_donation(field, donor_cell[0, 0], donor_frac[0, 0, 0], turn_parts)
+    section_one, donation = advance(field, *section(field, donation), field, lon_w, lat_w, turn_parts, True)
+    new_field = advance(section_one, *section(section_one, donation), field, lon_w, lat_w, turn_parts, False)
     return new_field.reshape(1, comps, levels, rows, cols)
 
 

time: 73.7 us -> 69.4 us (0.942)
  matrix products: 7.57 us -> 3.45 us
  Pallas kernels: 6.88 us -> 10.1 us
  waiting for transfers between devices: 22.7 us -> 21.3 us
  other arithmetic: 3.9 us -> 2.95 us
  local copies, waits for them, and re-layouts: 17.6 us -> 16.7 us
    dot_general x2 -> x0, matrix products: 4.12 us -> none  [donate(): along = jnp.einsum('kij,sj->kis', flat, weight_lon, precision=HIGHEST)]
    pallas_call x0 -> x1, Pallas kernels: none -> 2.58 us  [first_donation(): pl.pallas_call(donation_kernel, out_shape=(jax.ShapeDtypeStruct((planes,...]
    ppermute x2, waiting for transfers between devices: 2.26 us -> 0.82 us  [section(): given = lax.ppermute(donation, 'panel', [(0, 1), (1, 0)])]
    slice x1 -> x0, local copies, waits for them, and re-layouts: 0.76 us -> none  [per_device(): frac_p = donor_frac[0, 0, 0, 1]]
  transfers between devices with their start and end apart: 10 -> 10, of which waited for: 9 -> 9; matrix products, arithmetic and copies ran while one was open for 13% -> 16% of each run, Pallas kernels for 0% -> 0%
where the time goes in v5:
time: 69.4 us; the launch traced here: 69 us
  waiting for transfers between devices  21.3 us (31%)
  local copies, waits for them, and re-layouts  16.7 us (24%)
  starting transfers between devices  14.1 us (20%)
  Pallas kernels  10.1 us (15%)
  matrix products  3.45 us (5%)
  other arithmetic  2.95 us (4%)
    ppermute x8, waiting for transfers between devices, gather(): other = lax.ppermute(held, axis, [(i, i ^ k) for i in range(size)])  20.5 us
    ppermute x8, starting transfers between devices, gather(): other = lax.ppermute(held, axis, [(i, i ^ k) for i in range(size)])  10.2 us
    pallas_call x2, Pallas kernels, advance(): pl.pallas_call(functools.partial(stencil_kernel, first=first), out_shape=...  7.48 us
    ppermute x2, starting transfers between devices, section(): given = lax.ppermute(donation, 'panel', [(0, 1), (1, 0)])  3.88 us
    reshape x2, local copies, waits for them, and re-layouts, section(): side_cols = lon_all[:, :, dons:].reshape(lon_count, comps, levels, rows, 4)  3.83 us
    dot_general x2, matrix products, section(): rim = jnp.dot(partner, pick, precision=HIGHEST).reshape(comps, levels, -1)  3.45 us
    slice x2, local copies, waits for them, and re-layouts, section(): side_cols = jnp.concatenate([flat[:, :, :2], flat[:, :, cols - 2:]], axis=2)  2.79 us
    pallas_call x1, Pallas kernels, first_donation(): pl.pallas_call(donation_kernel, out_shape=(jax.ShapeDtypeStruct((planes,...  2.58 us
  transfers between devices with their start and end apart: 10, of which 9 were waited for; matrix products, arithmetic and copies ran while one was open for 16% of the time, Pallas kernels for 0%

profile of v5, /device:TPU:0, one launch (start us, length us, event | category | flops | bytes accessed | tf_op | source)
XLA Modules:
  0.0 69.0 jit_solution(2784920249964851436)
XLA Ops:
  1.3 2.6 %shard_map.55 = (f32[14,192]{1,0:T(8,128)}, f32[128,192]{1,0:T(8,128)}, f32[64,192]{1,0:T(8,128)}) custom-call(f32[14,64,128]{2,1,0:T(8,128)} %bitcast.81, s32[1,192]{1,0:T(1,128)} %bitcast.107, f32[2,192]{1,0:T(2,128)} %bitcast.106, f32[2,192]{1,0:T(2,128)} %pad_maximum_fusion.4.turn_ref), custom_call_target="tpu_custom_call" | custom-call | tf_op jit(solution)/shard_map/pallas_call | solution.py:146
  3.9 3.0 %collective-permute-start = (f32[14,192]{1,0:T(8,128)}, f32[14,192]{1,0:T(8,128)S(1)}, u32[]{:S(2)}, u32[]{:S(2)}) collective-permute-start(f32[14,192]{1,0:T(8,128)} %get-tuple-element.10), channel_id=1, source_target_pairs={{0,16},{16,0},{1,17},{17,1},{2,18},{18,2},{3,19},{19,3},{4,20},{20... | collective-permute-start | bytes 32264 | tf_op jit(solution)/shard_map/ppermute | solution.py:213
  7.7 1.4 %fusion.12 = (f32[14,64,2]{2,1,0:T(8,128)S(1)}, f32[14,64,2]{2,1,0:T(8,128)S(1)}) fusion(f32[14,64,128]{2,1,0:T(8,128)} %bitcast.83), kind=kLoop, calls=%fused_computation.53 | loop fusion | bytes 28672 | tf_op jit(solution)/shard_map/slice | solution.py:215
  10.1 1.1 %collective-permute-done.1 = f32[1,14,448]{2,1,0:T(8,128)S(1)} collective-permute-done((f32[1,14,448]{2,1,0:T(8,128)S(1)}, f32[1,14,448]{2,1,0:T(8,128)S(1)}, u32[]{:S(2)}, u32[]{:S(2)}) %collective-permute-start.1) | collective-permute-done | bytes 25120 | tf_op jit(solution)/shard_map/ppermute | solution.py:205
  11.3 1.5 %collective-permute-start.2 = (f32[2,14,448]{2,0,1:T(2,128)S(1)}, f32[2,14,448]{2,0,1:T(2,128)S(1)}, u32[]{:S(2)}, u32[]{:S(2)}) collective-permute-start(f32[2,14,448]{2,0,1:T(2,128)S(1)} %maximum_select_fusion.6), channel_id=1, source_target_pairs={{0,2},{1,3},{2,0},{3,1},{4,6},{5,7},{6,4},{7,5},{8,10},{9,11},{10,... | collective-permute-start | bytes 150536 | tf_op jit(solution)/shard_map/ppermute | solution.py:205
  13.0 2.6 %collective-permute-done.2 = f32[2,14,448]{2,0,1:T(2,128)S(1)} collective-permute-done((f32[2,14,448]{2,0,1:T(2,128)S(1)}, f32[2,14,448]{2,0,1:T(2,128)S(1)}, u32[]{:S(2)}, u32[]{:S(2)}) %collective-permute-start.2) | collective-permute-done | bytes 50208 | tf_op jit(solution)/shard_map/ppermute | solution.py:205
  15.8 1.6 %collective-permute-start.3 = (f32[1,14,1280]{2,1,0:T(8,128)S(1)}, f32[1,14,1280]{2,1,0:T(8,128)S(1)}, u32[]{:S(2)}, u32[]{:S(2)}) collective-permute-start(f32[1,14,1280]{2,1,0:T(8,128)S(1)} %maximum_bitcast_fusion), channel_id=1, source_target_pairs={{0,4},{4,0},{8,12},{12,8},{1,5},{5,1},{9,13},{13,9},{2,6},{6,2},{1... | collective-permute-start | bytes 215048 | tf_op jit(solution)/shard_map/ppermute | solution.py:205
  17.4 2.9 %collective-permute-done.3 = f32[1,14,1280]{2,1,0:T(8,128)S(1)} collective-permute-done((f32[1,14,1280]{2,1,0:T(8,128)S(1)}, f32[1,14,1280]{2,1,0:T(8,128)S(1)}, u32[]{:S(2)}, u32[]{:S(2)}) %collective-permute-start.3) | collective-permute-done | bytes 71712 | tf_op jit(solution)/shard_map/ppermute | solution.py:205
  20.3 2.6 %collective-permute-start.4 = (f32[2,14,1280]{2,1,0:T(8,128)S(1)}, f32[2,14,1280]{2,1,0:T(8,128)S(1)}, u32[]{:S(2)}, u32[]{:S(2)}) collective-permute-start(f32[2,14,1280]{2,1,0:T(8,128)S(1)} %maximum_select_fusion.2), channel_id=1, source_target_pairs={{0,8},{4,12},{8,0},{12,4},{1,9},{5,13},{9,1},{13,5},{2,10},{6,14},... | collective-permute-start | bytes 430088 | tf_op jit(solution)/shard_map/ppermute | solution.py:205
  23.1 1.9 %reshape.120 = f32[4,7,2,64,4]{4,3,0,2,1:T(8,128)S(1)} reshape(f32[4,14,256]{2,0,1:T(4,128)S(1)} %slice.143) | data formatting | bytes 114688 | tf_op jit(solution)/shard_map/reshape | solution.py:219
  25.5 3.3 %collective-permute-done.4 = f32[2,14,1280]{2,1,0:T(8,128)S(1)} collective-permute-done((f32[2,14,1280]{2,1,0:T(8,128)S(1)}, f32[2,14,1280]{2,1,0:T(8,128)S(1)}, u32[]{:S(2)}, u32[]{:S(2)}) %collective-permute-start.4) | collective-permute-done | bytes 143392 | tf_op jit(solution)/shard_map/ppermute | solution.py:205
  29.1 1.7 %fusion.3 = f32[7,2,384]{2,0,1:T(8,128)S(1)} fusion(s32[384]{0:T(512)S(1)} %pad_add_fusion, f32[7,2,3072]{2,1,0:T(2,128)S(1)} %dot_general.10), kind=kOutput, calls=%fused_computation.3 | convolution fusion | flops 199360512 | bytes 195072 | tf_op jit(solution)/shard_map/dot_general | solution.py:230
  31.1 1.0 %copy.86 = f32[7,2,64,2]{3,2,1,0:T(8,128)} copy(f32[7,2,64,2]{2,3,1,0:T(2,128)S(1)} %get-tuple-element.35) | data formatting | bytes 14336 | tf_op jit(solution)/shard_map/jit(_where)/select_n | solution.py:236
  33.7 4.0 %shard_map.56 = (f32[14,64,128]{2,1,0:T(8,128)}, f32[14,192]{1,0:T(8,128)}) custom-call(f32[14,64,128]{2,1,0:T(8,128)} %bitcast.84, f32[14,2,128]{2,1,0:T(2,128)} %bitcast.102, f32[14,2,128]{2,1,0:T(2,128)} %bitcast.101, f32[14,64,2]{2,1,0:T(8,128)} %bitcast.88, f32[14,64,2]{2,1,0:T(8,128)} %bitcast.87, f32[14,64,128]{2,1,0:T(8,128)} %bitcast.85, ...), custom_call_target="tpu_custom_call" | custom-call | tf_op jit(solution)/shard_map/pallas_call | solution.py:94
  38.6 1.4 %fusion.10 = (f32[14,64,2]{2,1,0:T(8,128)S(1)}, f32[14,64,2]{2,1,0:T(8,128)S(1)}) fusion(f32[14,64,128]{2,1,0:T(8,128)} %get-tuple-element.13.f_ref), kind=kLoop, calls=%fused_computation.51 | loop fusion | bytes 28672 | tf_op jit(solution)/shard_map/slice | solution.py:215
  43.1 1.5 %collective-permute-start.7 = (f32[2,14,448]{2,0,1:T(2,128)S(1)}, f32[2,14,448]{2,0,1:T(2,128)S(1)}, u32[]{:S(2)}, u32[]{:S(2)}) collective-permute-start(f32[2,14,448]{2,0,1:T(2,128)S(1)} %maximum_select_fusion.7), channel_id=1, source_target_pairs={{0,2},{1,3},{2,0},{3,1},{4,6},{5,7},{6,4},{7,5},{8,10},{9,11},{10,... | collective-permute-start | bytes 150536 | tf_op jit(solution)/shard_map/ppermute | solution.py:205
  44.7 2.6 %collective-permute-done.7 = f32[2,14,448]{2,0,1:T(2,128)S(1)} collective-permute-done((f32[2,14,448]{2,0,1:T(2,128)S(1)}, f32[2,14,448]{2,0,1:T(2,128)S(1)}, u32[]{:S(2)}, u32[]{:S(2)}) %collective-permute-start.7) | collective-permute-done | bytes 50208 | tf_op jit(solution)/shard_map/ppermute | solution.py:205
  48.3 3.8 %collective-permute-done.8 = f32[1,14,1280]{2,1,0:T(8,128)S(1)} collective-permute-done((f32[1,14,1280]{2,1,0:T(8,128)S(1)}, f32[1,14,1280]{2,1,0:T(8,128)S(1)}, u32[]{:S(2)}, u32[]{:S(2)}) %collective-permute-start.8) | collective-permute-done | bytes 71712 | tf_op jit(solution)/shard_map/ppermute | solution.py:205
  52.1 2.1 %collective-permute-start.9 = (f32[2,14,1280]{2,1,0:T(8,128)S(1)}, f32[2,14,1280]{2,1,0:T(8,128)S(1)}, u32[]{:S(2)}, u32[]{:S(2)}) collective-permute-start(f32[2,14,1280]{2,1,0:T(8,128)S(1)} %maximum_select_fusion.3), channel_id=1, source_target_pairs={{0,8},{4,12},{8,0},{12,4},{1,9},{5,13},{9,1},{13,5},{2,10},{6,14},... | collective-permute-start | bytes 430088 | tf_op jit(solution)/shard_map/ppermute | solution.py:205
  54.2 1.9 %reshape.131 = f32[4,7,2,64,4]{4,3,0,2,1:T(8,128)S(1)} reshape(f32[4,14,256]{2,0,1:T(4,128)S(1)} %slice.153) | data formatting | bytes 114688 | tf_op jit(solution)/shard_map/reshape | solution.py:219
  56.7 3.9 %collective-permute-done.9 = f32[2,14,1280]{2,1,0:T(8,128)S(1)} collective-permute-done((f32[2,14,1280]{2,1,0:T(8,128)S(1)}, f32[2,14,1280]{2,1,0:T(8,128)S(1)}, u32[]{:S(2)}, u32[]{:S(2)}) %collective-permute-start.9) | collective-permute-done | bytes 143392 | tf_op jit(solution)/shard_map/ppermute | solution.py:205
  60.9 1.7 %fusion.1 = f32[7,2,384]{2,0,1:T(8,128)S(1)} fusion(s32[384]{0:T(512)S(1)} %pad_add_fusion, f32[7,2,3072]{2,1,0:T(2,128)S(1)} %dot_general.12), kind=kOutput, calls=%fused_computation.2 | convolution fusion | flops 199360512 | bytes 195072 | tf_op jit(solution)/shard_map/dot_general | solution.py:230
  62.9 1.0 %copy.101 = f32[7,2,64,2]{3,2,1,0:T(8,128)} copy(f32[7,2,64,2]{2,3,1,0:T(2,128)S(1)} %get-tuple-element.31) | data formatting | bytes 14336 | tf_op jit(solution)/shard_map/jit(_where)/select_n | solution.py:236
  65.5 3.5 %shard_map.57 = f32[14,64,128]{2,1,0:T(8,128)} custom-call(f32[14,64,128]{2,1,0:T(8,128)} %get-tuple-element.13.f_ref, f32[14,2,128]{2,1,0:T(2,128)} %bitcast.104, f32[14,2,128]{2,1,0:T(2,128)} %bitcast.103, f32[14,64,2]{2,1,0:T(8,128)} %bitcast.90, f32[14,64,2]{2,1,0:T(8,128)} %bitcast.89, f32[14,64,128]{2,1,0:T(8,128)} %bitcast.86, ...), custom_call_target="tpu_custom_call" | custom-call | tf_op jit(solution)/shard_map/pallas_call | solution.py:94
  (84 shorter events, 13.8 us)
Async XLA Ops:
  3.9 6.0 %collective-permute-start = (f32[14,192]{1,0:T(8,128)}, f32[14,192]{1,0:T(8,128)S(1)}, u32[]{:S(2)}, u32[]{:S(2)}) collective-permute-start(f32[14,192]{1,0:T(8,128)} %get-tuple-element.10), channel_id=1, source_target_pairs={{0,16},{16,0},{1,17},{17,1},{2,18},{18,2},{3,19},{19,3},{4,20},{20... | collective-permute-start | bytes 32264 | tf_op jit(solution)/shard_map/ppermute | solution.py:213
  7.7 2.3 %copy-start = (s32[1,1,1,768]{3,2,1,0:T(1,128)S(1)}, s32[1,1,1,768]{3,2,1,0:T(1,128)}, u32[]{:S(2)}) copy-start(s32[1,1,1,768]{3,2,1,0:T(1,128)} %param.6) | copy-start | bytes 9220
  10.0 1.2 %collective-permute-start.1 = (f32[1,14,448]{2,1,0:T(8,128)S(1)}, f32[1,14,448]{2,1,0:T(8,128)S(1)}, u32[]{:S(2)}, u32[]{:S(2)}) collective-permute-start(f32[1,14,448]{2,1,0:T(8,128)S(1)} %maximum_bitcast_fusion.2), channel_id=1, source_target_pairs={{0,1},{1,0},{2,3},{3,2},{4,5},{5,4},{6,7},{7,6},{8,9},{9,8},{10,11... | collective-permute-start | bytes 75272 | tf_op jit(solution)/shard_map/ppermute | solution.py:205
  11.3 4.2 %collective-permute-start.2 = (f32[2,14,448]{2,0,1:T(2,128)S(1)}, f32[2,14,448]{2,0,1:T(2,128)S(1)}, u32[]{:S(2)}, u32[]{:S(2)}) collective-permute-start(f32[2,14,448]{2,0,1:T(2,128)S(1)} %maximum_select_fusion.6), channel_id=1, source_target_pairs={{0,2},{1,3},{2,0},{3,1},{4,6},{5,7},{6,4},{7,5},{8,10},{9,11},{10,... | collective-permute-start | bytes 150536 | tf_op jit(solution)/shard_map/ppermute | solution.py:205
  15.8 4.5 %collective-permute-start.3 = (f32[1,14,1280]{2,1,0:T(8,128)S(1)}, f32[1,14,1280]{2,1,0:T(8,128)S(1)}, u32[]{:S(2)}, u32[]{:S(2)}) collective-permute-start(f32[1,14,1280]{2,1,0:T(8,128)S(1)} %maximum_bitcast_fusion), channel_id=1, source_target_pairs={{0,4},{4,0},{8,12},{12,8},{1,5},{5,1},{9,13},{13,9},{2,6},{6,2},{1... | collective-permute-start | bytes 215048 | tf_op jit(solution)/shard_map/ppermute | solution.py:205
  20.3 8.4 %collective-permute-start.4 = (f32[2,14,1280]{2,1,0:T(8,128)S(1)}, f32[2,14,1280]{2,1,0:T(8,128)S(1)}, u32[]{:S(2)}, u32[]{:S(2)}) collective-permute-start(f32[2,14,1280]{2,1,0:T(8,128)S(1)} %maximum_select_fusion.2), channel_id=1, source_target_pairs={{0,8},{4,12},{8,0},{12,4},{1,9},{5,13},{9,1},{13,5},{2,10},{6,14},... | collective-permute-start | bytes 430088 | tf_op jit(solution)/shard_map/ppermute | solution.py:205
  37.7 3.9 %collective-permute-start.5 = (f32[14,192]{1,0:T(8,128)}, f32[14,192]{1,0:T(8,128)S(1)}, u32[]{:S(2)}, u32[]{:S(2)}) collective-permute-start(f32[14,192]{1,0:T(8,128)} %get-tuple-element.14), channel_id=1, source_target_pairs={{0,16},{16,0},{1,17},{17,1},{2,18},{18,2},{3,19},{19,3},{4,20},{20... | collective-permute-start | bytes 32264 | tf_op jit(solution)/shard_map/ppermute | solution.py:213
  41.7 1.2 %collective-permute-start.6 = (f32[1,14,448]{2,1,0:T(8,128)S(1)}, f32[1,14,448]{2,1,0:T(8,128)S(1)}, u32[]{:S(2)}, u32[]{:S(2)}) collective-permute-start(f32[1,14,448]{2,1,0:T(8,128)S(1)} %maximum_bitcast_fusion.3), channel_id=1, source_target_pairs={{0,1},{1,0},{2,3},{3,2},{4,5},{5,4},{6,7},{7,6},{8,9},{9,8},{10,11... | collective-permute-start | bytes 75272 | tf_op jit(solution)/shard_map/ppermute | solution.py:205
  43.1 4.2 %collective-permute-start.7 = (f32[2,14,448]{2,0,1:T(2,128)S(1)}, f32[2,14,448]{2,0,1:T(2,128)S(1)}, u32[]{:S(2)}, u32[]{:S(2)}) collective-permute-start(f32[2,14,448]{2,0,1:T(2,128)S(1)} %maximum_select_fusion.7), channel_id=1, source_target_pairs={{0,2},{1,3},{2,0},{3,1},{4,6},{5,7},{6,4},{7,5},{8,10},{9,11},{10,... | collective-permute-start | bytes 150536 | tf_op jit(solution)/shard_map/ppermute | solution.py:205
  47.5 4.5 %collective-permute-start.8 = (f32[1,14,1280]{2,1,0:T(8,128)S(1)}, f32[1,14,1280]{2,1,0:T(8,128)S(1)}, u32[]{:S(2)}, u32[]{:S(2)}) collective-permute-start(f32[1,14,1280]{2,1,0:T(8,128)S(1)} %maximum_bitcast_fusion.1), channel_id=1, source_target_pairs={{0,4},{4,0},{8,12},{12,8},{1,5},{5,1},{9,13},{13,9},{2,6},{6,2},{1... | collective-permute-start | bytes 215048 | tf_op jit(solution)/shard_map/ppermute | solution.py:205
  52.1 8.5 %collective-permute-start.9 = (f32[2,14,1280]{2,1,0:T(8,128)S(1)}, f32[2,14,1280]{2,1,0:T(8,128)S(1)}, u32[]{:S(2)}, u32[]{:S(2)}) collective-permute-start(f32[2,14,1280]{2,1,0:T(8,128)S(1)} %maximum_select_fusion.3), channel_id=1, source_target_pairs={{0,8},{4,12},{8,0},{12,4},{1,9},{5,13},{9,1},{13,5},{2,10},{6,14},... | collective-permute-start | bytes 430088 | tf_op jit(solution)/shard_map/ppermute | solution.py:205

commit v6 on v5

--- a/solution.py
+++ b/solution.py
@@ -23,12 +23,32 @@
     row = lax.broadcasted_iota(jnp.int32, (height, width), 0)
     col = lax.broadcasted_iota(jnp.int32, (height, width), 1)
 
+    eye = jnp.where(
+        lax.broadcasted_iota(jnp.int32, (height, height), 0) == lax.broadcasted_iota(jnp.int32, (height, height), 1),
+        1.0,
+        0.0,
+    )
+    pick_row = lax.broadcasted_iota(jnp.int32, (width, height), 0)
+
+    def columns(k):
+        left = left_ref[k]
+        right = right_ref[k]
+        rows_of = jnp.where(
+            pick_row == 0,
+            left[0:1, :],
+            jnp.where(pick_row == 1, left[1:2, :], jnp.where(pick_row == 2, right[0:1, :], jnp.where(pick_row == 3, right[1:2, :], 0.0))),
+        )
+        return lax.dot_general(
+            eye, rows_of, (((1,), (1,)), ((), ())), precision=HIGHEST, preferred_element_type=jnp.float32
+        )
+
     def terms(k):
         x = f_ref[k]
         up = up_ref[k]
         down = down_ref[k]
-        left = left_ref[k]
-        right = right_ref[k]
+        sides = columns(k)
+        left = sides[:, 0:2]
+        right = sides[:, 2:4]
         lat_m1 = jnp.where(row == 0, up[1:2, :], pltpu.roll(x, 1, 0))
         lat_m2 = jnp.where(row == 0, up[0:1, :], jnp.where(row == 1, up[1:2, :], pltpu.roll(x, 2, 0)))
         lat_p1 = jnp.where(row == height - 1, down[0:1, :], pltpu.roll(x, height - 1, 0))
@@ -232,8 +252,8 @@
         rim_lon = jnp.transpose(rim[:, :, band:].reshape(comps, levels, 2, rows), (0, 1, 3, 2))
         up = jnp.where(on_top, rim_lat, up).reshape(comps * levels, 2, cols)
         down = jnp.where(on_bottom, rim_lat, down).reshape(comps * levels, 2, cols)
-        left = jnp.where(on_left, rim_lon, left).reshape(comps * levels, rows, 2)
-        right = jnp.where(on_right, rim_lon, right).reshape(comps * levels, rows, 2)
+        left = jnp.swapaxes(jnp.where(on_left, rim_lon, left).reshape(comps * levels, rows, 2), 1, 2)
+        right = jnp.swapaxes(jnp.where(on_right, rim_lon, right).reshape(comps * levels, rows, 2), 1, 2)
         return up, down, left, right
 
     field = state[0].reshape(comps * levels, rows, cols)

time: 69.4 us -> 66.7 us (0.961)
  local copies, waits for them, and re-layouts: 16.7 us -> 12.7 us
  other arithmetic: 2.95 us -> 4.16 us
    select_n x4 -> x0, local copies, waits for them, and re-layouts: 4.06 us -> none  [the longest x2 2.05 us: section(): right = jnp.where(on_right, rim_lon, right).reshape(comps * levels, rows, 2)]
    select_n x2, other arithmetic: 0.04 us -> 1.25 us  [section(): jnp.where(on_right, rim_lon, right).reshape(comps * levels, rows, 2)]
  transfers between devices with their start and end apart: 10 -> 10, of which waited for: 9 -> 9; matrix products, arithmetic and copies ran while one was open for 16% -> 17% of each run, Pallas kernels for 0% -> 0%
where the time goes in v6:
time: 66.7 us; the launch traced here: 66.4 us
  waiting for transfers between devices  21.4 us (32%)
  starting transfers between devices  14 us (21%)
  local copies, waits for them, and re-layouts  12.7 us (19%)
  Pallas kernels  10 us (15%)
  other arithmetic  4.16 us (6%)
  matrix products  3.62 us (5%)
    ppermute x8, waiting for transfers between devices, gather(): other = lax.ppermute(held, axis, [(i, i ^ k) for i in range(size)])  20.5 us
    ppermute x8, starting transfers between devices, gather(): other = lax.ppermute(held, axis, [(i, i ^ k) for i in range(size)])  10.2 us
    pallas_call x2, Pallas kernels, advance(): pl.pallas_call(functools.partial(stencil_kernel, first=first), out_shape=...  7.44 us
    ppermute x2, starting transfers between devices, section(): given = lax.ppermute(donation, 'panel', [(0, 1), (1, 0)])  3.83 us
    reshape x2, local copies, waits for them, and re-layouts, section(): side_cols = lon_all[:, :, dons:].reshape(lon_count, comps, levels, rows, 4)  3.83 us
    dot_general x2, matrix products, section(): rim = jnp.dot(partner, pick, precision=HIGHEST).reshape(comps, levels, -1)  3.62 us
    slice x2, local copies, waits for them, and re-layouts, section(): side_cols = jnp.concatenate([flat[:, :, :2], flat[:, :, cols - 2:]], axis=2)  2.83 us
    pallas_call x1, Pallas kernels, first_donation(): pl.pallas_call(donation_kernel, out_shape=(jax.ShapeDtypeStruct((planes,...  2.58 us
  transfers between devices with their start and end apart: 10, of which 9 were waited for; matrix products, arithmetic and copies ran while one was open for 17% of the time, Pallas kernels for 0%

profile of v6, /device:TPU:0, one launch (start us, length us, event | category | flops | bytes accessed | tf_op | source)
XLA Modules:
  0.0 66.4 jit_solution(2953360319338715455)
XLA Ops:
  1.3 2.6 %shard_map.55 = (f32[14,192]{1,0:T(8,128)}, f32[128,192]{1,0:T(8,128)}, f32[64,192]{1,0:T(8,128)}) custom-call(f32[14,64,128]{2,1,0:T(8,128)} %bitcast.89, s32[1,192]{1,0:T(1,128)} %bitcast.115, f32[2,192]{1,0:T(2,128)} %bitcast.114, f32[2,192]{1,0:T(2,128)} %pad_maximum_fusion.4.turn_ref), custom_call_target="tpu_custom_call" | custom-call | tf_op jit(solution)/shard_map/pallas_call | solution.py:166
  3.9 3.0 %collective-permute-start = (f32[14,192]{1,0:T(8,128)}, f32[14,192]{1,0:T(8,128)S(1)}, u32[]{:S(2)}, u32[]{:S(2)}) collective-permute-start(f32[14,192]{1,0:T(8,128)} %get-tuple-element.10), channel_id=1, source_target_pairs={{0,16},{16,0},{1,17},{17,1},{2,18},{18,2},{3,19},{19,3},{4,20},{20... | collective-permute-start | bytes 32264 | tf_op jit(solution)/shard_map/ppermute | solution.py:233
  7.7 1.4 %fusion.12 = (f32[14,64,2]{2,1,0:T(8,128)S(1)}, f32[14,64,2]{2,1,0:T(8,128)S(1)}) fusion(f32[14,64,128]{2,1,0:T(8,128)} %bitcast.91), kind=kLoop, calls=%fused_computation.53 | loop fusion | bytes 28672 | tf_op jit(solution)/shard_map/slice | solution.py:235
  10.1 1.1 %collective-permute-done.1 = f32[1,14,448]{2,1,0:T(8,128)S(1)} collective-permute-done((f32[1,14,448]{2,1,0:T(8,128)S(1)}, f32[1,14,448]{2,1,0:T(8,128)S(1)}, u32[]{:S(2)}, u32[]{:S(2)}) %collective-permute-start.1) | collective-permute-done | bytes 25120 | tf_op jit(solution)/shard_map/ppermute | solution.py:225
  11.4 1.5 %collective-permute-start.2 = (f32[2,14,448]{2,0,1:T(2,128)S(1)}, f32[2,14,448]{2,0,1:T(2,128)S(1)}, u32[]{:S(2)}, u32[]{:S(2)}) collective-permute-start(f32[2,14,448]{2,0,1:T(2,128)S(1)} %maximum_select_fusion.6), channel_id=1, source_target_pairs={{0,2},{1,3},{2,0},{3,1},{4,6},{5,7},{6,4},{7,5},{8,10},{9,11},{10,... | collective-permute-start | bytes 150536 | tf_op jit(solution)/shard_map/ppermute | solution.py:225
  13.0 2.6 %collective-permute-done.2 = f32[2,14,448]{2,0,1:T(2,128)S(1)} collective-permute-done((f32[2,14,448]{2,0,1:T(2,128)S(1)}, f32[2,14,448]{2,0,1:T(2,128)S(1)}, u32[]{:S(2)}, u32[]{:S(2)}) %collective-permute-start.2) | collective-permute-done | bytes 50208 | tf_op jit(solution)/shard_map/ppermute | solution.py:225
  15.8 1.6 %collective-permute-start.3 = (f32[1,14,1280]{2,1,0:T(8,128)S(1)}, f32[1,14,1280]{2,1,0:T(8,128)S(1)}, u32[]{:S(2)}, u32[]{:S(2)}) collective-permute-start(f32[1,14,1280]{2,1,0:T(8,128)S(1)} %maximum_bitcast_fusion), channel_id=1, source_target_pairs={{0,4},{4,0},{8,12},{12,8},{1,5},{5,1},{9,13},{13,9},{2,6},{6,2},{1... | collective-permute-start | bytes 215048 | tf_op jit(solution)/shard_map/ppermute | solution.py:225
  17.5 2.9 %collective-permute-done.3 = f32[1,14,1280]{2,1,0:T(8,128)S(1)} collective-permute-done((f32[1,14,1280]{2,1,0:T(8,128)S(1)}, f32[1,14,1280]{2,1,0:T(8,128)S(1)}, u32[]{:S(2)}, u32[]{:S(2)}) %collective-permute-start.3) | collective-permute-done | bytes 71712 | tf_op jit(solution)/shard_map/ppermute | solution.py:225
  20.4 2.6 %collective-permute-start.4 = (f32[2,14,1280]{2,1,0:T(8,128)S(1)}, f32[2,14,1280]{2,1,0:T(8,128)S(1)}, u32[]{:S(2)}, u32[]{:S(2)}) collective-permute-start(f32[2,14,1280]{2,1,0:T(8,128)S(1)} %maximum_select_fusion.2), channel_id=1, source_target_pairs={{0,8},{4,12},{8,0},{12,4},{1,9},{5,13},{9,1},{13,5},{2,10},{6,14},... | collective-permute-start | bytes 430088 | tf_op jit(solution)/shard_map/ppermute | solution.py:225
  23.1 1.9 %reshape.120 = f32[4,7,2,64,4]{4,3,0,2,1:T(8,128)S(1)} reshape(f32[4,14,256]{2,0,1:T(4,128)S(1)} %slice.143) | data formatting | bytes 114688 | tf_op jit(solution)/shard_map/reshape | solution.py:239
  25.5 3.3 %collective-permute-done.4 = f32[2,14,1280]{2,1,0:T(8,128)S(1)} collective-permute-done((f32[2,14,1280]{2,1,0:T(8,128)S(1)}, f32[2,14,1280]{2,1,0:T(8,128)S(1)}, u32[]{:S(2)}, u32[]{:S(2)}) %collective-permute-start.4) | collective-permute-done | bytes 143392 | tf_op jit(solution)/shard_map/ppermute | solution.py:225
  29.1 1.7 %fusion.3 = f32[7,2,384]{2,0,1:T(8,128)S(1)} fusion(s32[384]{0:T(512)S(1)} %pad_add_fusion, f32[7,2,3072]{2,1,0:T(2,128)S(1)} %dot_general.10), kind=kOutput, calls=%fused_computation.3 | convolution fusion | flops 199360512 | bytes 195072 | tf_op jit(solution)/shard_map/dot_general | solution.py:250
  32.3 3.9 %shard_map.56 = (f32[14,64,128]{2,1,0:T(8,128)}, f32[14,192]{1,0:T(8,128)}) custom-call(f32[14,64,128]{2,1,0:T(8,128)} %bitcast.92, f32[14,2,128]{2,1,0:T(2,128)} %bitcast.108, f32[14,2,128]{2,1,0:T(2,128)} %bitcast.107, f32[14,2,64]{2,1,0:T(2,128)} %bitcast.112, f32[14,2,64]{2,1,0:T(2,128)} %bitcast.111, f32[14,64,128]{2,1,0:T(8,128)} %bitcast.93, ...), custom_call_target="tpu_custom_call" | custom-call | tf_op jit(solution)/shard_map/pallas_call | solution.py:114
  36.3 0.9 %collective-permute-start.5 = (f32[14,192]{1,0:T(8,128)}, f32[14,192]{1,0:T(8,128)S(1)}, u32[]{:S(2)}, u32[]{:S(2)}) collective-permute-start(f32[14,192]{1,0:T(8,128)} %get-tuple-element.14), channel_id=1, source_target_pairs={{0,16},{16,0},{1,17},{17,1},{2,18},{18,2},{3,19},{19,3},{4,20},{20... | collective-permute-start | bytes 32264 | tf_op jit(solution)/shard_map/ppermute | solution.py:233
  37.1 1.4 %fusion.10 = (f32[14,64,2]{2,1,0:T(8,128)S(1)}, f32[14,64,2]{2,1,0:T(8,128)S(1)}) fusion(f32[14,64,128]{2,1,0:T(8,128)} %get-tuple-element.13.f_ref), kind=kLoop, calls=%fused_computation.51 | loop fusion | bytes 28672 | tf_op jit(solution)/shard_map/slice | solution.py:235
  40.3 0.9 %fusion.11 = (f32[14,2,128]{2,1,0:T(2,128)S(1)}, f32[14,2,128]{2,1,0:T(2,128)S(1)}) fusion(f32[14,64,128]{2,1,0:T(8,128)} %get-tuple-element.13.f_ref), kind=kLoop, calls=%fused_computation.52 | loop fusion | bytes 57344 | tf_op jit(solution)/shard_map/slice | solution.py:240
  41.6 1.5 %collective-permute-start.7 = (f32[2,14,448]{2,0,1:T(2,128)S(1)}, f32[2,14,448]{2,0,1:T(2,128)S(1)}, u32[]{:S(2)}, u32[]{:S(2)}) collective-permute-start(f32[2,14,448]{2,0,1:T(2,128)S(1)} %maximum_select_fusion.7), channel_id=1, source_target_pairs={{0,2},{1,3},{2,0},{3,1},{4,6},{5,7},{6,4},{7,5},{8,10},{9,11},{10,... | collective-permute-start | bytes 150536 | tf_op jit(solution)/shard_map/ppermute | solution.py:225
  43.2 2.7 %collective-permute-done.7 = f32[2,14,448]{2,0,1:T(2,128)S(1)} collective-permute-done((f32[2,14,448]{2,0,1:T(2,128)S(1)}, f32[2,14,448]{2,0,1:T(2,128)S(1)}, u32[]{:S(2)}, u32[]{:S(2)}) %collective-permute-start.7) | collective-permute-done | bytes 50208 | tf_op jit(solution)/shard_map/ppermute | solution.py:225
  46.8 3.8 %collective-permute-done.8 = f32[1,14,1280]{2,1,0:T(8,128)S(1)} collective-permute-done((f32[1,14,1280]{2,1,0:T(8,128)S(1)}, f32[1,14,1280]{2,1,0:T(8,128)S(1)}, u32[]{:S(2)}, u32[]{:S(2)}) %collective-permute-start.8) | collective-permute-done | bytes 71712 | tf_op jit(solution)/shard_map/ppermute | solution.py:225
  50.6 2.1 %collective-permute-start.9 = (f32[2,14,1280]{2,1,0:T(8,128)S(1)}, f32[2,14,1280]{2,1,0:T(8,128)S(1)}, u32[]{:S(2)}, u32[]{:S(2)}) collective-permute-start(f32[2,14,1280]{2,1,0:T(8,128)S(1)} %maximum_select_fusion.3), channel_id=1, source_target_pairs={{0,8},{4,12},{8,0},{12,4},{1,9},{5,13},{9,1},{13,5},{2,10},{6,14},... | collective-permute-start | bytes 430088 | tf_op jit(solution)/shard_map/ppermute | solution.py:225
  52.8 1.9 %reshape.131 = f32[4,7,2,64,4]{4,3,0,2,1:T(8,128)S(1)} reshape(f32[4,14,256]{2,0,1:T(4,128)S(1)} %slice.153) | data formatting | bytes 114688 | tf_op jit(solution)/shard_map/reshape | solution.py:239
  55.2 3.9 %collective-permute-done.9 = f32[2,14,1280]{2,1,0:T(8,128)S(1)} collective-permute-done((f32[2,14,1280]{2,1,0:T(8,128)S(1)}, f32[2,14,1280]{2,1,0:T(8,128)S(1)}, u32[]{:S(2)}, u32[]{:S(2)}) %collective-permute-start.9) | collective-permute-done | bytes 143392 | tf_op jit(solution)/shard_map/ppermute | solution.py:225
  59.5 1.9 %fusion.1 = f32[7,2,384]{2,0,1:T(8,128)S(1)} fusion(s32[384]{0:T(512)S(1)} %pad_add_fusion, f32[7,2,3072]{2,1,0:T(2,128)S(1)} %dot_general.12), kind=kOutput, calls=%fused_computation.2 | convolution fusion | flops 199360512 | bytes 195072 | tf_op jit(solution)/shard_map/dot_general | solution.py:250
  62.8 3.5 %shard_map.57 = f32[14,64,128]{2,1,0:T(8,128)} custom-call(f32[14,64,128]{2,1,0:T(8,128)} %get-tuple-element.13.f_ref, f32[14,2,128]{2,1,0:T(2,128)} %bitcast.106, f32[14,2,128]{2,1,0:T(2,128)} %bitcast.105, f32[14,2,64]{2,1,0:T(2,128)} %bitcast.110, f32[14,2,64]{2,1,0:T(2,128)} %bitcast.109, f32[14,64,128]{2,1,0:T(8,128)} %bitcast.94, ...), custom_call_target="tpu_custom_call" | custom-call | tf_op jit(solution)/shard_map/pallas_call | solution.py:114
  (80 shorter events, 11.3 us)
Async XLA Ops:
  3.9 6.0 %collective-permute-start = (f32[14,192]{1,0:T(8,128)}, f32[14,192]{1,0:T(8,128)S(1)}, u32[]{:S(2)}, u32[]{:S(2)}) collective-permute-start(f32[14,192]{1,0:T(8,128)} %get-tuple-element.10), channel_id=1, source_target_pairs={{0,16},{16,0},{1,17},{17,1},{2,18},{18,2},{3,19},{19,3},{4,20},{20... | collective-permute-start | bytes 32264 | tf_op jit(solution)/shard_map/ppermute | solution.py:233
  7.7 2.3 %copy-start = (s32[1,1,1,768]{3,2,1,0:T(1,128)S(1)}, s32[1,1,1,768]{3,2,1,0:T(1,128)}, u32[]{:S(2)}) copy-start(s32[1,1,1,768]{3,2,1,0:T(1,128)} %param.6) | copy-start | bytes 9220
  10.0 1.2 %collective-permute-start.1 = (f32[1,14,448]{2,1,0:T(8,128)S(1)}, f32[1,14,448]{2,1,0:T(8,128)S(1)}, u32[]{:S(2)}, u32[]{:S(2)}) collective-permute-start(f32[1,14,448]{2,1,0:T(8,128)S(1)} %maximum_bitcast_fusion.2), channel_id=1, source_target_pairs={{0,1},{1,0},{2,3},{3,2},{4,5},{5,4},{6,7},{7,6},{8,9},{9,8},{10,11... | collective-permute-start | bytes 75272 | tf_op jit(solution)/shard_map/ppermute | solution.py:225
  11.4 4.2 %collective-permute-start.2 = (f32[2,14,448]{2,0,1:T(2,128)S(1)}, f32[2,14,448]{2,0,1:T(2,128)S(1)}, u32[]{:S(2)}, u32[]{:S(2)}) collective-permute-start(f32[2,14,448]{2,0,1:T(2,128)S(1)} %maximum_select_fusion.6), channel_id=1, source_target_pairs={{0,2},{1,3},{2,0},{3,1},{4,6},{5,7},{6,4},{7,5},{8,10},{9,11},{10,... | collective-permute-start | bytes 150536 | tf_op jit(solution)/shard_map/ppermute | solution.py:225
  15.8 4.5 %collective-permute-start.3 = (f32[1,14,1280]{2,1,0:T(8,128)S(1)}, f32[1,14,1280]{2,1,0:T(8,128)S(1)}, u32[]{:S(2)}, u32[]{:S(2)}) collective-permute-start(f32[1,14,1280]{2,1,0:T(8,128)S(1)} %maximum_bitcast_fusion), channel_id=1, source_target_pairs={{0,4},{4,0},{8,12},{12,8},{1,5},{5,1},{9,13},{13,9},{2,6},{6,2},{1... | collective-permute-start | bytes 215048 | tf_op jit(solution)/shard_map/ppermute | solution.py:225
  20.4 8.4 %collective-permute-start.4 = (f32[2,14,1280]{2,1,0:T(8,128)S(1)}, f32[2,14,1280]{2,1,0:T(8,128)S(1)}, u32[]{:S(2)}, u32[]{:S(2)}) collective-permute-start(f32[2,14,1280]{2,1,0:T(8,128)S(1)} %maximum_select_fusion.2), channel_id=1, source_target_pairs={{0,8},{4,12},{8,0},{12,4},{1,9},{5,13},{9,1},{13,5},{2,10},{6,14},... | collective-permute-start | bytes 430088 | tf_op jit(solution)/shard_map/ppermute | solution.py:225
  36.3 3.9 %collective-permute-start.5 = (f32[14,192]{1,0:T(8,128)}, f32[14,192]{1,0:T(8,128)S(1)}, u32[]{:S(2)}, u32[]{:S(2)}) collective-permute-start(f32[14,192]{1,0:T(8,128)} %get-tuple-element.14), channel_id=1, source_target_pairs={{0,16},{16,0},{1,17},{17,1},{2,18},{18,2},{3,19},{19,3},{4,20},{20... | collective-permute-start | bytes 32264 | tf_op jit(solution)/shard_map/ppermute | solution.py:233
  40.3 1.2 %collective-permute-start.6 = (f32[1,14,448]{2,1,0:T(8,128)S(1)}, f32[1,14,448]{2,1,0:T(8,128)S(1)}, u32[]{:S(2)}, u32[]{:S(2)}) collective-permute-start(f32[1,14,448]{2,1,0:T(8,128)S(1)} %maximum_bitcast_fusion.3), channel_id=1, source_target_pairs={{0,1},{1,0},{2,3},{3,2},{4,5},{5,4},{6,7},{7,6},{8,9},{9,8},{10,11... | collective-permute-start | bytes 75272 | tf_op jit(solution)/shard_map/ppermute | solution.py:225
  41.6 4.2 %collective-permute-start.7 = (f32[2,14,448]{2,0,1:T(2,128)S(1)}, f32[2,14,448]{2,0,1:T(2,128)S(1)}, u32[]{:S(2)}, u32[]{:S(2)}) collective-permute-start(f32[2,14,448]{2,0,1:T(2,128)S(1)} %maximum_select_fusion.7), channel_id=1, source_target_pairs={{0,2},{1,3},{2,0},{3,1},{4,6},{5,7},{6,4},{7,5},{8,10},{9,11},{10,... | collective-permute-start | bytes 150536 | tf_op jit(solution)/shard_map/ppermute | solution.py:225
  46.1 4.5 %collective-permute-start.8 = (f32[1,14,1280]{2,1,0:T(8,128)S(1)}, f32[1,14,1280]{2,1,0:T(8,128)S(1)}, u32[]{:S(2)}, u32[]{:S(2)}) collective-permute-start(f32[1,14,1280]{2,1,0:T(8,128)S(1)} %maximum_bitcast_fusion.1), channel_id=1, source_target_pairs={{0,4},{4,0},{8,12},{12,8},{1,5},{5,1},{9,13},{13,9},{2,6},{6,2},{1... | collective-permute-start | bytes 215048 | tf_op jit(solution)/shard_map/ppermute | solution.py:225
  50.6 8.5 %collective-permute-start.9 = (f32[2,14,1280]{2,1,0:T(8,128)S(1)}, f32[2,14,1280]{2,1,0:T(8,128)S(1)}, u32[]{:S(2)}, u32[]{:S(2)}) collective-permute-start(f32[2,14,1280]{2,1,0:T(8,128)S(1)} %maximum_select_fusion.3), channel_id=1, source_target_pairs={{0,8},{4,12},{8,0},{12,4},{1,9},{5,13},{9,1},{13,5},{2,10},{6,14},... | collective-permute-start | bytes 430088 | tf_op jit(solution)/shard_map/ppermute | solution.py:225

commit v7 on v6

--- a/solution.py
+++ b/solution.py
@@ -17,7 +17,9 @@
 HIGHEST = lax.Precision.HIGHEST
 
 
-def stencil_kernel(f_ref, up_ref, down_ref, left_ref, right_ref, base_ref, lon_ref, lat_ref, turn_ref, o_ref, *rest, first):
+def stencil_kernel(
+    flags_ref, f_ref, rim_ref, up_ref, down_ref, left_ref, right_ref, base_ref, lon_ref, lat_ref, turn_ref, o_ref, *rest, first
+):
     planes, height, width = f_ref.shape
     comps = planes // 2
     row = lax.broadcasted_iota(jnp.int32, (height, width), 0)
@@ -30,9 +32,28 @@
     )
     pick_row = lax.broadcasted_iota(jnp.int32, (width, height), 0)
 
+    on_top = flags_ref[0] == 1
+    on_bottom = flags_ref[1] == 1
+    on_left = flags_ref[2] == 1
+    on_right = flags_ref[3] == 1
+    band = 2 * width
+    group = rim_ref.shape[1] - band
+
+    def edge(flag, rim, halo):
+        return jnp.where(jnp.broadcast_to(flag, halo.shape), rim, halo)
+
+    def halo_rows(k):
+        rim = jnp.concatenate([rim_ref[k : k + 1, 0:width], rim_ref[k : k + 1, width:band]], axis=0)
+        return edge(on_top, rim, up_ref[k]), edge(on_bottom, rim, down_ref[k])
+
     def columns(k):
-        left = left_ref[k]
-        right = right_ref[k]
+        start = band
+        rim = jnp.concatenate(
+            [rim_ref[k : k + 1, start : start + height], rim_ref[k : k + 1, start + group // 2 : start + group // 2 + height]],
+            axis=0,
+        )
+        left = edge(on_left, rim, left_ref[k])
+        right = edge(on_right, rim, right_ref[k])
         rows_of = jnp.where(
             pick_row == 0,
             left[0:1, :],
@@ -44,8 +65,7 @@
 
     def terms(k):
         x = f_ref[k]
-        up = up_ref[k]
-        down = down_ref[k]
+        up, down = halo_rows(k)
         sides = columns(k)
         left = sides[:, 0:2]
         right = sides[:, 2:4]
@@ -107,15 +127,18 @@
         donate_planes(lambda k: o_ref[k], planes, lon_ref[...], lat_ref[...], turn_ref, rest[0])
 
 
-def advance(field, up, down, left, right, base, lon, lat, turn, first):
+def advance(field, flags, rim, up, down, left, right, base, lon, lat, turn, first):
     shape = jax.ShapeDtypeStruct(field.shape, field.dtype)
     if first:
         shape = (shape, jax.ShapeDtypeStruct((field.shape[0], lon.shape[1]), jnp.float32))
+    vmem = pl.BlockSpec(memory_space=pltpu.VMEM)
     return pl.pallas_call(
         functools.partial(stencil_kernel, first=first),
         out_shape=shape,
+        in_specs=[pl.BlockSpec(memory_space=pltpu.SMEM)] + [vmem] * 10,
+        out_specs=(vmem, vmem) if first else vmem,
         interpret=INTERPRET,
-    )(field, up, down, left, right, base, lon, lat, turn)
+    )(flags, field, rim, up, down, left, right, base, lon, lat, turn)
 
 
 def donation_weights(cells_ref, frac_ref, rows, cols):
@@ -212,7 +235,10 @@
     side = 2 * rows
     lat_slots = jnp.where(on_top, slots[0:band], slots[band : 2 * band])
     lon_slots = jnp.where(on_left, slots[2 * band : 2 * band + side], slots[2 * band + side :])
-    wanted = jnp.concatenate([lat_slots, lon_slots])
+    group = -(-rows // 128) * 128
+    filler = jnp.zeros((group - rows,), jnp.int32)
+    wanted = jnp.concatenate([lat_slots, lon_slots[:rows], filler, lon_slots[rows:], filler])
+    flags = jnp.stack([on_top, on_bottom, on_left, on_right]).astype(jnp.int32)
     total = lat_count * lon_count * cells.shape[0]
     pick = (jnp.arange(total, dtype=jnp.int32)[:, None] == wanted[None, :]).astype(jnp.float32)
 
@@ -247,14 +273,12 @@
         down = lax.dynamic_index_in_dim(side_rows, jnp.minimum(lat_pos + 1, lat_count - 1), keepdims=False)[:, :, :2]
         left = lax.dynamic_index_in_dim(side_cols, jnp.maximum(lon_pos - 1, 0), keepdims=False)[..., 2:]
         right = lax.dynamic_index_in_dim(side_cols, jnp.minimum(lon_pos + 1, lon_count - 1), keepdims=False)[..., :2]
-        rim = jnp.dot(partner, pick, precision=HIGHEST).reshape(comps, levels, -1)
-        rim_lat = rim[:, :, :band].reshape(comps, levels, 2, cols)
-        rim_lon = jnp.transpose(rim[:, :, band:].reshape(comps, levels, 2, rows), (0, 1, 3, 2))
-        up = jnp.where(on_top, rim_lat, up).reshape(comps * levels, 2, cols)
-        down = jnp.where(on_bottom, rim_lat, down).reshape(comps * levels, 2, cols)
-        left = jnp.swapaxes(jnp.where(on_left, rim_lon, left).reshape(comps * levels, rows, 2), 1, 2)
-        right = jnp.swapaxes(jnp.where(on_right, rim_lon, right).reshape(comps * levels, rows, 2), 1, 2)
-        return up, down, left, right
+        rim = jnp.dot(partner, pick, precision=HIGHEST)
+        up = up.reshape(comps * levels, 2, cols)
+        down = down.reshape(comps * levels, 2, cols)
+        left = jnp.swapaxes(left.reshape(comps * levels, rows, 2), 1, 2)
+        right = jnp.swapaxes(right.reshape(comps * levels, rows, 2), 1, 2)
+        return flags, rim, up, down, left, right
 
     field = state[0].reshape(comps * levels, rows, cols)
     turn_parts = jnp.concatenate([jnp.cos(donor_turn[0, 0]), jnp.sin(donor_turn[0, 0])])

time: 66.7 us -> 67.9 us (1.018)
  local copies, waits for them, and re-layouts: 12.7 us -> 17.3 us
  waiting for transfers between devices: 21.4 us -> 18.1 us
  other arithmetic: 4.16 us -> 2.31 us
  matrix products: 3.62 us -> 5.15 us
    slice x6 -> x9, local copies, waits for them, and re-layouts: 0.02 us -> 5 us  [the longest x2 1.26 us: section(): lax.dynamic_index_in_dim(side_cols, jnp.minimum(lon_pos + 1, lon_count -...]
    ppermute x8, waiting for transfers between devices: 20.5 us -> 17.2 us  [gather(): other = lax.ppermute(held, axis, [(i, i ^ k) for i in range(size)])]
    select_n x4 -> x0, other arithmetic: 2.51 us -> none  [the longest x2 1.26 us: section(): down = jnp.where(on_bottom, rim_lat, down).reshape(comps * levels, 2, cols)]
    dot_general x2, matrix products: 3.62 us -> 5.15 us  [section(): rim = jnp.dot(partner, pick, precision=HIGHEST)]
  transfers between devices with their start and end apart: 10 -> 10, of which waited for: 9 -> 9; matrix products, arithmetic and copies ran while one was open for 17% -> 21% of each run, Pallas kernels for 0% -> 0%
where the time goes in v7:
time: 67.9 us; the launch traced here: 67.5 us
  waiting for transfers between devices  18.1 us (27%)
  local copies, waits for them, and re-layouts  17.3 us (25%)
  starting transfers between devices  14.1 us (21%)
  Pallas kernels  10.1 us (15%)
  matrix products  5.15 us (8%)
  other arithmetic  2.31 us (3%)
    ppermute x8, waiting for transfers between devices, gather(): other = lax.ppermute(held, axis, [(i, i ^ k) for i in range(size)])  17.2 us
    ppermute x8, starting transfers between devices, gather(): other = lax.ppermute(held, axis, [(i, i ^ k) for i in range(size)])  10.3 us
    pallas_call x2, Pallas kernels, advance(): pl.pallas_call(functools.partial(stencil_kernel, first=first), out_shape=...  7.55 us
    dot_general x2, matrix products, section(): rim = jnp.dot(partner, pick, precision=HIGHEST)  5.15 us
    reshape x2, local copies, waits for them, and re-layouts, section(): side_cols = lon_all[:, :, dons:].reshape(lon_count, comps, levels, rows, 4)  3.83 us
    ppermute x2, starting transfers between devices, section(): given = lax.ppermute(donation, 'panel', [(0, 1), (1, 0)])  3.82 us
    slice x2, local copies, waits for them, and re-layouts, section(): side_cols = jnp.concatenate([flat[:, :, :2], flat[:, :, cols - 2:]], axis=2)  2.76 us
    pallas_call x1, Pallas kernels, first_donation(): pl.pallas_call(donation_kernel, out_shape=(jax.ShapeDtypeStruct((planes,...  2.57 us
  transfers between devices with their start and end apart: 10, of which 9 were waited for; matrix products, arithmetic and copies ran while one was open for 21% of the time, Pallas kernels for 0%

profile of v7, /device:TPU:0, one launch (start us, length us, event | category | flops | bytes accessed | tf_op | source)
XLA Modules:
  0.0 67.5 jit_solution(18108502511214747992)
XLA Ops:
  1.3 2.6 %shard_map.55 = (f32[14,192]{1,0:T(8,128)}, f32[128,192]{1,0:T(8,128)}, f32[64,192]{1,0:T(8,128)}) custom-call(f32[14,64,128]{2,1,0:T(8,128)} %bitcast.89, s32[1,192]{1,0:T(1,128)} %bitcast.119, f32[2,192]{1,0:T(2,128)} %bitcast.118, f32[2,192]{1,0:T(2,128)} %pad_maximum_fusion.4.turn_ref), custom_call_target="tpu_custom_call" | custom-call | tf_op jit(solution)/shard_map/pallas_call | solution.py:189
  3.9 3.0 %collective-permute-start = (f32[14,192]{1,0:T(8,128)}, f32[14,192]{1,0:T(8,128)S(1)}, u32[]{:S(2)}, u32[]{:S(2)}) collective-permute-start(f32[14,192]{1,0:T(8,128)} %get-tuple-element.10), channel_id=1, source_target_pairs={{0,16},{16,0},{1,17},{17,1},{2,18},{18,2},{3,19},{19,3},{4,20},{20... | collective-permute-start | bytes 32264 | tf_op jit(solution)/shard_map/ppermute | solution.py:259
  7.8 1.4 %fusion.6 = (f32[14,64,2]{2,1,0:T(8,128)S(1)}, f32[14,64,2]{2,1,0:T(8,128)S(1)}) fusion(f32[14,64,128]{2,1,0:T(8,128)} %bitcast.91), kind=kLoop, calls=%fused_computation.43 | loop fusion | bytes 28672 | tf_op jit(solution)/shard_map/slice | solution.py:261
  10.2 1.1 %collective-permute-done.1 = f32[1,14,448]{2,1,0:T(8,128)S(1)} collective-permute-done((f32[1,14,448]{2,1,0:T(8,128)S(1)}, f32[1,14,448]{2,1,0:T(8,128)S(1)}, u32[]{:S(2)}, u32[]{:S(2)}) %collective-permute-start.1) | collective-permute-done | bytes 25120 | tf_op jit(solution)/shard_map/ppermute | solution.py:251
  11.4 1.6 %collective-permute-start.2 = (f32[2,14,448]{2,0,1:T(2,128)S(1)}, f32[2,14,448]{2,0,1:T(2,128)S(1)}, u32[]{:S(2)}, u32[]{:S(2)}) collective-permute-start(f32[2,14,448]{2,0,1:T(2,128)S(1)} %maximum_select_fusion.6), channel_id=1, source_target_pairs={{0,2},{1,3},{2,0},{3,1},{4,6},{5,7},{6,4},{7,5},{8,10},{9,11},{10,... | collective-permute-start | bytes 150536 | tf_op jit(solution)/shard_map/ppermute | solution.py:251
  13.0 2.6 %collective-permute-done.2 = f32[2,14,448]{2,0,1:T(2,128)S(1)} collective-permute-done((f32[2,14,448]{2,0,1:T(2,128)S(1)}, f32[2,14,448]{2,0,1:T(2,128)S(1)}, u32[]{:S(2)}, u32[]{:S(2)}) %collective-permute-start.2) | collective-permute-done | bytes 50208 | tf_op jit(solution)/shard_map/ppermute | solution.py:251
  15.9 1.6 %collective-permute-start.3 = (f32[1,14,1280]{2,1,0:T(8,128)S(1)}, f32[1,14,1280]{2,1,0:T(8,128)S(1)}, u32[]{:S(2)}, u32[]{:S(2)}) collective-permute-start(f32[1,14,1280]{2,1,0:T(8,128)S(1)} %maximum_bitcast_fusion), channel_id=1, source_target_pairs={{0,4},{4,0},{8,12},{12,8},{1,5},{5,1},{9,13},{13,9},{2,6},{6,2},{1... | collective-permute-start | bytes 215048 | tf_op jit(solution)/shard_map/ppermute | solution.py:251
  17.6 2.8 %collective-permute-done.3 = f32[1,14,1280]{2,1,0:T(8,128)S(1)} collective-permute-done((f32[1,14,1280]{2,1,0:T(8,128)S(1)}, f32[1,14,1280]{2,1,0:T(8,128)S(1)}, u32[]{:S(2)}, u32[]{:S(2)}) %collective-permute-start.3) | collective-permute-done | bytes 71712 | tf_op jit(solution)/shard_map/ppermute | solution.py:251
  20.4 2.7 %collective-permute-start.4 = (f32[2,14,1280]{2,1,0:T(8,128)S(1)}, f32[2,14,1280]{2,1,0:T(8,128)S(1)}, u32[]{:S(2)}, u32[]{:S(2)}) collective-permute-start(f32[2,14,1280]{2,1,0:T(8,128)S(1)} %maximum_select_fusion.2), channel_id=1, source_target_pairs={{0,8},{4,12},{8,0},{12,4},{1,9},{5,13},{9,1},{13,5},{2,10},{6,14},... | collective-permute-start | bytes 430088 | tf_op jit(solution)/shard_map/ppermute | solution.py:251
  23.9 1.9 %reshape.107 = f32[4,7,2,64,4]{4,3,0,2,1:T(8,128)S(1)} reshape(f32[4,14,256]{2,0,1:T(4,128)S(1)} %slice.141) | data formatting | bytes 114688 | tf_op jit(solution)/shard_map/reshape | solution.py:265
  27.6 1.3 %collective-permute-done.4 = f32[2,14,1280]{2,1,0:T(8,128)S(1)} collective-permute-done((f32[2,14,1280]{2,1,0:T(8,128)S(1)}, f32[2,14,1280]{2,1,0:T(8,128)S(1)}, u32[]{:S(2)}, u32[]{:S(2)}) %collective-permute-start.4) | collective-permute-done | bytes 143392 | tf_op jit(solution)/shard_map/ppermute | solution.py:251
  30.4 2.6 %fusion.1.rim_ref = f32[14,512]{1,0:T(8,128)} fusion(f32[14,3072]{1,0:T(8,128)S(1)} %bitcast.100, s32[512]{0:T(512)S(1)} %concatenate.91), kind=kOutput, calls=%fused_computation.2 | convolution fusion | flops 265814016 | bytes 202752 | tf_op jit(solution)/shard_map/dot_general | solution.py:276
  33.0 4.0 %shard_map.56 = (f32[14,64,128]{2,1,0:T(8,128)}, f32[14,192]{1,0:T(8,128)}) custom-call(s32[4]{0:T(128)} %add_convert_fusion.flags_ref, f32[14,64,128]{2,1,0:T(8,128)} %bitcast.92, f32[14,512]{1,0:T(8,128)} %fusion.1.rim_ref, f32[14,2,128]{2,1,0:T(2,128)} %bitcast.116, f32[14,2,128]{2,1,0:T(2,128)} %bitcast.115, f32[14,2,64]{2,1,0:T(2,128)} %bitcast.112, ...), custom_call_target="tpu_custom_call" | custom-call | tf_op jit(solution)/shard_map/pallas_call | solution.py:135
  37.8 1.4 %fusion.4 = (f32[14,64,2]{2,1,0:T(8,128)S(1)}, f32[14,64,2]{2,1,0:T(8,128)S(1)}) fusion(f32[14,64,128]{2,1,0:T(8,128)} %get-tuple-element.13.f_ref), kind=kLoop, calls=%fused_computation.41 | loop fusion | bytes 28672 | tf_op jit(solution)/shard_map/slice | solution.py:261
  40.0 0.9 %collective-permute-done.5 = f32[14,192]{1,0:T(8,128)S(1)} collective-permute-done((f32[14,192]{1,0:T(8,128)}, f32[14,192]{1,0:T(8,128)S(1)}, u32[]{:S(2)}, u32[]{:S(2)}) %collective-permute-start.5) | collective-permute-done | bytes 10784 | tf_op jit(solution)/shard_map/ppermute | solution.py:259
  41.0 0.9 %fusion.5 = (f32[14,2,128]{2,1,0:T(2,128)S(1)}, f32[14,2,128]{2,1,0:T(2,128)S(1)}) fusion(f32[14,64,128]{2,1,0:T(8,128)} %get-tuple-element.13.f_ref), kind=kLoop, calls=%fused_computation.42 | loop fusion | bytes 57344 | tf_op jit(solution)/shard_map/slice | solution.py:266
  42.3 1.6 %collective-permute-start.7 = (f32[2,14,448]{2,0,1:T(2,128)S(1)}, f32[2,14,448]{2,0,1:T(2,128)S(1)}, u32[]{:S(2)}, u32[]{:S(2)}) collective-permute-start(f32[2,14,448]{2,0,1:T(2,128)S(1)} %maximum_select_fusion.7), channel_id=1, source_target_pairs={{0,2},{1,3},{2,0},{3,1},{4,6},{5,7},{6,4},{7,5},{8,10},{9,11},{10,... | collective-permute-start | bytes 150536 | tf_op jit(solution)/shard_map/ppermute | solution.py:251
  43.9 2.6 %collective-permute-done.7 = f32[2,14,448]{2,0,1:T(2,128)S(1)} collective-permute-done((f32[2,14,448]{2,0,1:T(2,128)S(1)}, f32[2,14,448]{2,0,1:T(2,128)S(1)}, u32[]{:S(2)}, u32[]{:S(2)}) %collective-permute-start.7) | collective-permute-done | bytes 50208 | tf_op jit(solution)/shard_map/ppermute | solution.py:251
  47.5 3.8 %collective-permute-done.8 = f32[1,14,1280]{2,1,0:T(8,128)S(1)} collective-permute-done((f32[1,14,1280]{2,1,0:T(8,128)S(1)}, f32[1,14,1280]{2,1,0:T(8,128)S(1)}, u32[]{:S(2)}, u32[]{:S(2)}) %collective-permute-start.8) | collective-permute-done | bytes 71712 | tf_op jit(solution)/shard_map/ppermute | solution.py:251
  51.3 2.1 %collective-permute-start.9 = (f32[2,14,1280]{2,1,0:T(8,128)S(1)}, f32[2,14,1280]{2,1,0:T(8,128)S(1)}, u32[]{:S(2)}, u32[]{:S(2)}) collective-permute-start(f32[2,14,1280]{2,1,0:T(8,128)S(1)} %maximum_select_fusion.3), channel_id=1, source_target_pairs={{0,8},{4,12},{8,0},{12,4},{1,9},{5,13},{9,1},{13,5},{2,10},{6,14},... | collective-permute-start | bytes 430088 | tf_op jit(solution)/shard_map/ppermute | solution.py:251
  53.5 1.9 %reshape.117 = f32[4,7,2,64,4]{4,3,0,2,1:T(8,128)S(1)} reshape(f32[4,14,256]{2,0,1:T(4,128)S(1)} %slice.149) | data formatting | bytes 114688 | tf_op jit(solution)/shard_map/reshape | solution.py:265
  57.2 2.6 %collective-permute-done.9 = f32[2,14,1280]{2,1,0:T(8,128)S(1)} collective-permute-done((f32[2,14,1280]{2,1,0:T(8,128)S(1)}, f32[2,14,1280]{2,1,0:T(8,128)S(1)}, u32[]{:S(2)}, u32[]{:S(2)}) %collective-permute-start.9) | collective-permute-done | bytes 143392 | tf_op jit(solution)/shard_map/ppermute | solution.py:251
  61.4 2.6 %fusion.rim_ref = f32[14,512]{1,0:T(8,128)} fusion(f32[14,3072]{1,0:T(8,128)S(1)} %bitcast.99, s32[512]{0:T(512)S(1)} %concatenate.91), kind=kOutput, calls=%fused_computation.1 | convolution fusion | flops 265814016 | bytes 202752 | tf_op jit(solution)/shard_map/dot_general | solution.py:276
  64.0 3.6 %shard_map.57 = f32[14,64,128]{2,1,0:T(8,128)} custom-call(s32[4]{0:T(128)} %add_convert_fusion.flags_ref, f32[14,64,128]{2,1,0:T(8,128)} %get-tuple-element.13.f_ref, f32[14,512]{1,0:T(8,128)} %fusion.rim_ref, f32[14,2,128]{2,1,0:T(2,128)} %bitcast.114, f32[14,2,128]{2,1,0:T(2,128)} %bitcast.113, f32[14,2,64]{2,1,0:T(2,128)} %bitcast.110, ...), custom_call_target="tpu_custom_call" | custom-call | tf_op jit(solution)/shard_map/pallas_call | solution.py:135
  (79 shorter events, 14.1 us)
Async XLA Ops:
  0.0 9.2 %copy-start = (s32[1,1,1,768]{3,2,1,0:T(1,128)S(1)}, s32[1,1,1,768]{3,2,1,0:T(1,128)}, u32[]{:S(2)}) copy-start(s32[1,1,1,768]{3,2,1,0:T(1,128)} %param.6) | copy-start | bytes 9220
  3.9 6.1 %collective-permute-start = (f32[14,192]{1,0:T(8,128)}, f32[14,192]{1,0:T(8,128)S(1)}, u32[]{:S(2)}, u32[]{:S(2)}) collective-permute-start(f32[14,192]{1,0:T(8,128)} %get-tuple-element.10), channel_id=1, source_target_pairs={{0,16},{16,0},{1,17},{17,1},{2,18},{18,2},{3,19},{19,3},{4,20},{20... | collective-permute-start | bytes 32264 | tf_op jit(solution)/shard_map/ppermute | solution.py:259
  10.1 1.2 %collective-permute-start.1 = (f32[1,14,448]{2,1,0:T(8,128)S(1)}, f32[1,14,448]{2,1,0:T(8,128)S(1)}, u32[]{:S(2)}, u32[]{:S(2)}) collective-permute-start(f32[1,14,448]{2,1,0:T(8,128)S(1)} %maximum_bitcast_fusion.2), channel_id=1, source_target_pairs={{0,1},{1,0},{2,3},{3,2},{4,5},{5,4},{6,7},{7,6},{8,9},{9,8},{10,11... | collective-permute-start | bytes 75272 | tf_op jit(solution)/shard_map/ppermute | solution.py:251
  11.4 4.2 %collective-permute-start.2 = (f32[2,14,448]{2,0,1:T(2,128)S(1)}, f32[2,14,448]{2,0,1:T(2,128)S(1)}, u32[]{:S(2)}, u32[]{:S(2)}) collective-permute-start(f32[2,14,448]{2,0,1:T(2,128)S(1)} %maximum_select_fusion.6), channel_id=1, source_target_pairs={{0,2},{1,3},{2,0},{3,1},{4,6},{5,7},{6,4},{7,5},{8,10},{9,11},{10,... | collective-permute-start | bytes 150536 | tf_op jit(solution)/shard_map/ppermute | solution.py:251
  15.9 4.5 %collective-permute-start.3 = (f32[1,14,1280]{2,1,0:T(8,128)S(1)}, f32[1,14,1280]{2,1,0:T(8,128)S(1)}, u32[]{:S(2)}, u32[]{:S(2)}) collective-permute-start(f32[1,14,1280]{2,1,0:T(8,128)S(1)} %maximum_bitcast_fusion), channel_id=1, source_target_pairs={{0,4},{4,0},{8,12},{12,8},{1,5},{5,1},{9,13},{13,9},{2,6},{6,2},{1... | collective-permute-start | bytes 215048 | tf_op jit(solution)/shard_map/ppermute | solution.py:251
  20.4 8.4 %collective-permute-start.4 = (f32[2,14,1280]{2,1,0:T(8,128)S(1)}, f32[2,14,1280]{2,1,0:T(8,128)S(1)}, u32[]{:S(2)}, u32[]{:S(2)}) collective-permute-start(f32[2,14,1280]{2,1,0:T(8,128)S(1)} %maximum_select_fusion.2), channel_id=1, source_target_pairs={{0,8},{4,12},{8,0},{12,4},{1,9},{5,13},{9,1},{13,5},{2,10},{6,14},... | collective-permute-start | bytes 430088 | tf_op jit(solution)/shard_map/ppermute | solution.py:251
  37.0 3.9 %collective-permute-start.5 = (f32[14,192]{1,0:T(8,128)}, f32[14,192]{1,0:T(8,128)S(1)}, u32[]{:S(2)}, u32[]{:S(2)}) collective-permute-start(f32[14,192]{1,0:T(8,128)} %get-tuple-element.14), channel_id=1, source_target_pairs={{0,16},{16,0},{1,17},{17,1},{2,18},{18,2},{3,19},{19,3},{4,20},{20... | collective-permute-start | bytes 32264 | tf_op jit(solution)/shard_map/ppermute | solution.py:259
  41.0 1.2 %collective-permute-start.6 = (f32[1,14,448]{2,1,0:T(8,128)S(1)}, f32[1,14,448]{2,1,0:T(8,128)S(1)}, u32[]{:S(2)}, u32[]{:S(2)}) collective-permute-start(f32[1,14,448]{2,1,0:T(8,128)S(1)} %maximum_bitcast_fusion.3), channel_id=1, source_target_pairs={{0,1},{1,0},{2,3},{3,2},{4,5},{5,4},{6,7},{7,6},{8,9},{9,8},{10,11... | collective-permute-start | bytes 75272 | tf_op jit(solution)/shard_map/ppermute | solution.py:251
  42.3 4.2 %collective-permute-start.7 = (f32[2,14,448]{2,0,1:T(2,128)S(1)}, f32[2,14,448]{2,0,1:T(2,128)S(1)}, u32[]{:S(2)}, u32[]{:S(2)}) collective-permute-start(f32[2,14,448]{2,0,1:T(2,128)S(1)} %maximum_select_fusion.7), channel_id=1, source_target_pairs={{0,2},{1,3},{2,0},{3,1},{4,6},{5,7},{6,4},{7,5},{8,10},{9,11},{10,... | collective-permute-start | bytes 150536 | tf_op jit(solution)/shard_map/ppermute | solution.py:251
  46.8 4.5 %collective-permute-start.8 = (f32[1,14,1280]{2,1,0:T(8,128)S(1)}, f32[1,14,1280]{2,1,0:T(8,128)S(1)}, u32[]{:S(2)}, u32[]{:S(2)}) collective-permute-start(f32[1,14,1280]{2,1,0:T(8,128)S(1)} %maximum_bitcast_fusion.1), channel_id=1, source_target_pairs={{0,4},{4,0},{8,12},{12,8},{1,5},{5,1},{9,13},{13,9},{2,6},{6,2},{1... | collective-permute-start | bytes 215048 | tf_op jit(solution)/shard_map/ppermute | solution.py:251
  51.3 8.5 %collective-permute-start.9 = (f32[2,14,1280]{2,1,0:T(8,128)S(1)}, f32[2,14,1280]{2,1,0:T(8,128)S(1)}, u32[]{:S(2)}, u32[]{:S(2)}) collective-permute-start(f32[2,14,1280]{2,1,0:T(8,128)S(1)} %maximum_select_fusion.3), channel_id=1, source_target_pairs={{0,8},{4,12},{8,0},{12,4},{1,9},{5,13},{9,1},{13,5},{2,10},{6,14},... | collective-permute-start | bytes 430088 | tf_op jit(solution)/shard_map/ppermute | solution.py:251

commit v8 on v6

--- a/solution.py
+++ b/solution.py
@@ -232,17 +232,18 @@
         flat = field
         given = lax.ppermute(donation, "panel", [(0, 1), (1, 0)])
         dons = given.shape[1]
+        side_rows = jnp.concatenate([flat[:, :2, :], flat[:, rows - 2 :, :]], axis=1)
+        lat_packet = jnp.concatenate([given, side_rows.reshape(comps * levels, -1)], axis=1)
+        lat_all = gather(lat_packet, "lat")
+        col_given = jnp.transpose(lat_all[:, :, :dons], (1, 0, 2)).reshape(comps * levels, -1)
+        side_rows = lat_all[:, :, dons:].reshape(lat_count, comps, levels, 4, cols)
         side_cols = jnp.concatenate([flat[:, :, :2], flat[:, :, cols - 2 :]], axis=2)
-        lon_packet = jnp.concatenate([given, side_cols.reshape(comps * levels, -1)], axis=1)
+        lon_packet = jnp.concatenate([col_given, side_cols.reshape(comps * levels, -1)], axis=1)
         lon_all = gather(lon_packet, "lon")
-        row_given = jnp.transpose(lon_all[:, :, :dons], (1, 0, 2)).reshape(comps * levels, -1)
-        side_cols = lon_all[:, :, dons:].reshape(lon_count, comps, levels, rows, 4)
-        side_rows = jnp.concatenate([flat[:, :2, :], flat[:, rows - 2 :, :]], axis=1)
-        lat_packet = jnp.concatenate([row_given, side_rows.reshape(comps * levels, -1)], axis=1)
-        lat_all = gather(lat_packet, "lat")
-        width = row_given.shape[1]
-        partner = jnp.transpose(lat_all[:, :, :width], (1, 0, 2)).reshape(comps * levels, -1)
-        side_rows = lat_all[:, :, width:].reshape(lat_count, comps, levels, 4, cols)
+        width = col_given.shape[1]
+        partner = lon_all[:, :, :width].reshape(lon_count, comps * levels, lat_count, dons)
+        partner = jnp.transpose(partner, (1, 2, 0, 3)).reshape(comps * levels, -1)
+        side_cols = lon_all[:, :, width:].reshape(lon_count, comps, levels, rows, 4)
         up = lax.dynamic_index_in_dim(side_rows, jnp.maximum(lat_pos - 1, 0), keepdims=False)[:, :, 2:]
         down = lax.dynamic_index_in_dim(side_rows, jnp.minimum(lat_pos + 1, lat_count - 1), keepdims=False)[:, :, :2]
         left = lax.dynamic_index_in_dim(side_cols, jnp.maximum(lon_pos - 1, 0), keepdims=False)[..., 2:]

time: 66.7 us -> 68 us (1.019)
  starting transfers between devices: 14 us -> 17.1 us
  waiting for transfers between devices: 21.4 us -> 18.4 us
  local copies, waits for them, and re-layouts: 12.7 us -> 13.6 us
    ppermute x8, waiting for transfers between devices: 20.5 us -> 17 us  [gather(): other = lax.ppermute(held, axis, [(i, i ^ k) for i in range(size)])]
    ppermute x8, starting transfers between devices: 10.2 us -> 12.6 us  [gather(): other = lax.ppermute(held, axis, [(i, i ^ k) for i in range(size)])]
    ppermute x2, starting transfers between devices: 3.83 us -> 4.55 us  [section(): given = lax.ppermute(donation, 'panel', [(0, 1), (1, 0)])]
    reshape x6 -> x8, local copies, waits for them, and re-layouts: 4.11 us -> 4.57 us  [the longest x2 3.81 us: section(): side_cols = lon_all[:, :, width:].reshape(lon_count, comps, levels, rows, 4)]
  transfers between devices with their start and end apart: 10 -> 10, of which waited for: 9 -> 9; matrix products, arithmetic and copies ran while one was open for 17% -> 10% of each run, Pallas kernels for 0% -> 0%
where the time goes in v8:
time: 68 us; the launch traced here: 67.7 us
  waiting for transfers between devices  18.4 us (27%)
  starting transfers between devices  17.1 us (25%)
  local copies, waits for them, and re-layouts  13.6 us (20%)
  Pallas kernels  10 us (15%)
  other arithmetic  4.32 us (6%)
  matrix products  3.63 us (5%)
    ppermute x8, waiting for transfers between devices, gather(): other = lax.ppermute(held, axis, [(i, i ^ k) for i in range(size)])  17 us
    ppermute x8, starting transfers between devices, gather(): other = lax.ppermute(held, axis, [(i, i ^ k) for i in range(size)])  12.6 us
    pallas_call x2, Pallas kernels, advance(): pl.pallas_call(functools.partial(stencil_kernel, first=first), out_shape=...  7.44 us
    ppermute x2, starting transfers between devices, section(): given = lax.ppermute(donation, 'panel', [(0, 1), (1, 0)])  4.55 us
    reshape x2, local copies, waits for them, and re-layouts, section(): side_cols = lon_all[:, :, width:].reshape(lon_count, comps, levels, rows, 4)  3.81 us
    dot_general x2, matrix products, section(): rim = jnp.dot(partner, pick, precision=HIGHEST).reshape(comps, levels, -1)  3.63 us
    slice x2, local copies, waits for them, and re-layouts, section(): side_cols = jnp.concatenate([flat[:, :, :2], flat[:, :, cols - 2:]], axis=2)  2.83 us
    pallas_call x1, Pallas kernels, first_donation(): pl.pallas_call(donation_kernel, out_shape=(jax.ShapeDtypeStruct((planes,...  2.57 us
  transfers between devices with their start and end apart: 10, of which 9 were waited for; matrix products, arithmetic and copies ran while one was open for 10% of the time, Pallas kernels for 0%

profile of v8, /device:TPU:0, one launch (start us, length us, event | category | flops | bytes accessed | tf_op | source)
XLA Modules:
  0.0 67.7 jit_solution(15256310707698287201)
XLA Ops:
  1.3 2.6 %shard_map.55 = (f32[14,192]{1,0:T(8,128)}, f32[128,192]{1,0:T(8,128)}, f32[64,192]{1,0:T(8,128)}) custom-call(f32[14,64,128]{2,1,0:T(8,128)} %bitcast.83, s32[1,192]{1,0:T(1,128)} %bitcast.111, f32[2,192]{1,0:T(2,128)} %bitcast.110, f32[2,192]{1,0:T(2,128)} %pad_maximum_fusion.6.turn_ref), custom_call_target="tpu_custom_call" | custom-call | tf_op jit(solution)/shard_map/pallas_call | solution.py:166
  3.9 3.0 %collective-permute-start = (f32[14,192]{1,0:T(8,128)}, f32[14,192]{1,0:T(8,128)S(1)}, u32[]{:S(2)}, u32[]{:S(2)}) collective-permute-start(f32[14,192]{1,0:T(8,128)} %get-tuple-element.10), channel_id=1, source_target_pairs={{0,16},{16,0},{1,17},{17,1},{2,18},{18,2},{3,19},{19,3},{4,20},{20... | collective-permute-start | bytes 32264 | tf_op jit(solution)/shard_map/ppermute | solution.py:233
  7.7 1.4 %fusion.12 = (f32[14,64,2]{2,1,0:T(8,128)S(1)}, f32[14,64,2]{2,1,0:T(8,128)S(1)}) fusion(f32[14,64,128]{2,1,0:T(8,128)} %bitcast.85), kind=kLoop, calls=%fused_computation.51 | loop fusion | bytes 28672 | tf_op jit(solution)/shard_map/slice | solution.py:240
  9.3 1.7 %collective-permute-start.1 = (f32[1,14,704]{2,0,1:T(1,128)S(1)}, f32[1,14,704]{2,0,1:T(1,128)S(1)}, u32[]{:S(2)}, u32[]{:S(2)}) collective-permute-start(f32[1,14,704]{2,0,1:T(1,128)S(1)} %broadcast_in_dim.14), channel_id=1, source_target_pairs={{0,4},{4,0},{8,12},{12,8},{1,5},{5,1},{9,13},{13,9},{2,6},{6,2},{1... | collective-permute-start | bytes 118280 | tf_op jit(solution)/shard_map/ppermute | solution.py:225
  11.1 2.4 %collective-permute-done.1 = f32[1,14,704]{2,0,1:T(1,128)S(1)} collective-permute-done((f32[1,14,704]{2,0,1:T(1,128)S(1)}, f32[1,14,704]{2,0,1:T(1,128)S(1)}, u32[]{:S(2)}, u32[]{:S(2)}) %collective-permute-start.1) | collective-permute-done | bytes 39456 | tf_op jit(solution)/shard_map/ppermute | solution.py:225
  13.6 2.7 %collective-permute-start.2 = (f32[2,14,704]{2,0,1:T(2,128)S(1)}, f32[2,14,704]{2,0,1:T(2,128)S(1)}, u32[]{:S(2)}, u32[]{:S(2)}) collective-permute-start(f32[2,14,704]{2,0,1:T(2,128)S(1)} %maximum_select_fusion.6), channel_id=1, source_target_pairs={{0,8},{4,12},{8,0},{12,4},{1,9},{5,13},{9,1},{13,5},{2,10},{6,14},... | collective-permute-start | bytes 236552 | tf_op jit(solution)/shard_map/ppermute | solution.py:225
  17.1 1.9 %collective-permute-done.2 = f32[2,14,704]{2,0,1:T(2,128)S(1)} collective-permute-done((f32[2,14,704]{2,0,1:T(2,128)S(1)}, f32[2,14,704]{2,0,1:T(2,128)S(1)}, u32[]{:S(2)}, u32[]{:S(2)}) %collective-permute-start.2) | collective-permute-done | bytes 78880 | tf_op jit(solution)/shard_map/ppermute | solution.py:225
  20.6 1.6 %collective-permute-start.4 = (f32[2,14,1024]{2,1,0:T(8,128)S(1)}, f32[2,14,1024]{2,1,0:T(8,128)S(1)}, u32[]{:S(2)}, u32[]{:S(2)}) collective-permute-start(f32[2,14,1024]{2,1,0:T(8,128)S(1)} %maximum_select_fusion.4), channel_id=1, source_target_pairs={{0,2},{1,3},{2,0},{3,1},{4,6},{5,7},{6,4},{7,5},{8,10},{9,11},{10,... | collective-permute-start | bytes 344072 | tf_op jit(solution)/shard_map/ppermute | solution.py:225
  22.5 3.8 %collective-permute-done.4 = f32[2,14,1024]{2,1,0:T(8,128)S(1)} collective-permute-done((f32[2,14,1024]{2,1,0:T(8,128)S(1)}, f32[2,14,1024]{2,1,0:T(8,128)S(1)}, u32[]{:S(2)}, u32[]{:S(2)}) %collective-permute-start.4) | collective-permute-done | bytes 114720 | tf_op jit(solution)/shard_map/ppermute | solution.py:225
  27.0 1.7 %fusion.3 = f32[7,2,384]{2,0,1:T(8,128)S(1)} fusion(s32[384]{0:T(512)S(1)} %pad_add_fusion, f32[7,2,3072]{2,1,0:T(2,128)S(1)} %dot_general.10), kind=kOutput, calls=%fused_computation.3 | convolution fusion | flops 199360512 | bytes 195072 | tf_op jit(solution)/shard_map/dot_general | solution.py:251
  28.9 1.9 %reshape.127 = f32[4,7,2,64,4]{4,3,0,2,1:T(8,128)S(1)} reshape(f32[4,14,256]{2,0,1:T(4,128)S(1)} %copy.63) | data formatting | bytes 114688 | tf_op jit(solution)/shard_map/reshape | solution.py:246
  32.6 3.9 %shard_map.56 = (f32[14,64,128]{2,1,0:T(8,128)}, f32[14,192]{1,0:T(8,128)}) custom-call(f32[14,64,128]{2,1,0:T(8,128)} %bitcast.86, f32[14,2,128]{2,1,0:T(2,128)} %bitcast.104, f32[14,2,128]{2,1,0:T(2,128)} %bitcast.103, f32[14,2,64]{2,1,0:T(2,128)} %bitcast.108, f32[14,2,64]{2,1,0:T(2,128)} %bitcast.107, f32[14,64,128]{2,1,0:T(8,128)} %bitcast.87, ...), custom_call_target="tpu_custom_call" | custom-call | tf_op jit(solution)/shard_map/pallas_call | solution.py:114
  36.5 1.6 %collective-permute-start.5 = (f32[14,192]{1,0:T(8,128)}, f32[14,192]{1,0:T(8,128)S(1)}, u32[]{:S(2)}, u32[]{:S(2)}) collective-permute-start(f32[14,192]{1,0:T(8,128)} %get-tuple-element.14), channel_id=1, source_target_pairs={{0,16},{16,0},{1,17},{17,1},{2,18},{18,2},{3,19},{19,3},{4,20},{20... | collective-permute-start | bytes 32264 | tf_op jit(solution)/shard_map/ppermute | solution.py:233
  39.0 1.4 %collective-permute-done.5 = f32[14,192]{1,0:T(8,128)S(1)} collective-permute-done((f32[14,192]{1,0:T(8,128)}, f32[14,192]{1,0:T(8,128)S(1)}, u32[]{:S(2)}, u32[]{:S(2)}) %collective-permute-start.5) | collective-permute-done | bytes 10784 | tf_op jit(solution)/shard_map/ppermute | solution.py:233
  40.6 1.7 %collective-permute-start.6 = (f32[1,14,704]{2,0,1:T(1,128)S(1)}, f32[1,14,704]{2,0,1:T(1,128)S(1)}, u32[]{:S(2)}, u32[]{:S(2)}) collective-permute-start(f32[1,14,704]{2,0,1:T(1,128)S(1)} %broadcast_in_dim.16), channel_id=1, source_target_pairs={{0,4},{4,0},{8,12},{12,8},{1,5},{5,1},{9,13},{13,9},{2,6},{6,2},{1... | collective-permute-start | bytes 118280 | tf_op jit(solution)/shard_map/ppermute | solution.py:225
  42.3 1.4 %fusion.10 = (f32[14,64,2]{2,1,0:T(8,128)S(1)}, f32[14,64,2]{2,1,0:T(8,128)S(1)}) fusion(f32[14,64,128]{2,1,0:T(8,128)} %get-tuple-element.13.f_ref), kind=kLoop, calls=%fused_computation.49 | loop fusion | bytes 28672 | tf_op jit(solution)/shard_map/slice | solution.py:240
  44.8 3.1 %collective-permute-start.7 = (f32[2,14,704]{2,0,1:T(2,128)S(1)}, f32[2,14,704]{2,0,1:T(2,128)S(1)}, u32[]{:S(2)}, u32[]{:S(2)}) collective-permute-start(f32[2,14,704]{2,0,1:T(2,128)S(1)} %maximum_select_fusion.7), channel_id=1, source_target_pairs={{0,8},{4,12},{8,0},{12,4},{1,9},{5,13},{9,1},{13,5},{2,10},{6,14},... | collective-permute-start | bytes 236552 | tf_op jit(solution)/shard_map/ppermute | solution.py:225
  48.7 1.7 %collective-permute-done.7 = f32[2,14,704]{2,0,1:T(2,128)S(1)} collective-permute-done((f32[2,14,704]{2,0,1:T(2,128)S(1)}, f32[2,14,704]{2,0,1:T(2,128)S(1)}, u32[]{:S(2)}, u32[]{:S(2)}) %collective-permute-start.7) | collective-permute-done | bytes 78880 | tf_op jit(solution)/shard_map/ppermute | solution.py:225
  50.7 1.2 %collective-permute-done.8 = f32[1,14,1024]{2,1,0:T(8,128)S(1)} collective-permute-done((f32[1,14,1024]{2,1,0:T(8,128)S(1)}, f32[1,14,1024]{2,1,0:T(8,128)S(1)}, u32[]{:S(2)}, u32[]{:S(2)}) %collective-permute-start.8) | collective-permute-done | bytes 57376 | tf_op jit(solution)/shard_map/ppermute | solution.py:225
  52.0 1.5 %collective-permute-start.9 = (f32[2,14,1024]{2,1,0:T(8,128)S(1)}, f32[2,14,1024]{2,1,0:T(8,128)S(1)}, u32[]{:S(2)}, u32[]{:S(2)}) collective-permute-start(f32[2,14,1024]{2,1,0:T(8,128)S(1)} %maximum_select_fusion.5), channel_id=1, source_target_pairs={{0,2},{1,3},{2,0},{3,1},{4,6},{5,7},{6,4},{7,5},{8,10},{9,11},{10,... | collective-permute-start | bytes 344072 | tf_op jit(solution)/shard_map/ppermute | solution.py:225
  53.7 3.8 %collective-permute-done.9 = f32[2,14,1024]{2,1,0:T(8,128)S(1)} collective-permute-done((f32[2,14,1024]{2,1,0:T(8,128)S(1)}, f32[2,14,1024]{2,1,0:T(8,128)S(1)}, u32[]{:S(2)}, u32[]{:S(2)}) %collective-permute-start.9) | collective-permute-done | bytes 114720 | tf_op jit(solution)/shard_map/ppermute | solution.py:225
  58.3 1.9 %fusion.1 = f32[7,2,384]{2,0,1:T(8,128)S(1)} fusion(s32[384]{0:T(512)S(1)} %pad_add_fusion, f32[7,2,3072]{2,1,0:T(2,128)S(1)} %dot_general.12), kind=kOutput, calls=%fused_computation.2 | convolution fusion | flops 199360512 | bytes 195072 | tf_op jit(solution)/shard_map/dot_general | solution.py:251
  60.4 1.9 %reshape.139 = f32[4,7,2,64,4]{4,3,0,2,1:T(8,128)S(1)} reshape(f32[4,14,256]{2,0,1:T(4,128)S(1)} %copy.73) | data formatting | bytes 114688 | tf_op jit(solution)/shard_map/reshape | solution.py:246
  64.1 3.5 %shard_map.57 = f32[14,64,128]{2,1,0:T(8,128)} custom-call(f32[14,64,128]{2,1,0:T(8,128)} %get-tuple-element.13.f_ref, f32[14,2,128]{2,1,0:T(2,128)} %bitcast.102, f32[14,2,128]{2,1,0:T(2,128)} %bitcast.101, f32[14,2,64]{2,1,0:T(2,128)} %bitcast.106, f32[14,2,64]{2,1,0:T(2,128)} %bitcast.105, f32[14,64,128]{2,1,0:T(8,128)} %bitcast.88, ...), custom_call_target="tpu_custom_call" | custom-call | tf_op jit(solution)/shard_map/pallas_call | solution.py:114
  (84 shorter events, 13.6 us)
Async XLA Ops:
  0.0 9.1 %copy-start = (s32[1,1,1,768]{3,2,1,0:T(1,128)S(1)}, s32[1,1,1,768]{3,2,1,0:T(1,128)}, u32[]{:S(2)}) copy-start(s32[1,1,1,768]{3,2,1,0:T(1,128)} %param.6) | copy-start | bytes 9220
  3.9 5.3 %collective-permute-start = (f32[14,192]{1,0:T(8,128)}, f32[14,192]{1,0:T(8,128)S(1)}, u32[]{:S(2)}, u32[]{:S(2)}) collective-permute-start(f32[14,192]{1,0:T(8,128)} %get-tuple-element.10), channel_id=1, source_target_pairs={{0,16},{16,0},{1,17},{17,1},{2,18},{18,2},{3,19},{19,3},{4,20},{20... | collective-permute-start | bytes 32264 | tf_op jit(solution)/shard_map/ppermute | solution.py:233
  9.3 4.1 %collective-permute-start.1 = (f32[1,14,704]{2,0,1:T(1,128)S(1)}, f32[1,14,704]{2,0,1:T(1,128)S(1)}, u32[]{:S(2)}, u32[]{:S(2)}) collective-permute-start(f32[1,14,704]{2,0,1:T(1,128)S(1)} %broadcast_in_dim.14), channel_id=1, source_target_pairs={{0,4},{4,0},{8,12},{12,8},{1,5},{5,1},{9,13},{13,9},{2,6},{6,2},{1... | collective-permute-start | bytes 118280 | tf_op jit(solution)/shard_map/ppermute | solution.py:225
  13.6 5.4 %collective-permute-start.2 = (f32[2,14,704]{2,0,1:T(2,128)S(1)}, f32[2,14,704]{2,0,1:T(2,128)S(1)}, u32[]{:S(2)}, u32[]{:S(2)}) collective-permute-start(f32[2,14,704]{2,0,1:T(2,128)S(1)} %maximum_select_fusion.6), channel_id=1, source_target_pairs={{0,8},{4,12},{8,0},{12,4},{1,9},{5,13},{9,1},{13,5},{2,10},{6,14},... | collective-permute-start | bytes 236552 | tf_op jit(solution)/shard_map/ppermute | solution.py:225
  19.3 1.3 %collective-permute-start.3 = (f32[1,14,1024]{2,1,0:T(8,128)S(1)}, f32[1,14,1024]{2,1,0:T(8,128)S(1)}, u32[]{:S(2)}, u32[]{:S(2)}) collective-permute-start(f32[1,14,1024]{2,1,0:T(8,128)S(1)} %maximum_bitcast_fusion), channel_id=1, source_target_pairs={{0,1},{1,0},{2,3},{3,2},{4,5},{5,4},{6,7},{7,6},{8,9},{9,8},{10,11... | collective-permute-start | bytes 172040 | tf_op jit(solution)/shard_map/ppermute | solution.py:225
  20.6 5.6 %collective-permute-start.4 = (f32[2,14,1024]{2,1,0:T(8,128)S(1)}, f32[2,14,1024]{2,1,0:T(8,128)S(1)}, u32[]{:S(2)}, u32[]{:S(2)}) collective-permute-start(f32[2,14,1024]{2,1,0:T(8,128)S(1)} %maximum_select_fusion.4), channel_id=1, source_target_pairs={{0,2},{1,3},{2,0},{3,1},{4,6},{5,7},{6,4},{7,5},{8,10},{9,11},{10,... | collective-permute-start | bytes 344072 | tf_op jit(solution)/shard_map/ppermute | solution.py:225
  36.5 3.9 %collective-permute-start.5 = (f32[14,192]{1,0:T(8,128)}, f32[14,192]{1,0:T(8,128)S(1)}, u32[]{:S(2)}, u32[]{:S(2)}) collective-permute-start(f32[14,192]{1,0:T(8,128)} %get-tuple-element.14), channel_id=1, source_target_pairs={{0,16},{16,0},{1,17},{17,1},{2,18},{18,2},{3,19},{19,3},{4,20},{20... | collective-permute-start | bytes 32264 | tf_op jit(solution)/shard_map/ppermute | solution.py:233
  40.6 4.1 %collective-permute-start.6 = (f32[1,14,704]{2,0,1:T(1,128)S(1)}, f32[1,14,704]{2,0,1:T(1,128)S(1)}, u32[]{:S(2)}, u32[]{:S(2)}) collective-permute-start(f32[1,14,704]{2,0,1:T(1,128)S(1)} %broadcast_in_dim.16), channel_id=1, source_target_pairs={{0,4},{4,0},{8,12},{12,8},{1,5},{5,1},{9,13},{13,9},{2,6},{6,2},{1... | collective-permute-start | bytes 118280 | tf_op jit(solution)/shard_map/ppermute | solution.py:225
  44.8 5.6 %collective-permute-start.7 = (f32[2,14,704]{2,0,1:T(2,128)S(1)}, f32[2,14,704]{2,0,1:T(2,128)S(1)}, u32[]{:S(2)}, u32[]{:S(2)}) collective-permute-start(f32[2,14,704]{2,0,1:T(2,128)S(1)} %maximum_select_fusion.7), channel_id=1, source_target_pairs={{0,8},{4,12},{8,0},{12,4},{1,9},{5,13},{9,1},{13,5},{2,10},{6,14},... | collective-permute-start | bytes 236552 | tf_op jit(solution)/shard_map/ppermute | solution.py:225
  50.6 1.3 %collective-permute-start.8 = (f32[1,14,1024]{2,1,0:T(8,128)S(1)}, f32[1,14,1024]{2,1,0:T(8,128)S(1)}, u32[]{:S(2)}, u32[]{:S(2)}) collective-permute-start(f32[1,14,1024]{2,1,0:T(8,128)S(1)} %maximum_bitcast_fusion.1), channel_id=1, source_target_pairs={{0,1},{1,0},{2,3},{3,2},{4,5},{5,4},{6,7},{7,6},{8,9},{9,8},{10,11... | collective-permute-start | bytes 172040 | tf_op jit(solution)/shard_map/ppermute | solution.py:225
  52.0 5.6 %collective-permute-start.9 = (f32[2,14,1024]{2,1,0:T(8,128)S(1)}, f32[2,14,1024]{2,1,0:T(8,128)S(1)}, u32[]{:S(2)}, u32[]{:S(2)}) collective-permute-start(f32[2,14,1024]{2,1,0:T(8,128)S(1)} %maximum_select_fusion.5), channel_id=1, source_target_pairs={{0,2},{1,3},{2,0},{3,1},{4,6},{5,7},{6,4},{7,5},{8,10},{9,11},{10,... | collective-permute-start | bytes 344072 | tf_op jit(solution)/shard_map/ppermute | solution.py:225

commit v9 on v8

--- a/solution.py
+++ b/solution.py
@@ -238,23 +238,24 @@
         col_given = jnp.transpose(lat_all[:, :, :dons], (1, 0, 2)).reshape(comps * levels, -1)
         side_rows = lat_all[:, :, dons:].reshape(lat_count, comps, levels, 4, cols)
         side_cols = jnp.concatenate([flat[:, :, :2], flat[:, :, cols - 2 :]], axis=2)
+        side_cols = jnp.swapaxes(side_cols, 1, 2)
         lon_packet = jnp.concatenate([col_given, side_cols.reshape(comps * levels, -1)], axis=1)
         lon_all = gather(lon_packet, "lon")
         width = col_given.shape[1]
         partner = lon_all[:, :, :width].reshape(lon_count, comps * levels, lat_count, dons)
         partner = jnp.transpose(partner, (1, 2, 0, 3)).reshape(comps * levels, -1)
-        side_cols = lon_all[:, :, width:].reshape(lon_count, comps, levels, rows, 4)
+        side_cols = lon_all[:, :, width:].reshape(lon_count, comps, levels, 4, rows)
         up = lax.dynamic_index_in_dim(side_rows, jnp.maximum(lat_pos - 1, 0), keepdims=False)[:, :, 2:]
         down = lax.dynamic_index_in_dim(side_rows, jnp.minimum(lat_pos + 1, lat_count - 1), keepdims=False)[:, :, :2]
-        left = lax.dynamic_index_in_dim(side_cols, jnp.maximum(lon_pos - 1, 0), keepdims=False)[..., 2:]
-        right = lax.dynamic_index_in_dim(side_cols, jnp.minimum(lon_pos + 1, lon_count - 1), keepdims=False)[..., :2]
+        left = lax.dynamic_index_in_dim(side_cols, jnp.maximum(lon_pos - 1, 0), keepdims=False)[:, :, 2:]
+        right = lax.dynamic_index_in_dim(side_cols, jnp.minimum(lon_pos + 1, lon_count - 1), keepdims=False)[:, :, :2]
         rim = jnp.dot(partner, pick, precision=HIGHEST).reshape(comps, levels, -1)
         rim_lat = rim[:, :, :band].reshape(comps, levels, 2, cols)
-        rim_lon = jnp.transpose(rim[:, :, band:].reshape(comps, levels, 2, rows), (0, 1, 3, 2))
+        rim_lon = rim[:, :, band:].reshape(comps, levels, 2, rows)
         up = jnp.where(on_top, rim_lat, up).reshape(comps * levels, 2, cols)
         down = jnp.where(on_bottom, rim_lat, down).reshape(comps * levels, 2, cols)
-        left = jnp.swapaxes(jnp.where(on_left, rim_lon, left).reshape(comps * levels, rows, 2), 1, 2)
-        right = jnp.swapaxes(jnp.where(on_right, rim_lon, right).reshape(comps * levels, rows, 2), 1, 2)
+        left = jnp.where(on_left, rim_lon, left).reshape(comps * levels, 2, rows)
+        right = jnp.where(on_right, rim_lon, right).reshape(comps * levels, 2, rows)
         return up, down, left, right
 
     field = state[0].reshape(comps * levels, rows, cols)

time: 68 us -> 64.9 us (0.954)
  local copies, waits for them, and re-layouts: 13.6 us -> 7.96 us
  starting transfers between devices: 17.1 us -> 18.8 us
  waiting for transfers between devices: 18.4 us -> 19.9 us
    reshape x4, local copies, waits for them, and re-layouts: 3.99 us -> 0.41 us  [the longest x2 0.23 us: section(): side_cols = lon_all[:, :, width:].reshape(lon_count, comps, levels, 4, rows)]
    ppermute x2, waiting for transfers between devices: 1.45 us -> 3.28 us  [section(): given = lax.ppermute(donation, 'panel', [(0, 1), (1, 0)])]
    ppermute x8, starting transfers between devices: 12.6 us -> 14 us  [gather(): other = lax.ppermute(held, axis, [(i, i ^ k) for i in range(size)])]
    unnamed x6 -> x12, local copies, waits for them, and re-layouts: 0.03 us -> 1.2 us
    concatenate x2 -> x0, local copies, waits for them, and re-layouts: 1.01 us -> none  [section(): side_cols = jnp.concatenate([flat[:, :, :2], flat[:, :, cols - 2:]], axis=2)]
    dynamic_slice x6 -> x0, local copies, waits for them, and re-layouts: 0.99 us -> none  [the longest x4 0.58 us: section(): lax.dynamic_index_in_dim(side_cols, jnp.minimum(lon_pos + 1, lon_count -...]
    slice x2, local copies, waits for them, and re-layouts: 1.72 us -> 0.87 us  [section(): side_rows = jnp.concatenate([flat[:, :2, :], flat[:, rows - 2:, :]], axis=1)]
    slice x2 -> x6, local copies, waits for them, and re-layouts: 2.83 us -> 2.33 us  [section(): side_cols = jnp.concatenate([flat[:, :, :2], flat[:, :, cols - 2:]], axis=2)]
  transfers between devices with their start and end apart: 10 -> 10, of which waited for: 9 -> 10; matrix products, arithmetic and copies ran while one was open for 10% -> 5% of each run, Pallas kernels for 0% -> 0%
where the time goes in v9:
time: 64.9 us; the launch traced here: 64.6 us
  waiting for transfers between devices  19.9 us (31%)
  starting transfers between devices  18.8 us (29%)
  Pallas kernels  10 us (15%)
  local copies, waits for them, and re-layouts  7.96 us (12%)
  other arithmetic  3.97 us (6%)
  matrix products  3.46 us (5%)
    ppermute x8, waiting for transfers between devices, gather(): other = lax.ppermute(held, axis, [(i, i ^ k) for i in range(size)])  16.6 us
    ppermute x8, starting transfers between devices, gather(): other = lax.ppermute(held, axis, [(i, i ^ k) for i in range(size)])  14 us
    pallas_call x2, Pallas kernels, advance(): pl.pallas_call(functools.partial(stencil_kernel, first=first), out_shape=...  7.45 us
    ppermute x2, starting transfers between devices, section(): given = lax.ppermute(donation, 'panel', [(0, 1), (1, 0)])  4.81 us
    dot_general x2, matrix products, section(): rim = jnp.dot(partner, pick, precision=HIGHEST).reshape(comps, levels, -1)  3.46 us
    ppermute x2, waiting for transfers between devices, section(): given = lax.ppermute(donation, 'panel', [(0, 1), (1, 0)])  3.28 us
    pallas_call x1, Pallas kernels, first_donation(): pl.pallas_call(donation_kernel, out_shape=(jax.ShapeDtypeStruct((planes,...  2.58 us
    slice x6, local copies, waits for them, and re-layouts, section(): side_cols = jnp.concatenate([flat[:, :, :2], flat[:, :, cols - 2:]], axis=2)  2.33 us
  transfers between devices with their start and end apart: 10, of which 10 were waited for; matrix products, arithmetic and copies ran while one was open for 5% of the time, Pallas kernels for 0%

profile of v9, /device:TPU:0, one launch (start us, length us, event | category | flops | bytes accessed | tf_op | source)
XLA Modules:
  0.0 64.6 jit_solution(5445533899464347465)
XLA Ops:
  1.4 2.6 %shard_map.55 = (f32[14,192]{1,0:T(8,128)}, f32[128,192]{1,0:T(8,128)}, f32[64,192]{1,0:T(8,128)}) custom-call(f32[14,64,128]{2,1,0:T(8,128)} %bitcast.75, s32[1,192]{1,0:T(1,128)} %bitcast.97, f32[2,192]{1,0:T(2,128)} %bitcast.96, f32[2,192]{1,0:T(2,128)} %pad_maximum_fusion.4.turn_ref), custom_call_target="tpu_custom_call" | custom-call | tf_op jit(solution)/shard_map/pallas_call | solution.py:166
  4.0 3.0 %collective-permute-start = (f32[14,192]{1,0:T(8,128)}, f32[14,192]{1,0:T(8,128)S(1)}, u32[]{:S(2)}, u32[]{:S(2)}) collective-permute-start(f32[14,192]{1,0:T(8,128)} %get-tuple-element.10), channel_id=1, source_target_pairs={{0,16},{16,0},{1,17},{17,1},{2,18},{18,2},{3,19},{19,3},{4,20},{20... | collective-permute-start | bytes 32264 | tf_op jit(solution)/shard_map/ppermute | solution.py:233
  7.7 1.2 %collective-permute-done = f32[14,192]{1,0:T(8,128)S(1)} collective-permute-done((f32[14,192]{1,0:T(8,128)}, f32[14,192]{1,0:T(8,128)S(1)}, u32[]{:S(2)}, u32[]{:S(2)}) %collective-permute-start) | collective-permute-done | bytes 10784 | tf_op jit(solution)/shard_map/ppermute | solution.py:233
  9.0 2.1 %collective-permute-start.1 = (f32[1,14,704]{2,0,1:T(1,128)S(1)}, f32[1,14,704]{2,0,1:T(1,128)S(1)}, u32[]{:S(2)}, u32[]{:S(2)}) collective-permute-start(f32[1,14,704]{2,0,1:T(1,128)S(1)} %broadcast_in_dim.14), channel_id=1, source_target_pairs={{0,4},{4,0},{8,12},{12,8},{1,5},{5,1},{9,13},{13,9},{2,6},{6,2},{1... | collective-permute-start | bytes 118280 | tf_op jit(solution)/shard_map/ppermute | solution.py:225
  11.5 1.6 %collective-permute-done.1 = f32[1,14,704]{2,0,1:T(1,128)S(1)} collective-permute-done((f32[1,14,704]{2,0,1:T(1,128)S(1)}, f32[1,14,704]{2,0,1:T(1,128)S(1)}, u32[]{:S(2)}, u32[]{:S(2)}) %collective-permute-start.1) | collective-permute-done | bytes 39456 | tf_op jit(solution)/shard_map/ppermute | solution.py:225
  13.2 3.1 %collective-permute-start.2 = (f32[2,14,704]{2,0,1:T(2,128)S(1)}, f32[2,14,704]{2,0,1:T(2,128)S(1)}, u32[]{:S(2)}, u32[]{:S(2)}) collective-permute-start(f32[2,14,704]{2,0,1:T(2,128)S(1)} %maximum_select_fusion.6), channel_id=1, source_target_pairs={{0,8},{4,12},{8,0},{12,4},{1,9},{5,13},{9,1},{13,5},{2,10},{6,14},... | collective-permute-start | bytes 236552 | tf_op jit(solution)/shard_map/ppermute | solution.py:225
  16.5 2.4 %collective-permute-done.2 = f32[2,14,704]{2,0,1:T(2,128)S(1)} collective-permute-done((f32[2,14,704]{2,0,1:T(2,128)S(1)}, f32[2,14,704]{2,0,1:T(2,128)S(1)}, u32[]{:S(2)}, u32[]{:S(2)}) %collective-permute-start.2) | collective-permute-done | bytes 78880 | tf_op jit(solution)/shard_map/ppermute | solution.py:225
  19.2 1.2 %collective-permute-done.3 = f32[1,14,1024]{2,1,0:T(8,128)S(1)} collective-permute-done((f32[1,14,1024]{2,1,0:T(8,128)S(1)}, f32[1,14,1024]{2,1,0:T(8,128)S(1)}, u32[]{:S(2)}, u32[]{:S(2)}) %collective-permute-start.3) | collective-permute-done | bytes 57376 | tf_op jit(solution)/shard_map/ppermute | solution.py:225
  20.4 1.9 %collective-permute-start.4 = (f32[2,14,1024]{2,1,0:T(8,128)S(1)}, f32[2,14,1024]{2,1,0:T(8,128)S(1)}, u32[]{:S(2)}, u32[]{:S(2)}) collective-permute-start(f32[2,14,1024]{2,1,0:T(8,128)S(1)} %maximum_select_fusion.4), channel_id=1, source_target_pairs={{0,2},{1,3},{2,0},{3,1},{4,6},{5,7},{6,4},{7,5},{8,10},{9,11},{10,... | collective-permute-start | bytes 344072 | tf_op jit(solution)/shard_map/ppermute | solution.py:225
  22.5 3.6 %collective-permute-done.4 = f32[2,14,1024]{2,1,0:T(8,128)S(1)} collective-permute-done((f32[2,14,1024]{2,1,0:T(8,128)S(1)}, f32[2,14,1024]{2,1,0:T(8,128)S(1)}, u32[]{:S(2)}, u32[]{:S(2)}) %collective-permute-start.4) | collective-permute-done | bytes 114720 | tf_op jit(solution)/shard_map/ppermute | solution.py:225
  27.2 1.7 %fusion.3 = f32[7,2,384]{2,0,1:T(8,128)S(1)} fusion(s32[384]{0:T(512)S(1)} %pad_add_fusion, f32[7,2,3072]{2,1,0:T(2,128)S(1)} %dot_general.10), kind=kOutput, calls=%fused_computation.3 | convolution fusion | flops 199360512 | bytes 195072 | tf_op jit(solution)/shard_map/dot_general | solution.py:252
  30.5 3.9 %shard_map.56 = (f32[14,64,128]{2,1,0:T(8,128)}, f32[14,192]{1,0:T(8,128)}) custom-call(f32[14,64,128]{2,1,0:T(8,128)} %bitcast.76, f32[14,2,128]{2,1,0:T(2,128)} %bitcast.94, f32[14,2,128]{2,1,0:T(2,128)} %bitcast.93, f32[14,2,64]{2,1,0:T(2,128)} %bitcast.90, f32[14,2,64]{2,1,0:T(2,128)} %bitcast.89, f32[14,64,128]{2,1,0:T(8,128)} %bitcast.77, ...), custom_call_target="tpu_custom_call" | custom-call | tf_op jit(solution)/shard_map/pallas_call | solution.py:114
  34.5 0.9 %fusion.11 = (f32[14,2,128]{2,1,0:T(2,128)S(1)}, f32[14,2,128]{2,1,0:T(2,128)S(1)}) fusion(f32[14,64,128]{2,1,0:T(8,128)} %get-tuple-element.13.f_ref), kind=kLoop, calls=%fused_computation.50 | loop fusion | bytes 57344 | tf_op jit(solution)/shard_map/slice | solution.py:235
  35.3 1.8 %collective-permute-start.5 = (f32[14,192]{1,0:T(8,128)}, f32[14,192]{1,0:T(8,128)S(1)}, u32[]{:S(2)}, u32[]{:S(2)}) collective-permute-start(f32[14,192]{1,0:T(8,128)} %get-tuple-element.14), channel_id=1, source_target_pairs={{0,16},{16,0},{1,17},{17,1},{2,18},{18,2},{3,19},{19,3},{4,20},{20... | collective-permute-start | bytes 32264 | tf_op jit(solution)/shard_map/ppermute | solution.py:233
  37.2 2.1 %collective-permute-done.5 = f32[14,192]{1,0:T(8,128)S(1)} collective-permute-done((f32[14,192]{1,0:T(8,128)}, f32[14,192]{1,0:T(8,128)S(1)}, u32[]{:S(2)}, u32[]{:S(2)}) %collective-permute-start.5) | collective-permute-done | bytes 10784 | tf_op jit(solution)/shard_map/ppermute | solution.py:233
  39.4 1.9 %collective-permute-start.6 = (f32[1,14,704]{2,0,1:T(1,128)S(1)}, f32[1,14,704]{2,0,1:T(1,128)S(1)}, u32[]{:S(2)}, u32[]{:S(2)}) collective-permute-start(f32[1,14,704]{2,0,1:T(1,128)S(1)} %broadcast_in_dim.16), channel_id=1, source_target_pairs={{0,4},{4,0},{8,12},{12,8},{1,5},{5,1},{9,13},{13,9},{2,6},{6,2},{1... | collective-permute-start | bytes 118280 | tf_op jit(solution)/shard_map/ppermute | solution.py:225
  41.4 1.3 %fusion.10 = (f32[14,64,2]{2,1,0:T(8,128)S(1)}, f32[14,64,2]{2,1,0:T(8,128)S(1)}) fusion(f32[14,64,128]{2,1,0:T(8,128)} %get-tuple-element.13.f_ref), kind=kLoop, calls=%fused_computation.49 | loop fusion | bytes 28672 | tf_op jit(solution)/shard_map/slice | solution.py:240
  43.7 3.3 %collective-permute-start.7 = (f32[2,14,704]{2,0,1:T(2,128)S(1)}, f32[2,14,704]{2,0,1:T(2,128)S(1)}, u32[]{:S(2)}, u32[]{:S(2)}) collective-permute-start(f32[2,14,704]{2,0,1:T(2,128)S(1)} %maximum_select_fusion.7), channel_id=1, source_target_pairs={{0,8},{4,12},{8,0},{12,4},{1,9},{5,13},{9,1},{13,5},{2,10},{6,14},... | collective-permute-start | bytes 236552 | tf_op jit(solution)/shard_map/ppermute | solution.py:225
  47.1 2.4 %collective-permute-done.7 = f32[2,14,704]{2,0,1:T(2,128)S(1)} collective-permute-done((f32[2,14,704]{2,0,1:T(2,128)S(1)}, f32[2,14,704]{2,0,1:T(2,128)S(1)}, u32[]{:S(2)}, u32[]{:S(2)}) %collective-permute-start.7) | collective-permute-done | bytes 78880 | tf_op jit(solution)/shard_map/ppermute | solution.py:225
  49.7 1.2 %collective-permute-done.8 = f32[1,14,1024]{2,1,0:T(8,128)S(1)} collective-permute-done((f32[1,14,1024]{2,1,0:T(8,128)S(1)}, f32[1,14,1024]{2,1,0:T(8,128)S(1)}, u32[]{:S(2)}, u32[]{:S(2)}) %collective-permute-start.8) | collective-permute-done | bytes 57376 | tf_op jit(solution)/shard_map/ppermute | solution.py:225
  51.0 1.6 %collective-permute-start.9 = (f32[2,14,1024]{2,1,0:T(8,128)S(1)}, f32[2,14,1024]{2,1,0:T(8,128)S(1)}, u32[]{:S(2)}, u32[]{:S(2)}) collective-permute-start(f32[2,14,1024]{2,1,0:T(8,128)S(1)} %maximum_select_fusion.5), channel_id=1, source_target_pairs={{0,2},{1,3},{2,0},{3,1},{4,6},{5,7},{6,4},{7,5},{8,10},{9,11},{10,... | collective-permute-start | bytes 344072 | tf_op jit(solution)/shard_map/ppermute | solution.py:225
  52.8 3.8 %collective-permute-done.9 = f32[2,14,1024]{2,1,0:T(8,128)S(1)} collective-permute-done((f32[2,14,1024]{2,1,0:T(8,128)S(1)}, f32[2,14,1024]{2,1,0:T(8,128)S(1)}, u32[]{:S(2)}, u32[]{:S(2)}) %collective-permute-start.9) | collective-permute-done | bytes 114720 | tf_op jit(solution)/shard_map/ppermute | solution.py:225
  57.7 1.7 %fusion.1 = f32[7,2,384]{2,0,1:T(8,128)S(1)} fusion(s32[384]{0:T(512)S(1)} %pad_add_fusion, f32[7,2,3072]{2,1,0:T(2,128)S(1)} %dot_general.12), kind=kOutput, calls=%fused_computation.2 | convolution fusion | flops 199360512 | bytes 195072 | tf_op jit(solution)/shard_map/dot_general | solution.py:252
  61.1 3.5 %shard_map.57 = f32[14,64,128]{2,1,0:T(8,128)} custom-call(f32[14,64,128]{2,1,0:T(8,128)} %get-tuple-element.13.f_ref, f32[14,2,128]{2,1,0:T(2,128)} %bitcast.92, f32[14,2,128]{2,1,0:T(2,128)} %bitcast.91, f32[14,2,64]{2,1,0:T(2,128)} %bitcast.88, f32[14,2,64]{2,1,0:T(2,128)} %bitcast.87, f32[14,64,128]{2,1,0:T(8,128)} %bitcast.78, ...), custom_call_target="tpu_custom_call" | custom-call | tf_op jit(solution)/shard_map/pallas_call | solution.py:114
  (90 shorter events, 10.3 us)
Async XLA Ops:
  0.0 6.9 %copy-start = (f32[1,7,2,64,128]{4,3,2,1,0:T(8,128)S(1)}, f32[1,7,2,64,128]{4,3,2,1,0:T(8,128)}, u32[]{:S(2)}) copy-start(f32[1,7,2,64,128]{4,3,2,1,0:T(8,128)} %param.5) | copy-start | bytes 1376260
  4.0 4.9 %collective-permute-start = (f32[14,192]{1,0:T(8,128)}, f32[14,192]{1,0:T(8,128)S(1)}, u32[]{:S(2)}, u32[]{:S(2)}) collective-permute-start(f32[14,192]{1,0:T(8,128)} %get-tuple-element.10), channel_id=1, source_target_pairs={{0,16},{16,0},{1,17},{17,1},{2,18},{18,2},{3,19},{19,3},{4,20},{20... | collective-permute-start | bytes 32264 | tf_op jit(solution)/shard_map/ppermute | solution.py:233
  6.9 0.7 %copy-start.3 = (s32[1,1,1,768]{3,2,1,0:T(1,128)S(1)}, s32[1,1,1,768]{3,2,1,0:T(1,128)}, u32[]{:S(2)}) copy-start(s32[1,1,1,768]{3,2,1,0:T(1,128)} %param.6) | copy-start | bytes 9220
  9.0 4.1 %collective-permute-start.1 = (f32[1,14,704]{2,0,1:T(1,128)S(1)}, f32[1,14,704]{2,0,1:T(1,128)S(1)}, u32[]{:S(2)}, u32[]{:S(2)}) collective-permute-start(f32[1,14,704]{2,0,1:T(1,128)S(1)} %broadcast_in_dim.14), channel_id=1, source_target_pairs={{0,4},{4,0},{8,12},{12,8},{1,5},{5,1},{9,13},{13,9},{2,6},{6,2},{1... | collective-permute-start | bytes 118280 | tf_op jit(solution)/shard_map/ppermute | solution.py:225
  13.2 5.6 %collective-permute-start.2 = (f32[2,14,704]{2,0,1:T(2,128)S(1)}, f32[2,14,704]{2,0,1:T(2,128)S(1)}, u32[]{:S(2)}, u32[]{:S(2)}) collective-permute-start(f32[2,14,704]{2,0,1:T(2,128)S(1)} %maximum_select_fusion.6), channel_id=1, source_target_pairs={{0,8},{4,12},{8,0},{12,4},{1,9},{5,13},{9,1},{13,5},{2,10},{6,14},... | collective-permute-start | bytes 236552 | tf_op jit(solution)/shard_map/ppermute | solution.py:225
  19.1 1.3 %collective-permute-start.3 = (f32[1,14,1024]{2,1,0:T(8,128)S(1)}, f32[1,14,1024]{2,1,0:T(8,128)S(1)}, u32[]{:S(2)}, u32[]{:S(2)}) collective-permute-start(f32[1,14,1024]{2,1,0:T(8,128)S(1)} %maximum_bitcast_fusion), channel_id=1, source_target_pairs={{0,1},{1,0},{2,3},{3,2},{4,5},{5,4},{6,7},{7,6},{8,9},{9,8},{10,11... | collective-permute-start | bytes 172040 | tf_op jit(solution)/shard_map/ppermute | solution.py:225
  20.4 5.7 %collective-permute-start.4 = (f32[2,14,1024]{2,1,0:T(8,128)S(1)}, f32[2,14,1024]{2,1,0:T(8,128)S(1)}, u32[]{:S(2)}, u32[]{:S(2)}) collective-permute-start(f32[2,14,1024]{2,1,0:T(8,128)S(1)} %maximum_select_fusion.4), channel_id=1, source_target_pairs={{0,2},{1,3},{2,0},{3,1},{4,6},{5,7},{6,4},{7,5},{8,10},{9,11},{10,... | collective-permute-start | bytes 344072 | tf_op jit(solution)/shard_map/ppermute | solution.py:225
  26.1 0.7 %copy-start.2 = (f32[4,14,1024]{2,1,0:T(8,128)}, f32[4,14,1024]{2,1,0:T(8,128)S(1)}, u32[]{:S(2)}) copy-start(f32[4,14,1024]{2,1,0:T(8,128)S(1)} %maximum_select_fusion) | copy-start | bytes 688132
  27.2 1.9 %slice-start.1 = ((f32[4,14,1024]{2,1,0:T(8,128)}), f32[4,14,256]{2,1,0:T(8,128)S(1)}, s32[]{:S(2)}) async-start(f32[4,14,1024]{2,1,0:T(8,128)} %copy-done.2), calls=%async_computation.1 | async-start | bytes 131072 | tf_op jit(solution)/shard_map/slice | solution.py:247
  35.3 4.0 %collective-permute-start.5 = (f32[14,192]{1,0:T(8,128)}, f32[14,192]{1,0:T(8,128)S(1)}, u32[]{:S(2)}, u32[]{:S(2)}) collective-permute-start(f32[14,192]{1,0:T(8,128)} %get-tuple-element.14), channel_id=1, source_target_pairs={{0,16},{16,0},{1,17},{17,1},{2,18},{18,2},{3,19},{19,3},{4,20},{20... | collective-permute-start | bytes 32264 | tf_op jit(solution)/shard_map/ppermute | solution.py:233
  39.4 4.1 %collective-permute-start.6 = (f32[1,14,704]{2,0,1:T(1,128)S(1)}, f32[1,14,704]{2,0,1:T(1,128)S(1)}, u32[]{:S(2)}, u32[]{:S(2)}) collective-permute-start(f32[1,14,704]{2,0,1:T(1,128)S(1)} %broadcast_in_dim.16), channel_id=1, source_target_pairs={{0,4},{4,0},{8,12},{12,8},{1,5},{5,1},{9,13},{13,9},{2,6},{6,2},{1... | collective-permute-start | bytes 118280 | tf_op jit(solution)/shard_map/ppermute | solution.py:225
  43.7 5.7 %collective-permute-start.7 = (f32[2,14,704]{2,0,1:T(2,128)S(1)}, f32[2,14,704]{2,0,1:T(2,128)S(1)}, u32[]{:S(2)}, u32[]{:S(2)}) collective-permute-start(f32[2,14,704]{2,0,1:T(2,128)S(1)} %maximum_select_fusion.7), channel_id=1, source_target_pairs={{0,8},{4,12},{8,0},{12,4},{1,9},{5,13},{9,1},{13,5},{2,10},{6,14},... | collective-permute-start | bytes 236552 | tf_op jit(solution)/shard_map/ppermute | solution.py:225
  49.7 1.3 %collective-permute-start.8 = (f32[1,14,1024]{2,1,0:T(8,128)S(1)}, f32[1,14,1024]{2,1,0:T(8,128)S(1)}, u32[]{:S(2)}, u32[]{:S(2)}) collective-permute-start(f32[1,14,1024]{2,1,0:T(8,128)S(1)} %maximum_bitcast_fusion.1), channel_id=1, source_target_pairs={{0,1},{1,0},{2,3},{3,2},{4,5},{5,4},{6,7},{7,6},{8,9},{9,8},{10,11... | collective-permute-start | bytes 172040 | tf_op jit(solution)/shard_map/ppermute | solution.py:225
  51.0 5.6 %collective-permute-start.9 = (f32[2,14,1024]{2,1,0:T(8,128)S(1)}, f32[2,14,1024]{2,1,0:T(8,128)S(1)}, u32[]{:S(2)}, u32[]{:S(2)}) collective-permute-start(f32[2,14,1024]{2,1,0:T(8,128)S(1)} %maximum_select_fusion.5), channel_id=1, source_target_pairs={{0,2},{1,3},{2,0},{3,1},{4,6},{5,7},{6,4},{7,5},{8,10},{9,11},{10,... | collective-permute-start | bytes 344072 | tf_op jit(solution)/shard_map/ppermute | solution.py:225
  56.7 0.7 %copy-start.1 = (f32[4,14,1024]{2,1,0:T(8,128)}, f32[4,14,1024]{2,1,0:T(8,128)S(1)}, u32[]{:S(2)}) copy-start(f32[4,14,1024]{2,1,0:T(8,128)S(1)} %maximum_select_fusion.1) | copy-start | bytes 688132
  57.7 1.9 %slice-start = ((f32[4,14,1024]{2,1,0:T(8,128)}), f32[4,14,256]{2,1,0:T(8,128)S(1)}, s32[]{:S(2)}) async-start(f32[4,14,1024]{2,1,0:T(8,128)} %copy-done.1), calls=%async_computation | async-start | bytes 131072 | tf_op jit(solution)/shard_map/slice | solution.py:247

commit v10 on v9

--- a/solution.py
+++ b/solution.py
@@ -17,12 +17,15 @@
 HIGHEST = lax.Precision.HIGHEST
 
 
-def stencil_kernel(f_ref, up_ref, down_ref, left_ref, right_ref, base_ref, lon_ref, lat_ref, turn_ref, o_ref, *rest, first):
-    planes, height, width = f_ref.shape
-    comps = planes // 2
+def stencil_kernel(*refs, first):
+    if first:
+        f_ref, other_ref, up_ref, down_ref, left_ref, right_ref, lon_ref, lat_ref, turn_ref, o_ref, don_ref = refs
+    else:
+        f_ref, other_ref, up_ref, down_ref, left_ref, right_ref, base_ref, lon_ref, lat_ref, turn_ref, o_ref = refs
+    comps, _, height, width = f_ref.shape
+    level = pl.program_id(0)
     row = lax.broadcasted_iota(jnp.int32, (height, width), 0)
     col = lax.broadcasted_iota(jnp.int32, (height, width), 1)
-
     eye = jnp.where(
         lax.broadcasted_iota(jnp.int32, (height, height), 0) == lax.broadcasted_iota(jnp.int32, (height, height), 1),
         1.0,
@@ -30,9 +33,9 @@
     )
     pick_row = lax.broadcasted_iota(jnp.int32, (width, height), 0)
 
-    def columns(k):
-        left = left_ref[k]
-        right = right_ref[k]
+    def columns(c):
+        left = left_ref[c, 0]
+        right = right_ref[c, 0]
         rows_of = jnp.where(
             pick_row == 0,
             left[0:1, :],
@@ -42,11 +45,11 @@
             eye, rows_of, (((1,), (1,)), ((), ())), precision=HIGHEST, preferred_element_type=jnp.float32
         )
 
-    def terms(k):
-        x = f_ref[k]
-        up = up_ref[k]
-        down = down_ref[k]
-        sides = columns(k)
+    def terms(c):
+        x = f_ref[c, 0]
+        up = up_ref[c, 0]
+        down = down_ref[c, 0]
+        sides = columns(c)
         left = sides[:, 0:2]
         right = sides[:, 2:4]
         lat_m1 = jnp.where(row == 0, up[1:2, :], pltpu.roll(x, 1, 0))
@@ -66,56 +69,91 @@
         lap = lat_p1 + lat_m1 + lon_p1 + lon_m1 - 4.0 * x
         return x, d_lat, d_lon, lap
 
-    for level in range(2):
-        def plane(c):
-            return c * 2 + level
-
-        def value(c):
-            return f_ref[plane(c)]
-
-        def lap_of(c, x, lap):
-            above = f_ref[c * 2 + 1] if level == 0 else 0.0
-            below = f_ref[c * 2] if level == 1 else 0.0
-            return lap + above + below - 2.0 * x
-
-        def store(c, x, rate):
-            section = x + time_step * rate
-            if first:
-                o_ref[plane(c)] = section
+    def lap_of(c, x, lap):
+        return lap + other_ref[c, 0] - 2.0 * x
+
+    def store(c, x, rate):
+        section = x + time_step * rate
+        if first:
+            o_ref[c, 0] = section
+        else:
+            o_ref[c, 0] = 0.5 * base_ref[c, 0] + 0.5 * section
+
+    u1, u2, u4, u5, u6 = (f_ref[c, 0] for c in (1, 2, 4, 5, 6))
+    for c in range(3):
+        xa, lat_a, lon_a, lap_a = terms(c)
+        xb, lat_b, lon_b, lap_b = terms(c + 3)
+        adv_u_a = u1 * lat_a + u2 * lon_a
+        adv_b_a = u4 * lat_a + u5 * lon_a
+        adv_u_b = u1 * lat_b + u2 * lon_b
+        adv_b_b = u4 * lat_b + u5 * lon_b
+        rate_a = -adv_u_a + adv_b_b + viscosity * lap_of(c, xa, lap_a)
+        if c == 0:
+            rate_a = rate_a + buoyancy * u6
+        rate_b = adv_b_a - adv_u_b + resistivity * lap_of(c + 3, xb, lap_b)
+        store(c, xa, rate_a)
+        store(c + 3, xb, rate_b)
+    x6, lat_6, lon_6, lap_6 = terms(6)
+    adv_u_6 = u1 * lat_6 + u2 * lon_6
+    store(6, x6, -adv_u_6 + diffusivity * lap_of(6, x6, lap_6))
+
+    if first:
+        weight_lon = lon_ref[...]
+        weight_lat = lat_ref[...]
+        cosine = turn_ref[0:1, :]
+        sine = turn_ref[1:2, :]
+        values = []
+        for c in range(comps):
+            along = jnp.dot(o_ref[c, 0], weight_lon, precision=HIGHEST, preferred_element_type=jnp.float32)
+            values.append(jnp.sum(along * weight_lat, axis=0, keepdims=True))
+        for c in range(comps):
+            if c in (1, 4):
+                value = cosine * values[c] - sine * values[c + 1]
+            elif c in (2, 5):
+                value = sine * values[c - 1] + cosine * values[c]
             else:
-                o_ref[plane(c)] = 0.5 * base_ref[plane(c)] + 0.5 * section
-
-        u1, u2, u4, u5, u6 = value(1), value(2), value(4), value(5), value(6)
-        for c in range(3):
-            xa, lat_a, lon_a, lap_a = terms(plane(c))
-            xb, lat_b, lon_b, lap_b = terms(plane(c + 3))
-            adv_u_a = u1 * lat_a + u2 * lon_a
-            adv_b_a = u4 * lat_a + u5 * lon_a
-            adv_u_b = u1 * lat_b + u2 * lon_b
-            adv_b_b = u4 * lat_b + u5 * lon_b
-            rate_a = -adv_u_a + adv_b_b + viscosity * lap_of(c, xa, lap_a)
-            if c == 0:
-                rate_a = rate_a + buoyancy * u6
-            rate_b = adv_b_a - adv_u_b + resistivity * lap_of(c + 3, xb, lap_b)
-            store(c, xa, rate_a)
-            store(c + 3, xb, rate_b)
-        x6, lat_6, lon_6, lap_6 = terms(plane(6))
-        adv_u_6 = u1 * lat_6 + u2 * lon_6
-        store(6, x6, -adv_u_6 + diffusivity * lap_of(6, x6, lap_6))
-
+                value = values[c]
+            don_ref[pl.ds(2 * c + level, 1), :] = value
+
+
+def advance(field, up, down, left, right, base, lon, lat, turn, first):
+    planes, height, width = field.shape
+    comps = planes // 2
+    field = field.reshape(comps, 2, height, width)
+
+    def by_level(shape, other=False):
+        if other:
+            return pl.BlockSpec((comps, 1) + shape, lambda r: (0, 1 - r, 0, 0))
+        return pl.BlockSpec((comps, 1) + shape, lambda r: (0, r, 0, 0))
+
+    def whole(shape):
+        return pl.BlockSpec(shape, lambda r: (0,) * len(shape))
+
+    args = [field, field, up.reshape(comps, 2, 2, width), down.reshape(comps, 2, 2, width)]
+    args += [left.reshape(comps, 2, 2, height), right.reshape(comps, 2, 2, height)]
+    specs = [by_level((height, width)), by_level((height, width), True), by_level((2, width)), by_level((2, width))]
+    specs += [by_level((2, height)), by_level((2, height))]
+    if not first:
+        args.append(base.reshape(comps, 2, height, width))
+        specs.append(by_level((height, width)))
+    args += [lon, lat, turn]
+    specs += [whole(lon.shape), whole(lat.shape), whole(turn.shape)]
+    shape = jax.ShapeDtypeStruct(field.shape, field.dtype)
+    out_specs = by_level((height, width))
     if first:
-        donate_planes(lambda k: o_ref[k], planes, lon_ref[...], lat_ref[...], turn_ref, rest[0])
-
-
-def advance(field, up, down, left, right, base, lon, lat, turn, first):
-    shape = jax.ShapeDtypeStruct(field.shape, field.dtype)
-    if first:
-        shape = (shape, jax.ShapeDtypeStruct((field.shape[0], lon.shape[1]), jnp.float32))
-    return pl.pallas_call(
+        shape = (shape, jax.ShapeDtypeStruct((planes, lon.shape[1]), jnp.float32))
+        out_specs = (out_specs, whole((planes, lon.shape[1])))
+    out = pl.pallas_call(
         functools.partial(stencil_kernel, first=first),
+        grid=(2,),
+        in_specs=specs,
+        out_specs=out_specs,
         out_shape=shape,
         interpret=INTERPRET,
-    )(field, up, down, left, right, base, lon, lat, turn)
+    )(*args)
+    if first:
+        return out[0].reshape(planes, height, width), out[1]
+    return out.reshape(planes, height, width)
 
 
 def donation_weights(cells_ref, frac_ref, rows, cols):

time: 64.9 us -> 65.5 us (level)
  Pallas kernels: 10 us -> 10.7 us
    pallas_call x2, Pallas kernels: 7.45 us -> 8.11 us  [advance(): pl.pallas_call(functools.partial(stencil_kernel, first=first), grid=(2,),...]
    slice x6 -> x4, local copies, waits for them, and re-layouts: 2.33 us -> 1.93 us  [section(): side_cols = jnp.concatenate([flat[:, :, :2], flat[:, :, cols - 2:]], axis=2)]
    unnamed x12 -> x14, local copies, waits for them, and re-layouts: 1.2 us -> 1.6 us
where the time goes in v10:
time: 65.5 us; the launch traced here: 65.2 us
  waiting for transfers between devices  19.9 us (30%)
  starting transfers between devices  18.8 us (29%)
  Pallas kernels  10.7 us (16%)
  local copies, waits for them, and re-layouts  7.96 us (12%)
  other arithmetic  3.97 us (6%)
  matrix products  3.46 us (5%)
    ppermute x8, waiting for transfers between devices, gather(): other = lax.ppermute(held, axis, [(i, i ^ k) for i in range(size)])  16.6 us
    ppermute x8, starting transfers between devices, gather(): other = lax.ppermute(held, axis, [(i, i ^ k) for i in range(size)])  14 us
    pallas_call x2, Pallas kernels, advance(): pl.pallas_call(functools.partial(stencil_kernel, first=first), grid=(2,),...  8.11 us
    ppermute x2, starting transfers between devices, section(): given = lax.ppermute(donation, 'panel', [(0, 1), (1, 0)])  4.81 us
    dot_general x2, matrix products, section(): rim = jnp.dot(partner, pick, precision=HIGHEST).reshape(comps, levels, -1)  3.46 us
    ppermute x2, waiting for transfers between devices, section(): given = lax.ppermute(donation, 'panel', [(0, 1), (1, 0)])  3.28 us
    pallas_call x1, Pallas kernels, first_donation(): pl.pallas_call(donation_kernel, out_shape=(jax.ShapeDtypeStruct((planes,...  2.58 us
    slice x4, local copies, waits for them, and re-layouts, section(): side_cols = jnp.concatenate([flat[:, :, :2], flat[:, :, cols - 2:]], axis=2)  1.93 us
  transfers between devices with their start and end apart: 10, of which 10 were waited for; matrix products, arithmetic and copies ran while one was open for 5% of the time, Pallas kernels for 0%

profile of v10, /device:TPU:0, one launch (start us, length us, event | category | flops | bytes accessed | tf_op | source)
XLA Modules:
  0.0 65.2 jit_solution(14471395600214162981)
XLA Ops:
  1.4 2.6 %shard_map.55 = (f32[14,192]{1,0:T(8,128)}, f32[128,192]{1,0:T(8,128)}, f32[64,192]{1,0:T(8,128)}) custom-call(f32[14,64,128]{2,1,0:T(8,128)} %bitcast.69, s32[1,192]{1,0:T(1,128)} %bitcast.85, f32[2,192]{1,0:T(2,128)} %bitcast.84, f32[2,192]{1,0:T(2,128)} %pad_maximum_fusion.4.turn_ref.refs_8_.refs_9_), custom_call_target="tpu_custom_call" | custom-call | tf_op jit(solution)/shard_map/pallas_call | solution.py:204
  4.0 3.0 %collective-permute-start = (f32[14,192]{1,0:T(8,128)}, f32[14,192]{1,0:T(8,128)S(1)}, u32[]{:S(2)}, u32[]{:S(2)}) collective-permute-start(f32[14,192]{1,0:T(8,128)} %get-tuple-element.10), channel_id=1, source_target_pairs={{0,16},{16,0},{1,17},{17,1},{2,18},{18,2},{3,19},{19,3},{4,20},{20... | collective-permute-start | bytes 32264 | tf_op jit(solution)/shard_map/ppermute | solution.py:271
  7.7 1.2 %collective-permute-done = f32[14,192]{1,0:T(8,128)S(1)} collective-permute-done((f32[14,192]{1,0:T(8,128)}, f32[14,192]{1,0:T(8,128)S(1)}, u32[]{:S(2)}, u32[]{:S(2)}) %collective-permute-start) | collective-permute-done | bytes 10784 | tf_op jit(solution)/shard_map/ppermute | solution.py:271
  9.0 2.1 %collective-permute-start.1 = (f32[1,14,704]{2,0,1:T(1,128)S(1)}, f32[1,14,704]{2,0,1:T(1,128)S(1)}, u32[]{:S(2)}, u32[]{:S(2)}) collective-permute-start(f32[1,14,704]{2,0,1:T(1,128)S(1)} %broadcast_in_dim.14), channel_id=1, source_target_pairs={{0,4},{4,0},{8,12},{12,8},{1,5},{5,1},{9,13},{13,9},{2,6},{6,2},{1... | collective-permute-start | bytes 118280 | tf_op jit(solution)/shard_map/ppermute | solution.py:263
  11.5 1.6 %collective-permute-done.1 = f32[1,14,704]{2,0,1:T(1,128)S(1)} collective-permute-done((f32[1,14,704]{2,0,1:T(1,128)S(1)}, f32[1,14,704]{2,0,1:T(1,128)S(1)}, u32[]{:S(2)}, u32[]{:S(2)}) %collective-permute-start.1) | collective-permute-done | bytes 39456 | tf_op jit(solution)/shard_map/ppermute | solution.py:263
  13.2 3.1 %collective-permute-start.2 = (f32[2,14,704]{2,0,1:T(2,128)S(1)}, f32[2,14,704]{2,0,1:T(2,128)S(1)}, u32[]{:S(2)}, u32[]{:S(2)}) collective-permute-start(f32[2,14,704]{2,0,1:T(2,128)S(1)} %maximum_select_fusion.6), channel_id=1, source_target_pairs={{0,8},{4,12},{8,0},{12,4},{1,9},{5,13},{9,1},{13,5},{2,10},{6,14},... | collective-permute-start | bytes 236552 | tf_op jit(solution)/shard_map/ppermute | solution.py:263
  16.5 2.4 %collective-permute-done.2 = f32[2,14,704]{2,0,1:T(2,128)S(1)} collective-permute-done((f32[2,14,704]{2,0,1:T(2,128)S(1)}, f32[2,14,704]{2,0,1:T(2,128)S(1)}, u32[]{:S(2)}, u32[]{:S(2)}) %collective-permute-start.2) | collective-permute-done | bytes 78880 | tf_op jit(solution)/shard_map/ppermute | solution.py:263
  19.2 1.2 %collective-permute-done.3 = f32[1,14,1024]{2,1,0:T(8,128)S(1)} collective-permute-done((f32[1,14,1024]{2,1,0:T(8,128)S(1)}, f32[1,14,1024]{2,1,0:T(8,128)S(1)}, u32[]{:S(2)}, u32[]{:S(2)}) %collective-permute-start.3) | collective-permute-done | bytes 57376 | tf_op jit(solution)/shard_map/ppermute | solution.py:263
  20.4 1.9 %collective-permute-start.4 = (f32[2,14,1024]{2,1,0:T(8,128)S(1)}, f32[2,14,1024]{2,1,0:T(8,128)S(1)}, u32[]{:S(2)}, u32[]{:S(2)}) collective-permute-start(f32[2,14,1024]{2,1,0:T(8,128)S(1)} %maximum_select_fusion.4), channel_id=1, source_target_pairs={{0,2},{1,3},{2,0},{3,1},{4,6},{5,7},{6,4},{7,5},{8,10},{9,11},{10,... | collective-permute-start | bytes 344072 | tf_op jit(solution)/shard_map/ppermute | solution.py:263
  22.5 3.6 %collective-permute-done.4 = f32[2,14,1024]{2,1,0:T(8,128)S(1)} collective-permute-done((f32[2,14,1024]{2,1,0:T(8,128)S(1)}, f32[2,14,1024]{2,1,0:T(8,128)S(1)}, u32[]{:S(2)}, u32[]{:S(2)}) %collective-permute-start.4) | collective-permute-done | bytes 114720 | tf_op jit(solution)/shard_map/ppermute | solution.py:263
  27.2 1.7 %fusion.3 = f32[7,2,384]{2,0,1:T(8,128)S(1)} fusion(s32[384]{0:T(512)S(1)} %pad_add_fusion, f32[7,2,3072]{2,1,0:T(2,128)S(1)} %dot_general.10), kind=kOutput, calls=%fused_computation.3 | convolution fusion | flops 199360512 | bytes 195072 | tf_op jit(solution)/shard_map/dot_general | solution.py:290
  30.5 4.4 %shard_map.56 = (f32[7,2,64,128]{3,2,1,0:T(8,128)}, f32[14,192]{1,0:T(8,128)}) custom-call(f32[7,2,64,128]{3,2,1,0:T(8,128)} %bitcast.70, f32[7,2,64,128]{3,2,1,0:T(8,128)} %bitcast.71, f32[7,2,2,128]{3,2,1,0:T(2,128)} %get-tuple-element.38.refs_2_, f32[7,2,2,128]{3,2,1,0:T(2,128)} %get-tuple-element.37.refs_3_, f32[7,2,2,64]{3,2,1,0:T(2,128)} %get-tuple-element.36.refs_4_, ...), custom_call_target="tpu_custom_call" | custom-call | tf_op jit(solution)/shard_map/pallas_call | solution.py:146
  35.0 0.9 %fusion.11 = (f32[14,2,128]{2,1,0:T(2,128)S(1)}, f32[14,2,128]{2,1,0:T(2,128)S(1)}) fusion(f32[14,64,128]{2,1,0:T(8,128)} %bitcast.75), kind=kLoop, calls=%fused_computation.50 | loop fusion | bytes 57344 | tf_op jit(solution)/shard_map/slice | solution.py:273
  35.8 1.8 %collective-permute-start.5 = (f32[14,192]{1,0:T(8,128)}, f32[14,192]{1,0:T(8,128)S(1)}, u32[]{:S(2)}, u32[]{:S(2)}) collective-permute-start(f32[14,192]{1,0:T(8,128)} %get-tuple-element.14), channel_id=1, source_target_pairs={{0,16},{16,0},{1,17},{17,1},{2,18},{18,2},{3,19},{19,3},{4,20},{20... | collective-permute-start | bytes 32264 | tf_op jit(solution)/shard_map/ppermute | solution.py:271
  37.7 2.1 %collective-permute-done.5 = f32[14,192]{1,0:T(8,128)S(1)} collective-permute-done((f32[14,192]{1,0:T(8,128)}, f32[14,192]{1,0:T(8,128)S(1)}, u32[]{:S(2)}, u32[]{:S(2)}) %collective-permute-start.5) | collective-permute-done | bytes 10784 | tf_op jit(solution)/shard_map/ppermute | solution.py:271
  39.9 1.9 %collective-permute-start.6 = (f32[1,14,704]{2,0,1:T(1,128)S(1)}, f32[1,14,704]{2,0,1:T(1,128)S(1)}, u32[]{:S(2)}, u32[]{:S(2)}) collective-permute-start(f32[1,14,704]{2,0,1:T(1,128)S(1)} %broadcast_in_dim.16), channel_id=1, source_target_pairs={{0,4},{4,0},{8,12},{12,8},{1,5},{5,1},{9,13},{13,9},{2,6},{6,2},{1... | collective-permute-start | bytes 118280 | tf_op jit(solution)/shard_map/ppermute | solution.py:263
  41.9 1.3 %fusion.10 = (f32[14,64,2]{2,1,0:T(8,128)S(1)}, f32[14,64,2]{2,1,0:T(8,128)S(1)}) fusion(f32[14,64,128]{2,1,0:T(8,128)} %bitcast.76), kind=kLoop, calls=%fused_computation.49 | loop fusion | bytes 28672 | tf_op jit(solution)/shard_map/slice | solution.py:278
  44.2 3.3 %collective-permute-start.7 = (f32[2,14,704]{2,0,1:T(2,128)S(1)}, f32[2,14,704]{2,0,1:T(2,128)S(1)}, u32[]{:S(2)}, u32[]{:S(2)}) collective-permute-start(f32[2,14,704]{2,0,1:T(2,128)S(1)} %maximum_select_fusion.7), channel_id=1, source_target_pairs={{0,8},{4,12},{8,0},{12,4},{1,9},{5,13},{9,1},{13,5},{2,10},{6,14},... | collective-permute-start | bytes 236552 | tf_op jit(solution)/shard_map/ppermute | solution.py:263
  47.6 2.4 %collective-permute-done.7 = f32[2,14,704]{2,0,1:T(2,128)S(1)} collective-permute-done((f32[2,14,704]{2,0,1:T(2,128)S(1)}, f32[2,14,704]{2,0,1:T(2,128)S(1)}, u32[]{:S(2)}, u32[]{:S(2)}) %collective-permute-start.7) | collective-permute-done | bytes 78880 | tf_op jit(solution)/shard_map/ppermute | solution.py:263
  50.2 1.2 %collective-permute-done.8 = f32[1,14,1024]{2,1,0:T(8,128)S(1)} collective-permute-done((f32[1,14,1024]{2,1,0:T(8,128)S(1)}, f32[1,14,1024]{2,1,0:T(8,128)S(1)}, u32[]{:S(2)}, u32[]{:S(2)}) %collective-permute-start.8) | collective-permute-done | bytes 57376 | tf_op jit(solution)/shard_map/ppermute | solution.py:263
  51.5 1.6 %collective-permute-start.9 = (f32[2,14,1024]{2,1,0:T(8,128)S(1)}, f32[2,14,1024]{2,1,0:T(8,128)S(1)}, u32[]{:S(2)}, u32[]{:S(2)}) collective-permute-start(f32[2,14,1024]{2,1,0:T(8,128)S(1)} %maximum_select_fusion.5), channel_id=1, source_target_pairs={{0,2},{1,3},{2,0},{3,1},{4,6},{5,7},{6,4},{7,5},{8,10},{9,11},{10,... | collective-permute-start | bytes 344072 | tf_op jit(solution)/shard_map/ppermute | solution.py:263
  53.3 3.8 %collective-permute-done.9 = f32[2,14,1024]{2,1,0:T(8,128)S(1)} collective-permute-done((f32[2,14,1024]{2,1,0:T(8,128)S(1)}, f32[2,14,1024]{2,1,0:T(8,128)S(1)}, u32[]{:S(2)}, u32[]{:S(2)}) %collective-permute-start.9) | collective-permute-done | bytes 114720 | tf_op jit(solution)/shard_map/ppermute | solution.py:263
  58.2 1.7 %fusion.1 = f32[7,2,384]{2,0,1:T(8,128)S(1)} fusion(s32[384]{0:T(512)S(1)} %pad_add_fusion, f32[7,2,3072]{2,1,0:T(2,128)S(1)} %dot_general.12), kind=kOutput, calls=%fused_computation.2 | convolution fusion | flops 199360512 | bytes 195072 | tf_op jit(solution)/shard_map/dot_general | solution.py:290
  61.5 3.7 %shard_map.57 = f32[7,2,64,128]{3,2,1,0:T(8,128)} custom-call(f32[7,2,64,128]{3,2,1,0:T(8,128)} %get-tuple-element.13.refs_0_.refs_1_, f32[7,2,64,128]{3,2,1,0:T(8,128)} %get-tuple-element.13.refs_0_.refs_1_, f32[7,2,2,128]{3,2,1,0:T(2,128)} %get-tuple-element.34.refs_2_, f32[7,2,2,128]{3,2,1,0:T(2,128)} %get-tuple-element.33.refs_3_, ...), custom_call_target="tpu_custom_call" | custom-call | tf_op jit(solution)/shard_map/pallas_call | solution.py:146
  (90 shorter events, 10.3 us)
Async XLA Ops:
  0.0 6.9 %copy-start = (f32[1,7,2,64,128]{4,3,2,1,0:T(8,128)S(1)}, f32[1,7,2,64,128]{4,3,2,1,0:T(8,128)}, u32[]{:S(2)}) copy-start(f32[1,7,2,64,128]{4,3,2,1,0:T(8,128)} %param.5) | copy-start | bytes 1376260
  4.0 4.9 %collective-permute-start = (f32[14,192]{1,0:T(8,128)}, f32[14,192]{1,0:T(8,128)S(1)}, u32[]{:S(2)}, u32[]{:S(2)}) collective-permute-start(f32[14,192]{1,0:T(8,128)} %get-tuple-element.10), channel_id=1, source_target_pairs={{0,16},{16,0},{1,17},{17,1},{2,18},{18,2},{3,19},{19,3},{4,20},{20... | collective-permute-start | bytes 32264 | tf_op jit(solution)/shard_map/ppermute | solution.py:271
  6.9 0.7 %copy-start.3 = (s32[1,1,1,768]{3,2,1,0:T(1,128)S(1)}, s32[1,1,1,768]{3,2,1,0:T(1,128)}, u32[]{:S(2)}) copy-start(s32[1,1,1,768]{3,2,1,0:T(1,128)} %param.6) | copy-start | bytes 9220
  9.0 4.1 %collective-permute-start.1 = (f32[1,14,704]{2,0,1:T(1,128)S(1)}, f32[1,14,704]{2,0,1:T(1,128)S(1)}, u32[]{:S(2)}, u32[]{:S(2)}) collective-permute-start(f32[1,14,704]{2,0,1:T(1,128)S(1)} %broadcast_in_dim.14), channel_id=1, source_target_pairs={{0,4},{4,0},{8,12},{12,8},{1,5},{5,1},{9,13},{13,9},{2,6},{6,2},{1... | collective-permute-start | bytes 118280 | tf_op jit(solution)/shard_map/ppermute | solution.py:263
  13.2 5.6 %collective-permute-start.2 = (f32[2,14,704]{2,0,1:T(2,128)S(1)}, f32[2,14,704]{2,0,1:T(2,128)S(1)}, u32[]{:S(2)}, u32[]{:S(2)}) collective-permute-start(f32[2,14,704]{2,0,1:T(2,128)S(1)} %maximum_select_fusion.6), channel_id=1, source_target_pairs={{0,8},{4,12},{8,0},{12,4},{1,9},{5,13},{9,1},{13,5},{2,10},{6,14},... | collective-permute-start | bytes 236552 | tf_op jit(solution)/shard_map/ppermute | solution.py:263
  19.1 1.3 %collective-permute-start.3 = (f32[1,14,1024]{2,1,0:T(8,128)S(1)}, f32[1,14,1024]{2,1,0:T(8,128)S(1)}, u32[]{:S(2)}, u32[]{:S(2)}) collective-permute-start(f32[1,14,1024]{2,1,0:T(8,128)S(1)} %maximum_bitcast_fusion), channel_id=1, source_target_pairs={{0,1},{1,0},{2,3},{3,2},{4,5},{5,4},{6,7},{7,6},{8,9},{9,8},{10,11... | collective-permute-start | bytes 172040 | tf_op jit(solution)/shard_map/ppermute | solution.py:263
  20.4 5.7 %collective-permute-start.4 = (f32[2,14,1024]{2,1,0:T(8,128)S(1)}, f32[2,14,1024]{2,1,0:T(8,128)S(1)}, u32[]{:S(2)}, u32[]{:S(2)}) collective-permute-start(f32[2,14,1024]{2,1,0:T(8,128)S(1)} %maximum_select_fusion.4), channel_id=1, source_target_pairs={{0,2},{1,3},{2,0},{3,1},{4,6},{5,7},{6,4},{7,5},{8,10},{9,11},{10,... | collective-permute-start | bytes 344072 | tf_op jit(solution)/shard_map/ppermute | solution.py:263
  26.1 0.7 %copy-start.2 = (f32[4,14,1024]{2,1,0:T(8,128)}, f32[4,14,1024]{2,1,0:T(8,128)S(1)}, u32[]{:S(2)}) copy-start(f32[4,14,1024]{2,1,0:T(8,128)S(1)} %maximum_select_fusion) | copy-start | bytes 688132
  27.2 1.9 %slice-start.1 = ((f32[4,14,1024]{2,1,0:T(8,128)}), f32[4,14,256]{2,1,0:T(8,128)S(1)}, s32[]{:S(2)}) async-start(f32[4,14,1024]{2,1,0:T(8,128)} %copy-done.2), calls=%async_computation.1 | async-start | bytes 131072 | tf_op jit(solution)/shard_map/slice | solution.py:285
  35.8 4.0 %collective-permute-start.5 = (f32[14,192]{1,0:T(8,128)}, f32[14,192]{1,0:T(8,128)S(1)}, u32[]{:S(2)}, u32[]{:S(2)}) collective-permute-start(f32[14,192]{1,0:T(8,128)} %get-tuple-element.14), channel_id=1, source_target_pairs={{0,16},{16,0},{1,17},{17,1},{2,18},{18,2},{3,19},{19,3},{4,20},{20... | collective-permute-start | bytes 32264 | tf_op jit(solution)/shard_map/ppermute | solution.py:271
  39.9 4.1 %collective-permute-start.6 = (f32[1,14,704]{2,0,1:T(1,128)S(1)}, f32[1,14,704]{2,0,1:T(1,128)S(1)}, u32[]{:S(2)}, u32[]{:S(2)}) collective-permute-start(f32[1,14,704]{2,0,1:T(1,128)S(1)} %broadcast_in_dim.16), channel_id=1, source_target_pairs={{0,4},{4,0},{8,12},{12,8},{1,5},{5,1},{9,13},{13,9},{2,6},{6,2},{1... | collective-permute-start | bytes 118280 | tf_op jit(solution)/shard_map/ppermute | solution.py:263
  44.2 5.7 %collective-permute-start.7 = (f32[2,14,704]{2,0,1:T(2,128)S(1)}, f32[2,14,704]{2,0,1:T(2,128)S(1)}, u32[]{:S(2)}, u32[]{:S(2)}) collective-permute-start(f32[2,14,704]{2,0,1:T(2,128)S(1)} %maximum_select_fusion.7), channel_id=1, source_target_pairs={{0,8},{4,12},{8,0},{12,4},{1,9},{5,13},{9,1},{13,5},{2,10},{6,14},... | collective-permute-start | bytes 236552 | tf_op jit(solution)/shard_map/ppermute | solution.py:263
  50.2 1.3 %collective-permute-start.8 = (f32[1,14,1024]{2,1,0:T(8,128)S(1)}, f32[1,14,1024]{2,1,0:T(8,128)S(1)}, u32[]{:S(2)}, u32[]{:S(2)}) collective-permute-start(f32[1,14,1024]{2,1,0:T(8,128)S(1)} %maximum_bitcast_fusion.1), channel_id=1, source_target_pairs={{0,1},{1,0},{2,3},{3,2},{4,5},{5,4},{6,7},{7,6},{8,9},{9,8},{10,11... | collective-permute-start | bytes 172040 | tf_op jit(solution)/shard_map/ppermute | solution.py:263
  51.5 5.6 %collective-permute-start.9 = (f32[2,14,1024]{2,1,0:T(8,128)S(1)}, f32[2,14,1024]{2,1,0:T(8,128)S(1)}, u32[]{:S(2)}, u32[]{:S(2)}) collective-permute-start(f32[2,14,1024]{2,1,0:T(8,128)S(1)} %maximum_select_fusion.5), channel_id=1, source_target_pairs={{0,2},{1,3},{2,0},{3,1},{4,6},{5,7},{6,4},{7,5},{8,10},{9,11},{10,... | collective-permute-start | bytes 344072 | tf_op jit(solution)/shard_map/ppermute | solution.py:263
  57.2 0.7 %copy-start.1 = (f32[4,14,1024]{2,1,0:T(8,128)}, f32[4,14,1024]{2,1,0:T(8,128)S(1)}, u32[]{:S(2)}) copy-start(f32[4,14,1024]{2,1,0:T(8,128)S(1)} %maximum_select_fusion.1) | copy-start | bytes 688132
  58.2 1.9 %slice-start = ((f32[4,14,1024]{2,1,0:T(8,128)}), f32[4,14,256]{2,1,0:T(8,128)S(1)}, s32[]{:S(2)}) async-start(f32[4,14,1024]{2,1,0:T(8,128)} %copy-done.1), calls=%async_computation | async-start | bytes 131072 | tf_op jit(solution)/shard_map/slice | solution.py:285

commit v11 on v9

--- a/solution.py
+++ b/solution.py
@@ -61,8 +61,8 @@
         lon_p2 = jnp.where(
             col == width - 1, right[:, 1:2], jnp.where(col == width - 2, right[:, 0:1], pltpu.roll(x, width - 2, 1))
         )
-        d_lat = (8.0 * (lat_p1 - lat_m1) - (lat_p2 - lat_m2)) / 12.0
-        d_lon = (8.0 * (lon_p1 - lon_m1) - (lon_p2 - lon_m2)) / 12.0
+        d_lat = (8.0 * (lat_p1 - lat_m1) - (lat_p2 - lat_m2)) * (1.0 / 12.0)
+        d_lon = (8.0 * (lon_p1 - lon_m1) - (lon_p2 - lon_m2)) * (1.0 / 12.0)
         lap = lat_p1 + lat_m1 + lon_p1 + lon_m1 - 4.0 * x
         return x, d_lat, d_lon, lap
 

time: 64.9 us -> 64.9 us (level)
  no operation moved by 1% of the time
where the time goes in v11:
time: 64.9 us; the launch traced here: 64.6 us
  waiting for transfers between devices  19.9 us (31%)
  starting transfers between devices  18.8 us (29%)
  Pallas kernels  10 us (15%)
  local copies, waits for them, and re-layouts  7.96 us (12%)
  other arithmetic  3.97 us (6%)
  matrix products  3.46 us (5%)
    ppermute x8, waiting for transfers between devices, gather(): other = lax.ppermute(held, axis, [(i, i ^ k) for i in range(size)])  16.6 us
    ppermute x8, starting transfers between devices, gather(): other = lax.ppermute(held, axis, [(i, i ^ k) for i in range(size)])  14 us
    pallas_call x2, Pallas kernels, advance(): pl.pallas_call(functools.partial(stencil_kernel, first=first), out_shape=...  7.45 us
    ppermute x2, starting transfers between devices, section(): given = lax.ppermute(donation, 'panel', [(0, 1), (1, 0)])  4.81 us
    dot_general x2, matrix products, section(): rim = jnp.dot(partner, pick, precision=HIGHEST).reshape(comps, levels, -1)  3.46 us
    ppermute x2, waiting for transfers between devices, section(): given = lax.ppermute(donation, 'panel', [(0, 1), (1, 0)])  3.28 us
    pallas_call x1, Pallas kernels, first_donation(): pl.pallas_call(donation_kernel, out_shape=(jax.ShapeDtypeStruct((planes,...  2.58 us
    slice x6, local copies, waits for them, and re-layouts, section(): side_cols = jnp.concatenate([flat[:, :, :2], flat[:, :, cols - 2:]], axis=2)  2.33 us
  transfers between devices with their start and end apart: 10, of which 10 were waited for; matrix products, arithmetic and copies ran while one was open for 5% of the time, Pallas kernels for 0%

profile of v11, /device:TPU:0, one launch (start us, length us, event | category | flops | bytes accessed | tf_op | source)
XLA Modules:
  0.0 64.6 jit_solution(5445533899464347465)
XLA Ops:
  1.4 2.6 %shard_map.55 = (f32[14,192]{1,0:T(8,128)}, f32[128,192]{1,0:T(8,128)}, f32[64,192]{1,0:T(8,128)}) custom-call(f32[14,64,128]{2,1,0:T(8,128)} %bitcast.75, s32[1,192]{1,0:T(1,128)} %bitcast.97, f32[2,192]{1,0:T(2,128)} %bitcast.96, f32[2,192]{1,0:T(2,128)} %pad_maximum_fusion.4.turn_ref), custom_call_target="tpu_custom_call" | custom-call | tf_op jit(solution)/shard_map/pallas_call | solution.py:166
  4.0 3.0 %collective-permute-start = (f32[14,192]{1,0:T(8,128)}, f32[14,192]{1,0:T(8,128)S(1)}, u32[]{:S(2)}, u32[]{:S(2)}) collective-permute-start(f32[14,192]{1,0:T(8,128)} %get-tuple-element.10), channel_id=1, source_target_pairs={{0,16},{16,0},{1,17},{17,1},{2,18},{18,2},{3,19},{19,3},{4,20},{20... | collective-permute-start | bytes 32264 | tf_op jit(solution)/shard_map/ppermute | solution.py:233
  7.7 1.2 %collective-permute-done = f32[14,192]{1,0:T(8,128)S(1)} collective-permute-done((f32[14,192]{1,0:T(8,128)}, f32[14,192]{1,0:T(8,128)S(1)}, u32[]{:S(2)}, u32[]{:S(2)}) %collective-permute-start) | collective-permute-done | bytes 10784 | tf_op jit(solution)/shard_map/ppermute | solution.py:233
  9.0 2.1 %collective-permute-start.1 = (f32[1,14,704]{2,0,1:T(1,128)S(1)}, f32[1,14,704]{2,0,1:T(1,128)S(1)}, u32[]{:S(2)}, u32[]{:S(2)}) collective-permute-start(f32[1,14,704]{2,0,1:T(1,128)S(1)} %broadcast_in_dim.14), channel_id=1, source_target_pairs={{0,4},{4,0},{8,12},{12,8},{1,5},{5,1},{9,13},{13,9},{2,6},{6,2},{1... | collective-permute-start | bytes 118280 | tf_op jit(solution)/shard_map/ppermute | solution.py:225
  11.5 1.6 %collective-permute-done.1 = f32[1,14,704]{2,0,1:T(1,128)S(1)} collective-permute-done((f32[1,14,704]{2,0,1:T(1,128)S(1)}, f32[1,14,704]{2,0,1:T(1,128)S(1)}, u32[]{:S(2)}, u32[]{:S(2)}) %collective-permute-start.1) | collective-permute-done | bytes 39456 | tf_op jit(solution)/shard_map/ppermute | solution.py:225
  13.2 3.1 %collective-permute-start.2 = (f32[2,14,704]{2,0,1:T(2,128)S(1)}, f32[2,14,704]{2,0,1:T(2,128)S(1)}, u32[]{:S(2)}, u32[]{:S(2)}) collective-permute-start(f32[2,14,704]{2,0,1:T(2,128)S(1)} %maximum_select_fusion.6), channel_id=1, source_target_pairs={{0,8},{4,12},{8,0},{12,4},{1,9},{5,13},{9,1},{13,5},{2,10},{6,14},... | collective-permute-start | bytes 236552 | tf_op jit(solution)/shard_map/ppermute | solution.py:225
  16.5 2.4 %collective-permute-done.2 = f32[2,14,704]{2,0,1:T(2,128)S(1)} collective-permute-done((f32[2,14,704]{2,0,1:T(2,128)S(1)}, f32[2,14,704]{2,0,1:T(2,128)S(1)}, u32[]{:S(2)}, u32[]{:S(2)}) %collective-permute-start.2) | collective-permute-done | bytes 78880 | tf_op jit(solution)/shard_map/ppermute | solution.py:225
  19.2 1.2 %collective-permute-done.3 = f32[1,14,1024]{2,1,0:T(8,128)S(1)} collective-permute-done((f32[1,14,1024]{2,1,0:T(8,128)S(1)}, f32[1,14,1024]{2,1,0:T(8,128)S(1)}, u32[]{:S(2)}, u32[]{:S(2)}) %collective-permute-start.3) | collective-permute-done | bytes 57376 | tf_op jit(solution)/shard_map/ppermute | solution.py:225
  20.4 1.9 %collective-permute-start.4 = (f32[2,14,1024]{2,1,0:T(8,128)S(1)}, f32[2,14,1024]{2,1,0:T(8,128)S(1)}, u32[]{:S(2)}, u32[]{:S(2)}) collective-permute-start(f32[2,14,1024]{2,1,0:T(8,128)S(1)} %maximum_select_fusion.4), channel_id=1, source_target_pairs={{0,2},{1,3},{2,0},{3,1},{4,6},{5,7},{6,4},{7,5},{8,10},{9,11},{10,... | collective-permute-start | bytes 344072 | tf_op jit(solution)/shard_map/ppermute | solution.py:225
  22.5 3.6 %collective-permute-done.4 = f32[2,14,1024]{2,1,0:T(8,128)S(1)} collective-permute-done((f32[2,14,1024]{2,1,0:T(8,128)S(1)}, f32[2,14,1024]{2,1,0:T(8,128)S(1)}, u32[]{:S(2)}, u32[]{:S(2)}) %collective-permute-start.4) | collective-permute-done | bytes 114720 | tf_op jit(solution)/shard_map/ppermute | solution.py:225
  27.2 1.7 %fusion.3 = f32[7,2,384]{2,0,1:T(8,128)S(1)} fusion(s32[384]{0:T(512)S(1)} %pad_add_fusion, f32[7,2,3072]{2,1,0:T(2,128)S(1)} %dot_general.10), kind=kOutput, calls=%fused_computation.3 | convolution fusion | flops 199360512 | bytes 195072 | tf_op jit(solution)/shard_map/dot_general | solution.py:252
  30.5 3.9 %shard_map.56 = (f32[14,64,128]{2,1,0:T(8,128)}, f32[14,192]{1,0:T(8,128)}) custom-call(f32[14,64,128]{2,1,0:T(8,128)} %bitcast.76, f32[14,2,128]{2,1,0:T(2,128)} %bitcast.94, f32[14,2,128]{2,1,0:T(2,128)} %bitcast.93, f32[14,2,64]{2,1,0:T(2,128)} %bitcast.90, f32[14,2,64]{2,1,0:T(2,128)} %bitcast.89, f32[14,64,128]{2,1,0:T(8,128)} %bitcast.77, ...), custom_call_target="tpu_custom_call" | custom-call | tf_op jit(solution)/shard_map/pallas_call | solution.py:114
  34.5 0.9 %fusion.11 = (f32[14,2,128]{2,1,0:T(2,128)S(1)}, f32[14,2,128]{2,1,0:T(2,128)S(1)}) fusion(f32[14,64,128]{2,1,0:T(8,128)} %get-tuple-element.13.f_ref), kind=kLoop, calls=%fused_computation.50 | loop fusion | bytes 57344 | tf_op jit(solution)/shard_map/slice | solution.py:235
  35.3 1.8 %collective-permute-start.5 = (f32[14,192]{1,0:T(8,128)}, f32[14,192]{1,0:T(8,128)S(1)}, u32[]{:S(2)}, u32[]{:S(2)}) collective-permute-start(f32[14,192]{1,0:T(8,128)} %get-tuple-element.14), channel_id=1, source_target_pairs={{0,16},{16,0},{1,17},{17,1},{2,18},{18,2},{3,19},{19,3},{4,20},{20... | collective-permute-start | bytes 32264 | tf_op jit(solution)/shard_map/ppermute | solution.py:233
  37.2 2.1 %collective-permute-done.5 = f32[14,192]{1,0:T(8,128)S(1)} collective-permute-done((f32[14,192]{1,0:T(8,128)}, f32[14,192]{1,0:T(8,128)S(1)}, u32[]{:S(2)}, u32[]{:S(2)}) %collective-permute-start.5) | collective-permute-done | bytes 10784 | tf_op jit(solution)/shard_map/ppermute | solution.py:233
  39.4 1.9 %collective-permute-start.6 = (f32[1,14,704]{2,0,1:T(1,128)S(1)}, f32[1,14,704]{2,0,1:T(1,128)S(1)}, u32[]{:S(2)}, u32[]{:S(2)}) collective-permute-start(f32[1,14,704]{2,0,1:T(1,128)S(1)} %broadcast_in_dim.16), channel_id=1, source_target_pairs={{0,4},{4,0},{8,12},{12,8},{1,5},{5,1},{9,13},{13,9},{2,6},{6,2},{1... | collective-permute-start | bytes 118280 | tf_op jit(solution)/shard_map/ppermute | solution.py:225
  41.4 1.3 %fusion.10 = (f32[14,64,2]{2,1,0:T(8,128)S(1)}, f32[14,64,2]{2,1,0:T(8,128)S(1)}) fusion(f32[14,64,128]{2,1,0:T(8,128)} %get-tuple-element.13.f_ref), kind=kLoop, calls=%fused_computation.49 | loop fusion | bytes 28672 | tf_op jit(solution)/shard_map/slice | solution.py:240
  43.7 3.3 %collective-permute-start.7 = (f32[2,14,704]{2,0,1:T(2,128)S(1)}, f32[2,14,704]{2,0,1:T(2,128)S(1)}, u32[]{:S(2)}, u32[]{:S(2)}) collective-permute-start(f32[2,14,704]{2,0,1:T(2,128)S(1)} %maximum_select_fusion.7), channel_id=1, source_target_pairs={{0,8},{4,12},{8,0},{12,4},{1,9},{5,13},{9,1},{13,5},{2,10},{6,14},... | collective-permute-start | bytes 236552 | tf_op jit(solution)/shard_map/ppermute | solution.py:225
  47.1 2.4 %collective-permute-done.7 = f32[2,14,704]{2,0,1:T(2,128)S(1)} collective-permute-done((f32[2,14,704]{2,0,1:T(2,128)S(1)}, f32[2,14,704]{2,0,1:T(2,128)S(1)}, u32[]{:S(2)}, u32[]{:S(2)}) %collective-permute-start.7) | collective-permute-done | bytes 78880 | tf_op jit(solution)/shard_map/ppermute | solution.py:225
  49.7 1.2 %collective-permute-done.8 = f32[1,14,1024]{2,1,0:T(8,128)S(1)} collective-permute-done((f32[1,14,1024]{2,1,0:T(8,128)S(1)}, f32[1,14,1024]{2,1,0:T(8,128)S(1)}, u32[]{:S(2)}, u32[]{:S(2)}) %collective-permute-start.8) | collective-permute-done | bytes 57376 | tf_op jit(solution)/shard_map/ppermute | solution.py:225
  51.0 1.6 %collective-permute-start.9 = (f32[2,14,1024]{2,1,0:T(8,128)S(1)}, f32[2,14,1024]{2,1,0:T(8,128)S(1)}, u32[]{:S(2)}, u32[]{:S(2)}) collective-permute-start(f32[2,14,1024]{2,1,0:T(8,128)S(1)} %maximum_select_fusion.5), channel_id=1, source_target_pairs={{0,2},{1,3},{2,0},{3,1},{4,6},{5,7},{6,4},{7,5},{8,10},{9,11},{10,... | collective-permute-start | bytes 344072 | tf_op jit(solution)/shard_map/ppermute | solution.py:225
  52.8 3.8 %collective-permute-done.9 = f32[2,14,1024]{2,1,0:T(8,128)S(1)} collective-permute-done((f32[2,14,1024]{2,1,0:T(8,128)S(1)}, f32[2,14,1024]{2,1,0:T(8,128)S(1)}, u32[]{:S(2)}, u32[]{:S(2)}) %collective-permute-start.9) | collective-permute-done | bytes 114720 | tf_op jit(solution)/shard_map/ppermute | solution.py:225
  57.7 1.7 %fusion.1 = f32[7,2,384]{2,0,1:T(8,128)S(1)} fusion(s32[384]{0:T(512)S(1)} %pad_add_fusion, f32[7,2,3072]{2,1,0:T(2,128)S(1)} %dot_general.12), kind=kOutput, calls=%fused_computation.2 | convolution fusion | flops 199360512 | bytes 195072 | tf_op jit(solution)/shard_map/dot_general | solution.py:252
  61.1 3.5 %shard_map.57 = f32[14,64,128]{2,1,0:T(8,128)} custom-call(f32[14,64,128]{2,1,0:T(8,128)} %get-tuple-element.13.f_ref, f32[14,2,128]{2,1,0:T(2,128)} %bitcast.92, f32[14,2,128]{2,1,0:T(2,128)} %bitcast.91, f32[14,2,64]{2,1,0:T(2,128)} %bitcast.88, f32[14,2,64]{2,1,0:T(2,128)} %bitcast.87, f32[14,64,128]{2,1,0:T(8,128)} %bitcast.78, ...), custom_call_target="tpu_custom_call" | custom-call | tf_op jit(solution)/shard_map/pallas_call | solution.py:114
  (90 shorter events, 10.3 us)
Async XLA Ops:
  0.0 6.9 %copy-start = (f32[1,7,2,64,128]{4,3,2,1,0:T(8,128)S(1)}, f32[1,7,2,64,128]{4,3,2,1,0:T(8,128)}, u32[]{:S(2)}) copy-start(f32[1,7,2,64,128]{4,3,2,1,0:T(8,128)} %param.5) | copy-start | bytes 1376260
  4.0 4.9 %collective-permute-start = (f32[14,192]{1,0:T(8,128)}, f32[14,192]{1,0:T(8,128)S(1)}, u32[]{:S(2)}, u32[]{:S(2)}) collective-permute-start(f32[14,192]{1,0:T(8,128)} %get-tuple-element.10), channel_id=1, source_target_pairs={{0,16},{16,0},{1,17},{17,1},{2,18},{18,2},{3,19},{19,3},{4,20},{20... | collective-permute-start | bytes 32264 | tf_op jit(solution)/shard_map/ppermute | solution.py:233
  6.9 0.7 %copy-start.3 = (s32[1,1,1,768]{3,2,1,0:T(1,128)S(1)}, s32[1,1,1,768]{3,2,1,0:T(1,128)}, u32[]{:S(2)}) copy-start(s32[1,1,1,768]{3,2,1,0:T(1,128)} %param.6) | copy-start | bytes 9220
  9.0 4.1 %collective-permute-start.1 = (f32[1,14,704]{2,0,1:T(1,128)S(1)}, f32[1,14,704]{2,0,1:T(1,128)S(1)}, u32[]{:S(2)}, u32[]{:S(2)}) collective-permute-start(f32[1,14,704]{2,0,1:T(1,128)S(1)} %broadcast_in_dim.14), channel_id=1, source_target_pairs={{0,4},{4,0},{8,12},{12,8},{1,5},{5,1},{9,13},{13,9},{2,6},{6,2},{1... | collective-permute-start | bytes 118280 | tf_op jit(solution)/shard_map/ppermute | solution.py:225
  13.2 5.6 %collective-permute-start.2 = (f32[2,14,704]{2,0,1:T(2,128)S(1)}, f32[2,14,704]{2,0,1:T(2,128)S(1)}, u32[]{:S(2)}, u32[]{:S(2)}) collective-permute-start(f32[2,14,704]{2,0,1:T(2,128)S(1)} %maximum_select_fusion.6), channel_id=1, source_target_pairs={{0,8},{4,12},{8,0},{12,4},{1,9},{5,13},{9,1},{13,5},{2,10},{6,14},... | collective-permute-start | bytes 236552 | tf_op jit(solution)/shard_map/ppermute | solution.py:225
  19.1 1.3 %collective-permute-start.3 = (f32[1,14,1024]{2,1,0:T(8,128)S(1)}, f32[1,14,1024]{2,1,0:T(8,128)S(1)}, u32[]{:S(2)}, u32[]{:S(2)}) collective-permute-start(f32[1,14,1024]{2,1,0:T(8,128)S(1)} %maximum_bitcast_fusion), channel_id=1, source_target_pairs={{0,1},{1,0},{2,3},{3,2},{4,5},{5,4},{6,7},{7,6},{8,9},{9,8},{10,11... | collective-permute-start | bytes 172040 | tf_op jit(solution)/shard_map/ppermute | solution.py:225
  20.4 5.7 %collective-permute-start.4 = (f32[2,14,1024]{2,1,0:T(8,128)S(1)}, f32[2,14,1024]{2,1,0:T(8,128)S(1)}, u32[]{:S(2)}, u32[]{:S(2)}) collective-permute-start(f32[2,14,1024]{2,1,0:T(8,128)S(1)} %maximum_select_fusion.4), channel_id=1, source_target_pairs={{0,2},{1,3},{2,0},{3,1},{4,6},{5,7},{6,4},{7,5},{8,10},{9,11},{10,... | collective-permute-start | bytes 344072 | tf_op jit(solution)/shard_map/ppermute | solution.py:225
  26.1 0.7 %copy-start.2 = (f32[4,14,1024]{2,1,0:T(8,128)}, f32[4,14,1024]{2,1,0:T(8,128)S(1)}, u32[]{:S(2)}) copy-start(f32[4,14,1024]{2,1,0:T(8,128)S(1)} %maximum_select_fusion) | copy-start | bytes 688132
  27.2 1.9 %slice-start.1 = ((f32[4,14,1024]{2,1,0:T(8,128)}), f32[4,14,256]{2,1,0:T(8,128)S(1)}, s32[]{:S(2)}) async-start(f32[4,14,1024]{2,1,0:T(8,128)} %copy-done.2), calls=%async_computation.1 | async-start | bytes 131072 | tf_op jit(solution)/shard_map/slice | solution.py:247
  35.3 4.0 %collective-permute-start.5 = (f32[14,192]{1,0:T(8,128)}, f32[14,192]{1,0:T(8,128)S(1)}, u32[]{:S(2)}, u32[]{:S(2)}) collective-permute-start(f32[14,192]{1,0:T(8,128)} %get-tuple-element.14), channel_id=1, source_target_pairs={{0,16},{16,0},{1,17},{17,1},{2,18},{18,2},{3,19},{19,3},{4,20},{20... | collective-permute-start | bytes 32264 | tf_op jit(solution)/shard_map/ppermute | solution.py:233
  39.4 4.1 %collective-permute-start.6 = (f32[1,14,704]{2,0,1:T(1,128)S(1)}, f32[1,14,704]{2,0,1:T(1,128)S(1)}, u32[]{:S(2)}, u32[]{:S(2)}) collective-permute-start(f32[1,14,704]{2,0,1:T(1,128)S(1)} %broadcast_in_dim.16), channel_id=1, source_target_pairs={{0,4},{4,0},{8,12},{12,8},{1,5},{5,1},{9,13},{13,9},{2,6},{6,2},{1... | collective-permute-start | bytes 118280 | tf_op jit(solution)/shard_map/ppermute | solution.py:225
  43.7 5.7 %collective-permute-start.7 = (f32[2,14,704]{2,0,1:T(2,128)S(1)}, f32[2,14,704]{2,0,1:T(2,128)S(1)}, u32[]{:S(2)}, u32[]{:S(2)}) collective-permute-start(f32[2,14,704]{2,0,1:T(2,128)S(1)} %maximum_select_fusion.7), channel_id=1, source_target_pairs={{0,8},{4,12},{8,0},{12,4},{1,9},{5,13},{9,1},{13,5},{2,10},{6,14},... | collective-permute-start | bytes 236552 | tf_op jit(solution)/shard_map/ppermute | solution.py:225
  49.7 1.3 %collective-permute-start.8 = (f32[1,14,1024]{2,1,0:T(8,128)S(1)}, f32[1,14,1024]{2,1,0:T(8,128)S(1)}, u32[]{:S(2)}, u32[]{:S(2)}) collective-permute-start(f32[1,14,1024]{2,1,0:T(8,128)S(1)} %maximum_bitcast_fusion.1), channel_id=1, source_target_pairs={{0,1},{1,0},{2,3},{3,2},{4,5},{5,4},{6,7},{7,6},{8,9},{9,8},{10,11... | collective-permute-start | bytes 172040 | tf_op jit(solution)/shard_map/ppermute | solution.py:225
  51.0 5.6 %collective-permute-start.9 = (f32[2,14,1024]{2,1,0:T(8,128)S(1)}, f32[2,14,1024]{2,1,0:T(8,128)S(1)}, u32[]{:S(2)}, u32[]{:S(2)}) collective-permute-start(f32[2,14,1024]{2,1,0:T(8,128)S(1)} %maximum_select_fusion.5), channel_id=1, source_target_pairs={{0,2},{1,3},{2,0},{3,1},{4,6},{5,7},{6,4},{7,5},{8,10},{9,11},{10,... | collective-permute-start | bytes 344072 | tf_op jit(solution)/shard_map/ppermute | solution.py:225
  56.7 0.7 %copy-start.1 = (f32[4,14,1024]{2,1,0:T(8,128)}, f32[4,14,1024]{2,1,0:T(8,128)S(1)}, u32[]{:S(2)}) copy-start(f32[4,14,1024]{2,1,0:T(8,128)S(1)} %maximum_select_fusion.1) | copy-start | bytes 688132
  57.7 1.9 %slice-start = ((f32[4,14,1024]{2,1,0:T(8,128)}), f32[4,14,256]{2,1,0:T(8,128)S(1)}, s32[]{:S(2)}) async-start(f32[4,14,1024]{2,1,0:T(8,128)} %copy-done.1), calls=%async_computation | async-start | bytes 131072 | tf_op jit(solution)/shard_map/slice | solution.py:247

commit v12 on v11

--- a/solution.py
+++ b/solution.py
@@ -214,7 +214,17 @@
     lon_slots = jnp.where(on_left, slots[2 * band : 2 * band + side], slots[2 * band + side :])
     wanted = jnp.concatenate([lat_slots, lon_slots])
     total = lat_count * lon_count * cells.shape[0]
-    pick = (jnp.arange(total, dtype=jnp.int32)[:, None] == wanted[None, :]).astype(jnp.float32)
+    pick = (jnp.arange(total, dtype=jnp.int32)[:, None] == wanted[None, :]).astype(jnp.bfloat16)
+
+    def select(values):
+        high = lax.reduce_precision(values, exponent_bits=8, mantissa_bits=7)
+        rest = values - high
+        middle = lax.reduce_precision(rest, exponent_bits=8, mantissa_bits=7)
+        low = rest - middle
+        parts = jnp.concatenate([high, middle, low]).astype(jnp.bfloat16)
+        picked = jnp.dot(parts, pick, preferred_element_type=jnp.float32)
+        count = values.shape[0]
+        return picked[:count] + (picked[count : 2 * count] + picked[2 * count :])
 
     def gather(packet, axis):
         size = lax.axis_size(axis)
@@ -249,7 +259,7 @@
         down = lax.dynamic_index_in_dim(side_rows, jnp.minimum(lat_pos + 1, lat_count - 1), keepdims=False)[:, :, :2]
         left = lax.dynamic_index_in_dim(side_cols, jnp.maximum(lon_pos - 1, 0), keepdims=False)[:, :, 2:]
         right = lax.dynamic_index_in_dim(side_cols, jnp.minimum(lon_pos + 1, lon_count - 1), keepdims=False)[:, :, :2]
-        rim = jnp.dot(partner, pick, precision=HIGHEST).reshape(comps, levels, -1)
+        rim = select(partner).reshape(comps, levels, -1)
         rim_lat = rim[:, :, :band].reshape(comps, levels, 2, cols)
         rim_lon = rim[:, :, band:].reshape(comps, levels, 2, rows)
         up = jnp.where(on_top, rim_lat, up).reshape(comps * levels, 2, cols)

time: 64.9 us -> 62.7 us (0.966)
  matrix products: 3.46 us -> 1.98 us
  local copies, waits for them, and re-layouts: 7.96 us -> 7.2 us
    dot_general x2, matrix products: 3.46 us -> 1.98 us  [select(): picked = jnp.dot(parts, pick, preferred_element_type=jnp.float32)]
    unnamed x12 -> x8, local copies, waits for them, and re-layouts: 1.2 us -> 0.5 us
where the time goes in v12:
time: 62.7 us; the launch traced here: 62.4 us
  waiting for transfers between devices  19.9 us (32%)
  starting transfers between devices  18.8 us (30%)
  Pallas kernels  10 us (16%)
  local copies, waits for them, and re-layouts  7.2 us (11%)
  other arithmetic  4.07 us (6%)
  matrix products  1.98 us (3%)
    ppermute x8, waiting for transfers between devices, gather(): other = lax.ppermute(held, axis, [(i, i ^ k) for i in range(size)])  16.6 us
    ppermute x8, starting transfers between devices, gather(): other = lax.ppermute(held, axis, [(i, i ^ k) for i in range(size)])  14 us
    pallas_call x2, Pallas kernels, advance(): pl.pallas_call(functools.partial(stencil_kernel, first=first), out_shape=...  7.44 us
    ppermute x2, starting transfers between devices, section(): given = lax.ppermute(donation, 'panel', [(0, 1), (1, 0)])  4.81 us
    ppermute x2, waiting for transfers between devices, section(): given = lax.ppermute(donation, 'panel', [(0, 1), (1, 0)])  3.31 us
    pallas_call x1, Pallas kernels, first_donation(): pl.pallas_call(donation_kernel, out_shape=(jax.ShapeDtypeStruct((planes,...  2.58 us
    slice x6, local copies, waits for them, and re-layouts, section(): side_cols = jnp.concatenate([flat[:, :, :2], flat[:, :, cols - 2:]], axis=2)  2.34 us
    dot_general x2, matrix products, select(): picked = jnp.dot(parts, pick, preferred_element_type=jnp.float32)  1.98 us
  transfers between devices with their start and end apart: 10, of which 10 were waited for; matrix products, arithmetic and copies ran while one was open for 5% of the time, Pallas kernels for 0%

profile of v12, /device:TPU:0, one launch (start us, length us, event | category | flops | bytes accessed | tf_op | source)
XLA Modules:
  0.0 62.4 jit_solution(8739597212308211480)
XLA Ops:
  1.4 2.6 %shard_map.55 = (f32[14,192]{1,0:T(8,128)}, f32[128,192]{1,0:T(8,128)}, f32[64,192]{1,0:T(8,128)}) custom-call(f32[14,64,128]{2,1,0:T(8,128)} %bitcast.67, s32[1,192]{1,0:T(1,128)} %bitcast.89, f32[2,192]{1,0:T(2,128)} %bitcast.88, f32[2,192]{1,0:T(2,128)} %pad_maximum_fusion.4.turn_ref), custom_call_target="tpu_custom_call" | custom-call | tf_op jit(solution)/shard_map/pallas_call | solution.py:166
  3.9 3.0 %collective-permute-start = (f32[14,192]{1,0:T(8,128)}, f32[14,192]{1,0:T(8,128)S(1)}, u32[]{:S(2)}, u32[]{:S(2)}) collective-permute-start(f32[14,192]{1,0:T(8,128)} %get-tuple-element.10), channel_id=1, source_target_pairs={{0,16},{16,0},{1,17},{17,1},{2,18},{18,2},{3,19},{19,3},{4,20},{20... | collective-permute-start | bytes 32264 | tf_op jit(solution)/shard_map/ppermute | solution.py:243
  7.7 1.2 %collective-permute-done = f32[14,192]{1,0:T(8,128)S(1)} collective-permute-done((f32[14,192]{1,0:T(8,128)}, f32[14,192]{1,0:T(8,128)S(1)}, u32[]{:S(2)}, u32[]{:S(2)}) %collective-permute-start) | collective-permute-done | bytes 10784 | tf_op jit(solution)/shard_map/ppermute | solution.py:243
  8.9 2.1 %collective-permute-start.1 = (f32[1,14,704]{2,0,1:T(1,128)S(1)}, f32[1,14,704]{2,0,1:T(1,128)S(1)}, u32[]{:S(2)}, u32[]{:S(2)}) collective-permute-start(f32[1,14,704]{2,0,1:T(1,128)S(1)} %broadcast_in_dim.14), channel_id=1, source_target_pairs={{0,4},{4,0},{8,12},{12,8},{1,5},{5,1},{9,13},{13,9},{2,6},{6,2},{1... | collective-permute-start | bytes 118280 | tf_op jit(solution)/shard_map/ppermute | solution.py:235
  11.5 1.6 %collective-permute-done.1 = f32[1,14,704]{2,0,1:T(1,128)S(1)} collective-permute-done((f32[1,14,704]{2,0,1:T(1,128)S(1)}, f32[1,14,704]{2,0,1:T(1,128)S(1)}, u32[]{:S(2)}, u32[]{:S(2)}) %collective-permute-start.1) | collective-permute-done | bytes 39456 | tf_op jit(solution)/shard_map/ppermute | solution.py:235
  13.2 3.1 %collective-permute-start.2 = (f32[2,14,704]{2,0,1:T(2,128)S(1)}, f32[2,14,704]{2,0,1:T(2,128)S(1)}, u32[]{:S(2)}, u32[]{:S(2)}) collective-permute-start(f32[2,14,704]{2,0,1:T(2,128)S(1)} %maximum_select_fusion.6), channel_id=1, source_target_pairs={{0,8},{4,12},{8,0},{12,4},{1,9},{5,13},{9,1},{13,5},{2,10},{6,14},... | collective-permute-start | bytes 236552 | tf_op jit(solution)/shard_map/ppermute | solution.py:235
  16.4 2.4 %collective-permute-done.2 = f32[2,14,704]{2,0,1:T(2,128)S(1)} collective-permute-done((f32[2,14,704]{2,0,1:T(2,128)S(1)}, f32[2,14,704]{2,0,1:T(2,128)S(1)}, u32[]{:S(2)}, u32[]{:S(2)}) %collective-permute-start.2) | collective-permute-done | bytes 78880 | tf_op jit(solution)/shard_map/ppermute | solution.py:235
  19.2 1.2 %collective-permute-done.3 = f32[1,14,1024]{2,1,0:T(8,128)S(1)} collective-permute-done((f32[1,14,1024]{2,1,0:T(8,128)S(1)}, f32[1,14,1024]{2,1,0:T(8,128)S(1)}, u32[]{:S(2)}, u32[]{:S(2)}) %collective-permute-start.3) | collective-permute-done | bytes 57376 | tf_op jit(solution)/shard_map/ppermute | solution.py:235
  20.4 1.9 %collective-permute-start.4 = (f32[2,14,1024]{2,1,0:T(8,128)S(1)}, f32[2,14,1024]{2,1,0:T(8,128)S(1)}, u32[]{:S(2)}, u32[]{:S(2)}) collective-permute-start(f32[2,14,1024]{2,1,0:T(8,128)S(1)} %maximum_select_fusion.4), channel_id=1, source_target_pairs={{0,2},{1,3},{2,0},{3,1},{4,6},{5,7},{6,4},{7,5},{8,10},{9,11},{10,... | collective-permute-start | bytes 344072 | tf_op jit(solution)/shard_map/ppermute | solution.py:235
  22.5 3.6 %collective-permute-done.4 = f32[2,14,1024]{2,1,0:T(8,128)S(1)} collective-permute-done((f32[2,14,1024]{2,1,0:T(8,128)S(1)}, f32[2,14,1024]{2,1,0:T(8,128)S(1)}, u32[]{:S(2)}, u32[]{:S(2)}) %collective-permute-start.4) | collective-permute-done | bytes 114720 | tf_op jit(solution)/shard_map/ppermute | solution.py:235
  26.8 1.0 %fusion.1 = f32[42,384]{1,0:T(8,128)S(1)} fusion(s32[384]{0:T(512)S(1)} %pad_add_fusion, bf16[14,3072]{1,0:T(8,128)(2,1)S(1)} %get-tuple-element.27, bf16[14,3072]{1,0:T(8,128)(2,1)S(1)} %get-tuple-element.28, bf16[14,3072]{1,0:T(8,128)(2,1)S(1)} %get-tuple-element.26), kind=kOutput, calls=%fused_computation.2 | convolution fusion | flops 101044224 | bytes 324096 | tf_op jit(solution)/shard_map/dot_general | solution.py:225
  29.5 3.9 %shard_map.56 = (f32[14,64,128]{2,1,0:T(8,128)}, f32[14,192]{1,0:T(8,128)}) custom-call(f32[14,64,128]{2,1,0:T(8,128)} %bitcast.68, f32[14,2,128]{2,1,0:T(2,128)} %bitcast.82, f32[14,2,128]{2,1,0:T(2,128)} %bitcast.81, f32[14,2,64]{2,1,0:T(2,128)} %bitcast.86, f32[14,2,64]{2,1,0:T(2,128)} %bitcast.85, f32[14,64,128]{2,1,0:T(8,128)} %bitcast.69, ...), custom_call_target="tpu_custom_call" | custom-call | tf_op jit(solution)/shard_map/pallas_call | solution.py:114
  33.4 0.9 %fusion.21 = (f32[14,2,128]{2,1,0:T(2,128)S(1)}, f32[14,2,128]{2,1,0:T(2,128)S(1)}) fusion(f32[14,64,128]{2,1,0:T(8,128)} %get-tuple-element.13.f_ref), kind=kLoop, calls=%fused_computation.72 | loop fusion | bytes 57344 | tf_op jit(solution)/shard_map/slice | solution.py:245
  34.2 1.8 %collective-permute-start.5 = (f32[14,192]{1,0:T(8,128)}, f32[14,192]{1,0:T(8,128)S(1)}, u32[]{:S(2)}, u32[]{:S(2)}) collective-permute-start(f32[14,192]{1,0:T(8,128)} %get-tuple-element.14), channel_id=1, source_target_pairs={{0,16},{16,0},{1,17},{17,1},{2,18},{18,2},{3,19},{19,3},{4,20},{20... | collective-permute-start | bytes 32264 | tf_op jit(solution)/shard_map/ppermute | solution.py:243
  36.1 2.1 %collective-permute-done.5 = f32[14,192]{1,0:T(8,128)S(1)} collective-permute-done((f32[14,192]{1,0:T(8,128)}, f32[14,192]{1,0:T(8,128)S(1)}, u32[]{:S(2)}, u32[]{:S(2)}) %collective-permute-start.5) | collective-permute-done | bytes 10784 | tf_op jit(solution)/shard_map/ppermute | solution.py:243
  38.4 1.9 %collective-permute-start.6 = (f32[1,14,704]{2,0,1:T(1,128)S(1)}, f32[1,14,704]{2,0,1:T(1,128)S(1)}, u32[]{:S(2)}, u32[]{:S(2)}) collective-permute-start(f32[1,14,704]{2,0,1:T(1,128)S(1)} %broadcast_in_dim.16), channel_id=1, source_target_pairs={{0,4},{4,0},{8,12},{12,8},{1,5},{5,1},{9,13},{13,9},{2,6},{6,2},{1... | collective-permute-start | bytes 118280 | tf_op jit(solution)/shard_map/ppermute | solution.py:235
  40.3 1.4 %fusion.22 = (f32[14,64,2]{2,1,0:T(8,128)S(1)}, f32[14,64,2]{2,1,0:T(8,128)S(1)}) fusion(f32[14,64,128]{2,1,0:T(8,128)} %get-tuple-element.13.f_ref), kind=kLoop, calls=%fused_computation.73 | loop fusion | bytes 28672 | tf_op jit(solution)/shard_map/slice | solution.py:250
  42.6 3.3 %collective-permute-start.7 = (f32[2,14,704]{2,0,1:T(2,128)S(1)}, f32[2,14,704]{2,0,1:T(2,128)S(1)}, u32[]{:S(2)}, u32[]{:S(2)}) collective-permute-start(f32[2,14,704]{2,0,1:T(2,128)S(1)} %maximum_select_fusion.7), channel_id=1, source_target_pairs={{0,8},{4,12},{8,0},{12,4},{1,9},{5,13},{9,1},{13,5},{2,10},{6,14},... | collective-permute-start | bytes 236552 | tf_op jit(solution)/shard_map/ppermute | solution.py:235
  46.0 2.4 %collective-permute-done.7 = f32[2,14,704]{2,0,1:T(2,128)S(1)} collective-permute-done((f32[2,14,704]{2,0,1:T(2,128)S(1)}, f32[2,14,704]{2,0,1:T(2,128)S(1)}, u32[]{:S(2)}, u32[]{:S(2)}) %collective-permute-start.7) | collective-permute-done | bytes 78880 | tf_op jit(solution)/shard_map/ppermute | solution.py:235
  48.7 1.2 %collective-permute-done.8 = f32[1,14,1024]{2,1,0:T(8,128)S(1)} collective-permute-done((f32[1,14,1024]{2,1,0:T(8,128)S(1)}, f32[1,14,1024]{2,1,0:T(8,128)S(1)}, u32[]{:S(2)}, u32[]{:S(2)}) %collective-permute-start.8) | collective-permute-done | bytes 57376 | tf_op jit(solution)/shard_map/ppermute | solution.py:235
  49.9 1.6 %collective-permute-start.9 = (f32[2,14,1024]{2,1,0:T(8,128)S(1)}, f32[2,14,1024]{2,1,0:T(8,128)S(1)}, u32[]{:S(2)}, u32[]{:S(2)}) collective-permute-start(f32[2,14,1024]{2,1,0:T(8,128)S(1)} %maximum_select_fusion.5), channel_id=1, source_target_pairs={{0,2},{1,3},{2,0},{3,1},{4,6},{5,7},{6,4},{7,5},{8,10},{9,11},{10,... | collective-permute-start | bytes 344072 | tf_op jit(solution)/shard_map/ppermute | solution.py:235
  51.7 3.8 %collective-permute-done.9 = f32[2,14,1024]{2,1,0:T(8,128)S(1)} collective-permute-done((f32[2,14,1024]{2,1,0:T(8,128)S(1)}, f32[2,14,1024]{2,1,0:T(8,128)S(1)}, u32[]{:S(2)}, u32[]{:S(2)}) %collective-permute-start.9) | collective-permute-done | bytes 114720 | tf_op jit(solution)/shard_map/ppermute | solution.py:235
  56.3 1.0 %fusion = f32[42,384]{1,0:T(8,128)S(1)} fusion(s32[384]{0:T(512)S(1)} %pad_add_fusion, bf16[14,3072]{1,0:T(8,128)(2,1)S(1)} %get-tuple-element.24, bf16[14,3072]{1,0:T(8,128)(2,1)S(1)} %get-tuple-element.25, bf16[14,3072]{1,0:T(8,128)(2,1)S(1)} %get-tuple-element.23), kind=kOutput, calls=%fused_computation.1 | convolution fusion | flops 101044224 | bytes 324096 | tf_op jit(solution)/shard_map/dot_general | solution.py:225
  58.9 3.5 %shard_map.57 = f32[14,64,128]{2,1,0:T(8,128)} custom-call(f32[14,64,128]{2,1,0:T(8,128)} %get-tuple-element.13.f_ref, f32[14,2,128]{2,1,0:T(2,128)} %bitcast.80, f32[14,2,128]{2,1,0:T(2,128)} %bitcast.79, f32[14,2,64]{2,1,0:T(2,128)} %bitcast.84, f32[14,2,64]{2,1,0:T(2,128)} %bitcast.83, f32[14,64,128]{2,1,0:T(8,128)} %bitcast.70, ...), custom_call_target="tpu_custom_call" | custom-call | tf_op jit(solution)/shard_map/pallas_call | solution.py:114
  (88 shorter events, 9.6 us)
Async XLA Ops:
  0.0 6.9 %copy-start = (f32[1,7,2,64,128]{4,3,2,1,0:T(8,128)S(1)}, f32[1,7,2,64,128]{4,3,2,1,0:T(8,128)}, u32[]{:S(2)}) copy-start(f32[1,7,2,64,128]{4,3,2,1,0:T(8,128)} %param.5) | copy-start | bytes 1376260
  3.9 4.9 %collective-permute-start = (f32[14,192]{1,0:T(8,128)}, f32[14,192]{1,0:T(8,128)S(1)}, u32[]{:S(2)}, u32[]{:S(2)}) collective-permute-start(f32[14,192]{1,0:T(8,128)} %get-tuple-element.10), channel_id=1, source_target_pairs={{0,16},{16,0},{1,17},{17,1},{2,18},{18,2},{3,19},{19,3},{4,20},{20... | collective-permute-start | bytes 32264 | tf_op jit(solution)/shard_map/ppermute | solution.py:243
  6.9 0.7 %copy-start.1 = (s32[1,1,1,768]{3,2,1,0:T(1,128)S(1)}, s32[1,1,1,768]{3,2,1,0:T(1,128)}, u32[]{:S(2)}) copy-start(s32[1,1,1,768]{3,2,1,0:T(1,128)} %param.6) | copy-start | bytes 9220
  8.9 4.1 %collective-permute-start.1 = (f32[1,14,704]{2,0,1:T(1,128)S(1)}, f32[1,14,704]{2,0,1:T(1,128)S(1)}, u32[]{:S(2)}, u32[]{:S(2)}) collective-permute-start(f32[1,14,704]{2,0,1:T(1,128)S(1)} %broadcast_in_dim.14), channel_id=1, source_target_pairs={{0,4},{4,0},{8,12},{12,8},{1,5},{5,1},{9,13},{13,9},{2,6},{6,2},{1... | collective-permute-start | bytes 118280 | tf_op jit(solution)/shard_map/ppermute | solution.py:235
  13.2 5.6 %collective-permute-start.2 = (f32[2,14,704]{2,0,1:T(2,128)S(1)}, f32[2,14,704]{2,0,1:T(2,128)S(1)}, u32[]{:S(2)}, u32[]{:S(2)}) collective-permute-start(f32[2,14,704]{2,0,1:T(2,128)S(1)} %maximum_select_fusion.6), channel_id=1, source_target_pairs={{0,8},{4,12},{8,0},{12,4},{1,9},{5,13},{9,1},{13,5},{2,10},{6,14},... | collective-permute-start | bytes 236552 | tf_op jit(solution)/shard_map/ppermute | solution.py:235
  19.1 1.3 %collective-permute-start.3 = (f32[1,14,1024]{2,1,0:T(8,128)S(1)}, f32[1,14,1024]{2,1,0:T(8,128)S(1)}, u32[]{:S(2)}, u32[]{:S(2)}) collective-permute-start(f32[1,14,1024]{2,1,0:T(8,128)S(1)} %maximum_bitcast_fusion), channel_id=1, source_target_pairs={{0,1},{1,0},{2,3},{3,2},{4,5},{5,4},{6,7},{7,6},{8,9},{9,8},{10,11... | collective-permute-start | bytes 172040 | tf_op jit(solution)/shard_map/ppermute | solution.py:235
  20.4 5.7 %collective-permute-start.4 = (f32[2,14,1024]{2,1,0:T(8,128)S(1)}, f32[2,14,1024]{2,1,0:T(8,128)S(1)}, u32[]{:S(2)}, u32[]{:S(2)}) collective-permute-start(f32[2,14,1024]{2,1,0:T(8,128)S(1)} %maximum_select_fusion.4), channel_id=1, source_target_pairs={{0,2},{1,3},{2,0},{3,1},{4,6},{5,7},{6,4},{7,5},{8,10},{9,11},{10,... | collective-permute-start | bytes 344072 | tf_op jit(solution)/shard_map/ppermute | solution.py:235
  34.2 4.0 %collective-permute-start.5 = (f32[14,192]{1,0:T(8,128)}, f32[14,192]{1,0:T(8,128)S(1)}, u32[]{:S(2)}, u32[]{:S(2)}) collective-permute-start(f32[14,192]{1,0:T(8,128)} %get-tuple-element.14), channel_id=1, source_target_pairs={{0,16},{16,0},{1,17},{17,1},{2,18},{18,2},{3,19},{19,3},{4,20},{20... | collective-permute-start | bytes 32264 | tf_op jit(solution)/shard_map/ppermute | solution.py:243
  38.4 4.1 %collective-permute-start.6 = (f32[1,14,704]{2,0,1:T(1,128)S(1)}, f32[1,14,704]{2,0,1:T(1,128)S(1)}, u32[]{:S(2)}, u32[]{:S(2)}) collective-permute-start(f32[1,14,704]{2,0,1:T(1,128)S(1)} %broadcast_in_dim.16), channel_id=1, source_target_pairs={{0,4},{4,0},{8,12},{12,8},{1,5},{5,1},{9,13},{13,9},{2,6},{6,2},{1... | collective-permute-start | bytes 118280 | tf_op jit(solution)/shard_map/ppermute | solution.py:235
  42.6 5.7 %collective-permute-start.7 = (f32[2,14,704]{2,0,1:T(2,128)S(1)}, f32[2,14,704]{2,0,1:T(2,128)S(1)}, u32[]{:S(2)}, u32[]{:S(2)}) collective-permute-start(f32[2,14,704]{2,0,1:T(2,128)S(1)} %maximum_select_fusion.7), channel_id=1, source_target_pairs={{0,8},{4,12},{8,0},{12,4},{1,9},{5,13},{9,1},{13,5},{2,10},{6,14},... | collective-permute-start | bytes 236552 | tf_op jit(solution)/shard_map/ppermute | solution.py:235
  48.6 1.3 %collective-permute-start.8 = (f32[1,14,1024]{2,1,0:T(8,128)S(1)}, f32[1,14,1024]{2,1,0:T(8,128)S(1)}, u32[]{:S(2)}, u32[]{:S(2)}) collective-permute-start(f32[1,14,1024]{2,1,0:T(8,128)S(1)} %maximum_bitcast_fusion.1), channel_id=1, source_target_pairs={{0,1},{1,0},{2,3},{3,2},{4,5},{5,4},{6,7},{7,6},{8,9},{9,8},{10,11... | collective-permute-start | bytes 172040 | tf_op jit(solution)/shard_map/ppermute | solution.py:235
  49.9 5.6 %collective-permute-start.9 = (f32[2,14,1024]{2,1,0:T(8,128)S(1)}, f32[2,14,1024]{2,1,0:T(8,128)S(1)}, u32[]{:S(2)}, u32[]{:S(2)}) collective-permute-start(f32[2,14,1024]{2,1,0:T(8,128)S(1)} %maximum_select_fusion.5), channel_id=1, source_target_pairs={{0,2},{1,3},{2,0},{3,1},{4,6},{5,7},{6,4},{7,5},{8,10},{9,11},{10,... | collective-permute-start | bytes 344072 | tf_op jit(solution)/shard_map/ppermute | solution.py:235

commit v13 on v12

--- a/solution.py
+++ b/solution.py
@@ -17,7 +17,7 @@
 HIGHEST = lax.Precision.HIGHEST
 
 
-def stencil_kernel(f_ref, up_ref, down_ref, left_ref, right_ref, base_ref, lon_ref, lat_ref, turn_ref, o_ref, *rest, first):
+def stencil_kernel(f_ref, halo_ref, base_ref, lon_ref, lat_ref, turn_ref, o_ref, *rest, first):
     planes, height, width = f_ref.shape
     comps = planes // 2
     row = lax.broadcasted_iota(jnp.int32, (height, width), 0)
@@ -31,8 +31,8 @@
     pick_row = lax.broadcasted_iota(jnp.int32, (width, height), 0)
 
     def columns(k):
-        left = left_ref[k]
-        right = right_ref[k]
+        left = halo_ref[k, 4:6, 0:height]
+        right = halo_ref[k, 6:8, 0:height]
         rows_of = jnp.where(
             pick_row == 0,
             left[0:1, :],
@@ -44,8 +44,8 @@
 
     def terms(k):
         x = f_ref[k]
-        up = up_ref[k]
-        down = down_ref[k]
+        up = halo_ref[k, 0:2, :]
+        down = halo_ref[k, 2:4, :]
         sides = columns(k)
         left = sides[:, 0:2]
         right = sides[:, 2:4]
@@ -107,7 +107,7 @@
         donate_planes(lambda k: o_ref[k], planes, lon_ref[...], lat_ref[...], turn_ref, rest[0])
 
 
-def advance(field, up, down, left, right, base, lon, lat, turn, first):
+def advance(field, halo, base, lon, lat, turn, first):
     shape = jax.ShapeDtypeStruct(field.shape, field.dtype)
     if first:
         shape = (shape, jax.ShapeDtypeStruct((field.shape[0], lon.shape[1]), jnp.float32))
@@ -115,7 +115,7 @@
         functools.partial(stencil_kernel, first=first),
         out_shape=shape,
         interpret=INTERPRET,
-    )(field, up, down, left, right, base, lon, lat, turn)
+    )(field, halo, base, lon, lat, turn)
 
 
 def donation_weights(cells_ref, frac_ref, rows, cols):
@@ -266,7 +266,8 @@
         down = jnp.where(on_bottom, rim_lat, down).reshape(comps * levels, 2, cols)
         left = jnp.where(on_left, rim_lon, left).reshape(comps * levels, 2, rows)
         right = jnp.where(on_right, rim_lon, right).reshape(comps * levels, 2, rows)
-        return up, down, left, right
+        sides = jnp.pad(jnp.concatenate([left, right], axis=1), ((0, 0), (0, 0), (0, cols - rows)))
+        return (jnp.concatenate([up, down, sides], axis=1),)
 
     field = state[0].reshape(comps * levels, rows, cols)
     turn_parts = jnp.concatenate([jnp.cos(donor_turn[0, 0]), jnp.sin(donor_turn[0, 0])])

time: 62.7 us -> 62.4 us (level)
  other arithmetic: 4.07 us -> 3.01 us
  local copies, waits for them, and re-layouts: 7.2 us -> 7.87 us
    select_n x4, other arithmetic: 2.52 us -> 0.09 us  [the longest x2 0.04 us: section(): left = jnp.where(on_left, rim_lon, left).reshape(comps * levels, 2, rows)]
    concatenate x0 -> x4, other arithmetic: none -> 1.35 us  [the longest x2 1.3 us: section(): return (jnp.concatenate([up, down, sides], axis=1),)]
    unnamed x8 -> x12, local copies, waits for them, and re-layouts: 0.5 us -> 1.18 us
where the time goes in v13:
time: 62.4 us; the launch traced here: 62.1 us
  waiting for transfers between devices  20 us (32%)
  starting transfers between devices  18.8 us (30%)
  Pallas kernels  9.98 us (16%)
  local copies, waits for them, and re-layouts  7.87 us (13%)
  other arithmetic  3.01 us (5%)
  matrix products  1.98 us (3%)
    ppermute x8, waiting for transfers between devices, gather(): other = lax.ppermute(held, axis, [(i, i ^ k) for i in range(size)])  16.6 us
    ppermute x8, starting transfers between devices, gather(): other = lax.ppermute(held, axis, [(i, i ^ k) for i in range(size)])  14 us
    pallas_call x2, Pallas kernels, advance(): pl.pallas_call(functools.partial(stencil_kernel, first=first), out_shape=...  7.4 us
    ppermute x2, starting transfers between devices, section(): given = lax.ppermute(donation, 'panel', [(0, 1), (1, 0)])  4.8 us
    ppermute x2, waiting for transfers between devices, section(): given = lax.ppermute(donation, 'panel', [(0, 1), (1, 0)])  3.31 us
    pallas_call x1, Pallas kernels, first_donation(): pl.pallas_call(donation_kernel, out_shape=(jax.ShapeDtypeStruct((planes,...  2.58 us
    slice x6, local copies, waits for them, and re-layouts, section(): side_cols = jnp.concatenate([flat[:, :, :2], flat[:, :, cols - 2:]], axis=2)  2.33 us
    dot_general x2, matrix products, select(): picked = jnp.dot(parts, pick, preferred_element_type=jnp.float32)  1.98 us
  transfers between devices with their start and end apart: 10, of which 10 were waited for; matrix products, arithmetic and copies ran while one was open for 5% of the time, Pallas kernels for 0%

profile of v13, /device:TPU:0, one launch (start us, length us, event | category | flops | bytes accessed | tf_op | source)
XLA Modules:
  0.0 62.1 jit_solution(1662601896990432605)
XLA Ops:
  1.4 2.6 %shard_map.55 = (f32[14,192]{1,0:T(8,128)}, f32[128,192]{1,0:T(8,128)}, f32[64,192]{1,0:T(8,128)}) custom-call(f32[14,64,128]{2,1,0:T(8,128)} %bitcast.67, s32[1,192]{1,0:T(1,128)} %bitcast.89, f32[2,192]{1,0:T(2,128)} %bitcast.88, f32[2,192]{1,0:T(2,128)} %pad_maximum_fusion.6.turn_ref), custom_call_target="tpu_custom_call" | custom-call | tf_op jit(solution)/shard_map/pallas_call | solution.py:166
  4.0 3.0 %collective-permute-start = (f32[14,192]{1,0:T(8,128)}, f32[14,192]{1,0:T(8,128)S(1)}, u32[]{:S(2)}, u32[]{:S(2)}) collective-permute-start(f32[14,192]{1,0:T(8,128)} %get-tuple-element.10), channel_id=1, source_target_pairs={{0,16},{16,0},{1,17},{17,1},{2,18},{18,2},{3,19},{19,3},{4,20},{20... | collective-permute-start | bytes 32264 | tf_op jit(solution)/shard_map/ppermute | solution.py:243
  7.7 1.2 %collective-permute-done = f32[14,192]{1,0:T(8,128)S(1)} collective-permute-done((f32[14,192]{1,0:T(8,128)}, f32[14,192]{1,0:T(8,128)S(1)}, u32[]{:S(2)}, u32[]{:S(2)}) %collective-permute-start) | collective-permute-done | bytes 10784 | tf_op jit(solution)/shard_map/ppermute | solution.py:243
  9.0 2.1 %collective-permute-start.1 = (f32[1,14,704]{2,0,1:T(1,128)S(1)}, f32[1,14,704]{2,0,1:T(1,128)S(1)}, u32[]{:S(2)}, u32[]{:S(2)}) collective-permute-start(f32[1,14,704]{2,0,1:T(1,128)S(1)} %broadcast_in_dim.14), channel_id=1, source_target_pairs={{0,4},{4,0},{8,12},{12,8},{1,5},{5,1},{9,13},{13,9},{2,6},{6,2},{1... | collective-permute-start | bytes 118280 | tf_op jit(solution)/shard_map/ppermute | solution.py:235
  11.5 1.6 %collective-permute-done.1 = f32[1,14,704]{2,0,1:T(1,128)S(1)} collective-permute-done((f32[1,14,704]{2,0,1:T(1,128)S(1)}, f32[1,14,704]{2,0,1:T(1,128)S(1)}, u32[]{:S(2)}, u32[]{:S(2)}) %collective-permute-start.1) | collective-permute-done | bytes 39456 | tf_op jit(solution)/shard_map/ppermute | solution.py:235
  13.3 3.1 %collective-permute-start.2 = (f32[2,14,704]{2,0,1:T(2,128)S(1)}, f32[2,14,704]{2,0,1:T(2,128)S(1)}, u32[]{:S(2)}, u32[]{:S(2)}) collective-permute-start(f32[2,14,704]{2,0,1:T(2,128)S(1)} %maximum_select_fusion.6), channel_id=1, source_target_pairs={{0,8},{4,12},{8,0},{12,4},{1,9},{5,13},{9,1},{13,5},{2,10},{6,14},... | collective-permute-start | bytes 236552 | tf_op jit(solution)/shard_map/ppermute | solution.py:235
  16.5 2.4 %collective-permute-done.2 = f32[2,14,704]{2,0,1:T(2,128)S(1)} collective-permute-done((f32[2,14,704]{2,0,1:T(2,128)S(1)}, f32[2,14,704]{2,0,1:T(2,128)S(1)}, u32[]{:S(2)}, u32[]{:S(2)}) %collective-permute-start.2) | collective-permute-done | bytes 78880 | tf_op jit(solution)/shard_map/ppermute | solution.py:235
  19.2 1.2 %collective-permute-done.3 = f32[1,14,1024]{2,1,0:T(8,128)S(1)} collective-permute-done((f32[1,14,1024]{2,1,0:T(8,128)S(1)}, f32[1,14,1024]{2,1,0:T(8,128)S(1)}, u32[]{:S(2)}, u32[]{:S(2)}) %collective-permute-start.3) | collective-permute-done | bytes 57376 | tf_op jit(solution)/shard_map/ppermute | solution.py:235
  20.4 1.9 %collective-permute-start.4 = (f32[2,14,1024]{2,1,0:T(8,128)S(1)}, f32[2,14,1024]{2,1,0:T(8,128)S(1)}, u32[]{:S(2)}, u32[]{:S(2)}) collective-permute-start(f32[2,14,1024]{2,1,0:T(8,128)S(1)} %maximum_select_fusion.4), channel_id=1, source_target_pairs={{0,2},{1,3},{2,0},{3,1},{4,6},{5,7},{6,4},{7,5},{8,10},{9,11},{10,... | collective-permute-start | bytes 344072 | tf_op jit(solution)/shard_map/ppermute | solution.py:235
  22.5 3.6 %collective-permute-done.4 = f32[2,14,1024]{2,1,0:T(8,128)S(1)} collective-permute-done((f32[2,14,1024]{2,1,0:T(8,128)S(1)}, f32[2,14,1024]{2,1,0:T(8,128)S(1)}, u32[]{:S(2)}, u32[]{:S(2)}) %collective-permute-start.4) | collective-permute-done | bytes 114720 | tf_op jit(solution)/shard_map/ppermute | solution.py:235
  27.2 1.0 %fusion.1 = f32[42,384]{1,0:T(8,128)S(1)} fusion(s32[384]{0:T(512)S(1)} %pad_add_fusion, bf16[14,3072]{1,0:T(8,128)(2,1)S(1)} %get-tuple-element.27, bf16[14,3072]{1,0:T(8,128)(2,1)S(1)} %get-tuple-element.28, bf16[14,3072]{1,0:T(8,128)(2,1)S(1)} %get-tuple-element.26), kind=kOutput, calls=%fused_computation.2 | convolution fusion | flops 101044224 | bytes 324096 | tf_op jit(solution)/shard_map/dot_general | solution.py:225
  29.3 3.9 %shard_map.56 = (f32[14,64,128]{2,1,0:T(8,128)}, f32[14,192]{1,0:T(8,128)}) custom-call(f32[14,64,128]{2,1,0:T(8,128)} %bitcast.68, f32[14,8,128]{2,1,0:T(8,128)} %pad_maximum_fusion.halo_ref, f32[14,64,128]{2,1,0:T(8,128)} %bitcast.69, f32[128,192]{1,0:T(8,128)} %get-tuple-element.11.lon_ref, f32[64,192]{1,0:T(8,128)} %get-tuple-element.12.lat_ref, ...), custom_call_target="tpu_custom_call" | custom-call | tf_op jit(solution)/shard_map/pallas_call | solution.py:114
  33.2 0.9 %fusion.21 = (f32[14,2,128]{2,1,0:T(2,128)S(1)}, f32[14,2,128]{2,1,0:T(2,128)S(1)}) fusion(f32[14,64,128]{2,1,0:T(8,128)} %get-tuple-element.13.f_ref), kind=kLoop, calls=%fused_computation.77 | loop fusion | bytes 57344 | tf_op jit(solution)/shard_map/slice | solution.py:245
  34.1 1.8 %collective-permute-start.5 = (f32[14,192]{1,0:T(8,128)}, f32[14,192]{1,0:T(8,128)S(1)}, u32[]{:S(2)}, u32[]{:S(2)}) collective-permute-start(f32[14,192]{1,0:T(8,128)} %get-tuple-element.14), channel_id=1, source_target_pairs={{0,16},{16,0},{1,17},{17,1},{2,18},{18,2},{3,19},{19,3},{4,20},{20... | collective-permute-start | bytes 32264 | tf_op jit(solution)/shard_map/ppermute | solution.py:243
  36.0 2.1 %collective-permute-done.5 = f32[14,192]{1,0:T(8,128)S(1)} collective-permute-done((f32[14,192]{1,0:T(8,128)}, f32[14,192]{1,0:T(8,128)S(1)}, u32[]{:S(2)}, u32[]{:S(2)}) %collective-permute-start.5) | collective-permute-done | bytes 10784 | tf_op jit(solution)/shard_map/ppermute | solution.py:243
  38.2 1.9 %collective-permute-start.6 = (f32[1,14,704]{2,0,1:T(1,128)S(1)}, f32[1,14,704]{2,0,1:T(1,128)S(1)}, u32[]{:S(2)}, u32[]{:S(2)}) collective-permute-start(f32[1,14,704]{2,0,1:T(1,128)S(1)} %broadcast_in_dim.16), channel_id=1, source_target_pairs={{0,4},{4,0},{8,12},{12,8},{1,5},{5,1},{9,13},{13,9},{2,6},{6,2},{1... | collective-permute-start | bytes 118280 | tf_op jit(solution)/shard_map/ppermute | solution.py:235
  40.1 1.3 %fusion.22 = (f32[14,64,2]{2,1,0:T(8,128)S(1)}, f32[14,64,2]{2,1,0:T(8,128)S(1)}) fusion(f32[14,64,128]{2,1,0:T(8,128)} %get-tuple-element.13.f_ref), kind=kLoop, calls=%fused_computation.78 | loop fusion | bytes 28672 | tf_op jit(solution)/shard_map/slice | solution.py:250
  42.4 3.3 %collective-permute-start.7 = (f32[2,14,704]{2,0,1:T(2,128)S(1)}, f32[2,14,704]{2,0,1:T(2,128)S(1)}, u32[]{:S(2)}, u32[]{:S(2)}) collective-permute-start(f32[2,14,704]{2,0,1:T(2,128)S(1)} %maximum_select_fusion.7), channel_id=1, source_target_pairs={{0,8},{4,12},{8,0},{12,4},{1,9},{5,13},{9,1},{13,5},{2,10},{6,14},... | collective-permute-start | bytes 236552 | tf_op jit(solution)/shard_map/ppermute | solution.py:235
  45.8 2.4 %collective-permute-done.7 = f32[2,14,704]{2,0,1:T(2,128)S(1)} collective-permute-done((f32[2,14,704]{2,0,1:T(2,128)S(1)}, f32[2,14,704]{2,0,1:T(2,128)S(1)}, u32[]{:S(2)}, u32[]{:S(2)}) %collective-permute-start.7) | collective-permute-done | bytes 78880 | tf_op jit(solution)/shard_map/ppermute | solution.py:235
  48.5 1.2 %collective-permute-done.8 = f32[1,14,1024]{2,1,0:T(8,128)S(1)} collective-permute-done((f32[1,14,1024]{2,1,0:T(8,128)S(1)}, f32[1,14,1024]{2,1,0:T(8,128)S(1)}, u32[]{:S(2)}, u32[]{:S(2)}) %collective-permute-start.8) | collective-permute-done | bytes 57376 | tf_op jit(solution)/shard_map/ppermute | solution.py:235
  49.8 1.6 %collective-permute-start.9 = (f32[2,14,1024]{2,1,0:T(8,128)S(1)}, f32[2,14,1024]{2,1,0:T(8,128)S(1)}, u32[]{:S(2)}, u32[]{:S(2)}) collective-permute-start(f32[2,14,1024]{2,1,0:T(8,128)S(1)} %maximum_select_fusion.5), channel_id=1, source_target_pairs={{0,2},{1,3},{2,0},{3,1},{4,6},{5,7},{6,4},{7,5},{8,10},{9,11},{10,... | collective-permute-start | bytes 344072 | tf_op jit(solution)/shard_map/ppermute | solution.py:235
  51.5 3.8 %collective-permute-done.9 = f32[2,14,1024]{2,1,0:T(8,128)S(1)} collective-permute-done((f32[2,14,1024]{2,1,0:T(8,128)S(1)}, f32[2,14,1024]{2,1,0:T(8,128)S(1)}, u32[]{:S(2)}, u32[]{:S(2)}) %collective-permute-start.9) | collective-permute-done | bytes 114720 | tf_op jit(solution)/shard_map/ppermute | solution.py:235
  56.5 1.0 %fusion = f32[42,384]{1,0:T(8,128)S(1)} fusion(s32[384]{0:T(512)S(1)} %pad_add_fusion, bf16[14,3072]{1,0:T(8,128)(2,1)S(1)} %get-tuple-element.24, bf16[14,3072]{1,0:T(8,128)(2,1)S(1)} %get-tuple-element.25, bf16[14,3072]{1,0:T(8,128)(2,1)S(1)} %get-tuple-element.23), kind=kOutput, calls=%fused_computation.1 | convolution fusion | flops 101044224 | bytes 324096 | tf_op jit(solution)/shard_map/dot_general | solution.py:225
  58.6 3.5 %shard_map.57 = f32[14,64,128]{2,1,0:T(8,128)} custom-call(f32[14,64,128]{2,1,0:T(8,128)} %get-tuple-element.13.f_ref, f32[14,8,128]{2,1,0:T(8,128)} %pad_maximum_fusion.1.halo_ref, f32[14,64,128]{2,1,0:T(8,128)} %bitcast.70, f32[128,192]{1,0:T(8,128)} %get-tuple-element.11.lon_ref, f32[64,192]{1,0:T(8,128)} %get-tuple-element.12.lat_ref, ...), custom_call_target="tpu_custom_call" | custom-call | tf_op jit(solution)/shard_map/pallas_call | solution.py:114
  (98 shorter events, 9.2 us)
Async XLA Ops:
  0.0 6.9 %copy-start = (f32[1,7,2,64,128]{4,3,2,1,0:T(8,128)S(1)}, f32[1,7,2,64,128]{4,3,2,1,0:T(8,128)}, u32[]{:S(2)}) copy-start(f32[1,7,2,64,128]{4,3,2,1,0:T(8,128)} %param.5) | copy-start | bytes 1376260
  4.0 4.9 %collective-permute-start = (f32[14,192]{1,0:T(8,128)}, f32[14,192]{1,0:T(8,128)S(1)}, u32[]{:S(2)}, u32[]{:S(2)}) collective-permute-start(f32[14,192]{1,0:T(8,128)} %get-tuple-element.10), channel_id=1, source_target_pairs={{0,16},{16,0},{1,17},{17,1},{2,18},{18,2},{3,19},{19,3},{4,20},{20... | collective-permute-start | bytes 32264 | tf_op jit(solution)/shard_map/ppermute | solution.py:243
  6.9 0.7 %copy-start.3 = (s32[1,1,1,768]{3,2,1,0:T(1,128)S(1)}, s32[1,1,1,768]{3,2,1,0:T(1,128)}, u32[]{:S(2)}) copy-start(s32[1,1,1,768]{3,2,1,0:T(1,128)} %param.6) | copy-start | bytes 9220
  9.0 4.1 %collective-permute-start.1 = (f32[1,14,704]{2,0,1:T(1,128)S(1)}, f32[1,14,704]{2,0,1:T(1,128)S(1)}, u32[]{:S(2)}, u32[]{:S(2)}) collective-permute-start(f32[1,14,704]{2,0,1:T(1,128)S(1)} %broadcast_in_dim.14), channel_id=1, source_target_pairs={{0,4},{4,0},{8,12},{12,8},{1,5},{5,1},{9,13},{13,9},{2,6},{6,2},{1... | collective-permute-start | bytes 118280 | tf_op jit(solution)/shard_map/ppermute | solution.py:235
  13.3 5.6 %collective-permute-start.2 = (f32[2,14,704]{2,0,1:T(2,128)S(1)}, f32[2,14,704]{2,0,1:T(2,128)S(1)}, u32[]{:S(2)}, u32[]{:S(2)}) collective-permute-start(f32[2,14,704]{2,0,1:T(2,128)S(1)} %maximum_select_fusion.6), channel_id=1, source_target_pairs={{0,8},{4,12},{8,0},{12,4},{1,9},{5,13},{9,1},{13,5},{2,10},{6,14},... | collective-permute-start | bytes 236552 | tf_op jit(solution)/shard_map/ppermute | solution.py:235
  19.1 1.3 %collective-permute-start.3 = (f32[1,14,1024]{2,1,0:T(8,128)S(1)}, f32[1,14,1024]{2,1,0:T(8,128)S(1)}, u32[]{:S(2)}, u32[]{:S(2)}) collective-permute-start(f32[1,14,1024]{2,1,0:T(8,128)S(1)} %maximum_bitcast_fusion), channel_id=1, source_target_pairs={{0,1},{1,0},{2,3},{3,2},{4,5},{5,4},{6,7},{7,6},{8,9},{9,8},{10,11... | collective-permute-start | bytes 172040 | tf_op jit(solution)/shard_map/ppermute | solution.py:235
  20.4 5.7 %collective-permute-start.4 = (f32[2,14,1024]{2,1,0:T(8,128)S(1)}, f32[2,14,1024]{2,1,0:T(8,128)S(1)}, u32[]{:S(2)}, u32[]{:S(2)}) collective-permute-start(f32[2,14,1024]{2,1,0:T(8,128)S(1)} %maximum_select_fusion.4), channel_id=1, source_target_pairs={{0,2},{1,3},{2,0},{3,1},{4,6},{5,7},{6,4},{7,5},{8,10},{9,11},{10,... | collective-permute-start | bytes 344072 | tf_op jit(solution)/shard_map/ppermute | solution.py:235
  26.2 0.7 %copy-start.2 = (f32[4,14,1024]{2,1,0:T(8,128)}, f32[4,14,1024]{2,1,0:T(8,128)S(1)}, u32[]{:S(2)}) copy-start(f32[4,14,1024]{2,1,0:T(8,128)S(1)} %maximum_select_fusion) | copy-start | bytes 688132
  27.2 1.2 %slice-start.1 = ((f32[4,14,1024]{2,1,0:T(8,128)}), f32[4,14,256]{2,1,0:T(8,128)S(1)}, s32[]{:S(2)}) async-start(f32[4,14,1024]{2,1,0:T(8,128)} %copy-done.2), calls=%async_computation.1 | async-start | bytes 131072 | tf_op jit(solution)/shard_map/slice | solution.py:257
  34.1 4.0 %collective-permute-start.5 = (f32[14,192]{1,0:T(8,128)}, f32[14,192]{1,0:T(8,128)S(1)}, u32[]{:S(2)}, u32[]{:S(2)}) collective-permute-start(f32[14,192]{1,0:T(8,128)} %get-tuple-element.14), channel_id=1, source_target_pairs={{0,16},{16,0},{1,17},{17,1},{2,18},{18,2},{3,19},{19,3},{4,20},{20... | collective-permute-start | bytes 32264 | tf_op jit(solution)/shard_map/ppermute | solution.py:243
  38.2 4.1 %collective-permute-start.6 = (f32[1,14,704]{2,0,1:T(1,128)S(1)}, f32[1,14,704]{2,0,1:T(1,128)S(1)}, u32[]{:S(2)}, u32[]{:S(2)}) collective-permute-start(f32[1,14,704]{2,0,1:T(1,128)S(1)} %broadcast_in_dim.16), channel_id=1, source_target_pairs={{0,4},{4,0},{8,12},{12,8},{1,5},{5,1},{9,13},{13,9},{2,6},{6,2},{1... | collective-permute-start | bytes 118280 | tf_op jit(solution)/shard_map/ppermute | solution.py:235
  42.4 5.7 %collective-permute-start.7 = (f32[2,14,704]{2,0,1:T(2,128)S(1)}, f32[2,14,704]{2,0,1:T(2,128)S(1)}, u32[]{:S(2)}, u32[]{:S(2)}) collective-permute-start(f32[2,14,704]{2,0,1:T(2,128)S(1)} %maximum_select_fusion.7), channel_id=1, source_target_pairs={{0,8},{4,12},{8,0},{12,4},{1,9},{5,13},{9,1},{13,5},{2,10},{6,14},... | collective-permute-start | bytes 236552 | tf_op jit(solution)/shard_map/ppermute | solution.py:235
  48.4 1.3 %collective-permute-start.8 = (f32[1,14,1024]{2,1,0:T(8,128)S(1)}, f32[1,14,1024]{2,1,0:T(8,128)S(1)}, u32[]{:S(2)}, u32[]{:S(2)}) collective-permute-start(f32[1,14,1024]{2,1,0:T(8,128)S(1)} %maximum_bitcast_fusion.1), channel_id=1, source_target_pairs={{0,1},{1,0},{2,3},{3,2},{4,5},{5,4},{6,7},{7,6},{8,9},{9,8},{10,11... | collective-permute-start | bytes 172040 | tf_op jit(solution)/shard_map/ppermute | solution.py:235
  49.8 5.6 %collective-permute-start.9 = (f32[2,14,1024]{2,1,0:T(8,128)S(1)}, f32[2,14,1024]{2,1,0:T(8,128)S(1)}, u32[]{:S(2)}, u32[]{:S(2)}) collective-permute-start(f32[2,14,1024]{2,1,0:T(8,128)S(1)} %maximum_select_fusion.5), channel_id=1, source_target_pairs={{0,2},{1,3},{2,0},{3,1},{4,6},{5,7},{6,4},{7,5},{8,10},{9,11},{10,... | collective-permute-start | bytes 344072 | tf_op jit(solution)/shard_map/ppermute | solution.py:235
  55.4 0.7 %copy-start.1 = (f32[4,14,1024]{2,1,0:T(8,128)}, f32[4,14,1024]{2,1,0:T(8,128)S(1)}, u32[]{:S(2)}) copy-start(f32[4,14,1024]{2,1,0:T(8,128)S(1)} %maximum_select_fusion.1) | copy-start | bytes 688132
  56.4 1.2 %slice-start = ((f32[4,14,1024]{2,1,0:T(8,128)}), f32[4,14,256]{2,1,0:T(8,128)S(1)}, s32[]{:S(2)}) async-start(f32[4,14,1024]{2,1,0:T(8,128)} %copy-done.1), calls=%async_computation | async-start | bytes 131072 | tf_op jit(solution)/shard_map/slice | solution.py:257

commit v14 on v13

--- a/solution.py
+++ b/solution.py
@@ -22,6 +22,7 @@
     comps = planes // 2
     row = lax.broadcasted_iota(jnp.int32, (height, width), 0)
     col = lax.broadcasted_iota(jnp.int32, (height, width), 1)
+    tile = lax.broadcasted_iota(jnp.int32, (8, width), 0)
 
     eye = jnp.where(
         lax.broadcasted_iota(jnp.int32, (height, height), 0) == lax.broadcasted_iota(jnp.int32, (height, height), 1),
@@ -49,12 +50,16 @@
         sides = columns(k)
         left = sides[:, 0:2]
         right = sides[:, 2:4]
-        lat_m1 = jnp.where(row == 0, up[1:2, :], pltpu.roll(x, 1, 0))
-        lat_m2 = jnp.where(row == 0, up[0:1, :], jnp.where(row == 1, up[1:2, :], pltpu.roll(x, 2, 0)))
-        lat_p1 = jnp.where(row == height - 1, down[0:1, :], pltpu.roll(x, height - 1, 0))
-        lat_p2 = jnp.where(
-            row == height - 1, down[1:2, :], jnp.where(row == height - 2, down[0:1, :], pltpu.roll(x, height - 2, 0))
-        )
+        rolled = pltpu.roll(x, 1, 0)
+        lat_m1 = jnp.concatenate([jnp.where(tile == 0, up[1:2, :], rolled[:8]), rolled[8:]], axis=0)
+        rolled = pltpu.roll(x, 2, 0)
+        top = jnp.where(tile == 0, up[0:1, :], jnp.where(tile == 1, up[1:2, :], rolled[:8]))
+        lat_m2 = jnp.concatenate([top, rolled[8:]], axis=0)
+        rolled = pltpu.roll(x, height - 1, 0)
+        lat_p1 = jnp.concatenate([rolled[: height - 8], jnp.where(tile == 7, down[0:1, :], rolled[height - 8 :])], axis=0)
+        rolled = pltpu.roll(x, height - 2, 0)
+        bottom = jnp.where(tile == 7, down[1:2, :], jnp.where(tile == 6, down[0:1, :], rolled[height - 8 :]))
+        lat_p2 = jnp.concatenate([rolled[: height - 8], bottom], axis=0)
         lon_m1 = jnp.where(col == 0, left[:, 1:2], pltpu.roll(x, 1, 1))
         lon_m2 = jnp.where(col == 0, left[:, 0:1], jnp.where(col == 1, left[:, 1:2], pltpu.roll(x, 2, 1)))
         lon_p1 = jnp.where(col == width - 1, right[:, 0:1], pltpu.roll(x, width - 1, 1))

time: 62.4 us -> 62.4 us (level)
  no operation moved by 1% of the time
where the time goes in v14:
time: 62.4 us; the launch traced here: 62.1 us
  waiting for transfers between devices  20 us (32%)
  starting transfers between devices  18.8 us (30%)
  Pallas kernels  9.99 us (16%)
  local copies, waits for them, and re-layouts  7.87 us (13%)
  other arithmetic  3.01 us (5%)
  matrix products  1.98 us (3%)
    ppermute x8, waiting for transfers between devices, gather(): other = lax.ppermute(held, axis, [(i, i ^ k) for i in range(size)])  16.7 us
    ppermute x8, starting transfers between devices, gather(): other = lax.ppermute(held, axis, [(i, i ^ k) for i in range(size)])  14 us
    pallas_call x2, Pallas kernels, advance(): pl.pallas_call(functools.partial(stencil_kernel, first=first), out_shape=...  7.41 us
    ppermute x2, starting transfers between devices, section(): given = lax.ppermute(donation, 'panel', [(0, 1), (1, 0)])  4.79 us
    ppermute x2, waiting for transfers between devices, section(): given = lax.ppermute(donation, 'panel', [(0, 1), (1, 0)])  3.32 us
    pallas_call x1, Pallas kernels, first_donation(): pl.pallas_call(donation_kernel, out_shape=(jax.ShapeDtypeStruct((planes,...  2.58 us
    slice x6, local copies, waits for them, and re-layouts, section(): side_cols = jnp.concatenate([flat[:, :, :2], flat[:, :, cols - 2:]], axis=2)  2.33 us
    dot_general x2, matrix products, select(): picked = jnp.dot(parts, pick, preferred_element_type=jnp.float32)  1.98 us
  transfers between devices with their start and end apart: 10, of which 10 were waited for; matrix products, arithmetic and copies ran while one was open for 5% of the time, Pallas kernels for 0%

profile of v14, /device:TPU:0, one launch (start us, length us, event | category | flops | bytes accessed | tf_op | source)
XLA Modules:
  0.0 62.1 jit_solution(3388717605372376847)
XLA Ops:
  1.4 2.6 %shard_map.55 = (f32[14,192]{1,0:T(8,128)}, f32[128,192]{1,0:T(8,128)}, f32[64,192]{1,0:T(8,128)}) custom-call(f32[14,64,128]{2,1,0:T(8,128)} %bitcast.67, s32[1,192]{1,0:T(1,128)} %bitcast.89, f32[2,192]{1,0:T(2,128)} %bitcast.88, f32[2,192]{1,0:T(2,128)} %pad_maximum_fusion.6.turn_ref), custom_call_target="tpu_custom_call" | custom-call | tf_op jit(solution)/shard_map/pallas_call | solution.py:171
  4.0 3.0 %collective-permute-start = (f32[14,192]{1,0:T(8,128)}, f32[14,192]{1,0:T(8,128)S(1)}, u32[]{:S(2)}, u32[]{:S(2)}) collective-permute-start(f32[14,192]{1,0:T(8,128)} %get-tuple-element.10), channel_id=1, source_target_pairs={{0,16},{16,0},{1,17},{17,1},{2,18},{18,2},{3,19},{19,3},{4,20},{20... | collective-permute-start | bytes 32264 | tf_op jit(solution)/shard_map/ppermute | solution.py:248
  7.7 1.2 %collective-permute-done = f32[14,192]{1,0:T(8,128)S(1)} collective-permute-done((f32[14,192]{1,0:T(8,128)}, f32[14,192]{1,0:T(8,128)S(1)}, u32[]{:S(2)}, u32[]{:S(2)}) %collective-permute-start) | collective-permute-done | bytes 10784 | tf_op jit(solution)/shard_map/ppermute | solution.py:248
  9.0 2.1 %collective-permute-start.1 = (f32[1,14,704]{2,0,1:T(1,128)S(1)}, f32[1,14,704]{2,0,1:T(1,128)S(1)}, u32[]{:S(2)}, u32[]{:S(2)}) collective-permute-start(f32[1,14,704]{2,0,1:T(1,128)S(1)} %broadcast_in_dim.14), channel_id=1, source_target_pairs={{0,4},{4,0},{8,12},{12,8},{1,5},{5,1},{9,13},{13,9},{2,6},{6,2},{1... | collective-permute-start | bytes 118280 | tf_op jit(solution)/shard_map/ppermute | solution.py:240
  11.5 1.6 %collective-permute-done.1 = f32[1,14,704]{2,0,1:T(1,128)S(1)} collective-permute-done((f32[1,14,704]{2,0,1:T(1,128)S(1)}, f32[1,14,704]{2,0,1:T(1,128)S(1)}, u32[]{:S(2)}, u32[]{:S(2)}) %collective-permute-start.1) | collective-permute-done | bytes 39456 | tf_op jit(solution)/shard_map/ppermute | solution.py:240
  13.3 3.1 %collective-permute-start.2 = (f32[2,14,704]{2,0,1:T(2,128)S(1)}, f32[2,14,704]{2,0,1:T(2,128)S(1)}, u32[]{:S(2)}, u32[]{:S(2)}) collective-permute-start(f32[2,14,704]{2,0,1:T(2,128)S(1)} %maximum_select_fusion.6), channel_id=1, source_target_pairs={{0,8},{4,12},{8,0},{12,4},{1,9},{5,13},{9,1},{13,5},{2,10},{6,14},... | collective-permute-start | bytes 236552 | tf_op jit(solution)/shard_map/ppermute | solution.py:240
  16.5 2.4 %collective-permute-done.2 = f32[2,14,704]{2,0,1:T(2,128)S(1)} collective-permute-done((f32[2,14,704]{2,0,1:T(2,128)S(1)}, f32[2,14,704]{2,0,1:T(2,128)S(1)}, u32[]{:S(2)}, u32[]{:S(2)}) %collective-permute-start.2) | collective-permute-done | bytes 78880 | tf_op jit(solution)/shard_map/ppermute | solution.py:240
  19.2 1.2 %collective-permute-done.3 = f32[1,14,1024]{2,1,0:T(8,128)S(1)} collective-permute-done((f32[1,14,1024]{2,1,0:T(8,128)S(1)}, f32[1,14,1024]{2,1,0:T(8,128)S(1)}, u32[]{:S(2)}, u32[]{:S(2)}) %collective-permute-start.3) | collective-permute-done | bytes 57376 | tf_op jit(solution)/shard_map/ppermute | solution.py:240
  20.4 1.9 %collective-permute-start.4 = (f32[2,14,1024]{2,1,0:T(8,128)S(1)}, f32[2,14,1024]{2,1,0:T(8,128)S(1)}, u32[]{:S(2)}, u32[]{:S(2)}) collective-permute-start(f32[2,14,1024]{2,1,0:T(8,128)S(1)} %maximum_select_fusion.4), channel_id=1, source_target_pairs={{0,2},{1,3},{2,0},{3,1},{4,6},{5,7},{6,4},{7,5},{8,10},{9,11},{10,... | collective-permute-start | bytes 344072 | tf_op jit(solution)/shard_map/ppermute | solution.py:240
  22.5 3.6 %collective-permute-done.4 = f32[2,14,1024]{2,1,0:T(8,128)S(1)} collective-permute-done((f32[2,14,1024]{2,1,0:T(8,128)S(1)}, f32[2,14,1024]{2,1,0:T(8,128)S(1)}, u32[]{:S(2)}, u32[]{:S(2)}) %collective-permute-start.4) | collective-permute-done | bytes 114720 | tf_op jit(solution)/shard_map/ppermute | solution.py:240
  27.2 1.0 %fusion.1 = f32[42,384]{1,0:T(8,128)S(1)} fusion(s32[384]{0:T(512)S(1)} %pad_add_fusion, bf16[14,3072]{1,0:T(8,128)(2,1)S(1)} %get-tuple-element.27, bf16[14,3072]{1,0:T(8,128)(2,1)S(1)} %get-tuple-element.28, bf16[14,3072]{1,0:T(8,128)(2,1)S(1)} %get-tuple-element.26), kind=kOutput, calls=%fused_computation.2 | convolution fusion | flops 101044224 | bytes 324096 | tf_op jit(solution)/shard_map/dot_general | solution.py:230
  29.3 3.9 %shard_map.56 = (f32[14,64,128]{2,1,0:T(8,128)}, f32[14,192]{1,0:T(8,128)}) custom-call(f32[14,64,128]{2,1,0:T(8,128)} %bitcast.68, f32[14,8,128]{2,1,0:T(8,128)} %pad_maximum_fusion.halo_ref, f32[14,64,128]{2,1,0:T(8,128)} %bitcast.69, f32[128,192]{1,0:T(8,128)} %get-tuple-element.11.lon_ref, f32[64,192]{1,0:T(8,128)} %get-tuple-element.12.lat_ref, ...), custom_call_target="tpu_custom_call" | custom-call | tf_op jit(solution)/shard_map/pallas_call | solution.py:119
  33.2 0.9 %fusion.21 = (f32[14,2,128]{2,1,0:T(2,128)S(1)}, f32[14,2,128]{2,1,0:T(2,128)S(1)}) fusion(f32[14,64,128]{2,1,0:T(8,128)} %get-tuple-element.13.f_ref), kind=kLoop, calls=%fused_computation.77 | loop fusion | bytes 57344 | tf_op jit(solution)/shard_map/slice | solution.py:250
  34.1 1.8 %collective-permute-start.5 = (f32[14,192]{1,0:T(8,128)}, f32[14,192]{1,0:T(8,128)S(1)}, u32[]{:S(2)}, u32[]{:S(2)}) collective-permute-start(f32[14,192]{1,0:T(8,128)} %get-tuple-element.14), channel_id=1, source_target_pairs={{0,16},{16,0},{1,17},{17,1},{2,18},{18,2},{3,19},{19,3},{4,20},{20... | collective-permute-start | bytes 32264 | tf_op jit(solution)/shard_map/ppermute | solution.py:248
  36.0 2.1 %collective-permute-done.5 = f32[14,192]{1,0:T(8,128)S(1)} collective-permute-done((f32[14,192]{1,0:T(8,128)}, f32[14,192]{1,0:T(8,128)S(1)}, u32[]{:S(2)}, u32[]{:S(2)}) %collective-permute-start.5) | collective-permute-done | bytes 10784 | tf_op jit(solution)/shard_map/ppermute | solution.py:248
  38.2 1.9 %collective-permute-start.6 = (f32[1,14,704]{2,0,1:T(1,128)S(1)}, f32[1,14,704]{2,0,1:T(1,128)S(1)}, u32[]{:S(2)}, u32[]{:S(2)}) collective-permute-start(f32[1,14,704]{2,0,1:T(1,128)S(1)} %broadcast_in_dim.16), channel_id=1, source_target_pairs={{0,4},{4,0},{8,12},{12,8},{1,5},{5,1},{9,13},{13,9},{2,6},{6,2},{1... | collective-permute-start | bytes 118280 | tf_op jit(solution)/shard_map/ppermute | solution.py:240
  40.1 1.3 %fusion.22 = (f32[14,64,2]{2,1,0:T(8,128)S(1)}, f32[14,64,2]{2,1,0:T(8,128)S(1)}) fusion(f32[14,64,128]{2,1,0:T(8,128)} %get-tuple-element.13.f_ref), kind=kLoop, calls=%fused_computation.78 | loop fusion | bytes 28672 | tf_op jit(solution)/shard_map/slice | solution.py:255
  42.4 3.3 %collective-permute-start.7 = (f32[2,14,704]{2,0,1:T(2,128)S(1)}, f32[2,14,704]{2,0,1:T(2,128)S(1)}, u32[]{:S(2)}, u32[]{:S(2)}) collective-permute-start(f32[2,14,704]{2,0,1:T(2,128)S(1)} %maximum_select_fusion.7), channel_id=1, source_target_pairs={{0,8},{4,12},{8,0},{12,4},{1,9},{5,13},{9,1},{13,5},{2,10},{6,14},... | collective-permute-start | bytes 236552 | tf_op jit(solution)/shard_map/ppermute | solution.py:240
  45.8 2.4 %collective-permute-done.7 = f32[2,14,704]{2,0,1:T(2,128)S(1)} collective-permute-done((f32[2,14,704]{2,0,1:T(2,128)S(1)}, f32[2,14,704]{2,0,1:T(2,128)S(1)}, u32[]{:S(2)}, u32[]{:S(2)}) %collective-permute-start.7) | collective-permute-done | bytes 78880 | tf_op jit(solution)/shard_map/ppermute | solution.py:240
  48.5 1.2 %collective-permute-done.8 = f32[1,14,1024]{2,1,0:T(8,128)S(1)} collective-permute-done((f32[1,14,1024]{2,1,0:T(8,128)S(1)}, f32[1,14,1024]{2,1,0:T(8,128)S(1)}, u32[]{:S(2)}, u32[]{:S(2)}) %collective-permute-start.8) | collective-permute-done | bytes 57376 | tf_op jit(solution)/shard_map/ppermute | solution.py:240
  49.8 1.5 %collective-permute-start.9 = (f32[2,14,1024]{2,1,0:T(8,128)S(1)}, f32[2,14,1024]{2,1,0:T(8,128)S(1)}, u32[]{:S(2)}, u32[]{:S(2)}) collective-permute-start(f32[2,14,1024]{2,1,0:T(8,128)S(1)} %maximum_select_fusion.5), channel_id=1, source_target_pairs={{0,2},{1,3},{2,0},{3,1},{4,6},{5,7},{6,4},{7,5},{8,10},{9,11},{10,... | collective-permute-start | bytes 344072 | tf_op jit(solution)/shard_map/ppermute | solution.py:240
  51.6 3.8 %collective-permute-done.9 = f32[2,14,1024]{2,1,0:T(8,128)S(1)} collective-permute-done((f32[2,14,1024]{2,1,0:T(8,128)S(1)}, f32[2,14,1024]{2,1,0:T(8,128)S(1)}, u32[]{:S(2)}, u32[]{:S(2)}) %collective-permute-start.9) | collective-permute-done | bytes 114720 | tf_op jit(solution)/shard_map/ppermute | solution.py:240
  56.5 1.0 %fusion = f32[42,384]{1,0:T(8,128)S(1)} fusion(s32[384]{0:T(512)S(1)} %pad_add_fusion, bf16[14,3072]{1,0:T(8,128)(2,1)S(1)} %get-tuple-element.24, bf16[14,3072]{1,0:T(8,128)(2,1)S(1)} %get-tuple-element.25, bf16[14,3072]{1,0:T(8,128)(2,1)S(1)} %get-tuple-element.23), kind=kOutput, calls=%fused_computation.1 | convolution fusion | flops 101044224 | bytes 324096 | tf_op jit(solution)/shard_map/dot_general | solution.py:230
  58.6 3.5 %shard_map.57 = f32[14,64,128]{2,1,0:T(8,128)} custom-call(f32[14,64,128]{2,1,0:T(8,128)} %get-tuple-element.13.f_ref, f32[14,8,128]{2,1,0:T(8,128)} %pad_maximum_fusion.1.halo_ref, f32[14,64,128]{2,1,0:T(8,128)} %bitcast.70, f32[128,192]{1,0:T(8,128)} %get-tuple-element.11.lon_ref, f32[64,192]{1,0:T(8,128)} %get-tuple-element.12.lat_ref, ...), custom_call_target="tpu_custom_call" | custom-call | tf_op jit(solution)/shard_map/pallas_call | solution.py:119
  (98 shorter events, 9.2 us)
Async XLA Ops:
  0.0 6.9 %copy-start = (f32[1,7,2,64,128]{4,3,2,1,0:T(8,128)S(1)}, f32[1,7,2,64,128]{4,3,2,1,0:T(8,128)}, u32[]{:S(2)}) copy-start(f32[1,7,2,64,128]{4,3,2,1,0:T(8,128)} %param.5) | copy-start | bytes 1376260
  4.0 4.9 %collective-permute-start = (f32[14,192]{1,0:T(8,128)}, f32[14,192]{1,0:T(8,128)S(1)}, u32[]{:S(2)}, u32[]{:S(2)}) collective-permute-start(f32[14,192]{1,0:T(8,128)} %get-tuple-element.10), channel_id=1, source_target_pairs={{0,16},{16,0},{1,17},{17,1},{2,18},{18,2},{3,19},{19,3},{4,20},{20... | collective-permute-start | bytes 32264 | tf_op jit(solution)/shard_map/ppermute | solution.py:248
  6.9 0.7 %copy-start.3 = (s32[1,1,1,768]{3,2,1,0:T(1,128)S(1)}, s32[1,1,1,768]{3,2,1,0:T(1,128)}, u32[]{:S(2)}) copy-start(s32[1,1,1,768]{3,2,1,0:T(1,128)} %param.6) | copy-start | bytes 9220
  9.0 4.1 %collective-permute-start.1 = (f32[1,14,704]{2,0,1:T(1,128)S(1)}, f32[1,14,704]{2,0,1:T(1,128)S(1)}, u32[]{:S(2)}, u32[]{:S(2)}) collective-permute-start(f32[1,14,704]{2,0,1:T(1,128)S(1)} %broadcast_in_dim.14), channel_id=1, source_target_pairs={{0,4},{4,0},{8,12},{12,8},{1,5},{5,1},{9,13},{13,9},{2,6},{6,2},{1... | collective-permute-start | bytes 118280 | tf_op jit(solution)/shard_map/ppermute | solution.py:240
  13.3 5.6 %collective-permute-start.2 = (f32[2,14,704]{2,0,1:T(2,128)S(1)}, f32[2,14,704]{2,0,1:T(2,128)S(1)}, u32[]{:S(2)}, u32[]{:S(2)}) collective-permute-start(f32[2,14,704]{2,0,1:T(2,128)S(1)} %maximum_select_fusion.6), channel_id=1, source_target_pairs={{0,8},{4,12},{8,0},{12,4},{1,9},{5,13},{9,1},{13,5},{2,10},{6,14},... | collective-permute-start | bytes 236552 | tf_op jit(solution)/shard_map/ppermute | solution.py:240
  19.1 1.3 %collective-permute-start.3 = (f32[1,14,1024]{2,1,0:T(8,128)S(1)}, f32[1,14,1024]{2,1,0:T(8,128)S(1)}, u32[]{:S(2)}, u32[]{:S(2)}) collective-permute-start(f32[1,14,1024]{2,1,0:T(8,128)S(1)} %maximum_bitcast_fusion), channel_id=1, source_target_pairs={{0,1},{1,0},{2,3},{3,2},{4,5},{5,4},{6,7},{7,6},{8,9},{9,8},{10,11... | collective-permute-start | bytes 172040 | tf_op jit(solution)/shard_map/ppermute | solution.py:240
  20.4 5.7 %collective-permute-start.4 = (f32[2,14,1024]{2,1,0:T(8,128)S(1)}, f32[2,14,1024]{2,1,0:T(8,128)S(1)}, u32[]{:S(2)}, u32[]{:S(2)}) collective-permute-start(f32[2,14,1024]{2,1,0:T(8,128)S(1)} %maximum_select_fusion.4), channel_id=1, source_target_pairs={{0,2},{1,3},{2,0},{3,1},{4,6},{5,7},{6,4},{7,5},{8,10},{9,11},{10,... | collective-permute-start | bytes 344072 | tf_op jit(solution)/shard_map/ppermute | solution.py:240
  26.2 0.7 %copy-start.2 = (f32[4,14,1024]{2,1,0:T(8,128)}, f32[4,14,1024]{2,1,0:T(8,128)S(1)}, u32[]{:S(2)}) copy-start(f32[4,14,1024]{2,1,0:T(8,128)S(1)} %maximum_select_fusion) | copy-start | bytes 688132
  27.2 1.2 %slice-start.1 = ((f32[4,14,1024]{2,1,0:T(8,128)}), f32[4,14,256]{2,1,0:T(8,128)S(1)}, s32[]{:S(2)}) async-start(f32[4,14,1024]{2,1,0:T(8,128)} %copy-done.2), calls=%async_computation.1 | async-start | bytes 131072 | tf_op jit(solution)/shard_map/slice | solution.py:262
  34.1 4.0 %collective-permute-start.5 = (f32[14,192]{1,0:T(8,128)}, f32[14,192]{1,0:T(8,128)S(1)}, u32[]{:S(2)}, u32[]{:S(2)}) collective-permute-start(f32[14,192]{1,0:T(8,128)} %get-tuple-element.14), channel_id=1, source_target_pairs={{0,16},{16,0},{1,17},{17,1},{2,18},{18,2},{3,19},{19,3},{4,20},{20... | collective-permute-start | bytes 32264 | tf_op jit(solution)/shard_map/ppermute | solution.py:248
  38.2 4.1 %collective-permute-start.6 = (f32[1,14,704]{2,0,1:T(1,128)S(1)}, f32[1,14,704]{2,0,1:T(1,128)S(1)}, u32[]{:S(2)}, u32[]{:S(2)}) collective-permute-start(f32[1,14,704]{2,0,1:T(1,128)S(1)} %broadcast_in_dim.16), channel_id=1, source_target_pairs={{0,4},{4,0},{8,12},{12,8},{1,5},{5,1},{9,13},{13,9},{2,6},{6,2},{1... | collective-permute-start | bytes 118280 | tf_op jit(solution)/shard_map/ppermute | solution.py:240
  42.4 5.7 %collective-permute-start.7 = (f32[2,14,704]{2,0,1:T(2,128)S(1)}, f32[2,14,704]{2,0,1:T(2,128)S(1)}, u32[]{:S(2)}, u32[]{:S(2)}) collective-permute-start(f32[2,14,704]{2,0,1:T(2,128)S(1)} %maximum_select_fusion.7), channel_id=1, source_target_pairs={{0,8},{4,12},{8,0},{12,4},{1,9},{5,13},{9,1},{13,5},{2,10},{6,14},... | collective-permute-start | bytes 236552 | tf_op jit(solution)/shard_map/ppermute | solution.py:240
  48.4 1.3 %collective-permute-start.8 = (f32[1,14,1024]{2,1,0:T(8,128)S(1)}, f32[1,14,1024]{2,1,0:T(8,128)S(1)}, u32[]{:S(2)}, u32[]{:S(2)}) collective-permute-start(f32[1,14,1024]{2,1,0:T(8,128)S(1)} %maximum_bitcast_fusion.1), channel_id=1, source_target_pairs={{0,1},{1,0},{2,3},{3,2},{4,5},{5,4},{6,7},{7,6},{8,9},{9,8},{10,11... | collective-permute-start | bytes 172040 | tf_op jit(solution)/shard_map/ppermute | solution.py:240
  49.8 5.6 %collective-permute-start.9 = (f32[2,14,1024]{2,1,0:T(8,128)S(1)}, f32[2,14,1024]{2,1,0:T(8,128)S(1)}, u32[]{:S(2)}, u32[]{:S(2)}) collective-permute-start(f32[2,14,1024]{2,1,0:T(8,128)S(1)} %maximum_select_fusion.5), channel_id=1, source_target_pairs={{0,2},{1,3},{2,0},{3,1},{4,6},{5,7},{6,4},{7,5},{8,10},{9,11},{10,... | collective-permute-start | bytes 344072 | tf_op jit(solution)/shard_map/ppermute | solution.py:240
  55.4 0.7 %copy-start.1 = (f32[4,14,1024]{2,1,0:T(8,128)}, f32[4,14,1024]{2,1,0:T(8,128)S(1)}, u32[]{:S(2)}) copy-start(f32[4,14,1024]{2,1,0:T(8,128)S(1)} %maximum_select_fusion.1) | copy-start | bytes 688132
  56.5 1.2 %slice-start = ((f32[4,14,1024]{2,1,0:T(8,128)}), f32[4,14,256]{2,1,0:T(8,128)S(1)}, s32[]{:S(2)}) async-start(f32[4,14,1024]{2,1,0:T(8,128)} %copy-done.1), calls=%async_computation | async-start | bytes 131072 | tf_op jit(solution)/shard_map/slice | solution.py:262

commit v15 on v14

--- a/solution.py
+++ b/solution.py
@@ -17,7 +17,11 @@
 HIGHEST = lax.Precision.HIGHEST
 
 
-def stencil_kernel(f_ref, halo_ref, base_ref, lon_ref, lat_ref, turn_ref, o_ref, *rest, first):
+def stencil_kernel(*refs, first):
+    if first:
+        f_ref, halo_ref, lon_ref, lat_ref, turn_ref, o_ref, don_ref = refs
+    else:
+        f_ref, halo_ref, base_ref, o_ref = refs
     planes, height, width = f_ref.shape
     comps = planes // 2
     row = lax.broadcasted_iota(jnp.int32, (height, width), 0)
@@ -109,7 +113,7 @@
         store(6, x6, -adv_u_6 + diffusivity * lap_of(6, x6, lap_6))
 
     if first:
-        donate_planes(lambda k: o_ref[k], planes, lon_ref[...], lat_ref[...], turn_ref, rest[0])
+        donate_planes(lambda k: o_ref[k], planes, lon_ref[...], lat_ref[...], turn_ref, don_ref)
 
 
 def advance(field, halo, base, lon, lat, turn, first):
@@ -120,7 +124,7 @@
         functools.partial(stencil_kernel, first=first),
         out_shape=shape,
         interpret=INTERPRET,
-    )(field, halo, base, lon, lat, turn)
+    )(*((field, halo, lon, lat, turn) if first else (field, halo, base)))
 
 
 def donation_weights(cells_ref, frac_ref, rows, cols):

time: 62.4 us -> 62.1 us (level)
  no operation moved by 1% of the time
where the time goes in v15:
time: 62.1 us; the launch traced here: 61.9 us
  waiting for transfers between devices  19.9 us (32%)
  starting transfers between devices  18.8 us (30%)
  Pallas kernels  9.75 us (16%)
  local copies, waits for them, and re-layouts  7.87 us (13%)
  other arithmetic  3 us (5%)
  matrix products  1.98 us (3%)
    ppermute x8, waiting for transfers between devices, gather(): other = lax.ppermute(held, axis, [(i, i ^ k) for i in range(size)])  16.6 us
    ppermute x8, starting transfers between devices, gather(): other = lax.ppermute(held, axis, [(i, i ^ k) for i in range(size)])  14 us
    pallas_call x2, Pallas kernels, advance(): pl.pallas_call(functools.partial(stencil_kernel, first=first), out_shape=...  7.18 us
    ppermute x2, starting transfers between devices, section(): given = lax.ppermute(donation, 'panel', [(0, 1), (1, 0)])  4.81 us
    ppermute x2, waiting for transfers between devices, section(): given = lax.ppermute(donation, 'panel', [(0, 1), (1, 0)])  3.31 us
    pallas_call x1, Pallas kernels, first_donation(): pl.pallas_call(donation_kernel, out_shape=(jax.ShapeDtypeStruct((planes,...  2.57 us
    slice x6, local copies, waits for them, and re-layouts, section(): side_cols = jnp.concatenate([flat[:, :, :2], flat[:, :, cols - 2:]], axis=2)  2.33 us
    dot_general x2, matrix products, select(): picked = jnp.dot(parts, pick, preferred_element_type=jnp.float32)  1.98 us
  transfers between devices with their start and end apart: 10, of which 10 were waited for; matrix products, arithmetic and copies ran while one was open for 5% of the time, Pallas kernels for 0%

profile of v15, /device:TPU:0, one launch (start us, length us, event | category | flops | bytes accessed | tf_op | source)
XLA Modules:
  0.0 61.9 jit_solution(10953558201938753750)
XLA Ops:
  1.4 2.6 %shard_map.55 = (f32[14,192]{1,0:T(8,128)}, f32[128,192]{1,0:T(8,128)}, f32[64,192]{1,0:T(8,128)}) custom-call(f32[14,64,128]{2,1,0:T(8,128)} %bitcast.67, s32[1,192]{1,0:T(1,128)} %bitcast.88, f32[2,192]{1,0:T(2,128)} %bitcast.87, f32[2,192]{1,0:T(2,128)} %pad_maximum_fusion.6.turn_ref.refs_4_), custom_call_target="tpu_custom_call" | custom-call | tf_op jit(solution)/shard_map/pallas_call | solution.py:175
  4.0 3.0 %collective-permute-start = (f32[14,192]{1,0:T(8,128)}, f32[14,192]{1,0:T(8,128)S(1)}, u32[]{:S(2)}, u32[]{:S(2)}) collective-permute-start(f32[14,192]{1,0:T(8,128)} %get-tuple-element.10), channel_id=1, source_target_pairs={{0,16},{16,0},{1,17},{17,1},{2,18},{18,2},{3,19},{19,3},{4,20},{20... | collective-permute-start | bytes 32264 | tf_op jit(solution)/shard_map/ppermute | solution.py:252
  7.7 1.2 %collective-permute-done = f32[14,192]{1,0:T(8,128)S(1)} collective-permute-done((f32[14,192]{1,0:T(8,128)}, f32[14,192]{1,0:T(8,128)S(1)}, u32[]{:S(2)}, u32[]{:S(2)}) %collective-permute-start) | collective-permute-done | bytes 10784 | tf_op jit(solution)/shard_map/ppermute | solution.py:252
  9.0 2.2 %collective-permute-start.1 = (f32[1,14,704]{2,0,1:T(1,128)S(1)}, f32[1,14,704]{2,0,1:T(1,128)S(1)}, u32[]{:S(2)}, u32[]{:S(2)}) collective-permute-start(f32[1,14,704]{2,0,1:T(1,128)S(1)} %broadcast_in_dim.14), channel_id=1, source_target_pairs={{0,4},{4,0},{8,12},{12,8},{1,5},{5,1},{9,13},{13,9},{2,6},{6,2},{1... | collective-permute-start | bytes 118280 | tf_op jit(solution)/shard_map/ppermute | solution.py:244
  11.5 1.6 %collective-permute-done.1 = f32[1,14,704]{2,0,1:T(1,128)S(1)} collective-permute-done((f32[1,14,704]{2,0,1:T(1,128)S(1)}, f32[1,14,704]{2,0,1:T(1,128)S(1)}, u32[]{:S(2)}, u32[]{:S(2)}) %collective-permute-start.1) | collective-permute-done | bytes 39456 | tf_op jit(solution)/shard_map/ppermute | solution.py:244
  13.3 3.1 %collective-permute-start.2 = (f32[2,14,704]{2,0,1:T(2,128)S(1)}, f32[2,14,704]{2,0,1:T(2,128)S(1)}, u32[]{:S(2)}, u32[]{:S(2)}) collective-permute-start(f32[2,14,704]{2,0,1:T(2,128)S(1)} %maximum_select_fusion.6), channel_id=1, source_target_pairs={{0,8},{4,12},{8,0},{12,4},{1,9},{5,13},{9,1},{13,5},{2,10},{6,14},... | collective-permute-start | bytes 236552 | tf_op jit(solution)/shard_map/ppermute | solution.py:244
  16.5 2.4 %collective-permute-done.2 = f32[2,14,704]{2,0,1:T(2,128)S(1)} collective-permute-done((f32[2,14,704]{2,0,1:T(2,128)S(1)}, f32[2,14,704]{2,0,1:T(2,128)S(1)}, u32[]{:S(2)}, u32[]{:S(2)}) %collective-permute-start.2) | collective-permute-done | bytes 78880 | tf_op jit(solution)/shard_map/ppermute | solution.py:244
  19.2 1.2 %collective-permute-done.3 = f32[1,14,1024]{2,1,0:T(8,128)S(1)} collective-permute-done((f32[1,14,1024]{2,1,0:T(8,128)S(1)}, f32[1,14,1024]{2,1,0:T(8,128)S(1)}, u32[]{:S(2)}, u32[]{:S(2)}) %collective-permute-start.3) | collective-permute-done | bytes 57376 | tf_op jit(solution)/shard_map/ppermute | solution.py:244
  20.4 1.9 %collective-permute-start.4 = (f32[2,14,1024]{2,1,0:T(8,128)S(1)}, f32[2,14,1024]{2,1,0:T(8,128)S(1)}, u32[]{:S(2)}, u32[]{:S(2)}) collective-permute-start(f32[2,14,1024]{2,1,0:T(8,128)S(1)} %maximum_select_fusion.4), channel_id=1, source_target_pairs={{0,2},{1,3},{2,0},{3,1},{4,6},{5,7},{6,4},{7,5},{8,10},{9,11},{10,... | collective-permute-start | bytes 344072 | tf_op jit(solution)/shard_map/ppermute | solution.py:244
  22.5 3.6 %collective-permute-done.4 = f32[2,14,1024]{2,1,0:T(8,128)S(1)} collective-permute-done((f32[2,14,1024]{2,1,0:T(8,128)S(1)}, f32[2,14,1024]{2,1,0:T(8,128)S(1)}, u32[]{:S(2)}, u32[]{:S(2)}) %collective-permute-start.4) | collective-permute-done | bytes 114720 | tf_op jit(solution)/shard_map/ppermute | solution.py:244
  27.2 1.0 %fusion.1 = f32[42,384]{1,0:T(8,128)S(1)} fusion(s32[384]{0:T(512)S(1)} %pad_add_fusion, bf16[14,3072]{1,0:T(8,128)(2,1)S(1)} %get-tuple-element.27, bf16[14,3072]{1,0:T(8,128)(2,1)S(1)} %get-tuple-element.28, bf16[14,3072]{1,0:T(8,128)(2,1)S(1)} %get-tuple-element.26), kind=kOutput, calls=%fused_computation.2 | convolution fusion | flops 101044224 | bytes 324096 | tf_op jit(solution)/shard_map/dot_general | solution.py:234
  29.3 3.8 %shard_map.56 = (f32[14,64,128]{2,1,0:T(8,128)}, f32[14,192]{1,0:T(8,128)}) custom-call(f32[14,64,128]{2,1,0:T(8,128)} %bitcast.68, f32[14,8,128]{2,1,0:T(8,128)} %pad_maximum_fusion.refs_1_, f32[128,192]{1,0:T(8,128)} %get-tuple-element.11.refs_2_, f32[64,192]{1,0:T(8,128)} %get-tuple-element.12.refs_3_, f32[2,192]{1,0:T(2,128)} %pad_maximum_fusion.6.turn_ref.refs_4_), custom_call_target="tpu_custom_call" | custom-call | tf_op jit(solution)/shard_map/pallas_call | solution.py:123
  33.1 0.9 %fusion.21 = (f32[14,2,128]{2,1,0:T(2,128)S(1)}, f32[14,2,128]{2,1,0:T(2,128)S(1)}) fusion(f32[14,64,128]{2,1,0:T(8,128)} %get-tuple-element.13.refs_0_), kind=kLoop, calls=%fused_computation.77 | loop fusion | bytes 57344 | tf_op jit(solution)/shard_map/slice | solution.py:254
  33.9 1.8 %collective-permute-start.5 = (f32[14,192]{1,0:T(8,128)}, f32[14,192]{1,0:T(8,128)S(1)}, u32[]{:S(2)}, u32[]{:S(2)}) collective-permute-start(f32[14,192]{1,0:T(8,128)} %get-tuple-element.14), channel_id=1, source_target_pairs={{0,16},{16,0},{1,17},{17,1},{2,18},{18,2},{3,19},{19,3},{4,20},{20... | collective-permute-start | bytes 32264 | tf_op jit(solution)/shard_map/ppermute | solution.py:252
  35.8 2.1 %collective-permute-done.5 = f32[14,192]{1,0:T(8,128)S(1)} collective-permute-done((f32[14,192]{1,0:T(8,128)}, f32[14,192]{1,0:T(8,128)S(1)}, u32[]{:S(2)}, u32[]{:S(2)}) %collective-permute-start.5) | collective-permute-done | bytes 10784 | tf_op jit(solution)/shard_map/ppermute | solution.py:252
  38.1 1.9 %collective-permute-start.6 = (f32[1,14,704]{2,0,1:T(1,128)S(1)}, f32[1,14,704]{2,0,1:T(1,128)S(1)}, u32[]{:S(2)}, u32[]{:S(2)}) collective-permute-start(f32[1,14,704]{2,0,1:T(1,128)S(1)} %broadcast_in_dim.16), channel_id=1, source_target_pairs={{0,4},{4,0},{8,12},{12,8},{1,5},{5,1},{9,13},{13,9},{2,6},{6,2},{1... | collective-permute-start | bytes 118280 | tf_op jit(solution)/shard_map/ppermute | solution.py:244
  40.0 1.3 %fusion.22 = (f32[14,64,2]{2,1,0:T(8,128)S(1)}, f32[14,64,2]{2,1,0:T(8,128)S(1)}) fusion(f32[14,64,128]{2,1,0:T(8,128)} %get-tuple-element.13.refs_0_), kind=kLoop, calls=%fused_computation.78 | loop fusion | bytes 28672 | tf_op jit(solution)/shard_map/slice | solution.py:259
  42.3 3.3 %collective-permute-start.7 = (f32[2,14,704]{2,0,1:T(2,128)S(1)}, f32[2,14,704]{2,0,1:T(2,128)S(1)}, u32[]{:S(2)}, u32[]{:S(2)}) collective-permute-start(f32[2,14,704]{2,0,1:T(2,128)S(1)} %maximum_select_fusion.7), channel_id=1, source_target_pairs={{0,8},{4,12},{8,0},{12,4},{1,9},{5,13},{9,1},{13,5},{2,10},{6,14},... | collective-permute-start | bytes 236552 | tf_op jit(solution)/shard_map/ppermute | solution.py:244
  45.7 2.4 %collective-permute-done.7 = f32[2,14,704]{2,0,1:T(2,128)S(1)} collective-permute-done((f32[2,14,704]{2,0,1:T(2,128)S(1)}, f32[2,14,704]{2,0,1:T(2,128)S(1)}, u32[]{:S(2)}, u32[]{:S(2)}) %collective-permute-start.7) | collective-permute-done | bytes 78880 | tf_op jit(solution)/shard_map/ppermute | solution.py:244
  48.4 1.2 %collective-permute-done.8 = f32[1,14,1024]{2,1,0:T(8,128)S(1)} collective-permute-done((f32[1,14,1024]{2,1,0:T(8,128)S(1)}, f32[1,14,1024]{2,1,0:T(8,128)S(1)}, u32[]{:S(2)}, u32[]{:S(2)}) %collective-permute-start.8) | collective-permute-done | bytes 57376 | tf_op jit(solution)/shard_map/ppermute | solution.py:244
  49.6 1.6 %collective-permute-start.9 = (f32[2,14,1024]{2,1,0:T(8,128)S(1)}, f32[2,14,1024]{2,1,0:T(8,128)S(1)}, u32[]{:S(2)}, u32[]{:S(2)}) collective-permute-start(f32[2,14,1024]{2,1,0:T(8,128)S(1)} %maximum_select_fusion.5), channel_id=1, source_target_pairs={{0,2},{1,3},{2,0},{3,1},{4,6},{5,7},{6,4},{7,5},{8,10},{9,11},{10,... | collective-permute-start | bytes 344072 | tf_op jit(solution)/shard_map/ppermute | solution.py:244
  51.4 3.8 %collective-permute-done.9 = f32[2,14,1024]{2,1,0:T(8,128)S(1)} collective-permute-done((f32[2,14,1024]{2,1,0:T(8,128)S(1)}, f32[2,14,1024]{2,1,0:T(8,128)S(1)}, u32[]{:S(2)}, u32[]{:S(2)}) %collective-permute-start.9) | collective-permute-done | bytes 114720 | tf_op jit(solution)/shard_map/ppermute | solution.py:244
  56.3 1.0 %fusion = f32[42,384]{1,0:T(8,128)S(1)} fusion(s32[384]{0:T(512)S(1)} %pad_add_fusion, bf16[14,3072]{1,0:T(8,128)(2,1)S(1)} %get-tuple-element.24, bf16[14,3072]{1,0:T(8,128)(2,1)S(1)} %get-tuple-element.25, bf16[14,3072]{1,0:T(8,128)(2,1)S(1)} %get-tuple-element.23), kind=kOutput, calls=%fused_computation.1 | convolution fusion | flops 101044224 | bytes 324096 | tf_op jit(solution)/shard_map/dot_general | solution.py:234
  58.4 3.4 %shard_map.57 = f32[14,64,128]{2,1,0:T(8,128)} custom-call(f32[14,64,128]{2,1,0:T(8,128)} %get-tuple-element.13.refs_0_, f32[14,8,128]{2,1,0:T(8,128)} %pad_maximum_fusion.1.refs_1_, f32[14,64,128]{2,1,0:T(8,128)} %bitcast.69), custom_call_target="tpu_custom_call" | custom-call | tf_op jit(solution)/shard_map/pallas_call | solution.py:123
  (98 shorter events, 9.2 us)
Async XLA Ops:
  0.0 6.9 %copy-start = (f32[1,7,2,64,128]{4,3,2,1,0:T(8,128)S(1)}, f32[1,7,2,64,128]{4,3,2,1,0:T(8,128)}, u32[]{:S(2)}) copy-start(f32[1,7,2,64,128]{4,3,2,1,0:T(8,128)} %param.5) | copy-start | bytes 1376260
  4.0 4.9 %collective-permute-start = (f32[14,192]{1,0:T(8,128)}, f32[14,192]{1,0:T(8,128)S(1)}, u32[]{:S(2)}, u32[]{:S(2)}) collective-permute-start(f32[14,192]{1,0:T(8,128)} %get-tuple-element.10), channel_id=1, source_target_pairs={{0,16},{16,0},{1,17},{17,1},{2,18},{18,2},{3,19},{19,3},{4,20},{20... | collective-permute-start | bytes 32264 | tf_op jit(solution)/shard_map/ppermute | solution.py:252
  6.9 0.7 %copy-start.3 = (s32[1,1,1,768]{3,2,1,0:T(1,128)S(1)}, s32[1,1,1,768]{3,2,1,0:T(1,128)}, u32[]{:S(2)}) copy-start(s32[1,1,1,768]{3,2,1,0:T(1,128)} %param.6) | copy-start | bytes 9220
  9.0 4.2 %collective-permute-start.1 = (f32[1,14,704]{2,0,1:T(1,128)S(1)}, f32[1,14,704]{2,0,1:T(1,128)S(1)}, u32[]{:S(2)}, u32[]{:S(2)}) collective-permute-start(f32[1,14,704]{2,0,1:T(1,128)S(1)} %broadcast_in_dim.14), channel_id=1, source_target_pairs={{0,4},{4,0},{8,12},{12,8},{1,5},{5,1},{9,13},{13,9},{2,6},{6,2},{1... | collective-permute-start | bytes 118280 | tf_op jit(solution)/shard_map/ppermute | solution.py:244
  13.3 5.6 %collective-permute-start.2 = (f32[2,14,704]{2,0,1:T(2,128)S(1)}, f32[2,14,704]{2,0,1:T(2,128)S(1)}, u32[]{:S(2)}, u32[]{:S(2)}) collective-permute-start(f32[2,14,704]{2,0,1:T(2,128)S(1)} %maximum_select_fusion.6), channel_id=1, source_target_pairs={{0,8},{4,12},{8,0},{12,4},{1,9},{5,13},{9,1},{13,5},{2,10},{6,14},... | collective-permute-start | bytes 236552 | tf_op jit(solution)/shard_map/ppermute | solution.py:244
  19.1 1.3 %collective-permute-start.3 = (f32[1,14,1024]{2,1,0:T(8,128)S(1)}, f32[1,14,1024]{2,1,0:T(8,128)S(1)}, u32[]{:S(2)}, u32[]{:S(2)}) collective-permute-start(f32[1,14,1024]{2,1,0:T(8,128)S(1)} %maximum_bitcast_fusion), channel_id=1, source_target_pairs={{0,1},{1,0},{2,3},{3,2},{4,5},{5,4},{6,7},{7,6},{8,9},{9,8},{10,11... | collective-permute-start | bytes 172040 | tf_op jit(solution)/shard_map/ppermute | solution.py:244
  20.4 5.7 %collective-permute-start.4 = (f32[2,14,1024]{2,1,0:T(8,128)S(1)}, f32[2,14,1024]{2,1,0:T(8,128)S(1)}, u32[]{:S(2)}, u32[]{:S(2)}) collective-permute-start(f32[2,14,1024]{2,1,0:T(8,128)S(1)} %maximum_select_fusion.4), channel_id=1, source_target_pairs={{0,2},{1,3},{2,0},{3,1},{4,6},{5,7},{6,4},{7,5},{8,10},{9,11},{10,... | collective-permute-start | bytes 344072 | tf_op jit(solution)/shard_map/ppermute | solution.py:244
  26.1 0.7 %copy-start.2 = (f32[4,14,1024]{2,1,0:T(8,128)}, f32[4,14,1024]{2,1,0:T(8,128)S(1)}, u32[]{:S(2)}) copy-start(f32[4,14,1024]{2,1,0:T(8,128)S(1)} %maximum_select_fusion) | copy-start | bytes 688132
  27.2 1.2 %slice-start.1 = ((f32[4,14,1024]{2,1,0:T(8,128)}), f32[4,14,256]{2,1,0:T(8,128)S(1)}, s32[]{:S(2)}) async-start(f32[4,14,1024]{2,1,0:T(8,128)} %copy-done.2), calls=%async_computation.1 | async-start | bytes 131072 | tf_op jit(solution)/shard_map/slice | solution.py:266
  33.9 4.0 %collective-permute-start.5 = (f32[14,192]{1,0:T(8,128)}, f32[14,192]{1,0:T(8,128)S(1)}, u32[]{:S(2)}, u32[]{:S(2)}) collective-permute-start(f32[14,192]{1,0:T(8,128)} %get-tuple-element.14), channel_id=1, source_target_pairs={{0,16},{16,0},{1,17},{17,1},{2,18},{18,2},{3,19},{19,3},{4,20},{20... | collective-permute-start | bytes 32264 | tf_op jit(solution)/shard_map/ppermute | solution.py:252
  38.1 4.1 %collective-permute-start.6 = (f32[1,14,704]{2,0,1:T(1,128)S(1)}, f32[1,14,704]{2,0,1:T(1,128)S(1)}, u32[]{:S(2)}, u32[]{:S(2)}) collective-permute-start(f32[1,14,704]{2,0,1:T(1,128)S(1)} %broadcast_in_dim.16), channel_id=1, source_target_pairs={{0,4},{4,0},{8,12},{12,8},{1,5},{5,1},{9,13},{13,9},{2,6},{6,2},{1... | collective-permute-start | bytes 118280 | tf_op jit(solution)/shard_map/ppermute | solution.py:244
  42.3 5.8 %collective-permute-start.7 = (f32[2,14,704]{2,0,1:T(2,128)S(1)}, f32[2,14,704]{2,0,1:T(2,128)S(1)}, u32[]{:S(2)}, u32[]{:S(2)}) collective-permute-start(f32[2,14,704]{2,0,1:T(2,128)S(1)} %maximum_select_fusion.7), channel_id=1, source_target_pairs={{0,8},{4,12},{8,0},{12,4},{1,9},{5,13},{9,1},{13,5},{2,10},{6,14},... | collective-permute-start | bytes 236552 | tf_op jit(solution)/shard_map/ppermute | solution.py:244
  48.3 1.3 %collective-permute-start.8 = (f32[1,14,1024]{2,1,0:T(8,128)S(1)}, f32[1,14,1024]{2,1,0:T(8,128)S(1)}, u32[]{:S(2)}, u32[]{:S(2)}) collective-permute-start(f32[1,14,1024]{2,1,0:T(8,128)S(1)} %maximum_bitcast_fusion.1), channel_id=1, source_target_pairs={{0,1},{1,0},{2,3},{3,2},{4,5},{5,4},{6,7},{7,6},{8,9},{9,8},{10,11... | collective-permute-start | bytes 172040 | tf_op jit(solution)/shard_map/ppermute | solution.py:244
  49.6 5.6 %collective-permute-start.9 = (f32[2,14,1024]{2,1,0:T(8,128)S(1)}, f32[2,14,1024]{2,1,0:T(8,128)S(1)}, u32[]{:S(2)}, u32[]{:S(2)}) collective-permute-start(f32[2,14,1024]{2,1,0:T(8,128)S(1)} %maximum_select_fusion.5), channel_id=1, source_target_pairs={{0,2},{1,3},{2,0},{3,1},{4,6},{5,7},{6,4},{7,5},{8,10},{9,11},{10,... | collective-permute-start | bytes 344072 | tf_op jit(solution)/shard_map/ppermute | solution.py:244
  55.3 0.7 %copy-start.1 = (f32[4,14,1024]{2,1,0:T(8,128)}, f32[4,14,1024]{2,1,0:T(8,128)S(1)}, u32[]{:S(2)}) copy-start(f32[4,14,1024]{2,1,0:T(8,128)S(1)} %maximum_select_fusion.1) | copy-start | bytes 688132
  56.3 1.2 %slice-start = ((f32[4,14,1024]{2,1,0:T(8,128)}), f32[4,14,256]{2,1,0:T(8,128)S(1)}, s32[]{:S(2)}) async-start(f32[4,14,1024]{2,1,0:T(8,128)} %copy-done.1), calls=%async_computation | async-start | bytes 131072 | tf_op jit(solution)/shard_map/slice | solution.py:266

commit v16 on v15

--- a/solution.py
+++ b/solution.py
@@ -113,7 +113,7 @@
         store(6, x6, -adv_u_6 + diffusivity * lap_of(6, x6, lap_6))
 
     if first:
-        donate_planes(lambda k: o_ref[k], planes, lon_ref[...], lat_ref[...], turn_ref, don_ref)
+        donate_planes(o_ref[...], lon_ref[...], lat_ref[...], turn_ref, don_ref)
 
 
 def advance(field, halo, base, lon, lat, turn, first):
@@ -143,13 +143,14 @@
     return weight_lon, weight_lat
 
 
-def donate_planes(plane_of, planes, weight_lon, weight_lat, turn_ref, out_ref):
+def donate_planes(field, weight_lon, weight_lat, turn_ref, out_ref):
+    planes, rows, cols = field.shape
     cosine = turn_ref[0:1, :]
     sine = turn_ref[1:2, :]
+    along = jnp.dot(field.reshape(planes * rows, cols), weight_lon, precision=HIGHEST, preferred_element_type=jnp.float32)
     values = []
     for k in range(planes):
-        along = jnp.dot(plane_of(k), weight_lon, precision=HIGHEST, preferred_element_type=jnp.float32)
-        values.append(jnp.sum(along * weight_lat, axis=0, keepdims=True))
+        values.append(jnp.sum(along[k * rows : (k + 1) * rows] * weight_lat, axis=0, keepdims=True))
     for k in range(planes):
         comp, level = divmod(k, 2)
         if comp in (1, 4):
@@ -166,7 +167,7 @@
     weight_lon, weight_lat = donation_weights(cells_ref, frac_ref, rows, cols)
     lon_ref[...] = weight_lon
     lat_ref[...] = weight_lat
-    donate_planes(lambda k: f_ref[k], planes, weight_lon, weight_lat, turn_ref, out_ref)
+    donate_planes(f_ref[...], weight_lon, weight_lat, turn_ref, out_ref)
 
 
 def first_donation(field, cells, frac, turn):

time: 62.1 us -> 62.3 us (level)
  no operation moved by 1% of the time
where the time goes in v16:
time: 62.3 us; the launch traced here: 62 us
  waiting for transfers between devices  20 us (32%)
  starting transfers between devices  18.8 us (30%)
  Pallas kernels  9.88 us (16%)
  local copies, waits for them, and re-layouts  7.87 us (13%)
  other arithmetic  3 us (5%)
  matrix products  1.98 us (3%)
    ppermute x8, waiting for transfers between devices, gather(): other = lax.ppermute(held, axis, [(i, i ^ k) for i in range(size)])  16.6 us
    ppermute x8, starting transfers between devices, gather(): other = lax.ppermute(held, axis, [(i, i ^ k) for i in range(size)])  14 us
    pallas_call x2, Pallas kernels, advance(): pl.pallas_call(functools.partial(stencil_kernel, first=first), out_shape=...  7.33 us
    ppermute x2, starting transfers between devices, section(): given = lax.ppermute(donation, 'panel', [(0, 1), (1, 0)])  4.8 us
    ppermute x2, waiting for transfers between devices, section(): given = lax.ppermute(donation, 'panel', [(0, 1), (1, 0)])  3.31 us
    pallas_call x1, Pallas kernels, first_donation(): pl.pallas_call(donation_kernel, out_shape=(jax.ShapeDtypeStruct((planes,...  2.55 us
    slice x6, local copies, waits for them, and re-layouts, section(): side_cols = jnp.concatenate([flat[:, :, :2], flat[:, :, cols - 2:]], axis=2)  2.33 us
    dot_general x2, matrix products, select(): picked = jnp.dot(parts, pick, preferred_element_type=jnp.float32)  1.98 us
  transfers between devices with their start and end apart: 10, of which 10 were waited for; matrix products, arithmetic and copies ran while one was open for 5% of the time, Pallas kernels for 0%

profile of v16, /device:TPU:0, one launch (start us, length us, event | category | flops | bytes accessed | tf_op | source)
XLA Modules:
  0.0 62.0 jit_solution(3479873126194465818)
XLA Ops:
  1.4 2.6 %shard_map.55 = (f32[14,192]{1,0:T(8,128)}, f32[128,192]{1,0:T(8,128)}, f32[64,192]{1,0:T(8,128)}) custom-call(f32[14,64,128]{2,1,0:T(8,128)} %bitcast.67, s32[1,192]{1,0:T(1,128)} %bitcast.88, f32[2,192]{1,0:T(2,128)} %bitcast.87, f32[2,192]{1,0:T(2,128)} %pad_maximum_fusion.6.turn_ref.refs_4_), custom_call_target="tpu_custom_call" | custom-call | tf_op jit(solution)/shard_map/pallas_call | solution.py:176
  3.9 3.0 %collective-permute-start = (f32[14,192]{1,0:T(8,128)}, f32[14,192]{1,0:T(8,128)S(1)}, u32[]{:S(2)}, u32[]{:S(2)}) collective-permute-start(f32[14,192]{1,0:T(8,128)} %get-tuple-element.10), channel_id=1, source_target_pairs={{0,16},{16,0},{1,17},{17,1},{2,18},{18,2},{3,19},{19,3},{4,20},{20... | collective-permute-start | bytes 32264 | tf_op jit(solution)/shard_map/ppermute | solution.py:253
  7.7 1.2 %collective-permute-done = f32[14,192]{1,0:T(8,128)S(1)} collective-permute-done((f32[14,192]{1,0:T(8,128)}, f32[14,192]{1,0:T(8,128)S(1)}, u32[]{:S(2)}, u32[]{:S(2)}) %collective-permute-start) | collective-permute-done | bytes 10784 | tf_op jit(solution)/shard_map/ppermute | solution.py:253
  9.0 2.1 %collective-permute-start.1 = (f32[1,14,704]{2,0,1:T(1,128)S(1)}, f32[1,14,704]{2,0,1:T(1,128)S(1)}, u32[]{:S(2)}, u32[]{:S(2)}) collective-permute-start(f32[1,14,704]{2,0,1:T(1,128)S(1)} %broadcast_in_dim.14), channel_id=1, source_target_pairs={{0,4},{4,0},{8,12},{12,8},{1,5},{5,1},{9,13},{13,9},{2,6},{6,2},{1... | collective-permute-start | bytes 118280 | tf_op jit(solution)/shard_map/ppermute | solution.py:245
  11.5 1.6 %collective-permute-done.1 = f32[1,14,704]{2,0,1:T(1,128)S(1)} collective-permute-done((f32[1,14,704]{2,0,1:T(1,128)S(1)}, f32[1,14,704]{2,0,1:T(1,128)S(1)}, u32[]{:S(2)}, u32[]{:S(2)}) %collective-permute-start.1) | collective-permute-done | bytes 39456 | tf_op jit(solution)/shard_map/ppermute | solution.py:245
  13.2 3.1 %collective-permute-start.2 = (f32[2,14,704]{2,0,1:T(2,128)S(1)}, f32[2,14,704]{2,0,1:T(2,128)S(1)}, u32[]{:S(2)}, u32[]{:S(2)}) collective-permute-start(f32[2,14,704]{2,0,1:T(2,128)S(1)} %maximum_select_fusion.6), channel_id=1, source_target_pairs={{0,8},{4,12},{8,0},{12,4},{1,9},{5,13},{9,1},{13,5},{2,10},{6,14},... | collective-permute-start | bytes 236552 | tf_op jit(solution)/shard_map/ppermute | solution.py:245
  16.5 2.4 %collective-permute-done.2 = f32[2,14,704]{2,0,1:T(2,128)S(1)} collective-permute-done((f32[2,14,704]{2,0,1:T(2,128)S(1)}, f32[2,14,704]{2,0,1:T(2,128)S(1)}, u32[]{:S(2)}, u32[]{:S(2)}) %collective-permute-start.2) | collective-permute-done | bytes 78880 | tf_op jit(solution)/shard_map/ppermute | solution.py:245
  19.2 1.2 %collective-permute-done.3 = f32[1,14,1024]{2,1,0:T(8,128)S(1)} collective-permute-done((f32[1,14,1024]{2,1,0:T(8,128)S(1)}, f32[1,14,1024]{2,1,0:T(8,128)S(1)}, u32[]{:S(2)}, u32[]{:S(2)}) %collective-permute-start.3) | collective-permute-done | bytes 57376 | tf_op jit(solution)/shard_map/ppermute | solution.py:245
  20.4 1.9 %collective-permute-start.4 = (f32[2,14,1024]{2,1,0:T(8,128)S(1)}, f32[2,14,1024]{2,1,0:T(8,128)S(1)}, u32[]{:S(2)}, u32[]{:S(2)}) collective-permute-start(f32[2,14,1024]{2,1,0:T(8,128)S(1)} %maximum_select_fusion.4), channel_id=1, source_target_pairs={{0,2},{1,3},{2,0},{3,1},{4,6},{5,7},{6,4},{7,5},{8,10},{9,11},{10,... | collective-permute-start | bytes 344072 | tf_op jit(solution)/shard_map/ppermute | solution.py:245
  22.5 3.6 %collective-permute-done.4 = f32[2,14,1024]{2,1,0:T(8,128)S(1)} collective-permute-done((f32[2,14,1024]{2,1,0:T(8,128)S(1)}, f32[2,14,1024]{2,1,0:T(8,128)S(1)}, u32[]{:S(2)}, u32[]{:S(2)}) %collective-permute-start.4) | collective-permute-done | bytes 114720 | tf_op jit(solution)/shard_map/ppermute | solution.py:245
  27.2 1.0 %fusion.1 = f32[42,384]{1,0:T(8,128)S(1)} fusion(s32[384]{0:T(512)S(1)} %pad_add_fusion, bf16[14,3072]{1,0:T(8,128)(2,1)S(1)} %get-tuple-element.27, bf16[14,3072]{1,0:T(8,128)(2,1)S(1)} %get-tuple-element.28, bf16[14,3072]{1,0:T(8,128)(2,1)S(1)} %get-tuple-element.26), kind=kOutput, calls=%fused_computation.2 | convolution fusion | flops 101044224 | bytes 324096 | tf_op jit(solution)/shard_map/dot_general | solution.py:235
  29.3 3.9 %shard_map.56 = (f32[14,64,128]{2,1,0:T(8,128)}, f32[14,192]{1,0:T(8,128)}) custom-call(f32[14,64,128]{2,1,0:T(8,128)} %bitcast.68, f32[14,8,128]{2,1,0:T(8,128)} %pad_maximum_fusion.refs_1_, f32[128,192]{1,0:T(8,128)} %get-tuple-element.11.refs_2_, f32[64,192]{1,0:T(8,128)} %get-tuple-element.12.refs_3_, f32[2,192]{1,0:T(2,128)} %pad_maximum_fusion.6.turn_ref.refs_4_), custom_call_target="tpu_custom_call" | custom-call | tf_op jit(solution)/shard_map/pallas_call | solution.py:123
  33.2 0.9 %fusion.21 = (f32[14,2,128]{2,1,0:T(2,128)S(1)}, f32[14,2,128]{2,1,0:T(2,128)S(1)}) fusion(f32[14,64,128]{2,1,0:T(8,128)} %get-tuple-element.13.refs_0_), kind=kLoop, calls=%fused_computation.77 | loop fusion | bytes 57344 | tf_op jit(solution)/shard_map/slice | solution.py:255
  34.1 1.8 %collective-permute-start.5 = (f32[14,192]{1,0:T(8,128)}, f32[14,192]{1,0:T(8,128)S(1)}, u32[]{:S(2)}, u32[]{:S(2)}) collective-permute-start(f32[14,192]{1,0:T(8,128)} %get-tuple-element.14), channel_id=1, source_target_pairs={{0,16},{16,0},{1,17},{17,1},{2,18},{18,2},{3,19},{19,3},{4,20},{20... | collective-permute-start | bytes 32264 | tf_op jit(solution)/shard_map/ppermute | solution.py:253
  35.9 2.1 %collective-permute-done.5 = f32[14,192]{1,0:T(8,128)S(1)} collective-permute-done((f32[14,192]{1,0:T(8,128)}, f32[14,192]{1,0:T(8,128)S(1)}, u32[]{:S(2)}, u32[]{:S(2)}) %collective-permute-start.5) | collective-permute-done | bytes 10784 | tf_op jit(solution)/shard_map/ppermute | solution.py:253
  38.2 1.9 %collective-permute-start.6 = (f32[1,14,704]{2,0,1:T(1,128)S(1)}, f32[1,14,704]{2,0,1:T(1,128)S(1)}, u32[]{:S(2)}, u32[]{:S(2)}) collective-permute-start(f32[1,14,704]{2,0,1:T(1,128)S(1)} %broadcast_in_dim.16), channel_id=1, source_target_pairs={{0,4},{4,0},{8,12},{12,8},{1,5},{5,1},{9,13},{13,9},{2,6},{6,2},{1... | collective-permute-start | bytes 118280 | tf_op jit(solution)/shard_map/ppermute | solution.py:245
  40.1 1.3 %fusion.22 = (f32[14,64,2]{2,1,0:T(8,128)S(1)}, f32[14,64,2]{2,1,0:T(8,128)S(1)}) fusion(f32[14,64,128]{2,1,0:T(8,128)} %get-tuple-element.13.refs_0_), kind=kLoop, calls=%fused_computation.78 | loop fusion | bytes 28672 | tf_op jit(solution)/shard_map/slice | solution.py:260
  42.4 3.3 %collective-permute-start.7 = (f32[2,14,704]{2,0,1:T(2,128)S(1)}, f32[2,14,704]{2,0,1:T(2,128)S(1)}, u32[]{:S(2)}, u32[]{:S(2)}) collective-permute-start(f32[2,14,704]{2,0,1:T(2,128)S(1)} %maximum_select_fusion.7), channel_id=1, source_target_pairs={{0,8},{4,12},{8,0},{12,4},{1,9},{5,13},{9,1},{13,5},{2,10},{6,14},... | collective-permute-start | bytes 236552 | tf_op jit(solution)/shard_map/ppermute | solution.py:245
  45.8 2.4 %collective-permute-done.7 = f32[2,14,704]{2,0,1:T(2,128)S(1)} collective-permute-done((f32[2,14,704]{2,0,1:T(2,128)S(1)}, f32[2,14,704]{2,0,1:T(2,128)S(1)}, u32[]{:S(2)}, u32[]{:S(2)}) %collective-permute-start.7) | collective-permute-done | bytes 78880 | tf_op jit(solution)/shard_map/ppermute | solution.py:245
  48.5 1.2 %collective-permute-done.8 = f32[1,14,1024]{2,1,0:T(8,128)S(1)} collective-permute-done((f32[1,14,1024]{2,1,0:T(8,128)S(1)}, f32[1,14,1024]{2,1,0:T(8,128)S(1)}, u32[]{:S(2)}, u32[]{:S(2)}) %collective-permute-start.8) | collective-permute-done | bytes 57376 | tf_op jit(solution)/shard_map/ppermute | solution.py:245
  49.7 1.6 %collective-permute-start.9 = (f32[2,14,1024]{2,1,0:T(8,128)S(1)}, f32[2,14,1024]{2,1,0:T(8,128)S(1)}, u32[]{:S(2)}, u32[]{:S(2)}) collective-permute-start(f32[2,14,1024]{2,1,0:T(8,128)S(1)} %maximum_select_fusion.5), channel_id=1, source_target_pairs={{0,2},{1,3},{2,0},{3,1},{4,6},{5,7},{6,4},{7,5},{8,10},{9,11},{10,... | collective-permute-start | bytes 344072 | tf_op jit(solution)/shard_map/ppermute | solution.py:245
  51.5 3.8 %collective-permute-done.9 = f32[2,14,1024]{2,1,0:T(8,128)S(1)} collective-permute-done((f32[2,14,1024]{2,1,0:T(8,128)S(1)}, f32[2,14,1024]{2,1,0:T(8,128)S(1)}, u32[]{:S(2)}, u32[]{:S(2)}) %collective-permute-start.9) | collective-permute-done | bytes 114720 | tf_op jit(solution)/shard_map/ppermute | solution.py:245
  56.4 1.0 %fusion = f32[42,384]{1,0:T(8,128)S(1)} fusion(s32[384]{0:T(512)S(1)} %pad_add_fusion, bf16[14,3072]{1,0:T(8,128)(2,1)S(1)} %get-tuple-element.24, bf16[14,3072]{1,0:T(8,128)(2,1)S(1)} %get-tuple-element.25, bf16[14,3072]{1,0:T(8,128)(2,1)S(1)} %get-tuple-element.23), kind=kOutput, calls=%fused_computation.1 | convolution fusion | flops 101044224 | bytes 324096 | tf_op jit(solution)/shard_map/dot_general | solution.py:235
  58.5 3.4 %shard_map.57 = f32[14,64,128]{2,1,0:T(8,128)} custom-call(f32[14,64,128]{2,1,0:T(8,128)} %get-tuple-element.13.refs_0_, f32[14,8,128]{2,1,0:T(8,128)} %pad_maximum_fusion.1.refs_1_, f32[14,64,128]{2,1,0:T(8,128)} %bitcast.69), custom_call_target="tpu_custom_call" | custom-call | tf_op jit(solution)/shard_map/pallas_call | solution.py:123
  (98 shorter events, 9.2 us)
Async XLA Ops:
  0.0 6.9 %copy-start = (f32[1,7,2,64,128]{4,3,2,1,0:T(8,128)S(1)}, f32[1,7,2,64,128]{4,3,2,1,0:T(8,128)}, u32[]{:S(2)}) copy-start(f32[1,7,2,64,128]{4,3,2,1,0:T(8,128)} %param.5) | copy-start | bytes 1376260
  3.9 4.9 %collective-permute-start = (f32[14,192]{1,0:T(8,128)}, f32[14,192]{1,0:T(8,128)S(1)}, u32[]{:S(2)}, u32[]{:S(2)}) collective-permute-start(f32[14,192]{1,0:T(8,128)} %get-tuple-element.10), channel_id=1, source_target_pairs={{0,16},{16,0},{1,17},{17,1},{2,18},{18,2},{3,19},{19,3},{4,20},{20... | collective-permute-start | bytes 32264 | tf_op jit(solution)/shard_map/ppermute | solution.py:253
  6.9 0.7 %copy-start.3 = (s32[1,1,1,768]{3,2,1,0:T(1,128)S(1)}, s32[1,1,1,768]{3,2,1,0:T(1,128)}, u32[]{:S(2)}) copy-start(s32[1,1,1,768]{3,2,1,0:T(1,128)} %param.6) | copy-start | bytes 9220
  9.0 4.2 %collective-permute-start.1 = (f32[1,14,704]{2,0,1:T(1,128)S(1)}, f32[1,14,704]{2,0,1:T(1,128)S(1)}, u32[]{:S(2)}, u32[]{:S(2)}) collective-permute-start(f32[1,14,704]{2,0,1:T(1,128)S(1)} %broadcast_in_dim.14), channel_id=1, source_target_pairs={{0,4},{4,0},{8,12},{12,8},{1,5},{5,1},{9,13},{13,9},{2,6},{6,2},{1... | collective-permute-start | bytes 118280 | tf_op jit(solution)/shard_map/ppermute | solution.py:245
  13.2 5.6 %collective-permute-start.2 = (f32[2,14,704]{2,0,1:T(2,128)S(1)}, f32[2,14,704]{2,0,1:T(2,128)S(1)}, u32[]{:S(2)}, u32[]{:S(2)}) collective-permute-start(f32[2,14,704]{2,0,1:T(2,128)S(1)} %maximum_select_fusion.6), channel_id=1, source_target_pairs={{0,8},{4,12},{8,0},{12,4},{1,9},{5,13},{9,1},{13,5},{2,10},{6,14},... | collective-permute-start | bytes 236552 | tf_op jit(solution)/shard_map/ppermute | solution.py:245
  19.1 1.3 %collective-permute-start.3 = (f32[1,14,1024]{2,1,0:T(8,128)S(1)}, f32[1,14,1024]{2,1,0:T(8,128)S(1)}, u32[]{:S(2)}, u32[]{:S(2)}) collective-permute-start(f32[1,14,1024]{2,1,0:T(8,128)S(1)} %maximum_bitcast_fusion), channel_id=1, source_target_pairs={{0,1},{1,0},{2,3},{3,2},{4,5},{5,4},{6,7},{7,6},{8,9},{9,8},{10,11... | collective-permute-start | bytes 172040 | tf_op jit(solution)/shard_map/ppermute | solution.py:245
  20.4 5.7 %collective-permute-start.4 = (f32[2,14,1024]{2,1,0:T(8,128)S(1)}, f32[2,14,1024]{2,1,0:T(8,128)S(1)}, u32[]{:S(2)}, u32[]{:S(2)}) collective-permute-start(f32[2,14,1024]{2,1,0:T(8,128)S(1)} %maximum_select_fusion.4), channel_id=1, source_target_pairs={{0,2},{1,3},{2,0},{3,1},{4,6},{5,7},{6,4},{7,5},{8,10},{9,11},{10,... | collective-permute-start | bytes 344072 | tf_op jit(solution)/shard_map/ppermute | solution.py:245
  26.1 0.7 %copy-start.2 = (f32[4,14,1024]{2,1,0:T(8,128)}, f32[4,14,1024]{2,1,0:T(8,128)S(1)}, u32[]{:S(2)}) copy-start(f32[4,14,1024]{2,1,0:T(8,128)S(1)} %maximum_select_fusion) | copy-start | bytes 688132
  27.2 1.2 %slice-start.1 = ((f32[4,14,1024]{2,1,0:T(8,128)}), f32[4,14,256]{2,1,0:T(8,128)S(1)}, s32[]{:S(2)}) async-start(f32[4,14,1024]{2,1,0:T(8,128)} %copy-done.2), calls=%async_computation.1 | async-start | bytes 131072 | tf_op jit(solution)/shard_map/slice | solution.py:267
  34.1 4.0 %collective-permute-start.5 = (f32[14,192]{1,0:T(8,128)}, f32[14,192]{1,0:T(8,128)S(1)}, u32[]{:S(2)}, u32[]{:S(2)}) collective-permute-start(f32[14,192]{1,0:T(8,128)} %get-tuple-element.14), channel_id=1, source_target_pairs={{0,16},{16,0},{1,17},{17,1},{2,18},{18,2},{3,19},{19,3},{4,20},{20... | collective-permute-start | bytes 32264 | tf_op jit(solution)/shard_map/ppermute | solution.py:253
  38.2 4.1 %collective-permute-start.6 = (f32[1,14,704]{2,0,1:T(1,128)S(1)}, f32[1,14,704]{2,0,1:T(1,128)S(1)}, u32[]{:S(2)}, u32[]{:S(2)}) collective-permute-start(f32[1,14,704]{2,0,1:T(1,128)S(1)} %broadcast_in_dim.16), channel_id=1, source_target_pairs={{0,4},{4,0},{8,12},{12,8},{1,5},{5,1},{9,13},{13,9},{2,6},{6,2},{1... | collective-permute-start | bytes 118280 | tf_op jit(solution)/shard_map/ppermute | solution.py:245
  42.4 5.7 %collective-permute-start.7 = (f32[2,14,704]{2,0,1:T(2,128)S(1)}, f32[2,14,704]{2,0,1:T(2,128)S(1)}, u32[]{:S(2)}, u32[]{:S(2)}) collective-permute-start(f32[2,14,704]{2,0,1:T(2,128)S(1)} %maximum_select_fusion.7), channel_id=1, source_target_pairs={{0,8},{4,12},{8,0},{12,4},{1,9},{5,13},{9,1},{13,5},{2,10},{6,14},... | collective-permute-start | bytes 236552 | tf_op jit(solution)/shard_map/ppermute | solution.py:245
  48.4 1.3 %collective-permute-start.8 = (f32[1,14,1024]{2,1,0:T(8,128)S(1)}, f32[1,14,1024]{2,1,0:T(8,128)S(1)}, u32[]{:S(2)}, u32[]{:S(2)}) collective-permute-start(f32[1,14,1024]{2,1,0:T(8,128)S(1)} %maximum_bitcast_fusion.1), channel_id=1, source_target_pairs={{0,1},{1,0},{2,3},{3,2},{4,5},{5,4},{6,7},{7,6},{8,9},{9,8},{10,11... | collective-permute-start | bytes 172040 | tf_op jit(solution)/shard_map/ppermute | solution.py:245
  49.7 5.6 %collective-permute-start.9 = (f32[2,14,1024]{2,1,0:T(8,128)S(1)}, f32[2,14,1024]{2,1,0:T(8,128)S(1)}, u32[]{:S(2)}, u32[]{:S(2)}) collective-permute-start(f32[2,14,1024]{2,1,0:T(8,128)S(1)} %maximum_select_fusion.5), channel_id=1, source_target_pairs={{0,2},{1,3},{2,0},{3,1},{4,6},{5,7},{6,4},{7,5},{8,10},{9,11},{10,... | collective-permute-start | bytes 344072 | tf_op jit(solution)/shard_map/ppermute | solution.py:245
  55.4 0.7 %copy-start.1 = (f32[4,14,1024]{2,1,0:T(8,128)}, f32[4,14,1024]{2,1,0:T(8,128)S(1)}, u32[]{:S(2)}) copy-start(f32[4,14,1024]{2,1,0:T(8,128)S(1)} %maximum_select_fusion.1) | copy-start | bytes 688132
  56.4 1.2 %slice-start = ((f32[4,14,1024]{2,1,0:T(8,128)}), f32[4,14,256]{2,1,0:T(8,128)S(1)}, s32[]{:S(2)}) async-start(f32[4,14,1024]{2,1,0:T(8,128)} %copy-done.1), calls=%async_computation | async-start | bytes 131072 | tf_op jit(solution)/shard_map/slice | solution.py:267

commit v17 on v15

--- a/solution.py
+++ b/solution.py
@@ -161,7 +161,10 @@
         out_ref[k : k + 1, :] = value
 
 
-def donation_kernel(f_ref, cells_ref, frac_ref, turn_ref, out_ref, lon_ref, lat_ref):
+def donation_kernel(f_ref, cells_ref, frac_ref, angle_ref, out_ref, lon_ref, lat_ref, turn_ref):
+    angle = angle_ref[...]
+    turn_ref[0:1, :] = jnp.cos(angle)
+    turn_ref[1:2, :] = jnp.sin(angle)
     planes, rows, cols = f_ref.shape
     weight_lon, weight_lat = donation_weights(cells_ref, frac_ref, rows, cols)
     lon_ref[...] = weight_lon
@@ -178,6 +181,7 @@
             jax.ShapeDtypeStruct((planes, dons), jnp.float32),
             jax.ShapeDtypeStruct((cols, dons), jnp.float32),
             jax.ShapeDtypeStruct((rows, dons), jnp.float32),
+            jax.ShapeDtypeStruct((2, dons), jnp.float32),
         ),
         interpret=INTERPRET,
     )(field, cells, frac, turn)
@@ -279,8 +283,7 @@
         return (jnp.concatenate([up, down, sides], axis=1),)
 
     field = state[0].reshape(comps * levels, rows, cols)
-    turn_parts = jnp.concatenate([jnp.cos(donor_turn[0, 0]), jnp.sin(donor_turn[0, 0])])
-    donation, lon_w, lat_w = first_donation(field, donor_cell[0, 0], donor_frac[0, 0, 0], turn_parts)
+    donation, lon_w, lat_w, turn_parts = first_donation(field, donor_cell[0, 0], donor_frac[0, 0, 0], donor_turn[0, 0])
     section_one, donation = advance(field, *section(field, donation), field, lon_w, lat_w, turn_parts, True)
     new_field = advance(section_one, *section(section_one, donation), field, lon_w, lat_w, turn_parts, False)
     return new_field.reshape(1, comps, levels, rows, cols)

time: 62.1 us -> 60.8 us (0.979)
  local copies, waits for them, and re-layouts: 7.87 us -> 7.09 us
    cos x1 -> x0, local copies, waits for them, and re-layouts: 0.78 us -> none  [per_device(): jnp.cos(donor_turn[0, 0])]
where the time goes in v17:
time: 60.8 us; the launch traced here: 60.5 us
  waiting for transfers between devices  20 us (33%)
  starting transfers between devices  18.8 us (31%)
  Pallas kernels  9.82 us (16%)
  local copies, waits for them, and re-layouts  7.09 us (12%)
  other arithmetic  2.39 us (4%)
  matrix products  1.98 us (3%)
    ppermute x8, waiting for transfers between devices, gather(): other = lax.ppermute(held, axis, [(i, i ^ k) for i in range(size)])  16.6 us
    ppermute x8, starting transfers between devices, gather(): other = lax.ppermute(held, axis, [(i, i ^ k) for i in range(size)])  14 us
    pallas_call x2, Pallas kernels, advance(): pl.pallas_call(functools.partial(stencil_kernel, first=first), out_shape=...  7.18 us
    ppermute x2, starting transfers between devices, section(): given = lax.ppermute(donation, 'panel', [(0, 1), (1, 0)])  4.79 us
    ppermute x2, waiting for transfers between devices, section(): given = lax.ppermute(donation, 'panel', [(0, 1), (1, 0)])  3.32 us
    pallas_call x1, Pallas kernels, first_donation(): pl.pallas_call(donation_kernel, out_shape=(jax.ShapeDtypeStruct((planes,...  2.64 us
    slice x6, local copies, waits for them, and re-layouts, section(): side_cols = jnp.concatenate([flat[:, :, :2], flat[:, :, cols - 2:]], axis=2)  2.33 us
    dot_general x2, matrix products, select(): picked = jnp.dot(parts, pick, preferred_element_type=jnp.float32)  1.98 us
  transfers between devices with their start and end apart: 10, of which 10 were waited for; matrix products, arithmetic and copies ran while one was open for 5% of the time, Pallas kernels for 0%

profile of v17, /device:TPU:0, one launch (start us, length us, event | category | flops | bytes accessed | tf_op | source)
XLA Modules:
  0.0 60.5 jit_solution(8582153135648024126)
XLA Ops:
  0.0 2.6 %shard_map.55 = (f32[14,192]{1,0:T(8,128)}, f32[128,192]{1,0:T(8,128)}, f32[64,192]{1,0:T(8,128)}, f32[2,192]{1,0:T(2,128)}) custom-call(f32[14,64,128]{2,1,0:T(8,128)} %bitcast.64, s32[1,192]{1,0:T(1,128)} %bitcast.85, f32[2,192]{1,0:T(2,128)} %bitcast.84, f32[1,192]{1,0:T(1,128)} %bitcast.86), custom_call_target="tpu_custom_call" | custom-call | tf_op jit(solution)/shard_map/pallas_call | solution.py:178
  2.6 3.0 %collective-permute-start = (f32[14,192]{1,0:T(8,128)}, f32[14,192]{1,0:T(8,128)S(1)}, u32[]{:S(2)}, u32[]{:S(2)}) collective-permute-start(f32[14,192]{1,0:T(8,128)} %get-tuple-element.11), channel_id=1, source_target_pairs={{0,16},{16,0},{1,17},{17,1},{2,18},{18,2},{3,19},{19,3},{4,20},{20... | collective-permute-start | bytes 32264 | tf_op jit(solution)/shard_map/ppermute | solution.py:256
  6.4 1.2 %collective-permute-done = f32[14,192]{1,0:T(8,128)S(1)} collective-permute-done((f32[14,192]{1,0:T(8,128)}, f32[14,192]{1,0:T(8,128)S(1)}, u32[]{:S(2)}, u32[]{:S(2)}) %collective-permute-start) | collective-permute-done | bytes 10784 | tf_op jit(solution)/shard_map/ppermute | solution.py:256
  7.7 2.1 %collective-permute-start.1 = (f32[1,14,704]{2,0,1:T(1,128)S(1)}, f32[1,14,704]{2,0,1:T(1,128)S(1)}, u32[]{:S(2)}, u32[]{:S(2)}) collective-permute-start(f32[1,14,704]{2,0,1:T(1,128)S(1)} %broadcast_in_dim.14), channel_id=1, source_target_pairs={{0,4},{4,0},{8,12},{12,8},{1,5},{5,1},{9,13},{13,9},{2,6},{6,2},{1... | collective-permute-start | bytes 118280 | tf_op jit(solution)/shard_map/ppermute | solution.py:248
  10.2 1.6 %collective-permute-done.1 = f32[1,14,704]{2,0,1:T(1,128)S(1)} collective-permute-done((f32[1,14,704]{2,0,1:T(1,128)S(1)}, f32[1,14,704]{2,0,1:T(1,128)S(1)}, u32[]{:S(2)}, u32[]{:S(2)}) %collective-permute-start.1) | collective-permute-done | bytes 39456 | tf_op jit(solution)/shard_map/ppermute | solution.py:248
  11.9 3.1 %collective-permute-start.2 = (f32[2,14,704]{2,0,1:T(2,128)S(1)}, f32[2,14,704]{2,0,1:T(2,128)S(1)}, u32[]{:S(2)}, u32[]{:S(2)}) collective-permute-start(f32[2,14,704]{2,0,1:T(2,128)S(1)} %maximum_select_fusion.6), channel_id=1, source_target_pairs={{0,8},{4,12},{8,0},{12,4},{1,9},{5,13},{9,1},{13,5},{2,10},{6,14},... | collective-permute-start | bytes 236552 | tf_op jit(solution)/shard_map/ppermute | solution.py:248
  15.1 2.4 %collective-permute-done.2 = f32[2,14,704]{2,0,1:T(2,128)S(1)} collective-permute-done((f32[2,14,704]{2,0,1:T(2,128)S(1)}, f32[2,14,704]{2,0,1:T(2,128)S(1)}, u32[]{:S(2)}, u32[]{:S(2)}) %collective-permute-start.2) | collective-permute-done | bytes 78880 | tf_op jit(solution)/shard_map/ppermute | solution.py:248
  17.9 1.2 %collective-permute-done.3 = f32[1,14,1024]{2,1,0:T(8,128)S(1)} collective-permute-done((f32[1,14,1024]{2,1,0:T(8,128)S(1)}, f32[1,14,1024]{2,1,0:T(8,128)S(1)}, u32[]{:S(2)}, u32[]{:S(2)}) %collective-permute-start.3) | collective-permute-done | bytes 57376 | tf_op jit(solution)/shard_map/ppermute | solution.py:248
  19.1 1.9 %collective-permute-start.4 = (f32[2,14,1024]{2,1,0:T(8,128)S(1)}, f32[2,14,1024]{2,1,0:T(8,128)S(1)}, u32[]{:S(2)}, u32[]{:S(2)}) collective-permute-start(f32[2,14,1024]{2,1,0:T(8,128)S(1)} %maximum_select_fusion.4), channel_id=1, source_target_pairs={{0,2},{1,3},{2,0},{3,1},{4,6},{5,7},{6,4},{7,5},{8,10},{9,11},{10,... | collective-permute-start | bytes 344072 | tf_op jit(solution)/shard_map/ppermute | solution.py:248
  21.2 3.6 %collective-permute-done.4 = f32[2,14,1024]{2,1,0:T(8,128)S(1)} collective-permute-done((f32[2,14,1024]{2,1,0:T(8,128)S(1)}, f32[2,14,1024]{2,1,0:T(8,128)S(1)}, u32[]{:S(2)}, u32[]{:S(2)}) %collective-permute-start.4) | collective-permute-done | bytes 114720 | tf_op jit(solution)/shard_map/ppermute | solution.py:248
  25.9 1.0 %fusion.1 = f32[42,384]{1,0:T(8,128)S(1)} fusion(s32[384]{0:T(512)S(1)} %pad_add_fusion, bf16[14,3072]{1,0:T(8,128)(2,1)S(1)} %get-tuple-element.29, bf16[14,3072]{1,0:T(8,128)(2,1)S(1)} %get-tuple-element.30, bf16[14,3072]{1,0:T(8,128)(2,1)S(1)} %get-tuple-element.28), kind=kOutput, calls=%fused_computation.2 | convolution fusion | flops 101044224 | bytes 324096 | tf_op jit(solution)/shard_map/dot_general | solution.py:238
  28.0 3.8 %shard_map.56 = (f32[14,64,128]{2,1,0:T(8,128)}, f32[14,192]{1,0:T(8,128)}) custom-call(f32[14,64,128]{2,1,0:T(8,128)} %bitcast.65, f32[14,8,128]{2,1,0:T(8,128)} %pad_maximum_fusion.refs_1_, f32[128,192]{1,0:T(8,128)} %get-tuple-element.12.refs_2_, f32[64,192]{1,0:T(8,128)} %get-tuple-element.13.refs_3_, f32[2,192]{1,0:T(2,128)} %get-tuple-element.14.refs_4_), custom_call_target="tpu_custom_call" | custom-call | tf_op jit(solution)/shard_map/pallas_call | solution.py:123
  31.7 0.9 %fusion.21 = (f32[14,2,128]{2,1,0:T(2,128)S(1)}, f32[14,2,128]{2,1,0:T(2,128)S(1)}) fusion(f32[14,64,128]{2,1,0:T(8,128)} %get-tuple-element.15.refs_0_), kind=kLoop, calls=%fused_computation.74 | loop fusion | bytes 57344 | tf_op jit(solution)/shard_map/slice | solution.py:258
  32.6 1.8 %collective-permute-start.5 = (f32[14,192]{1,0:T(8,128)}, f32[14,192]{1,0:T(8,128)S(1)}, u32[]{:S(2)}, u32[]{:S(2)}) collective-permute-start(f32[14,192]{1,0:T(8,128)} %get-tuple-element.16), channel_id=1, source_target_pairs={{0,16},{16,0},{1,17},{17,1},{2,18},{18,2},{3,19},{19,3},{4,20},{20... | collective-permute-start | bytes 32264 | tf_op jit(solution)/shard_map/ppermute | solution.py:256
  34.5 2.1 %collective-permute-done.5 = f32[14,192]{1,0:T(8,128)S(1)} collective-permute-done((f32[14,192]{1,0:T(8,128)}, f32[14,192]{1,0:T(8,128)S(1)}, u32[]{:S(2)}, u32[]{:S(2)}) %collective-permute-start.5) | collective-permute-done | bytes 10784 | tf_op jit(solution)/shard_map/ppermute | solution.py:256
  36.7 1.9 %collective-permute-start.6 = (f32[1,14,704]{2,0,1:T(1,128)S(1)}, f32[1,14,704]{2,0,1:T(1,128)S(1)}, u32[]{:S(2)}, u32[]{:S(2)}) collective-permute-start(f32[1,14,704]{2,0,1:T(1,128)S(1)} %broadcast_in_dim.16), channel_id=1, source_target_pairs={{0,4},{4,0},{8,12},{12,8},{1,5},{5,1},{9,13},{13,9},{2,6},{6,2},{1... | collective-permute-start | bytes 118280 | tf_op jit(solution)/shard_map/ppermute | solution.py:248
  38.6 1.3 %fusion.22 = (f32[14,64,2]{2,1,0:T(8,128)S(1)}, f32[14,64,2]{2,1,0:T(8,128)S(1)}) fusion(f32[14,64,128]{2,1,0:T(8,128)} %get-tuple-element.15.refs_0_), kind=kLoop, calls=%fused_computation.75 | loop fusion | bytes 28672 | tf_op jit(solution)/shard_map/slice | solution.py:263
  41.0 3.3 %collective-permute-start.7 = (f32[2,14,704]{2,0,1:T(2,128)S(1)}, f32[2,14,704]{2,0,1:T(2,128)S(1)}, u32[]{:S(2)}, u32[]{:S(2)}) collective-permute-start(f32[2,14,704]{2,0,1:T(2,128)S(1)} %maximum_select_fusion.7), channel_id=1, source_target_pairs={{0,8},{4,12},{8,0},{12,4},{1,9},{5,13},{9,1},{13,5},{2,10},{6,14},... | collective-permute-start | bytes 236552 | tf_op jit(solution)/shard_map/ppermute | solution.py:248
  44.3 2.4 %collective-permute-done.7 = f32[2,14,704]{2,0,1:T(2,128)S(1)} collective-permute-done((f32[2,14,704]{2,0,1:T(2,128)S(1)}, f32[2,14,704]{2,0,1:T(2,128)S(1)}, u32[]{:S(2)}, u32[]{:S(2)}) %collective-permute-start.7) | collective-permute-done | bytes 78880 | tf_op jit(solution)/shard_map/ppermute | solution.py:248
  47.0 1.2 %collective-permute-done.8 = f32[1,14,1024]{2,1,0:T(8,128)S(1)} collective-permute-done((f32[1,14,1024]{2,1,0:T(8,128)S(1)}, f32[1,14,1024]{2,1,0:T(8,128)S(1)}, u32[]{:S(2)}, u32[]{:S(2)}) %collective-permute-start.8) | collective-permute-done | bytes 57376 | tf_op jit(solution)/shard_map/ppermute | solution.py:248
  48.3 1.6 %collective-permute-start.9 = (f32[2,14,1024]{2,1,0:T(8,128)S(1)}, f32[2,14,1024]{2,1,0:T(8,128)S(1)}, u32[]{:S(2)}, u32[]{:S(2)}) collective-permute-start(f32[2,14,1024]{2,1,0:T(8,128)S(1)} %maximum_select_fusion.5), channel_id=1, source_target_pairs={{0,2},{1,3},{2,0},{3,1},{4,6},{5,7},{6,4},{7,5},{8,10},{9,11},{10,... | collective-permute-start | bytes 344072 | tf_op jit(solution)/shard_map/ppermute | solution.py:248
  50.1 3.8 %collective-permute-done.9 = f32[2,14,1024]{2,1,0:T(8,128)S(1)} collective-permute-done((f32[2,14,1024]{2,1,0:T(8,128)S(1)}, f32[2,14,1024]{2,1,0:T(8,128)S(1)}, u32[]{:S(2)}, u32[]{:S(2)}) %collective-permute-start.9) | collective-permute-done | bytes 114720 | tf_op jit(solution)/shard_map/ppermute | solution.py:248
  55.0 1.0 %fusion = f32[42,384]{1,0:T(8,128)S(1)} fusion(s32[384]{0:T(512)S(1)} %pad_add_fusion, bf16[14,3072]{1,0:T(8,128)(2,1)S(1)} %get-tuple-element.26, bf16[14,3072]{1,0:T(8,128)(2,1)S(1)} %get-tuple-element.27, bf16[14,3072]{1,0:T(8,128)(2,1)S(1)} %get-tuple-element.25), kind=kOutput, calls=%fused_computation.1 | convolution fusion | flops 101044224 | bytes 324096 | tf_op jit(solution)/shard_map/dot_general | solution.py:238
  57.1 3.4 %shard_map.57 = f32[14,64,128]{2,1,0:T(8,128)} custom-call(f32[14,64,128]{2,1,0:T(8,128)} %get-tuple-element.15.refs_0_, f32[14,8,128]{2,1,0:T(8,128)} %pad_maximum_fusion.1.refs_1_, f32[14,64,128]{2,1,0:T(8,128)} %bitcast.66), custom_call_target="tpu_custom_call" | custom-call | tf_op jit(solution)/shard_map/pallas_call | solution.py:123
  (96 shorter events, 7.8 us)
Async XLA Ops:
  0.0 5.6 %copy-start = (f32[1,7,2,64,128]{4,3,2,1,0:T(8,128)S(1)}, f32[1,7,2,64,128]{4,3,2,1,0:T(8,128)}, u32[]{:S(2)}) copy-start(f32[1,7,2,64,128]{4,3,2,1,0:T(8,128)} %param.5) | copy-start | bytes 1376260
  2.6 4.9 %collective-permute-start = (f32[14,192]{1,0:T(8,128)}, f32[14,192]{1,0:T(8,128)S(1)}, u32[]{:S(2)}, u32[]{:S(2)}) collective-permute-start(f32[14,192]{1,0:T(8,128)} %get-tuple-element.11), channel_id=1, source_target_pairs={{0,16},{16,0},{1,17},{17,1},{2,18},{18,2},{3,19},{19,3},{4,20},{20... | collective-permute-start | bytes 32264 | tf_op jit(solution)/shard_map/ppermute | solution.py:256
  5.6 0.7 %copy-start.3 = (s32[1,1,1,768]{3,2,1,0:T(1,128)S(1)}, s32[1,1,1,768]{3,2,1,0:T(1,128)}, u32[]{:S(2)}) copy-start(s32[1,1,1,768]{3,2,1,0:T(1,128)} %param.6) | copy-start | bytes 9220
  7.7 4.1 %collective-permute-start.1 = (f32[1,14,704]{2,0,1:T(1,128)S(1)}, f32[1,14,704]{2,0,1:T(1,128)S(1)}, u32[]{:S(2)}, u32[]{:S(2)}) collective-permute-start(f32[1,14,704]{2,0,1:T(1,128)S(1)} %broadcast_in_dim.14), channel_id=1, source_target_pairs={{0,4},{4,0},{8,12},{12,8},{1,5},{5,1},{9,13},{13,9},{2,6},{6,2},{1... | collective-permute-start | bytes 118280 | tf_op jit(solution)/shard_map/ppermute | solution.py:248
  11.9 5.6 %collective-permute-start.2 = (f32[2,14,704]{2,0,1:T(2,128)S(1)}, f32[2,14,704]{2,0,1:T(2,128)S(1)}, u32[]{:S(2)}, u32[]{:S(2)}) collective-permute-start(f32[2,14,704]{2,0,1:T(2,128)S(1)} %maximum_select_fusion.6), channel_id=1, source_target_pairs={{0,8},{4,12},{8,0},{12,4},{1,9},{5,13},{9,1},{13,5},{2,10},{6,14},... | collective-permute-start | bytes 236552 | tf_op jit(solution)/shard_map/ppermute | solution.py:248
  17.8 1.3 %collective-permute-start.3 = (f32[1,14,1024]{2,1,0:T(8,128)S(1)}, f32[1,14,1024]{2,1,0:T(8,128)S(1)}, u32[]{:S(2)}, u32[]{:S(2)}) collective-permute-start(f32[1,14,1024]{2,1,0:T(8,128)S(1)} %maximum_bitcast_fusion), channel_id=1, source_target_pairs={{0,1},{1,0},{2,3},{3,2},{4,5},{5,4},{6,7},{7,6},{8,9},{9,8},{10,11... | collective-permute-start | bytes 172040 | tf_op jit(solution)/shard_map/ppermute | solution.py:248
  19.1 5.7 %collective-permute-start.4 = (f32[2,14,1024]{2,1,0:T(8,128)S(1)}, f32[2,14,1024]{2,1,0:T(8,128)S(1)}, u32[]{:S(2)}, u32[]{:S(2)}) collective-permute-start(f32[2,14,1024]{2,1,0:T(8,128)S(1)} %maximum_select_fusion.4), channel_id=1, source_target_pairs={{0,2},{1,3},{2,0},{3,1},{4,6},{5,7},{6,4},{7,5},{8,10},{9,11},{10,... | collective-permute-start | bytes 344072 | tf_op jit(solution)/shard_map/ppermute | solution.py:248
  24.8 0.7 %copy-start.2 = (f32[4,14,1024]{2,1,0:T(8,128)}, f32[4,14,1024]{2,1,0:T(8,128)S(1)}, u32[]{:S(2)}) copy-start(f32[4,14,1024]{2,1,0:T(8,128)S(1)} %maximum_select_fusion) | copy-start | bytes 688132
  25.9 1.2 %slice-start.1 = ((f32[4,14,1024]{2,1,0:T(8,128)}), f32[4,14,256]{2,1,0:T(8,128)S(1)}, s32[]{:S(2)}) async-start(f32[4,14,1024]{2,1,0:T(8,128)} %copy-done.2), calls=%async_computation.1 | async-start | bytes 131072 | tf_op jit(solution)/shard_map/slice | solution.py:270
  32.6 4.0 %collective-permute-start.5 = (f32[14,192]{1,0:T(8,128)}, f32[14,192]{1,0:T(8,128)S(1)}, u32[]{:S(2)}, u32[]{:S(2)}) collective-permute-start(f32[14,192]{1,0:T(8,128)} %get-tuple-element.16), channel_id=1, source_target_pairs={{0,16},{16,0},{1,17},{17,1},{2,18},{18,2},{3,19},{19,3},{4,20},{20... | collective-permute-start | bytes 32264 | tf_op jit(solution)/shard_map/ppermute | solution.py:256
  36.7 4.1 %collective-permute-start.6 = (f32[1,14,704]{2,0,1:T(1,128)S(1)}, f32[1,14,704]{2,0,1:T(1,128)S(1)}, u32[]{:S(2)}, u32[]{:S(2)}) collective-permute-start(f32[1,14,704]{2,0,1:T(1,128)S(1)} %broadcast_in_dim.16), channel_id=1, source_target_pairs={{0,4},{4,0},{8,12},{12,8},{1,5},{5,1},{9,13},{13,9},{2,6},{6,2},{1... | collective-permute-start | bytes 118280 | tf_op jit(solution)/shard_map/ppermute | solution.py:248
  41.0 5.7 %collective-permute-start.7 = (f32[2,14,704]{2,0,1:T(2,128)S(1)}, f32[2,14,704]{2,0,1:T(2,128)S(1)}, u32[]{:S(2)}, u32[]{:S(2)}) collective-permute-start(f32[2,14,704]{2,0,1:T(2,128)S(1)} %maximum_select_fusion.7), channel_id=1, source_target_pairs={{0,8},{4,12},{8,0},{12,4},{1,9},{5,13},{9,1},{13,5},{2,10},{6,14},... | collective-permute-start | bytes 236552 | tf_op jit(solution)/shard_map/ppermute | solution.py:248
  47.0 1.3 %collective-permute-start.8 = (f32[1,14,1024]{2,1,0:T(8,128)S(1)}, f32[1,14,1024]{2,1,0:T(8,128)S(1)}, u32[]{:S(2)}, u32[]{:S(2)}) collective-permute-start(f32[1,14,1024]{2,1,0:T(8,128)S(1)} %maximum_bitcast_fusion.1), channel_id=1, source_target_pairs={{0,1},{1,0},{2,3},{3,2},{4,5},{5,4},{6,7},{7,6},{8,9},{9,8},{10,11... | collective-permute-start | bytes 172040 | tf_op jit(solution)/shard_map/ppermute | solution.py:248
  48.3 5.6 %collective-permute-start.9 = (f32[2,14,1024]{2,1,0:T(8,128)S(1)}, f32[2,14,1024]{2,1,0:T(8,128)S(1)}, u32[]{:S(2)}, u32[]{:S(2)}) collective-permute-start(f32[2,14,1024]{2,1,0:T(8,128)S(1)} %maximum_select_fusion.5), channel_id=1, source_target_pairs={{0,2},{1,3},{2,0},{3,1},{4,6},{5,7},{6,4},{7,5},{8,10},{9,11},{10,... | collective-permute-start | bytes 344072 | tf_op jit(solution)/shard_map/ppermute | solution.py:248
  53.9 0.7 %copy-start.1 = (f32[4,14,1024]{2,1,0:T(8,128)}, f32[4,14,1024]{2,1,0:T(8,128)S(1)}, u32[]{:S(2)}) copy-start(f32[4,14,1024]{2,1,0:T(8,128)S(1)} %maximum_select_fusion.1) | copy-start | bytes 688132
  55.0 1.2 %slice-start = ((f32[4,14,1024]{2,1,0:T(8,128)}), f32[4,14,256]{2,1,0:T(8,128)S(1)}, s32[]{:S(2)}) async-start(f32[4,14,1024]{2,1,0:T(8,128)} %copy-done.1), calls=%async_computation | async-start | bytes 131072 | tf_op jit(solution)/shard_map/slice | solution.py:270

commit v18 on v17

--- a/solution.py
+++ b/solution.py
@@ -19,7 +19,7 @@
 
 def stencil_kernel(*refs, first):
     if first:
-        f_ref, halo_ref, lon_ref, lat_ref, turn_ref, o_ref, don_ref = refs
+        f_ref, halo_ref, lon_ref, lat_ref, turn_ref, o_ref, don_ref, rows_ref = refs
     else:
         f_ref, halo_ref, base_ref, o_ref = refs
     planes, height, width = f_ref.shape
@@ -91,6 +91,9 @@
             section = x + time_step * rate
             if first:
                 o_ref[plane(c)] = section
+                k = plane(c)
+                for slot, line in enumerate((0, 1, height - 2, height - 1)):
+                    rows_ref[k : k + 1, slot * width : (slot + 1) * width] = section[line : line + 1, :]
             else:
                 o_ref[plane(c)] = 0.5 * base_ref[plane(c)] + 0.5 * section
 
@@ -119,7 +122,11 @@
 def advance(field, halo, base, lon, lat, turn, first):
     shape = jax.ShapeDtypeStruct(field.shape, field.dtype)
     if first:
-        shape = (shape, jax.ShapeDtypeStruct((field.shape[0], lon.shape[1]), jnp.float32))
+        shape = (
+            shape,
+            jax.ShapeDtypeStruct((field.shape[0], lon.shape[1]), jnp.float32),
+            jax.ShapeDtypeStruct((field.shape[0], 4 * field.shape[2]), jnp.float32),
+        )
     return pl.pallas_call(
         functools.partial(stencil_kernel, first=first),
         out_shape=shape,
@@ -251,12 +258,13 @@
             k *= 2
         return held
 
-    def section(field, donation):
+    def section(field, donation, edge_rows=None):
         flat = field
         given = lax.ppermute(donation, "panel", [(0, 1), (1, 0)])
         dons = given.shape[1]
-        side_rows = jnp.concatenate([flat[:, :2, :], flat[:, rows - 2 :, :]], axis=1)
-        lat_packet = jnp.concatenate([given, side_rows.reshape(comps * levels, -1)], axis=1)
+        if edge_rows is None:
+            edge_rows = jnp.concatenate([flat[:, :2, :], flat[:, rows - 2 :, :]], axis=1).reshape(comps * levels, -1)
+        lat_packet = jnp.concatenate([given, edge_rows], axis=1)
         lat_all = gather(lat_packet, "lat")
         col_given = jnp.transpose(lat_all[:, :, :dons], (1, 0, 2)).reshape(comps * levels, -1)
         side_rows = lat_all[:, :, dons:].reshape(lat_count, comps, levels, 4, cols)
@@ -284,8 +292,8 @@
 
     field = state[0].reshape(comps * levels, rows, cols)
     donation, lon_w, lat_w, turn_parts = first_donation(field, donor_cell[0, 0], donor_frac[0, 0, 0], donor_turn[0, 0])
-    section_one, donation = advance(field, *section(field, donation), field, lon_w, lat_w, turn_parts, True)
-    new_field = advance(section_one, *section(section_one, donation), field, lon_w, lat_w, turn_parts, False)
+    section_one, donation, edge_rows = advance(field, *section(field, donation), field, lon_w, lat_w, turn_parts, True)
+    new_field = advance(section_one, *section(section_one, donation, edge_rows), field, lon_w, lat_w, turn_parts, False)
     return new_field.reshape(1, comps, levels, rows, cols)
 
 

time: 60.8 us -> 60.7 us (level)
  local copies, waits for them, and re-layouts: 7.09 us -> 6.12 us
    broadcast_in_dim x2 -> x4, other arithmetic: 0.02 us -> 0.93 us  [gather(): held = packet[None]]
    slice x2 -> x1, local copies, waits for them, and re-layouts: 0.87 us -> 0.01 us  [section(): flat[:, :2, :]]
where the time goes in v18:
time: 60.7 us; the launch traced here: 60.4 us
  waiting for transfers between devices  20.4 us (34%)
  starting transfers between devices  18.9 us (31%)
  Pallas kernels  9.83 us (16%)
  local copies, waits for them, and re-layouts  6.12 us (10%)
  other arithmetic  2.66 us (4%)
  matrix products  1.98 us (3%)
    ppermute x8, waiting for transfers between devices, gather(): other = lax.ppermute(held, axis, [(i, i ^ k) for i in range(size)])  17 us
    ppermute x8, starting transfers between devices, gather(): other = lax.ppermute(held, axis, [(i, i ^ k) for i in range(size)])  14.2 us
    pallas_call x2, Pallas kernels, advance(): pl.pallas_call(functools.partial(stencil_kernel, first=first), out_shape=...  7.19 us
    ppermute x2, starting transfers between devices, section(): given = lax.ppermute(donation, 'panel', [(0, 1), (1, 0)])  4.73 us
    ppermute x2, waiting for transfers between devices, section(): given = lax.ppermute(donation, 'panel', [(0, 1), (1, 0)])  3.37 us
    pallas_call x1, Pallas kernels, first_donation(): pl.pallas_call(donation_kernel, out_shape=(jax.ShapeDtypeStruct((planes,...  2.64 us
    slice x6, local copies, waits for them, and re-layouts, section(): side_cols = jnp.concatenate([flat[:, :, :2], flat[:, :, cols - 2:]], axis=2)  2.33 us
    dot_general x2, matrix products, select(): picked = jnp.dot(parts, pick, preferred_element_type=jnp.float32)  1.98 us
  transfers between devices with their start and end apart: 10, of which 10 were waited for; matrix products, arithmetic and copies ran while one was open for 5% of the time, Pallas kernels for 0%

profile of v18, /device:TPU:0, one launch (start us, length us, event | category | flops | bytes accessed | tf_op | source)
XLA Modules:
  0.0 60.4 jit_solution(13845045471165495957)
XLA Ops:
  0.0 2.6 %shard_map.55 = (f32[14,192]{1,0:T(8,128)}, f32[128,192]{1,0:T(8,128)}, f32[64,192]{1,0:T(8,128)}, f32[2,192]{1,0:T(2,128)}) custom-call(f32[14,64,128]{2,1,0:T(8,128)} %bitcast.69, s32[1,192]{1,0:T(1,128)} %bitcast.88, f32[2,192]{1,0:T(2,128)} %bitcast.87, f32[1,192]{1,0:T(1,128)} %bitcast.89), custom_call_target="tpu_custom_call" | custom-call | tf_op jit(solution)/shard_map/pallas_call | solution.py:185
  2.6 3.0 %collective-permute-start = (f32[14,192]{1,0:T(8,128)}, f32[14,192]{1,0:T(8,128)S(1)}, u32[]{:S(2)}, u32[]{:S(2)}) collective-permute-start(f32[14,192]{1,0:T(8,128)} %get-tuple-element.12), channel_id=1, source_target_pairs={{0,16},{16,0},{1,17},{17,1},{2,18},{18,2},{3,19},{19,3},{4,20},{20... | collective-permute-start | bytes 32264 | tf_op jit(solution)/shard_map/ppermute | solution.py:263
  6.4 1.2 %collective-permute-done = f32[14,192]{1,0:T(8,128)S(1)} collective-permute-done((f32[14,192]{1,0:T(8,128)}, f32[14,192]{1,0:T(8,128)S(1)}, u32[]{:S(2)}, u32[]{:S(2)}) %collective-permute-start) | collective-permute-done | bytes 10784 | tf_op jit(solution)/shard_map/ppermute | solution.py:263
  7.6 2.1 %collective-permute-start.1 = (f32[1,14,704]{2,1,0:T(8,128)S(1)}, f32[1,14,704]{2,1,0:T(8,128)S(1)}, u32[]{:S(2)}, u32[]{:S(2)}) collective-permute-start(f32[1,14,704]{2,1,0:T(8,128)S(1)} %maximum_bitcast_fusion.2), channel_id=1, source_target_pairs={{0,4},{4,0},{8,12},{12,8},{1,5},{5,1},{9,13},{13,9},{2,6},{6,2},{1... | collective-permute-start | bytes 118280 | tf_op jit(solution)/shard_map/ppermute | solution.py:255
  10.1 1.7 %collective-permute-done.1 = f32[1,14,704]{2,1,0:T(8,128)S(1)} collective-permute-done((f32[1,14,704]{2,1,0:T(8,128)S(1)}, f32[1,14,704]{2,1,0:T(8,128)S(1)}, u32[]{:S(2)}, u32[]{:S(2)}) %collective-permute-start.1) | collective-permute-done | bytes 39456 | tf_op jit(solution)/shard_map/ppermute | solution.py:255
  11.8 3.1 %collective-permute-start.2 = (f32[2,14,704]{2,1,0:T(8,128)S(1)}, f32[2,14,704]{2,1,0:T(8,128)S(1)}, u32[]{:S(2)}, u32[]{:S(2)}) collective-permute-start(f32[2,14,704]{2,1,0:T(8,128)S(1)} %maximum_select_fusion.6), channel_id=1, source_target_pairs={{0,8},{4,12},{8,0},{12,4},{1,9},{5,13},{9,1},{13,5},{2,10},{6,14},... | collective-permute-start | bytes 236552 | tf_op jit(solution)/shard_map/ppermute | solution.py:255
  15.0 2.5 %collective-permute-done.2 = f32[2,14,704]{2,1,0:T(8,128)S(1)} collective-permute-done((f32[2,14,704]{2,1,0:T(8,128)S(1)}, f32[2,14,704]{2,1,0:T(8,128)S(1)}, u32[]{:S(2)}, u32[]{:S(2)}) %collective-permute-start.2) | collective-permute-done | bytes 78880 | tf_op jit(solution)/shard_map/ppermute | solution.py:255
  17.8 1.2 %collective-permute-done.3 = f32[1,14,1024]{2,1,0:T(8,128)S(1)} collective-permute-done((f32[1,14,1024]{2,1,0:T(8,128)S(1)}, f32[1,14,1024]{2,1,0:T(8,128)S(1)}, u32[]{:S(2)}, u32[]{:S(2)}) %collective-permute-start.3) | collective-permute-done | bytes 57376 | tf_op jit(solution)/shard_map/ppermute | solution.py:255
  19.0 1.9 %collective-permute-start.4 = (f32[2,14,1024]{2,1,0:T(8,128)S(1)}, f32[2,14,1024]{2,1,0:T(8,128)S(1)}, u32[]{:S(2)}, u32[]{:S(2)}) collective-permute-start(f32[2,14,1024]{2,1,0:T(8,128)S(1)} %maximum_select_fusion.4), channel_id=1, source_target_pairs={{0,2},{1,3},{2,0},{3,1},{4,6},{5,7},{6,4},{7,5},{8,10},{9,11},{10,... | collective-permute-start | bytes 344072 | tf_op jit(solution)/shard_map/ppermute | solution.py:255
  21.1 3.6 %collective-permute-done.4 = f32[2,14,1024]{2,1,0:T(8,128)S(1)} collective-permute-done((f32[2,14,1024]{2,1,0:T(8,128)S(1)}, f32[2,14,1024]{2,1,0:T(8,128)S(1)}, u32[]{:S(2)}, u32[]{:S(2)}) %collective-permute-start.4) | collective-permute-done | bytes 114720 | tf_op jit(solution)/shard_map/ppermute | solution.py:255
  25.8 1.0 %fusion.1 = f32[42,384]{1,0:T(8,128)S(1)} fusion(s32[384]{0:T(512)S(1)} %pad_add_fusion, bf16[14,3072]{1,0:T(8,128)(2,1)S(1)} %get-tuple-element.29, bf16[14,3072]{1,0:T(8,128)(2,1)S(1)} %get-tuple-element.30, bf16[14,3072]{1,0:T(8,128)(2,1)S(1)} %get-tuple-element.28), kind=kOutput, calls=%fused_computation.2 | convolution fusion | flops 101044224 | bytes 324096 | tf_op jit(solution)/shard_map/dot_general | solution.py:245
  27.9 3.8 %shard_map.56 = (f32[14,64,128]{2,1,0:T(8,128)}, f32[14,192]{1,0:T(8,128)}, f32[14,512]{1,0:T(8,128)}) custom-call(f32[14,64,128]{2,1,0:T(8,128)} %bitcast.70, f32[14,8,128]{2,1,0:T(8,128)} %pad_maximum_fusion.refs_1_, f32[128,192]{1,0:T(8,128)} %get-tuple-element.13.refs_2_, f32[64,192]{1,0:T(8,128)} %get-tuple-element.14.refs_3_, ...), custom_call_target="tpu_custom_call" | custom-call | tf_op jit(solution)/shard_map/pallas_call | solution.py:130
  31.7 1.8 %collective-permute-start.5 = (f32[14,192]{1,0:T(8,128)}, f32[14,192]{1,0:T(8,128)S(1)}, u32[]{:S(2)}, u32[]{:S(2)}) collective-permute-start(f32[14,192]{1,0:T(8,128)} %get-tuple-element.17), channel_id=1, source_target_pairs={{0,16},{16,0},{1,17},{17,1},{2,18},{18,2},{3,19},{19,3},{4,20},{20... | collective-permute-start | bytes 32264 | tf_op jit(solution)/shard_map/ppermute | solution.py:263
  33.4 2.2 %collective-permute-done.5 = f32[14,192]{1,0:T(8,128)S(1)} collective-permute-done((f32[14,192]{1,0:T(8,128)}, f32[14,192]{1,0:T(8,128)S(1)}, u32[]{:S(2)}, u32[]{:S(2)}) %collective-permute-start.5) | collective-permute-done | bytes 10784 | tf_op jit(solution)/shard_map/ppermute | solution.py:263
  35.6 0.8 %maximum_bitcast_fusion.3 = f32[1,14,704]{2,1,0:T(8,128)S(1)} fusion(f32[14,512]{1,0:T(8,128)} %get-tuple-element.18, f32[14,192]{1,0:T(8,128)S(1)} %collective-permute-done.5), kind=kLoop, calls=%fused_computation.40 | loop fusion | flops 9856 | bytes 78848 | tf_op jit(solution)/shard_map/broadcast_in_dim | solution.py:252
  36.5 2.0 %collective-permute-start.6 = (f32[1,14,704]{2,1,0:T(8,128)S(1)}, f32[1,14,704]{2,1,0:T(8,128)S(1)}, u32[]{:S(2)}, u32[]{:S(2)}) collective-permute-start(f32[1,14,704]{2,1,0:T(8,128)S(1)} %maximum_bitcast_fusion.3), channel_id=1, source_target_pairs={{0,4},{4,0},{8,12},{12,8},{1,5},{5,1},{9,13},{13,9},{2,6},{6,2},{1... | collective-permute-start | bytes 118280 | tf_op jit(solution)/shard_map/ppermute | solution.py:255
  38.4 1.3 %fusion.21 = (f32[14,64,2]{2,1,0:T(8,128)S(1)}, f32[14,64,2]{2,1,0:T(8,128)S(1)}) fusion(f32[14,64,128]{2,1,0:T(8,128)} %get-tuple-element.16.refs_0_), kind=kLoop, calls=%fused_computation.73 | loop fusion | bytes 28672 | tf_op jit(solution)/shard_map/slice | solution.py:271
  40.6 3.5 %collective-permute-start.7 = (f32[2,14,704]{2,1,0:T(8,128)S(1)}, f32[2,14,704]{2,1,0:T(8,128)S(1)}, u32[]{:S(2)}, u32[]{:S(2)}) collective-permute-start(f32[2,14,704]{2,1,0:T(8,128)S(1)} %maximum_select_fusion.7), channel_id=1, source_target_pairs={{0,8},{4,12},{8,0},{12,4},{1,9},{5,13},{9,1},{13,5},{2,10},{6,14},... | collective-permute-start | bytes 236552 | tf_op jit(solution)/shard_map/ppermute | solution.py:255
  44.1 2.5 %collective-permute-done.7 = f32[2,14,704]{2,1,0:T(8,128)S(1)} collective-permute-done((f32[2,14,704]{2,1,0:T(8,128)S(1)}, f32[2,14,704]{2,1,0:T(8,128)S(1)}, u32[]{:S(2)}, u32[]{:S(2)}) %collective-permute-start.7) | collective-permute-done | bytes 78880 | tf_op jit(solution)/shard_map/ppermute | solution.py:255
  46.9 1.2 %collective-permute-done.8 = f32[1,14,1024]{2,1,0:T(8,128)S(1)} collective-permute-done((f32[1,14,1024]{2,1,0:T(8,128)S(1)}, f32[1,14,1024]{2,1,0:T(8,128)S(1)}, u32[]{:S(2)}, u32[]{:S(2)}) %collective-permute-start.8) | collective-permute-done | bytes 57376 | tf_op jit(solution)/shard_map/ppermute | solution.py:255
  48.2 1.6 %collective-permute-start.9 = (f32[2,14,1024]{2,1,0:T(8,128)S(1)}, f32[2,14,1024]{2,1,0:T(8,128)S(1)}, u32[]{:S(2)}, u32[]{:S(2)}) collective-permute-start(f32[2,14,1024]{2,1,0:T(8,128)S(1)} %maximum_select_fusion.5), channel_id=1, source_target_pairs={{0,2},{1,3},{2,0},{3,1},{4,6},{5,7},{6,4},{7,5},{8,10},{9,11},{10,... | collective-permute-start | bytes 344072 | tf_op jit(solution)/shard_map/ppermute | solution.py:255
  49.9 3.9 %collective-permute-done.9 = f32[2,14,1024]{2,1,0:T(8,128)S(1)} collective-permute-done((f32[2,14,1024]{2,1,0:T(8,128)S(1)}, f32[2,14,1024]{2,1,0:T(8,128)S(1)}, u32[]{:S(2)}, u32[]{:S(2)}) %collective-permute-start.9) | collective-permute-done | bytes 114720 | tf_op jit(solution)/shard_map/ppermute | solution.py:255
  54.8 1.0 %fusion = f32[42,384]{1,0:T(8,128)S(1)} fusion(s32[384]{0:T(512)S(1)} %pad_add_fusion, bf16[14,3072]{1,0:T(8,128)(2,1)S(1)} %get-tuple-element.26, bf16[14,3072]{1,0:T(8,128)(2,1)S(1)} %get-tuple-element.27, bf16[14,3072]{1,0:T(8,128)(2,1)S(1)} %get-tuple-element.25), kind=kOutput, calls=%fused_computation.1 | convolution fusion | flops 101044224 | bytes 324096 | tf_op jit(solution)/shard_map/dot_general | solution.py:245
  57.0 3.4 %shard_map.57 = f32[14,64,128]{2,1,0:T(8,128)} custom-call(f32[14,64,128]{2,1,0:T(8,128)} %get-tuple-element.16.refs_0_, f32[14,8,128]{2,1,0:T(8,128)} %pad_maximum_fusion.1.refs_1_, f32[14,64,128]{2,1,0:T(8,128)} %bitcast.71), custom_call_target="tpu_custom_call" | custom-call | tf_op jit(solution)/shard_map/pallas_call | solution.py:130
  (92 shorter events, 7.1 us)
Async XLA Ops:
  0.0 5.6 %copy-start = (f32[1,7,2,64,128]{4,3,2,1,0:T(8,128)S(1)}, f32[1,7,2,64,128]{4,3,2,1,0:T(8,128)}, u32[]{:S(2)}) copy-start(f32[1,7,2,64,128]{4,3,2,1,0:T(8,128)} %param.5) | copy-start | bytes 1376260
  2.6 4.9 %collective-permute-start = (f32[14,192]{1,0:T(8,128)}, f32[14,192]{1,0:T(8,128)S(1)}, u32[]{:S(2)}, u32[]{:S(2)}) collective-permute-start(f32[14,192]{1,0:T(8,128)} %get-tuple-element.12), channel_id=1, source_target_pairs={{0,16},{16,0},{1,17},{17,1},{2,18},{18,2},{3,19},{19,3},{4,20},{20... | collective-permute-start | bytes 32264 | tf_op jit(solution)/shard_map/ppermute | solution.py:263
  5.6 0.7 %copy-start.3 = (s32[1,1,1,768]{3,2,1,0:T(1,128)S(1)}, s32[1,1,1,768]{3,2,1,0:T(1,128)}, u32[]{:S(2)}) copy-start(s32[1,1,1,768]{3,2,1,0:T(1,128)} %param.6) | copy-start | bytes 9220
  7.6 4.1 %collective-permute-start.1 = (f32[1,14,704]{2,1,0:T(8,128)S(1)}, f32[1,14,704]{2,1,0:T(8,128)S(1)}, u32[]{:S(2)}, u32[]{:S(2)}) collective-permute-start(f32[1,14,704]{2,1,0:T(8,128)S(1)} %maximum_bitcast_fusion.2), channel_id=1, source_target_pairs={{0,4},{4,0},{8,12},{12,8},{1,5},{5,1},{9,13},{13,9},{2,6},{6,2},{1... | collective-permute-start | bytes 118280 | tf_op jit(solution)/shard_map/ppermute | solution.py:255
  11.8 5.7 %collective-permute-start.2 = (f32[2,14,704]{2,1,0:T(8,128)S(1)}, f32[2,14,704]{2,1,0:T(8,128)S(1)}, u32[]{:S(2)}, u32[]{:S(2)}) collective-permute-start(f32[2,14,704]{2,1,0:T(8,128)S(1)} %maximum_select_fusion.6), channel_id=1, source_target_pairs={{0,8},{4,12},{8,0},{12,4},{1,9},{5,13},{9,1},{13,5},{2,10},{6,14},... | collective-permute-start | bytes 236552 | tf_op jit(solution)/shard_map/ppermute | solution.py:255
  17.7 1.3 %collective-permute-start.3 = (f32[1,14,1024]{2,1,0:T(8,128)S(1)}, f32[1,14,1024]{2,1,0:T(8,128)S(1)}, u32[]{:S(2)}, u32[]{:S(2)}) collective-permute-start(f32[1,14,1024]{2,1,0:T(8,128)S(1)} %maximum_bitcast_fusion), channel_id=1, source_target_pairs={{0,1},{1,0},{2,3},{3,2},{4,5},{5,4},{6,7},{7,6},{8,9},{9,8},{10,11... | collective-permute-start | bytes 172040 | tf_op jit(solution)/shard_map/ppermute | solution.py:255
  19.0 5.7 %collective-permute-start.4 = (f32[2,14,1024]{2,1,0:T(8,128)S(1)}, f32[2,14,1024]{2,1,0:T(8,128)S(1)}, u32[]{:S(2)}, u32[]{:S(2)}) collective-permute-start(f32[2,14,1024]{2,1,0:T(8,128)S(1)} %maximum_select_fusion.4), channel_id=1, source_target_pairs={{0,2},{1,3},{2,0},{3,1},{4,6},{5,7},{6,4},{7,5},{8,10},{9,11},{10,... | collective-permute-start | bytes 344072 | tf_op jit(solution)/shard_map/ppermute | solution.py:255
  24.7 0.7 %copy-start.2 = (f32[4,14,1024]{2,1,0:T(8,128)}, f32[4,14,1024]{2,1,0:T(8,128)S(1)}, u32[]{:S(2)}) copy-start(f32[4,14,1024]{2,1,0:T(8,128)S(1)} %maximum_select_fusion) | copy-start | bytes 688132
  25.8 1.2 %slice-start.1 = ((f32[4,14,1024]{2,1,0:T(8,128)}), f32[4,14,256]{2,1,0:T(8,128)S(1)}, s32[]{:S(2)}) async-start(f32[4,14,1024]{2,1,0:T(8,128)} %copy-done.2), calls=%async_computation.1 | async-start | bytes 131072 | tf_op jit(solution)/shard_map/slice | solution.py:278
  31.7 3.9 %collective-permute-start.5 = (f32[14,192]{1,0:T(8,128)}, f32[14,192]{1,0:T(8,128)S(1)}, u32[]{:S(2)}, u32[]{:S(2)}) collective-permute-start(f32[14,192]{1,0:T(8,128)} %get-tuple-element.17), channel_id=1, source_target_pairs={{0,16},{16,0},{1,17},{17,1},{2,18},{18,2},{3,19},{19,3},{4,20},{20... | collective-permute-start | bytes 32264 | tf_op jit(solution)/shard_map/ppermute | solution.py:263
  36.5 4.1 %collective-permute-start.6 = (f32[1,14,704]{2,1,0:T(8,128)S(1)}, f32[1,14,704]{2,1,0:T(8,128)S(1)}, u32[]{:S(2)}, u32[]{:S(2)}) collective-permute-start(f32[1,14,704]{2,1,0:T(8,128)S(1)} %maximum_bitcast_fusion.3), channel_id=1, source_target_pairs={{0,4},{4,0},{8,12},{12,8},{1,5},{5,1},{9,13},{13,9},{2,6},{6,2},{1... | collective-permute-start | bytes 118280 | tf_op jit(solution)/shard_map/ppermute | solution.py:255
  40.6 6.1 %collective-permute-start.7 = (f32[2,14,704]{2,1,0:T(8,128)S(1)}, f32[2,14,704]{2,1,0:T(8,128)S(1)}, u32[]{:S(2)}, u32[]{:S(2)}) collective-permute-start(f32[2,14,704]{2,1,0:T(8,128)S(1)} %maximum_select_fusion.7), channel_id=1, source_target_pairs={{0,8},{4,12},{8,0},{12,4},{1,9},{5,13},{9,1},{13,5},{2,10},{6,14},... | collective-permute-start | bytes 236552 | tf_op jit(solution)/shard_map/ppermute | solution.py:255
  46.8 1.3 %collective-permute-start.8 = (f32[1,14,1024]{2,1,0:T(8,128)S(1)}, f32[1,14,1024]{2,1,0:T(8,128)S(1)}, u32[]{:S(2)}, u32[]{:S(2)}) collective-permute-start(f32[1,14,1024]{2,1,0:T(8,128)S(1)} %maximum_bitcast_fusion.1), channel_id=1, source_target_pairs={{0,1},{1,0},{2,3},{3,2},{4,5},{5,4},{6,7},{7,6},{8,9},{9,8},{10,11... | collective-permute-start | bytes 172040 | tf_op jit(solution)/shard_map/ppermute | solution.py:255
  48.2 5.6 %collective-permute-start.9 = (f32[2,14,1024]{2,1,0:T(8,128)S(1)}, f32[2,14,1024]{2,1,0:T(8,128)S(1)}, u32[]{:S(2)}, u32[]{:S(2)}) collective-permute-start(f32[2,14,1024]{2,1,0:T(8,128)S(1)} %maximum_select_fusion.5), channel_id=1, source_target_pairs={{0,2},{1,3},{2,0},{3,1},{4,6},{5,7},{6,4},{7,5},{8,10},{9,11},{10,... | collective-permute-start | bytes 344072 | tf_op jit(solution)/shard_map/ppermute | solution.py:255
  53.8 0.7 %copy-start.1 = (f32[4,14,1024]{2,1,0:T(8,128)}, f32[4,14,1024]{2,1,0:T(8,128)S(1)}, u32[]{:S(2)}) copy-start(f32[4,14,1024]{2,1,0:T(8,128)S(1)} %maximum_select_fusion.1) | copy-start | bytes 688132
  54.8 1.2 %slice-start = ((f32[4,14,1024]{2,1,0:T(8,128)}), f32[4,14,256]{2,1,0:T(8,128)S(1)}, s32[]{:S(2)}) async-start(f32[4,14,1024]{2,1,0:T(8,128)} %copy-done.1), calls=%async_computation | async-start | bytes 131072 | tf_op jit(solution)/shard_map/slice | solution.py:278

commit v19 on v17

--- a/solution.py
+++ b/solution.py
@@ -91,6 +91,9 @@
             section = x + time_step * rate
             if first:
                 o_ref[plane(c)] = section
+                k = plane(c)
+                for slot, line in enumerate((0, 1, height - 2, height - 1)):
+                    don_ref[k : k + 1, slot * width : (slot + 1) * width] = section[line : line + 1, :]
             else:
                 o_ref[plane(c)] = 0.5 * base_ref[plane(c)] + 0.5 * section
 
@@ -113,13 +116,16 @@
         store(6, x6, -adv_u_6 + diffusivity * lap_of(6, x6, lap_6))
 
     if first:
-        donate_planes(lambda k: o_ref[k], planes, lon_ref[...], lat_ref[...], turn_ref, don_ref)
+        donate_planes(lambda k: o_ref[k], planes, lon_ref[...], lat_ref[...], turn_ref, don_ref, 4 * width)
 
 
 def advance(field, halo, base, lon, lat, turn, first):
     shape = jax.ShapeDtypeStruct(field.shape, field.dtype)
     if first:
-        shape = (shape, jax.ShapeDtypeStruct((field.shape[0], lon.shape[1]), jnp.float32))
+        shape = (
+            shape,
+            jax.ShapeDtypeStruct((field.shape[0], 4 * field.shape[2] + lon.shape[1]), jnp.float32),
+        )
     return pl.pallas_call(
         functools.partial(stencil_kernel, first=first),
         out_shape=shape,
@@ -143,7 +149,7 @@
     return weight_lon, weight_lat
 
 
-def donate_planes(plane_of, planes, weight_lon, weight_lat, turn_ref, out_ref):
+def donate_planes(plane_of, planes, weight_lon, weight_lat, turn_ref, out_ref, start):
     cosine = turn_ref[0:1, :]
     sine = turn_ref[1:2, :]
     values = []
@@ -158,7 +164,7 @@
             value = sine * values[k - 2] + cosine * values[k]
         else:
             value = values[k]
-        out_ref[k : k + 1, :] = value
+        out_ref[k : k + 1, start : start + value.shape[1]] = value
 
 
 def donation_kernel(f_ref, cells_ref, frac_ref, angle_ref, out_ref, lon_ref, lat_ref, turn_ref):
@@ -169,7 +175,10 @@
     weight_lon, weight_lat = donation_weights(cells_ref, frac_ref, rows, cols)
     lon_ref[...] = weight_lon
     lat_ref[...] = weight_lat
-    donate_planes(lambda k: f_ref[k], planes, weight_lon, weight_lat, turn_ref, out_ref)
+    for k in range(planes):
+        for slot, line in enumerate((0, 1, rows - 2, rows - 1)):
+            out_ref[k : k + 1, slot * cols : (slot + 1) * cols] = f_ref[k, line : line + 1, :]
+    donate_planes(lambda k: f_ref[k], planes, weight_lon, weight_lat, turn_ref, out_ref, 4 * cols)
 
 
 def first_donation(field, cells, frac, turn):
@@ -178,7 +187,7 @@
     return pl.pallas_call(
         donation_kernel,
         out_shape=(
-            jax.ShapeDtypeStruct((planes, dons), jnp.float32),
+            jax.ShapeDtypeStruct((planes, 4 * cols + dons), jnp.float32),
             jax.ShapeDtypeStruct((cols, dons), jnp.float32),
             jax.ShapeDtypeStruct((rows, dons), jnp.float32),
             jax.ShapeDtypeStruct((2, dons), jnp.float32),
@@ -251,22 +260,21 @@
             k *= 2
         return held
 
-    def section(field, donation):
+    def section(field, packet):
         flat = field
-        given = lax.ppermute(donation, "panel", [(0, 1), (1, 0)])
-        dons = given.shape[1]
-        side_rows = jnp.concatenate([flat[:, :2, :], flat[:, rows - 2 :, :]], axis=1)
-        lat_packet = jnp.concatenate([given, side_rows.reshape(comps * levels, -1)], axis=1)
-        lat_all = gather(lat_packet, "lat")
-        col_given = jnp.transpose(lat_all[:, :, :dons], (1, 0, 2)).reshape(comps * levels, -1)
-        side_rows = lat_all[:, :, dons:].reshape(lat_count, comps, levels, 4, cols)
+        edge = 4 * cols
+        dons = packet.shape[1] - edge
+        lat_all = gather(packet, "lat")
+        side_rows = lat_all[:, :, :edge].reshape(lat_count, comps, levels, 4, cols)
+        col_given = jnp.transpose(lat_all[:, :, edge:], (1, 0, 2)).reshape(comps * levels, -1)
         side_cols = jnp.concatenate([flat[:, :, :2], flat[:, :, cols - 2 :]], axis=2)
         side_cols = jnp.swapaxes(side_cols, 1, 2)
         lon_packet = jnp.concatenate([col_given, side_cols.reshape(comps * levels, -1)], axis=1)
         lon_all = gather(lon_packet, "lon")
         width = col_given.shape[1]
-        partner = lon_all[:, :, :width].reshape(lon_count, comps * levels, lat_count, dons)
-        partner = jnp.transpose(partner, (1, 2, 0, 3)).reshape(comps * levels, -1)
+        own = lon_all[:, :, :width].reshape(lon_count, comps * levels, lat_count, dons)
+        own = jnp.transpose(own, (1, 2, 0, 3)).reshape(comps * levels, -1)
+        partner = lax.ppermute(own, "panel", [(0, 1), (1, 0)])
         side_cols = lon_all[:, :, width:].reshape(lon_count, comps, levels, 4, rows)
         up = lax.dynamic_index_in_dim(side_rows, jnp.maximum(lat_pos - 1, 0), keepdims=False)[:, :, 2:]
         down = lax.dynamic_index_in_dim(side_rows, jnp.minimum(lat_pos + 1, lat_count - 1), keepdims=False)[:, :, :2]

time: 60.8 us -> 63.4 us (1.043)
  waiting for transfers between devices: 20 us -> 26.1 us
  local copies, waits for them, and re-layouts: 7.09 us -> 4.78 us
  other arithmetic: 2.39 us -> 1.73 us
    ppermute x2, waiting for transfers between devices: 3.32 us -> 8.59 us  [section(): partner = lax.ppermute(own, 'panel', [(0, 1), (1, 0)])]
    ppermute x2, starting transfers between devices: 4.79 us -> 3.39 us  [section(): partner = lax.ppermute(own, 'panel', [(0, 1), (1, 0)])]
    unnamed x12 -> x8, local copies, waits for them, and re-layouts: 1.18 us -> 0.02 us
    slice x4 -> x2, local copies, waits for them, and re-layouts: 1.1 us -> 0.02 us  [section(): side_rows = lat_all[:, :, :edge].reshape(lat_count, comps, levels, 4, cols)]
    ppermute x8, starting transfers between devices: 14 us -> 14.9 us  [gather(): other = lax.ppermute(held, axis, [(i, i ^ k) for i in range(size)])]
    ppermute x8, waiting for transfers between devices: 16.6 us -> 17.5 us  [gather(): other = lax.ppermute(held, axis, [(i, i ^ k) for i in range(size)])]
where the time goes in v19:
time: 63.4 us; the launch traced here: 63.2 us
  waiting for transfers between devices  26.1 us (41%)
  starting transfers between devices  18.3 us (29%)
  Pallas kernels  9.83 us (16%)
  local copies, waits for them, and re-layouts  4.78 us (8%)
  matrix products  1.98 us (3%)
  other arithmetic  1.73 us (3%)
    ppermute x8, waiting for transfers between devices, gather(): other = lax.ppermute(held, axis, [(i, i ^ k) for i in range(size)])  17.5 us
    ppermute x8, starting transfers between devices, gather(): other = lax.ppermute(held, axis, [(i, i ^ k) for i in range(size)])  14.9 us
    ppermute x2, waiting for transfers between devices, section(): partner = lax.ppermute(own, 'panel', [(0, 1), (1, 0)])  8.59 us
    pallas_call x2, Pallas kernels, advance(): pl.pallas_call(functools.partial(stencil_kernel, first=first), out_shape=...  7.19 us
    ppermute x2, starting transfers between devices, section(): partner = lax.ppermute(own, 'panel', [(0, 1), (1, 0)])  3.39 us
    pallas_call x1, Pallas kernels, first_donation(): pl.pallas_call(donation_kernel, out_shape=(jax.ShapeDtypeStruct((planes,...  2.64 us
    slice x6, local copies, waits for them, and re-layouts, section(): side_cols = jnp.concatenate([flat[:, :, :2], flat[:, :, cols - 2:]], axis=2)  2.34 us
    dot_general x2, matrix products, select(): picked = jnp.dot(parts, pick, preferred_element_type=jnp.float32)  1.98 us
  transfers between devices with their start and end apart: 10, of which 10 were waited for; matrix products, arithmetic and copies ran while one was open for 5% of the time, Pallas kernels for 0%

profile of v19, /device:TPU:0, one launch (start us, length us, event | category | flops | bytes accessed | tf_op | source)
XLA Modules:
  0.0 63.2 jit_solution(8797273804968318187)
XLA Ops:
  0.0 2.6 %shard_map.55 = (f32[14,704]{1,0:T(8,128)}, f32[128,192]{1,0:T(8,128)}, f32[64,192]{1,0:T(8,128)}, f32[2,192]{1,0:T(2,128)}) custom-call(f32[14,64,128]{2,1,0:T(8,128)} %bitcast.64, s32[1,192]{1,0:T(1,128)} %bitcast.84, f32[2,192]{1,0:T(2,128)} %bitcast.83, f32[1,192]{1,0:T(1,128)} %bitcast.85), custom_call_target="tpu_custom_call" | custom-call | tf_op jit(solution)/shard_map/pallas_call | solution.py:187
  2.6 3.0 %collective-permute-start = (f32[1,14,704]{2,1,0:T(8,128)}, f32[1,14,704]{2,1,0:T(8,128)S(1)}, u32[]{:S(2)}, u32[]{:S(2)}) collective-permute-start(f32[1,14,704]{2,1,0:T(8,128)} %bitcast.78), channel_id=1, source_target_pairs={{0,4},{4,0},{8,12},{12,8},{1,5},{5,1},{9,13},{13,9},{2,6},{6,2},{1... | collective-permute-start | bytes 118280 | tf_op jit(solution)/shard_map/ppermute | solution.py:257
  6.3 1.6 %collective-permute-done = f32[1,14,704]{2,1,0:T(8,128)S(1)} collective-permute-done((f32[1,14,704]{2,1,0:T(8,128)}, f32[1,14,704]{2,1,0:T(8,128)S(1)}, u32[]{:S(2)}, u32[]{:S(2)}) %collective-permute-start) | collective-permute-done | bytes 39456 | tf_op jit(solution)/shard_map/ppermute | solution.py:257
  8.0 3.1 %collective-permute-start.1 = (f32[2,14,704]{2,1,0:T(8,128)S(1)}, f32[2,14,704]{2,1,0:T(8,128)S(1)}, u32[]{:S(2)}, u32[]{:S(2)}) collective-permute-start(f32[2,14,704]{2,1,0:T(8,128)S(1)} %maximum_select_fusion.6), channel_id=1, source_target_pairs={{0,8},{4,12},{8,0},{12,4},{1,9},{5,13},{9,1},{13,5},{2,10},{6,14},... | collective-permute-start | bytes 236552 | tf_op jit(solution)/shard_map/ppermute | solution.py:257
  11.2 2.6 %collective-permute-done.1 = f32[2,14,704]{2,1,0:T(8,128)S(1)} collective-permute-done((f32[2,14,704]{2,1,0:T(8,128)S(1)}, f32[2,14,704]{2,1,0:T(8,128)S(1)}, u32[]{:S(2)}, u32[]{:S(2)}) %collective-permute-start.1) | collective-permute-done | bytes 78880 | tf_op jit(solution)/shard_map/ppermute | solution.py:257
  14.1 1.2 %collective-permute-done.2 = f32[1,14,1024]{2,1,0:T(8,128)S(1)} collective-permute-done((f32[1,14,1024]{2,1,0:T(8,128)S(1)}, f32[1,14,1024]{2,1,0:T(8,128)S(1)}, u32[]{:S(2)}, u32[]{:S(2)}) %collective-permute-start.2) | collective-permute-done | bytes 57376 | tf_op jit(solution)/shard_map/ppermute | solution.py:257
  15.3 1.8 %collective-permute-start.3 = (f32[2,14,1024]{2,1,0:T(8,128)S(1)}, f32[2,14,1024]{2,1,0:T(8,128)S(1)}, u32[]{:S(2)}, u32[]{:S(2)}) collective-permute-start(f32[2,14,1024]{2,1,0:T(8,128)S(1)} %maximum_select_fusion.4), channel_id=1, source_target_pairs={{0,2},{1,3},{2,0},{3,1},{4,6},{5,7},{6,4},{7,5},{8,10},{9,11},{10,... | collective-permute-start | bytes 344072 | tf_op jit(solution)/shard_map/ppermute | solution.py:257
  17.2 3.8 %collective-permute-done.3 = f32[2,14,1024]{2,1,0:T(8,128)S(1)} collective-permute-done((f32[2,14,1024]{2,1,0:T(8,128)S(1)}, f32[2,14,1024]{2,1,0:T(8,128)S(1)}, u32[]{:S(2)}, u32[]{:S(2)}) %collective-permute-start.3) | collective-permute-done | bytes 114720 | tf_op jit(solution)/shard_map/ppermute | solution.py:257
  21.6 1.8 %collective-permute-start.4 = (f32[14,3072]{1,0:T(8,128)S(1)}, f32[14,3072]{1,0:T(8,128)S(1)}, u32[]{:S(2)}, u32[]{:S(2)}) collective-permute-start(f32[14,3072]{1,0:T(8,128)S(1)} %reshape.93), channel_id=1, source_target_pairs={{0,16},{16,0},{1,17},{17,1},{2,18},{18,2},{3,19},{19,3},{4,20},{20... | collective-permute-start | bytes 516104 | tf_op jit(solution)/shard_map/ppermute | solution.py:277
  23.6 4.2 %collective-permute-done.4 = f32[14,3072]{1,0:T(8,128)S(1)} collective-permute-done((f32[14,3072]{1,0:T(8,128)S(1)}, f32[14,3072]{1,0:T(8,128)S(1)}, u32[]{:S(2)}, u32[]{:S(2)}) %collective-permute-start.4) | collective-permute-done | bytes 172064 | tf_op jit(solution)/shard_map/ppermute | solution.py:277
  27.8 1.0 %fusion.1 = f32[42,384]{1,0:T(8,128)S(1)} fusion(s32[384]{0:T(512)S(1)} %pad_add_fusion, bf16[14,3072]{1,0:T(8,128)(2,1)S(1)} %get-tuple-element.25, bf16[14,3072]{1,0:T(8,128)(2,1)S(1)} %get-tuple-element.26, bf16[14,3072]{1,0:T(8,128)(2,1)S(1)} %get-tuple-element.24), kind=kOutput, calls=%fused_computation.2 | convolution fusion | flops 101044224 | bytes 324096 | tf_op jit(solution)/shard_map/dot_general | solution.py:247
  29.1 0.7 %pad_maximum_fusion.refs_1_ = f32[14,8,128]{2,1,0:T(8,128)} fusion(f32[14,4,128]{2,1,0:T(4,128)S(1)} %select_maximum_fusion.1, f32[14,2,128]{2,1,0:T(2,128)S(1)} %bitcast.75, f32[14,2,128]{2,1,0:T(2,128)S(1)} %bitcast.74), kind=kLoop, calls=%fused_computation.37 | loop fusion | flops 28672 | bytes 114688 | tf_op jit(solution)/shard_map/concatenate | solution.py:291
  29.8 3.8 %shard_map.56 = (f32[14,64,128]{2,1,0:T(8,128)}, f32[14,704]{1,0:T(8,128)}) custom-call(f32[14,64,128]{2,1,0:T(8,128)} %bitcast.65, f32[14,8,128]{2,1,0:T(8,128)} %pad_maximum_fusion.refs_1_, f32[128,192]{1,0:T(8,128)} %get-tuple-element.12.refs_2_, f32[64,192]{1,0:T(8,128)} %get-tuple-element.13.refs_3_, f32[2,192]{1,0:T(2,128)} %get-tuple-element.14.refs_4_), custom_call_target="tpu_custom_call" | custom-call | tf_op jit(solution)/shard_map/pallas_call | solution.py:129
  33.5 1.9 %collective-permute-start.5 = (f32[1,14,704]{2,1,0:T(8,128)}, f32[1,14,704]{2,1,0:T(8,128)S(1)}, u32[]{:S(2)}, u32[]{:S(2)}) collective-permute-start(f32[1,14,704]{2,1,0:T(8,128)} %bitcast.80), channel_id=1, source_target_pairs={{0,4},{4,0},{8,12},{12,8},{1,5},{5,1},{9,13},{13,9},{2,6},{6,2},{1... | collective-permute-start | bytes 118280 | tf_op jit(solution)/shard_map/ppermute | solution.py:257
  35.5 1.4 %fusion.21 = (f32[14,64,2]{2,1,0:T(8,128)S(1)}, f32[14,64,2]{2,1,0:T(8,128)S(1)}) fusion(f32[14,64,128]{2,1,0:T(8,128)} %get-tuple-element.15.refs_0_), kind=kLoop, calls=%fused_computation.70 | loop fusion | bytes 28672 | tf_op jit(solution)/shard_map/slice | solution.py:270
  37.8 3.4 %collective-permute-start.6 = (f32[2,14,704]{2,1,0:T(8,128)S(1)}, f32[2,14,704]{2,1,0:T(8,128)S(1)}, u32[]{:S(2)}, u32[]{:S(2)}) collective-permute-start(f32[2,14,704]{2,1,0:T(8,128)S(1)} %maximum_select_fusion.7), channel_id=1, source_target_pairs={{0,8},{4,12},{8,0},{12,4},{1,9},{5,13},{9,1},{13,5},{2,10},{6,14},... | collective-permute-start | bytes 236552 | tf_op jit(solution)/shard_map/ppermute | solution.py:257
  41.3 2.5 %collective-permute-done.6 = f32[2,14,704]{2,1,0:T(8,128)S(1)} collective-permute-done((f32[2,14,704]{2,1,0:T(8,128)S(1)}, f32[2,14,704]{2,1,0:T(8,128)S(1)}, u32[]{:S(2)}, u32[]{:S(2)}) %collective-permute-start.6) | collective-permute-done | bytes 78880 | tf_op jit(solution)/shard_map/ppermute | solution.py:257
  44.1 1.2 %collective-permute-done.7 = f32[1,14,1024]{2,1,0:T(8,128)S(1)} collective-permute-done((f32[1,14,1024]{2,1,0:T(8,128)S(1)}, f32[1,14,1024]{2,1,0:T(8,128)S(1)}, u32[]{:S(2)}, u32[]{:S(2)}) %collective-permute-start.7) | collective-permute-done | bytes 57376 | tf_op jit(solution)/shard_map/ppermute | solution.py:257
  45.3 1.6 %collective-permute-start.8 = (f32[2,14,1024]{2,1,0:T(8,128)S(1)}, f32[2,14,1024]{2,1,0:T(8,128)S(1)}, u32[]{:S(2)}, u32[]{:S(2)}) collective-permute-start(f32[2,14,1024]{2,1,0:T(8,128)S(1)} %maximum_select_fusion.5), channel_id=1, source_target_pairs={{0,2},{1,3},{2,0},{3,1},{4,6},{5,7},{6,4},{7,5},{8,10},{9,11},{10,... | collective-permute-start | bytes 344072 | tf_op jit(solution)/shard_map/ppermute | solution.py:257
  46.9 4.0 %collective-permute-done.8 = f32[2,14,1024]{2,1,0:T(8,128)S(1)} collective-permute-done((f32[2,14,1024]{2,1,0:T(8,128)S(1)}, f32[2,14,1024]{2,1,0:T(8,128)S(1)}, u32[]{:S(2)}, u32[]{:S(2)}) %collective-permute-start.8) | collective-permute-done | bytes 114720 | tf_op jit(solution)/shard_map/ppermute | solution.py:257
  51.6 1.6 %collective-permute-start.9 = (f32[14,3072]{1,0:T(8,128)S(1)}, f32[14,3072]{1,0:T(8,128)S(1)}, u32[]{:S(2)}, u32[]{:S(2)}) collective-permute-start(f32[14,3072]{1,0:T(8,128)S(1)} %reshape.106), channel_id=1, source_target_pairs={{0,16},{16,0},{1,17},{17,1},{2,18},{18,2},{3,19},{19,3},{4,20},{20... | collective-permute-start | bytes 516104 | tf_op jit(solution)/shard_map/ppermute | solution.py:277
  53.4 4.4 %collective-permute-done.9 = f32[14,3072]{1,0:T(8,128)S(1)} collective-permute-done((f32[14,3072]{1,0:T(8,128)S(1)}, f32[14,3072]{1,0:T(8,128)S(1)}, u32[]{:S(2)}, u32[]{:S(2)}) %collective-permute-start.9) | collective-permute-done | bytes 172064 | tf_op jit(solution)/shard_map/ppermute | solution.py:277
  57.8 1.0 %fusion = f32[42,384]{1,0:T(8,128)S(1)} fusion(s32[384]{0:T(512)S(1)} %pad_add_fusion, bf16[14,3072]{1,0:T(8,128)(2,1)S(1)} %get-tuple-element.22, bf16[14,3072]{1,0:T(8,128)(2,1)S(1)} %get-tuple-element.23, bf16[14,3072]{1,0:T(8,128)(2,1)S(1)} %get-tuple-element.21), kind=kOutput, calls=%fused_computation.1 | convolution fusion | flops 101044224 | bytes 324096 | tf_op jit(solution)/shard_map/dot_general | solution.py:247
  59.8 3.4 %shard_map.57 = f32[14,64,128]{2,1,0:T(8,128)} custom-call(f32[14,64,128]{2,1,0:T(8,128)} %get-tuple-element.15.refs_0_, f32[14,8,128]{2,1,0:T(8,128)} %pad_maximum_fusion.1.refs_1_, f32[14,64,128]{2,1,0:T(8,128)} %bitcast.66), custom_call_target="tpu_custom_call" | custom-call | tf_op jit(solution)/shard_map/pallas_call | solution.py:129
  (84 shorter events, 5.2 us)
Async XLA Ops:
  0.0 5.7 %copy-start = (f32[1,7,2,64,128]{4,3,2,1,0:T(8,128)S(1)}, f32[1,7,2,64,128]{4,3,2,1,0:T(8,128)}, u32[]{:S(2)}) copy-start(f32[1,7,2,64,128]{4,3,2,1,0:T(8,128)} %param.5) | copy-start | bytes 1376260
  2.6 5.3 %collective-permute-start = (f32[1,14,704]{2,1,0:T(8,128)}, f32[1,14,704]{2,1,0:T(8,128)S(1)}, u32[]{:S(2)}, u32[]{:S(2)}) collective-permute-start(f32[1,14,704]{2,1,0:T(8,128)} %bitcast.78), channel_id=1, source_target_pairs={{0,4},{4,0},{8,12},{12,8},{1,5},{5,1},{9,13},{13,9},{2,6},{6,2},{1... | collective-permute-start | bytes 118280 | tf_op jit(solution)/shard_map/ppermute | solution.py:257
  5.9 2.1 %copy-start.1 = (f32[14,704]{1,0:T(8,128)S(1)}, f32[14,704]{1,0:T(8,128)}, u32[]{:S(2)}) copy-start(f32[14,704]{1,0:T(8,128)} %get-tuple-element.11) | copy-start | bytes 118276
  8.0 5.8 %collective-permute-start.1 = (f32[2,14,704]{2,1,0:T(8,128)S(1)}, f32[2,14,704]{2,1,0:T(8,128)S(1)}, u32[]{:S(2)}, u32[]{:S(2)}) collective-permute-start(f32[2,14,704]{2,1,0:T(8,128)S(1)} %maximum_select_fusion.6), channel_id=1, source_target_pairs={{0,8},{4,12},{8,0},{12,4},{1,9},{5,13},{9,1},{13,5},{2,10},{6,14},... | collective-permute-start | bytes 236552 | tf_op jit(solution)/shard_map/ppermute | solution.py:257
  11.1 3.0 %copy-start.3 = (s32[1,1,1,768]{3,2,1,0:T(1,128)S(1)}, s32[1,1,1,768]{3,2,1,0:T(1,128)}, u32[]{:S(2)}) copy-start(s32[1,1,1,768]{3,2,1,0:T(1,128)} %param.6) | copy-start | bytes 9220
  14.0 1.3 %collective-permute-start.2 = (f32[1,14,1024]{2,1,0:T(8,128)S(1)}, f32[1,14,1024]{2,1,0:T(8,128)S(1)}, u32[]{:S(2)}, u32[]{:S(2)}) collective-permute-start(f32[1,14,1024]{2,1,0:T(8,128)S(1)} %maximum_bitcast_fusion), channel_id=1, source_target_pairs={{0,1},{1,0},{2,3},{3,2},{4,5},{5,4},{6,7},{7,6},{8,9},{9,8},{10,11... | collective-permute-start | bytes 172040 | tf_op jit(solution)/shard_map/ppermute | solution.py:257
  15.3 5.6 %collective-permute-start.3 = (f32[2,14,1024]{2,1,0:T(8,128)S(1)}, f32[2,14,1024]{2,1,0:T(8,128)S(1)}, u32[]{:S(2)}, u32[]{:S(2)}) collective-permute-start(f32[2,14,1024]{2,1,0:T(8,128)S(1)} %maximum_select_fusion.4), channel_id=1, source_target_pairs={{0,2},{1,3},{2,0},{3,1},{4,6},{5,7},{6,4},{7,5},{8,10},{9,11},{10,... | collective-permute-start | bytes 344072 | tf_op jit(solution)/shard_map/ppermute | solution.py:257
  21.6 6.2 %collective-permute-start.4 = (f32[14,3072]{1,0:T(8,128)S(1)}, f32[14,3072]{1,0:T(8,128)S(1)}, u32[]{:S(2)}, u32[]{:S(2)}) collective-permute-start(f32[14,3072]{1,0:T(8,128)S(1)} %reshape.93), channel_id=1, source_target_pairs={{0,16},{16,0},{1,17},{17,1},{2,18},{18,2},{3,19},{19,3},{4,20},{20... | collective-permute-start | bytes 516104 | tf_op jit(solution)/shard_map/ppermute | solution.py:277
  33.5 4.3 %collective-permute-start.5 = (f32[1,14,704]{2,1,0:T(8,128)}, f32[1,14,704]{2,1,0:T(8,128)S(1)}, u32[]{:S(2)}, u32[]{:S(2)}) collective-permute-start(f32[1,14,704]{2,1,0:T(8,128)} %bitcast.80), channel_id=1, source_target_pairs={{0,4},{4,0},{8,12},{12,8},{1,5},{5,1},{9,13},{13,9},{2,6},{6,2},{1... | collective-permute-start | bytes 118280 | tf_op jit(solution)/shard_map/ppermute | solution.py:257
  36.8 1.0 %copy-start.2 = (f32[14,704]{1,0:T(8,128)S(1)}, f32[14,704]{1,0:T(8,128)}, u32[]{:S(2)}) copy-start(f32[14,704]{1,0:T(8,128)} %get-tuple-element.16) | copy-start | bytes 118276
  37.8 6.0 %collective-permute-start.6 = (f32[2,14,704]{2,1,0:T(8,128)S(1)}, f32[2,14,704]{2,1,0:T(8,128)S(1)}, u32[]{:S(2)}, u32[]{:S(2)}) collective-permute-start(f32[2,14,704]{2,1,0:T(8,128)S(1)} %maximum_select_fusion.7), channel_id=1, source_target_pairs={{0,8},{4,12},{8,0},{12,4},{1,9},{5,13},{9,1},{13,5},{2,10},{6,14},... | collective-permute-start | bytes 236552 | tf_op jit(solution)/shard_map/ppermute | solution.py:257
  44.0 1.3 %collective-permute-start.7 = (f32[1,14,1024]{2,1,0:T(8,128)S(1)}, f32[1,14,1024]{2,1,0:T(8,128)S(1)}, u32[]{:S(2)}, u32[]{:S(2)}) collective-permute-start(f32[1,14,1024]{2,1,0:T(8,128)S(1)} %maximum_bitcast_fusion.1), channel_id=1, source_target_pairs={{0,1},{1,0},{2,3},{3,2},{4,5},{5,4},{6,7},{7,6},{8,9},{9,8},{10,11... | collective-permute-start | bytes 172040 | tf_op jit(solution)/shard_map/ppermute | solution.py:257
  45.3 5.6 %collective-permute-start.8 = (f32[2,14,1024]{2,1,0:T(8,128)S(1)}, f32[2,14,1024]{2,1,0:T(8,128)S(1)}, u32[]{:S(2)}, u32[]{:S(2)}) collective-permute-start(f32[2,14,1024]{2,1,0:T(8,128)S(1)} %maximum_select_fusion.5), channel_id=1, source_target_pairs={{0,2},{1,3},{2,0},{3,1},{4,6},{5,7},{6,4},{7,5},{8,10},{9,11},{10,... | collective-permute-start | bytes 344072 | tf_op jit(solution)/shard_map/ppermute | solution.py:257
  51.6 6.2 %collective-permute-start.9 = (f32[14,3072]{1,0:T(8,128)S(1)}, f32[14,3072]{1,0:T(8,128)S(1)}, u32[]{:S(2)}, u32[]{:S(2)}) collective-permute-start(f32[14,3072]{1,0:T(8,128)S(1)} %reshape.106), channel_id=1, source_target_pairs={{0,16},{16,0},{1,17},{17,1},{2,18},{18,2},{3,19},{19,3},{4,20},{20... | collective-permute-start | bytes 516104 | tf_op jit(solution)/shard_map/ppermute | solution.py:277

commit v20 on v17

--- a/solution.py
+++ b/solution.py
@@ -227,9 +227,20 @@
     lon_slots = jnp.where(on_left, slots[2 * band : 2 * band + side], slots[2 * band + side :])
     wanted = jnp.concatenate([lat_slots, lon_slots])
     total = lat_count * lon_count * cells.shape[0]
-    pick = (jnp.arange(total, dtype=jnp.int32)[:, None] == wanted[None, :]).astype(jnp.bfloat16)
-
-    def select(values):
+    dons_each = cells.shape[0]
+    half = lon_count // 2
+    chunk = jnp.arange(half * lat_count * dons_each, dtype=jnp.int32)
+
+    def pick_for(base):
+        block = chunk // (lat_count * dons_each)
+        lat_of = chunk // dons_each % lat_count
+        index = (lat_of * lon_count + base + block) * dons_each + chunk % dons_each
+        return (index[:, None] == wanted[None, :]).astype(jnp.bfloat16)
+
+    pick_held = pick_for(lon_pos // half * half)
+    pick_new = pick_for((lon_pos ^ half) // half * half)
+
+    def select(values, pick):
         high = lax.reduce_precision(values, exponent_bits=8, mantissa_bits=7)
         rest = values - high
         middle = lax.reduce_precision(rest, exponent_bits=8, mantissa_bits=7)
@@ -245,11 +256,12 @@
         held = packet[None]
         k = 1
         while k < size:
+            before = held
             other = lax.ppermute(held, axis, [(i, i ^ k) for i in range(size)])
             low = (pos // k) % 2 == 0
             held = jnp.where(low, jnp.concatenate([held, other]), jnp.concatenate([other, held]))
             k *= 2
-        return held
+        return held, before, other
 
     def section(field, donation):
         flat = field
@@ -257,22 +269,22 @@
         dons = given.shape[1]
         side_rows = jnp.concatenate([flat[:, :2, :], flat[:, rows - 2 :, :]], axis=1)
         lat_packet = jnp.concatenate([given, side_rows.reshape(comps * levels, -1)], axis=1)
-        lat_all = gather(lat_packet, "lat")
+        lat_all = gather(lat_packet, "lat")[0]
         col_given = jnp.transpose(lat_all[:, :, :dons], (1, 0, 2)).reshape(comps * levels, -1)
         side_rows = lat_all[:, :, dons:].reshape(lat_count, comps, levels, 4, cols)
         side_cols = jnp.concatenate([flat[:, :, :2], flat[:, :, cols - 2 :]], axis=2)
         side_cols = jnp.swapaxes(side_cols, 1, 2)
         lon_packet = jnp.concatenate([col_given, side_cols.reshape(comps * levels, -1)], axis=1)
-        lon_all = gather(lon_packet, "lon")
+        lon_all, lon_held, lon_new = gather(lon_packet, "lon")
         width = col_given.shape[1]
-        partner = lon_all[:, :, :width].reshape(lon_count, comps * levels, lat_count, dons)
-        partner = jnp.transpose(partner, (1, 2, 0, 3)).reshape(comps * levels, -1)
+        held_part = jnp.transpose(lon_held[:, :, :width], (1, 0, 2)).reshape(comps * levels, -1)
+        new_part = jnp.transpose(lon_new[:, :, :width], (1, 0, 2)).reshape(comps * levels, -1)
         side_cols = lon_all[:, :, width:].reshape(lon_count, comps, levels, 4, rows)
         up = lax.dynamic_index_in_dim(side_rows, jnp.maximum(lat_pos - 1, 0), keepdims=False)[:, :, 2:]
         down = lax.dynamic_index_in_dim(side_rows, jnp.minimum(lat_pos + 1, lat_count - 1), keepdims=False)[:, :, :2]
         left = lax.dynamic_index_in_dim(side_cols, jnp.maximum(lon_pos - 1, 0), keepdims=False)[:, :, 2:]
         right = lax.dynamic_index_in_dim(side_cols, jnp.minimum(lon_pos + 1, lon_count - 1), keepdims=False)[:, :, :2]
-        rim = select(partner).reshape(comps, levels, -1)
+        rim = (select(held_part, pick_held) + select(new_part, pick_new)).reshape(comps, levels, -1)
         rim_lat = rim[:, :, :band].reshape(comps, levels, 2, cols)
         rim_lon = rim[:, :, band:].reshape(comps, levels, 2, rows)
         up = jnp.where(on_top, rim_lat, up).reshape(comps * levels, 2, cols)

time: 60.8 us -> 58.5 us (0.962)
  waiting for transfers between devices: 20 us -> 18.5 us
  local copies, waits for them, and re-layouts: 7.09 us -> 5.64 us
    ppermute x8, waiting for transfers between devices: 16.6 us -> 15.7 us  [gather(): other = lax.ppermute(held, axis, [(i, i ^ k) for i in range(size)])]
    reshape x6 -> x2, local copies, waits for them, and re-layouts: 0.88 us -> 0.03 us  [section(): (select(held_part, pick_held) + select(new_part, pick_new)).reshape(comps...]
    dot_general x2 -> x4, matrix products: 1.98 us -> 2.34 us  [select(): picked = jnp.dot(parts, pick, preferred_element_type=jnp.float32)]
  transfers between devices with their start and end apart: 10 -> 10, of which waited for: 10 -> 10; matrix products, arithmetic and copies ran while one was open for 5% -> 7% of each run, Pallas kernels for 0% -> 0%
where the time goes in v20:
time: 58.5 us; the launch traced here: 58.2 us
  starting transfers between devices  18.8 us (32%)
  waiting for transfers between devices  18.5 us (32%)
  Pallas kernels  9.81 us (17%)
  local copies, waits for them, and re-layouts  5.64 us (10%)
  other arithmetic  2.44 us (4%)
  matrix products  2.34 us (4%)
  between operations  0.62 us (1%)
    ppermute x8, waiting for transfers between devices, gather(): other = lax.ppermute(held, axis, [(i, i ^ k) for i in range(size)])  15.7 us
    ppermute x8, starting transfers between devices, gather(): other = lax.ppermute(held, axis, [(i, i ^ k) for i in range(size)])  14 us
    pallas_call x2, Pallas kernels, advance(): pl.pallas_call(functools.partial(stencil_kernel, first=first), out_shape=...  7.18 us
    ppermute x2, starting transfers between devices, section(): given = lax.ppermute(donation, 'panel', [(0, 1), (1, 0)])  4.8 us
    ppermute x2, waiting for transfers between devices, section(): given = lax.ppermute(donation, 'panel', [(0, 1), (1, 0)])  2.82 us
    pallas_call x1, Pallas kernels, first_donation(): pl.pallas_call(donation_kernel, out_shape=(jax.ShapeDtypeStruct((planes,...  2.63 us
    dot_general x4, matrix products, select(): picked = jnp.dot(parts, pick, preferred_element_type=jnp.float32)  2.34 us
    slice x6, local copies, waits for them, and re-layouts, section(): side_cols = jnp.concatenate([flat[:, :, :2], flat[:, :, cols - 2:]], axis=2)  2.33 us
  transfers between devices with their start and end apart: 10, of which 10 were waited for; matrix products, arithmetic and copies ran while one was open for 7% of the time, Pallas kernels for 0%

profile of v20, /device:TPU:0, one launch (start us, length us, event | category | flops | bytes accessed | tf_op | source)
XLA Modules:
  0.0 58.2 jit_solution(16250750984455743575)
XLA Ops:
  0.0 2.6 %shard_map.55 = (f32[14,192]{1,0:T(8,128)}, f32[128,192]{1,0:T(8,128)}, f32[64,192]{1,0:T(8,128)}, f32[2,192]{1,0:T(2,128)}) custom-call(f32[14,64,128]{2,1,0:T(8,128)} %bitcast.78, s32[1,192]{1,0:T(1,128)} %bitcast.105, f32[2,192]{1,0:T(2,128)} %bitcast.104, f32[1,192]{1,0:T(1,128)} %bitcast.106), custom_call_target="tpu_custom_call" | custom-call | tf_op jit(solution)/shard_map/pallas_call | solution.py:178
  2.6 3.0 %collective-permute-start = (f32[14,192]{1,0:T(8,128)}, f32[14,192]{1,0:T(8,128)S(1)}, u32[]{:S(2)}, u32[]{:S(2)}) collective-permute-start(f32[14,192]{1,0:T(8,128)} %get-tuple-element.11), channel_id=1, source_target_pairs={{0,16},{16,0},{1,17},{17,1},{2,18},{18,2},{3,19},{19,3},{4,20},{20... | collective-permute-start | bytes 32264 | tf_op jit(solution)/shard_map/ppermute | solution.py:268
  6.8 0.7 %collective-permute-done = f32[14,192]{1,0:T(8,128)S(1)} collective-permute-done((f32[14,192]{1,0:T(8,128)}, f32[14,192]{1,0:T(8,128)S(1)}, u32[]{:S(2)}, u32[]{:S(2)}) %collective-permute-start) | collective-permute-done | bytes 10784 | tf_op jit(solution)/shard_map/ppermute | solution.py:268
  7.6 2.1 %collective-permute-start.1 = (f32[1,14,704]{2,0,1:T(1,128)S(1)}, f32[1,14,704]{2,0,1:T(1,128)S(1)}, u32[]{:S(2)}, u32[]{:S(2)}) collective-permute-start(f32[1,14,704]{2,0,1:T(1,128)S(1)} %broadcast_in_dim.16), channel_id=1, source_target_pairs={{0,4},{4,0},{8,12},{12,8},{1,5},{5,1},{9,13},{13,9},{2,6},{6,2},{1... | collective-permute-start | bytes 118280 | tf_op jit(solution)/shard_map/ppermute | solution.py:260
  9.9 1.8 %collective-permute-done.1 = f32[1,14,704]{2,0,1:T(1,128)S(1)} collective-permute-done((f32[1,14,704]{2,0,1:T(1,128)S(1)}, f32[1,14,704]{2,0,1:T(1,128)S(1)}, u32[]{:S(2)}, u32[]{:S(2)}) %collective-permute-start.1) | collective-permute-done | bytes 39456 | tf_op jit(solution)/shard_map/ppermute | solution.py:260
  11.9 3.1 %collective-permute-start.2 = (f32[2,14,704]{2,0,1:T(2,128)S(1)}, f32[2,14,704]{2,0,1:T(2,128)S(1)}, u32[]{:S(2)}, u32[]{:S(2)}) collective-permute-start(f32[2,14,704]{2,0,1:T(2,128)S(1)} %maximum_select_fusion.4), channel_id=1, source_target_pairs={{0,8},{4,12},{8,0},{12,4},{1,9},{5,13},{9,1},{13,5},{2,10},{6,14},... | collective-permute-start | bytes 236552 | tf_op jit(solution)/shard_map/ppermute | solution.py:260
  15.0 2.5 %collective-permute-done.2 = f32[2,14,704]{2,0,1:T(2,128)S(1)} collective-permute-done((f32[2,14,704]{2,0,1:T(2,128)S(1)}, f32[2,14,704]{2,0,1:T(2,128)S(1)}, u32[]{:S(2)}, u32[]{:S(2)}) %collective-permute-start.2) | collective-permute-done | bytes 78880 | tf_op jit(solution)/shard_map/ppermute | solution.py:260
  18.1 1.1 %collective-permute-done.3 = f32[1,14,1024]{2,1,0:T(8,128)S(1)} collective-permute-done((f32[1,14,1024]{2,1,0:T(8,128)S(1)}, f32[1,14,1024]{2,1,0:T(8,128)S(1)}, u32[]{:S(2)}, u32[]{:S(2)}) %collective-permute-start.3) | collective-permute-done | bytes 57376 | tf_op jit(solution)/shard_map/ppermute | solution.py:260
  19.2 1.9 %collective-permute-start.4 = (f32[2,14,1024]{2,1,0:T(8,128)S(1)}, f32[2,14,1024]{2,1,0:T(8,128)S(1)}, u32[]{:S(2)}, u32[]{:S(2)}) collective-permute-start(f32[2,14,1024]{2,1,0:T(8,128)S(1)} %maximum_select_fusion.2), channel_id=1, source_target_pairs={{0,2},{1,3},{2,0},{3,1},{4,6},{5,7},{6,4},{7,5},{8,10},{9,11},{10,... | collective-permute-start | bytes 344072 | tf_op jit(solution)/shard_map/ppermute | solution.py:260
  21.9 3.1 %collective-permute-done.4 = f32[2,14,1024]{2,1,0:T(8,128)S(1)} collective-permute-done((f32[2,14,1024]{2,1,0:T(8,128)S(1)}, f32[2,14,1024]{2,1,0:T(8,128)S(1)}, u32[]{:S(2)}, u32[]{:S(2)}) %collective-permute-start.4) | collective-permute-done | bytes 114720 | tf_op jit(solution)/shard_map/ppermute | solution.py:260
  26.2 0.6 %pad_maximum_fusion.4.refs_1_ = f32[14,8,128]{2,1,0:T(8,128)} fusion(f32[14,4,128]{2,1,0:T(4,128)S(1)} %select_maximum_fusion.1, f32[14,2,128]{2,1,0:T(2,128)S(1)} %bitcast.100, f32[14,2,128]{2,1,0:T(2,128)S(1)} %bitcast.99), kind=kLoop, calls=%fused_computation.76 | loop fusion | flops 28672 | bytes 114688 | tf_op jit(solution)/shard_map/concatenate | solution.py:295
  26.8 3.8 %shard_map.56 = (f32[14,64,128]{2,1,0:T(8,128)}, f32[14,192]{1,0:T(8,128)}) custom-call(f32[14,64,128]{2,1,0:T(8,128)} %bitcast.79, f32[14,8,128]{2,1,0:T(8,128)} %pad_maximum_fusion.4.refs_1_, f32[128,192]{1,0:T(8,128)} %get-tuple-element.12.refs_2_, f32[64,192]{1,0:T(8,128)} %get-tuple-element.13.refs_3_, f32[2,192]{1,0:T(2,128)} %get-tuple-element.14.refs_4_), custom_call_target="tpu_custom_call" | custom-call | tf_op jit(solution)/shard_map/pallas_call | solution.py:123
  30.6 0.9 %fusion.66 = (f32[14,2,128]{2,1,0:T(2,128)S(1)}, f32[14,2,128]{2,1,0:T(2,128)S(1)}) fusion(f32[14,64,128]{2,1,0:T(8,128)} %get-tuple-element.15.refs_0_), kind=kLoop, calls=%fused_computation.144 | loop fusion | bytes 57344 | tf_op jit(solution)/shard_map/slice | solution.py:270
  31.4 1.8 %collective-permute-start.5 = (f32[14,192]{1,0:T(8,128)}, f32[14,192]{1,0:T(8,128)S(1)}, u32[]{:S(2)}, u32[]{:S(2)}) collective-permute-start(f32[14,192]{1,0:T(8,128)} %get-tuple-element.16), channel_id=1, source_target_pairs={{0,16},{16,0},{1,17},{17,1},{2,18},{18,2},{3,19},{19,3},{4,20},{20... | collective-permute-start | bytes 32264 | tf_op jit(solution)/shard_map/ppermute | solution.py:268
  33.3 2.1 %collective-permute-done.5 = f32[14,192]{1,0:T(8,128)S(1)} collective-permute-done((f32[14,192]{1,0:T(8,128)}, f32[14,192]{1,0:T(8,128)S(1)}, u32[]{:S(2)}, u32[]{:S(2)}) %collective-permute-start.5) | collective-permute-done | bytes 10784 | tf_op jit(solution)/shard_map/ppermute | solution.py:268
  35.6 1.9 %collective-permute-start.6 = (f32[1,14,704]{2,0,1:T(1,128)S(1)}, f32[1,14,704]{2,0,1:T(1,128)S(1)}, u32[]{:S(2)}, u32[]{:S(2)}) collective-permute-start(f32[1,14,704]{2,0,1:T(1,128)S(1)} %broadcast_in_dim.18), channel_id=1, source_target_pairs={{0,4},{4,0},{8,12},{12,8},{1,5},{5,1},{9,13},{13,9},{2,6},{6,2},{1... | collective-permute-start | bytes 118280 | tf_op jit(solution)/shard_map/ppermute | solution.py:260
  37.5 1.3 %fusion.67 = (f32[14,64,2]{2,1,0:T(8,128)S(1)}, f32[14,64,2]{2,1,0:T(8,128)S(1)}) fusion(f32[14,64,128]{2,1,0:T(8,128)} %get-tuple-element.15.refs_0_), kind=kLoop, calls=%fused_computation.145 | loop fusion | bytes 28672 | tf_op jit(solution)/shard_map/slice | solution.py:275
  39.8 3.3 %collective-permute-start.7 = (f32[2,14,704]{2,0,1:T(2,128)S(1)}, f32[2,14,704]{2,0,1:T(2,128)S(1)}, u32[]{:S(2)}, u32[]{:S(2)}) collective-permute-start(f32[2,14,704]{2,0,1:T(2,128)S(1)} %maximum_select_fusion.5), channel_id=1, source_target_pairs={{0,8},{4,12},{8,0},{12,4},{1,9},{5,13},{9,1},{13,5},{2,10},{6,14},... | collective-permute-start | bytes 236552 | tf_op jit(solution)/shard_map/ppermute | solution.py:260
  43.2 2.4 %collective-permute-done.7 = f32[2,14,704]{2,0,1:T(2,128)S(1)} collective-permute-done((f32[2,14,704]{2,0,1:T(2,128)S(1)}, f32[2,14,704]{2,0,1:T(2,128)S(1)}, u32[]{:S(2)}, u32[]{:S(2)}) %collective-permute-start.7) | collective-permute-done | bytes 78880 | tf_op jit(solution)/shard_map/ppermute | solution.py:260
  46.1 1.1 %collective-permute-done.8 = f32[1,14,1024]{2,1,0:T(8,128)S(1)} collective-permute-done((f32[1,14,1024]{2,1,0:T(8,128)S(1)}, f32[1,14,1024]{2,1,0:T(8,128)S(1)}, u32[]{:S(2)}, u32[]{:S(2)}) %collective-permute-start.8) | collective-permute-done | bytes 57376 | tf_op jit(solution)/shard_map/ppermute | solution.py:260
  47.2 1.6 %collective-permute-start.9 = (f32[2,14,1024]{2,1,0:T(8,128)S(1)}, f32[2,14,1024]{2,1,0:T(8,128)S(1)}, u32[]{:S(2)}, u32[]{:S(2)}) collective-permute-start(f32[2,14,1024]{2,1,0:T(8,128)S(1)} %maximum_select_fusion.3), channel_id=1, source_target_pairs={{0,2},{1,3},{2,0},{3,1},{4,6},{5,7},{6,4},{7,5},{8,10},{9,11},{10,... | collective-permute-start | bytes 344072 | tf_op jit(solution)/shard_map/ppermute | solution.py:260
  49.6 3.3 %collective-permute-done.9 = f32[2,14,1024]{2,1,0:T(8,128)S(1)} collective-permute-done((f32[2,14,1024]{2,1,0:T(8,128)S(1)}, f32[2,14,1024]{2,1,0:T(8,128)S(1)}, u32[]{:S(2)}, u32[]{:S(2)}) %collective-permute-start.9) | collective-permute-done | bytes 114720 | tf_op jit(solution)/shard_map/ppermute | solution.py:260
  54.1 0.6 %pad_maximum_fusion.5.refs_1_ = f32[14,8,128]{2,1,0:T(8,128)} fusion(f32[14,4,128]{2,1,0:T(4,128)S(1)} %select_maximum_fusion, f32[14,2,128]{2,1,0:T(2,128)S(1)} %bitcast.96, f32[14,2,128]{2,1,0:T(2,128)S(1)} %bitcast.95), kind=kLoop, calls=%fused_computation.77 | loop fusion | flops 28672 | bytes 114688 | tf_op jit(solution)/shard_map/concatenate | solution.py:295
  54.8 3.4 %shard_map.57 = f32[14,64,128]{2,1,0:T(8,128)} custom-call(f32[14,64,128]{2,1,0:T(8,128)} %get-tuple-element.15.refs_0_, f32[14,8,128]{2,1,0:T(8,128)} %pad_maximum_fusion.5.refs_1_, f32[14,64,128]{2,1,0:T(8,128)} %bitcast.80), custom_call_target="tpu_custom_call" | custom-call | tf_op jit(solution)/shard_map/pallas_call | solution.py:123
  (100 shorter events, 7.5 us)
Async XLA Ops:
  0.0 5.6 %copy-start = (f32[1,7,2,64,128]{4,3,2,1,0:T(8,128)S(1)}, f32[1,7,2,64,128]{4,3,2,1,0:T(8,128)}, u32[]{:S(2)}) copy-start(f32[1,7,2,64,128]{4,3,2,1,0:T(8,128)} %param.5) | copy-start | bytes 1376260
  2.6 4.9 %collective-permute-start = (f32[14,192]{1,0:T(8,128)}, f32[14,192]{1,0:T(8,128)S(1)}, u32[]{:S(2)}, u32[]{:S(2)}) collective-permute-start(f32[14,192]{1,0:T(8,128)} %get-tuple-element.11), channel_id=1, source_target_pairs={{0,16},{16,0},{1,17},{17,1},{2,18},{18,2},{3,19},{19,3},{4,20},{20... | collective-permute-start | bytes 32264 | tf_op jit(solution)/shard_map/ppermute | solution.py:268
  5.6 0.7 %copy-start.1 = (s32[1,1,1,768]{3,2,1,0:T(1,128)S(1)}, s32[1,1,1,768]{3,2,1,0:T(1,128)}, u32[]{:S(2)}) copy-start(s32[1,1,1,768]{3,2,1,0:T(1,128)} %param.6) | copy-start | bytes 9220
  7.6 4.1 %collective-permute-start.1 = (f32[1,14,704]{2,0,1:T(1,128)S(1)}, f32[1,14,704]{2,0,1:T(1,128)S(1)}, u32[]{:S(2)}, u32[]{:S(2)}) collective-permute-start(f32[1,14,704]{2,0,1:T(1,128)S(1)} %broadcast_in_dim.16), channel_id=1, source_target_pairs={{0,4},{4,0},{8,12},{12,8},{1,5},{5,1},{9,13},{13,9},{2,6},{6,2},{1... | collective-permute-start | bytes 118280 | tf_op jit(solution)/shard_map/ppermute | solution.py:260
  11.9 5.6 %collective-permute-start.2 = (f32[2,14,704]{2,0,1:T(2,128)S(1)}, f32[2,14,704]{2,0,1:T(2,128)S(1)}, u32[]{:S(2)}, u32[]{:S(2)}) collective-permute-start(f32[2,14,704]{2,0,1:T(2,128)S(1)} %maximum_select_fusion.4), channel_id=1, source_target_pairs={{0,8},{4,12},{8,0},{12,4},{1,9},{5,13},{9,1},{13,5},{2,10},{6,14},... | collective-permute-start | bytes 236552 | tf_op jit(solution)/shard_map/ppermute | solution.py:260
  17.9 1.3 %collective-permute-start.3 = (f32[1,14,1024]{2,1,0:T(8,128)S(1)}, f32[1,14,1024]{2,1,0:T(8,128)S(1)}, u32[]{:S(2)}, u32[]{:S(2)}) collective-permute-start(f32[1,14,1024]{2,1,0:T(8,128)S(1)} %maximum_bitcast_fusion), channel_id=1, source_target_pairs={{0,1},{1,0},{2,3},{3,2},{4,5},{5,4},{6,7},{7,6},{8,9},{9,8},{10,11... | collective-permute-start | bytes 172040 | tf_op jit(solution)/shard_map/ppermute | solution.py:260
  19.2 5.7 %collective-permute-start.4 = (f32[2,14,1024]{2,1,0:T(8,128)S(1)}, f32[2,14,1024]{2,1,0:T(8,128)S(1)}, u32[]{:S(2)}, u32[]{:S(2)}) collective-permute-start(f32[2,14,1024]{2,1,0:T(8,128)S(1)} %maximum_select_fusion.2), channel_id=1, source_target_pairs={{0,2},{1,3},{2,0},{3,1},{4,6},{5,7},{6,4},{7,5},{8,10},{9,11},{10,... | collective-permute-start | bytes 344072 | tf_op jit(solution)/shard_map/ppermute | solution.py:260
  31.4 4.0 %collective-permute-start.5 = (f32[14,192]{1,0:T(8,128)}, f32[14,192]{1,0:T(8,128)S(1)}, u32[]{:S(2)}, u32[]{:S(2)}) collective-permute-start(f32[14,192]{1,0:T(8,128)} %get-tuple-element.16), channel_id=1, source_target_pairs={{0,16},{16,0},{1,17},{17,1},{2,18},{18,2},{3,19},{19,3},{4,20},{20... | collective-permute-start | bytes 32264 | tf_op jit(solution)/shard_map/ppermute | solution.py:268
  35.6 4.1 %collective-permute-start.6 = (f32[1,14,704]{2,0,1:T(1,128)S(1)}, f32[1,14,704]{2,0,1:T(1,128)S(1)}, u32[]{:S(2)}, u32[]{:S(2)}) collective-permute-start(f32[1,14,704]{2,0,1:T(1,128)S(1)} %broadcast_in_dim.18), channel_id=1, source_target_pairs={{0,4},{4,0},{8,12},{12,8},{1,5},{5,1},{9,13},{13,9},{2,6},{6,2},{1... | collective-permute-start | bytes 118280 | tf_op jit(solution)/shard_map/ppermute | solution.py:260
  39.8 5.7 %collective-permute-start.7 = (f32[2,14,704]{2,0,1:T(2,128)S(1)}, f32[2,14,704]{2,0,1:T(2,128)S(1)}, u32[]{:S(2)}, u32[]{:S(2)}) collective-permute-start(f32[2,14,704]{2,0,1:T(2,128)S(1)} %maximum_select_fusion.5), channel_id=1, source_target_pairs={{0,8},{4,12},{8,0},{12,4},{1,9},{5,13},{9,1},{13,5},{2,10},{6,14},... | collective-permute-start | bytes 236552 | tf_op jit(solution)/shard_map/ppermute | solution.py:260
  45.9 1.3 %collective-permute-start.8 = (f32[1,14,1024]{2,1,0:T(8,128)S(1)}, f32[1,14,1024]{2,1,0:T(8,128)S(1)}, u32[]{:S(2)}, u32[]{:S(2)}) collective-permute-start(f32[1,14,1024]{2,1,0:T(8,128)S(1)} %maximum_bitcast_fusion.1), channel_id=1, source_target_pairs={{0,1},{1,0},{2,3},{3,2},{4,5},{5,4},{6,7},{7,6},{8,9},{9,8},{10,11... | collective-permute-start | bytes 172040 | tf_op jit(solution)/shard_map/ppermute | solution.py:260
  47.2 5.6 %collective-permute-start.9 = (f32[2,14,1024]{2,1,0:T(8,128)S(1)}, f32[2,14,1024]{2,1,0:T(8,128)S(1)}, u32[]{:S(2)}, u32[]{:S(2)}) collective-permute-start(f32[2,14,1024]{2,1,0:T(8,128)S(1)} %maximum_select_fusion.3), channel_id=1, source_target_pairs={{0,2},{1,3},{2,0},{3,1},{4,6},{5,7},{6,4},{7,5},{8,10},{9,11},{10,... | collective-permute-start | bytes 344072 | tf_op jit(solution)/shard_map/ppermute | solution.py:260

commit v21 on v20

--- a/solution.py
+++ b/solution.py
@@ -231,14 +231,20 @@
     half = lon_count // 2
     chunk = jnp.arange(half * lat_count * dons_each, dtype=jnp.int32)
 
-    def pick_for(base):
+    lon_bits = lon_count.bit_length() - 1
+
+    def reverse(value, bits):
+        return sum(((value >> i) & 1) << (bits - 1 - i) for i in range(bits))
+
+    def pick_for(low_bit):
         block = chunk // (lat_count * dons_each)
+        device = low_bit + reverse(block, lon_bits - 1) * 2
         lat_of = chunk // dons_each % lat_count
-        index = (lat_of * lon_count + base + block) * dons_each + chunk % dons_each
+        index = (lat_of * lon_count + device) * dons_each + chunk % dons_each
         return (index[:, None] == wanted[None, :]).astype(jnp.bfloat16)
 
-    pick_held = pick_for(lon_pos // half * half)
-    pick_new = pick_for((lon_pos ^ half) // half * half)
+    pick_held = pick_for(lon_pos % 2)
+    pick_new = pick_for(1 - lon_pos % 2)
 
     def select(values, pick):
         high = lax.reduce_precision(values, exponent_bits=8, mantissa_bits=7)
@@ -250,17 +256,22 @@
         count = values.shape[0]
         return picked[:count] + (picked[count : 2 * count] + picked[2 * count :])
 
-    def gather(packet, axis):
+    def gather(packet, axis, far_first=False):
         size = lax.axis_size(axis)
         pos = lax.axis_index(axis)
         held = packet[None]
+        steps = []
         k = 1
         while k < size:
+            steps.append(k)
+            k *= 2
+        if far_first:
+            steps.reverse()
+        for k in steps:
             before = held
             other = lax.ppermute(held, axis, [(i, i ^ k) for i in range(size)])
             low = (pos // k) % 2 == 0
             held = jnp.where(low, jnp.concatenate([held, other]), jnp.concatenate([other, held]))
-            k *= 2
         return held, before, other
 
     def section(field, donation):
@@ -275,15 +286,17 @@
         side_cols = jnp.concatenate([flat[:, :, :2], flat[:, :, cols - 2 :]], axis=2)
         side_cols = jnp.swapaxes(side_cols, 1, 2)
         lon_packet = jnp.concatenate([col_given, side_cols.reshape(comps * levels, -1)], axis=1)
-        lon_all, lon_held, lon_new = gather(lon_packet, "lon")
+        lon_all, lon_held, lon_new = gather(lon_packet, "lon", far_first=True)
         width = col_given.shape[1]
         held_part = jnp.transpose(lon_held[:, :, :width], (1, 0, 2)).reshape(comps * levels, -1)
         new_part = jnp.transpose(lon_new[:, :, :width], (1, 0, 2)).reshape(comps * levels, -1)
         side_cols = lon_all[:, :, width:].reshape(lon_count, comps, levels, 4, rows)
         up = lax.dynamic_index_in_dim(side_rows, jnp.maximum(lat_pos - 1, 0), keepdims=False)[:, :, 2:]
         down = lax.dynamic_index_in_dim(side_rows, jnp.minimum(lat_pos + 1, lat_count - 1), keepdims=False)[:, :, :2]
-        left = lax.dynamic_index_in_dim(side_cols, jnp.maximum(lon_pos - 1, 0), keepdims=False)[:, :, 2:]
-        right = lax.dynamic_index_in_dim(side_cols, jnp.minimum(lon_pos + 1, lon_count - 1), keepdims=False)[:, :, :2]
+        left_at = reverse(jnp.maximum(lon_pos - 1, 0), lon_bits)
+        right_at = reverse(jnp.minimum(lon_pos + 1, lon_count - 1), lon_bits)
+        left = lax.dynamic_index_in_dim(side_cols, left_at, keepdims=False)[:, :, 2:]
+        right = lax.dynamic_index_in_dim(side_cols, right_at, keepdims=False)[:, :, :2]
         rim = (select(held_part, pick_held) + select(new_part, pick_new)).reshape(comps, levels, -1)
         rim_lat = rim[:, :, :band].reshape(comps, levels, 2, cols)
         rim_lon = rim[:, :, band:].reshape(comps, levels, 2, rows)

time: 58.5 us -> 56.1 us (0.959)
  waiting for transfers between devices: 18.5 us -> 15.9 us
    ppermute x8, waiting for transfers between devices: 15.7 us -> 13.1 us  [gather(): other = lax.ppermute(held, axis, [(i, i ^ k) for i in range(size)])]
  transfers between devices with their start and end apart: 10 -> 10, of which waited for: 10 -> 10; matrix products, arithmetic and copies ran while one was open for 7% -> 8% of each run, Pallas kernels for 0% -> 0%
where the time goes in v21:
time: 56.1 us; the launch traced here: 55.8 us
  starting transfers between devices  19 us (34%)
  waiting for transfers between devices  15.9 us (28%)
  Pallas kernels  9.81 us (17%)
  local copies, waits for them, and re-layouts  5.64 us (10%)
  other arithmetic  2.44 us (4%)
  matrix products  2.34 us (4%)
  between operations  0.63 us (1%)
    ppermute x8, starting transfers between devices, gather(): other = lax.ppermute(held, axis, [(i, i ^ k) for i in range(size)])  14.2 us
    ppermute x8, waiting for transfers between devices, gather(): other = lax.ppermute(held, axis, [(i, i ^ k) for i in range(size)])  13.1 us
    pallas_call x2, Pallas kernels, advance(): pl.pallas_call(functools.partial(stencil_kernel, first=first), out_shape=...  7.18 us
    ppermute x2, starting transfers between devices, section(): given = lax.ppermute(donation, 'panel', [(0, 1), (1, 0)])  4.87 us
    ppermute x2, waiting for transfers between devices, section(): given = lax.ppermute(donation, 'panel', [(0, 1), (1, 0)])  2.78 us
    pallas_call x1, Pallas kernels, first_donation(): pl.pallas_call(donation_kernel, out_shape=(jax.ShapeDtypeStruct((planes,...  2.63 us
    dot_general x4, matrix products, select(): picked = jnp.dot(parts, pick, preferred_element_type=jnp.float32)  2.34 us
    slice x6, local copies, waits for them, and re-layouts, section(): side_cols = jnp.concatenate([flat[:, :, :2], flat[:, :, cols - 2:]], axis=2)  2.33 us
  transfers between devices with their start and end apart: 10, of which 10 were waited for; matrix products, arithmetic and copies ran while one was open for 8% of the time, Pallas kernels for 0%

profile of v21, /device:TPU:0, one launch (start us, length us, event | category | flops | bytes accessed | tf_op | source)
XLA Modules:
  0.0 55.8 jit_solution(8054758935031313388)
XLA Ops:
  0.0 2.6 %shard_map.55 = (f32[14,192]{1,0:T(8,128)}, f32[128,192]{1,0:T(8,128)}, f32[64,192]{1,0:T(8,128)}, f32[2,192]{1,0:T(2,128)}) custom-call(f32[14,64,128]{2,1,0:T(8,128)} %bitcast.78, s32[1,192]{1,0:T(1,128)} %bitcast.105, f32[2,192]{1,0:T(2,128)} %bitcast.104, f32[1,192]{1,0:T(1,128)} %bitcast.106), custom_call_target="tpu_custom_call" | custom-call | tf_op jit(solution)/shard_map/pallas_call | solution.py:178
  2.6 3.0 %collective-permute-start = (f32[14,192]{1,0:T(8,128)}, f32[14,192]{1,0:T(8,128)S(1)}, u32[]{:S(2)}, u32[]{:S(2)}) collective-permute-start(f32[14,192]{1,0:T(8,128)} %get-tuple-element.11), channel_id=1, source_target_pairs={{0,16},{16,0},{1,17},{17,1},{2,18},{18,2},{3,19},{19,3},{4,20},{20... | collective-permute-start | bytes 32264 | tf_op jit(solution)/shard_map/ppermute | solution.py:279
  6.8 0.7 %collective-permute-done = f32[14,192]{1,0:T(8,128)S(1)} collective-permute-done((f32[14,192]{1,0:T(8,128)}, f32[14,192]{1,0:T(8,128)S(1)}, u32[]{:S(2)}, u32[]{:S(2)}) %collective-permute-start) | collective-permute-done | bytes 10784 | tf_op jit(solution)/shard_map/ppermute | solution.py:279
  7.6 2.1 %collective-permute-start.1 = (f32[1,14,704]{2,0,1:T(1,128)S(1)}, f32[1,14,704]{2,0,1:T(1,128)S(1)}, u32[]{:S(2)}, u32[]{:S(2)}) collective-permute-start(f32[1,14,704]{2,0,1:T(1,128)S(1)} %broadcast_in_dim.16), channel_id=1, source_target_pairs={{0,4},{4,0},{8,12},{12,8},{1,5},{5,1},{9,13},{13,9},{2,6},{6,2},{1... | collective-permute-start | bytes 118280 | tf_op jit(solution)/shard_map/ppermute | solution.py:272
  10.0 1.8 %collective-permute-done.1 = f32[1,14,704]{2,0,1:T(1,128)S(1)} collective-permute-done((f32[1,14,704]{2,0,1:T(1,128)S(1)}, f32[1,14,704]{2,0,1:T(1,128)S(1)}, u32[]{:S(2)}, u32[]{:S(2)}) %collective-permute-start.1) | collective-permute-done | bytes 39456 | tf_op jit(solution)/shard_map/ppermute | solution.py:272
  11.9 3.1 %collective-permute-start.2 = (f32[2,14,704]{2,0,1:T(2,128)S(1)}, f32[2,14,704]{2,0,1:T(2,128)S(1)}, u32[]{:S(2)}, u32[]{:S(2)}) collective-permute-start(f32[2,14,704]{2,0,1:T(2,128)S(1)} %maximum_select_fusion.4), channel_id=1, source_target_pairs={{0,8},{4,12},{8,0},{12,4},{1,9},{5,13},{9,1},{13,5},{2,10},{6,14},... | collective-permute-start | bytes 236552 | tf_op jit(solution)/shard_map/ppermute | solution.py:272
  15.0 2.5 %collective-permute-done.2 = f32[2,14,704]{2,0,1:T(2,128)S(1)} collective-permute-done((f32[2,14,704]{2,0,1:T(2,128)S(1)}, f32[2,14,704]{2,0,1:T(2,128)S(1)}, u32[]{:S(2)}, u32[]{:S(2)}) %collective-permute-start.2) | collective-permute-done | bytes 78880 | tf_op jit(solution)/shard_map/ppermute | solution.py:272
  17.9 1.9 %collective-permute-start.3 = (f32[1,14,1024]{2,1,0:T(8,128)S(1)}, f32[1,14,1024]{2,1,0:T(8,128)S(1)}, u32[]{:S(2)}, u32[]{:S(2)}) collective-permute-start(f32[1,14,1024]{2,1,0:T(8,128)S(1)} %maximum_bitcast_fusion), channel_id=1, source_target_pairs={{0,2},{1,3},{2,0},{3,1},{4,6},{5,7},{6,4},{7,5},{8,10},{9,11},{10,... | collective-permute-start | bytes 172040 | tf_op jit(solution)/shard_map/ppermute | solution.py:272
  19.9 2.3 %collective-permute-done.3 = f32[1,14,1024]{2,1,0:T(8,128)S(1)} collective-permute-done((f32[1,14,1024]{2,1,0:T(8,128)S(1)}, f32[1,14,1024]{2,1,0:T(8,128)S(1)}, u32[]{:S(2)}, u32[]{:S(2)}) %collective-permute-start.3) | collective-permute-done | bytes 57376 | tf_op jit(solution)/shard_map/ppermute | solution.py:272
  22.5 0.6 %fusion.6 = f32[42,384]{1,0:T(8,128)S(1)} fusion(s32[384]{0:T(512)S(1)} %pad_add_fusion, s32[1536]{0:T(1024)S(1)} %fusion.62, bf16[14,1536]{1,0:T(8,128)(2,1)S(1)} %get-tuple-element.40, bf16[14,1536]{1,0:T(8,128)(2,1)S(1)} %get-tuple-element.41, bf16[14,1536]{1,0:T(8,128)(2,1)S(1)} %get-tuple-element.39), kind=kOutput, calls=%fused_computation.6 | convolution fusion | flops 50522112 | bytes 201216 | tf_op jit(solution)/shard_map/dot_general | solution.py:255
  24.9 0.6 %pad_maximum_fusion.4.refs_1_ = f32[14,8,128]{2,1,0:T(8,128)} fusion(f32[14,4,128]{2,1,0:T(4,128)S(1)} %select_maximum_fusion.1, f32[14,2,128]{2,1,0:T(2,128)S(1)} %bitcast.100, f32[14,2,128]{2,1,0:T(2,128)S(1)} %bitcast.99), kind=kLoop, calls=%fused_computation.76 | loop fusion | flops 28672 | bytes 114688 | tf_op jit(solution)/shard_map/concatenate | solution.py:308
  25.5 3.8 %shard_map.56 = (f32[14,64,128]{2,1,0:T(8,128)}, f32[14,192]{1,0:T(8,128)}) custom-call(f32[14,64,128]{2,1,0:T(8,128)} %bitcast.79, f32[14,8,128]{2,1,0:T(8,128)} %pad_maximum_fusion.4.refs_1_, f32[128,192]{1,0:T(8,128)} %get-tuple-element.12.refs_2_, f32[64,192]{1,0:T(8,128)} %get-tuple-element.13.refs_3_, f32[2,192]{1,0:T(2,128)} %get-tuple-element.14.refs_4_), custom_call_target="tpu_custom_call" | custom-call | tf_op jit(solution)/shard_map/pallas_call | solution.py:123
  29.3 0.9 %fusion.70 = (f32[14,2,128]{2,1,0:T(2,128)S(1)}, f32[14,2,128]{2,1,0:T(2,128)S(1)}) fusion(f32[14,64,128]{2,1,0:T(8,128)} %get-tuple-element.15.refs_0_), kind=kLoop, calls=%fused_computation.148 | loop fusion | bytes 57344 | tf_op jit(solution)/shard_map/slice | solution.py:281
  30.1 1.9 %collective-permute-start.5 = (f32[14,192]{1,0:T(8,128)}, f32[14,192]{1,0:T(8,128)S(1)}, u32[]{:S(2)}, u32[]{:S(2)}) collective-permute-start(f32[14,192]{1,0:T(8,128)} %get-tuple-element.16), channel_id=1, source_target_pairs={{0,16},{16,0},{1,17},{17,1},{2,18},{18,2},{3,19},{19,3},{4,20},{20... | collective-permute-start | bytes 32264 | tf_op jit(solution)/shard_map/ppermute | solution.py:279
  32.1 2.1 %collective-permute-done.5 = f32[14,192]{1,0:T(8,128)S(1)} collective-permute-done((f32[14,192]{1,0:T(8,128)}, f32[14,192]{1,0:T(8,128)S(1)}, u32[]{:S(2)}, u32[]{:S(2)}) %collective-permute-start.5) | collective-permute-done | bytes 10784 | tf_op jit(solution)/shard_map/ppermute | solution.py:279
  34.3 2.0 %collective-permute-start.6 = (f32[1,14,704]{2,0,1:T(1,128)S(1)}, f32[1,14,704]{2,0,1:T(1,128)S(1)}, u32[]{:S(2)}, u32[]{:S(2)}) collective-permute-start(f32[1,14,704]{2,0,1:T(1,128)S(1)} %broadcast_in_dim.18), channel_id=1, source_target_pairs={{0,4},{4,0},{8,12},{12,8},{1,5},{5,1},{9,13},{13,9},{2,6},{6,2},{1... | collective-permute-start | bytes 118280 | tf_op jit(solution)/shard_map/ppermute | solution.py:272
  36.3 1.3 %fusion.71 = (f32[14,64,2]{2,1,0:T(8,128)S(1)}, f32[14,64,2]{2,1,0:T(8,128)S(1)}) fusion(f32[14,64,128]{2,1,0:T(8,128)} %get-tuple-element.15.refs_0_), kind=kLoop, calls=%fused_computation.149 | loop fusion | bytes 28672 | tf_op jit(solution)/shard_map/slice | solution.py:286
  38.5 3.3 %collective-permute-start.7 = (f32[2,14,704]{2,0,1:T(2,128)S(1)}, f32[2,14,704]{2,0,1:T(2,128)S(1)}, u32[]{:S(2)}, u32[]{:S(2)}) collective-permute-start(f32[2,14,704]{2,0,1:T(2,128)S(1)} %maximum_select_fusion.5), channel_id=1, source_target_pairs={{0,8},{4,12},{8,0},{12,4},{1,9},{5,13},{9,1},{13,5},{2,10},{6,14},... | collective-permute-start | bytes 236552 | tf_op jit(solution)/shard_map/ppermute | solution.py:272
  42.0 2.4 %collective-permute-done.7 = f32[2,14,704]{2,0,1:T(2,128)S(1)} collective-permute-done((f32[2,14,704]{2,0,1:T(2,128)S(1)}, f32[2,14,704]{2,0,1:T(2,128)S(1)}, u32[]{:S(2)}, u32[]{:S(2)}) %collective-permute-start.7) | collective-permute-done | bytes 78880 | tf_op jit(solution)/shard_map/ppermute | solution.py:272
  44.7 1.6 %collective-permute-start.8 = (f32[1,14,1024]{2,1,0:T(8,128)S(1)}, f32[1,14,1024]{2,1,0:T(8,128)S(1)}, u32[]{:S(2)}, u32[]{:S(2)}) collective-permute-start(f32[1,14,1024]{2,1,0:T(8,128)S(1)} %maximum_bitcast_fusion.1), channel_id=1, source_target_pairs={{0,2},{1,3},{2,0},{3,1},{4,6},{5,7},{6,4},{7,5},{8,10},{9,11},{10,... | collective-permute-start | bytes 172040 | tf_op jit(solution)/shard_map/ppermute | solution.py:272
  46.4 2.7 %collective-permute-done.8 = f32[1,14,1024]{2,1,0:T(8,128)S(1)} collective-permute-done((f32[1,14,1024]{2,1,0:T(8,128)S(1)}, f32[1,14,1024]{2,1,0:T(8,128)S(1)}, u32[]{:S(2)}, u32[]{:S(2)}) %collective-permute-start.8) | collective-permute-done | bytes 57376 | tf_op jit(solution)/shard_map/ppermute | solution.py:272
  49.3 0.6 %fusion.4 = f32[42,384]{1,0:T(8,128)S(1)} fusion(s32[384]{0:T(512)S(1)} %pad_add_fusion, s32[1536]{0:T(1024)S(1)} %fusion.62, bf16[14,1536]{1,0:T(8,128)(2,1)S(1)} %get-tuple-element.34, bf16[14,1536]{1,0:T(8,128)(2,1)S(1)} %get-tuple-element.35, bf16[14,1536]{1,0:T(8,128)(2,1)S(1)} %get-tuple-element.33), kind=kOutput, calls=%fused_computation.4 | convolution fusion | flops 50522112 | bytes 201216 | tf_op jit(solution)/shard_map/dot_general | solution.py:255
  51.7 0.6 %pad_maximum_fusion.5.refs_1_ = f32[14,8,128]{2,1,0:T(8,128)} fusion(f32[14,4,128]{2,1,0:T(4,128)S(1)} %select_maximum_fusion, f32[14,2,128]{2,1,0:T(2,128)S(1)} %bitcast.96, f32[14,2,128]{2,1,0:T(2,128)S(1)} %bitcast.95), kind=kLoop, calls=%fused_computation.77 | loop fusion | flops 28672 | bytes 114688 | tf_op jit(solution)/shard_map/concatenate | solution.py:308
  52.4 3.4 %shard_map.57 = f32[14,64,128]{2,1,0:T(8,128)} custom-call(f32[14,64,128]{2,1,0:T(8,128)} %get-tuple-element.15.refs_0_, f32[14,8,128]{2,1,0:T(8,128)} %pad_maximum_fusion.5.refs_1_, f32[14,64,128]{2,1,0:T(8,128)} %bitcast.80), custom_call_target="tpu_custom_call" | custom-call | tf_op jit(solution)/shard_map/pallas_call | solution.py:123
  (100 shorter events, 7.4 us)
Async XLA Ops:
  0.0 5.6 %copy-start = (f32[1,7,2,64,128]{4,3,2,1,0:T(8,128)S(1)}, f32[1,7,2,64,128]{4,3,2,1,0:T(8,128)}, u32[]{:S(2)}) copy-start(f32[1,7,2,64,128]{4,3,2,1,0:T(8,128)} %param.5) | copy-start | bytes 1376260
  2.6 4.9 %collective-permute-start = (f32[14,192]{1,0:T(8,128)}, f32[14,192]{1,0:T(8,128)S(1)}, u32[]{:S(2)}, u32[]{:S(2)}) collective-permute-start(f32[14,192]{1,0:T(8,128)} %get-tuple-element.11), channel_id=1, source_target_pairs={{0,16},{16,0},{1,17},{17,1},{2,18},{18,2},{3,19},{19,3},{4,20},{20... | collective-permute-start | bytes 32264 | tf_op jit(solution)/shard_map/ppermute | solution.py:279
  5.6 0.7 %copy-start.1 = (s32[1,1,1,768]{3,2,1,0:T(1,128)S(1)}, s32[1,1,1,768]{3,2,1,0:T(1,128)}, u32[]{:S(2)}) copy-start(s32[1,1,1,768]{3,2,1,0:T(1,128)} %param.6) | copy-start | bytes 9220
  7.6 4.1 %collective-permute-start.1 = (f32[1,14,704]{2,0,1:T(1,128)S(1)}, f32[1,14,704]{2,0,1:T(1,128)S(1)}, u32[]{:S(2)}, u32[]{:S(2)}) collective-permute-start(f32[1,14,704]{2,0,1:T(1,128)S(1)} %broadcast_in_dim.16), channel_id=1, source_target_pairs={{0,4},{4,0},{8,12},{12,8},{1,5},{5,1},{9,13},{13,9},{2,6},{6,2},{1... | collective-permute-start | bytes 118280 | tf_op jit(solution)/shard_map/ppermute | solution.py:272
  11.9 5.6 %collective-permute-start.2 = (f32[2,14,704]{2,0,1:T(2,128)S(1)}, f32[2,14,704]{2,0,1:T(2,128)S(1)}, u32[]{:S(2)}, u32[]{:S(2)}) collective-permute-start(f32[2,14,704]{2,0,1:T(2,128)S(1)} %maximum_select_fusion.4), channel_id=1, source_target_pairs={{0,8},{4,12},{8,0},{12,4},{1,9},{5,13},{9,1},{13,5},{2,10},{6,14},... | collective-permute-start | bytes 236552 | tf_op jit(solution)/shard_map/ppermute | solution.py:272
  17.9 4.3 %collective-permute-start.3 = (f32[1,14,1024]{2,1,0:T(8,128)S(1)}, f32[1,14,1024]{2,1,0:T(8,128)S(1)}, u32[]{:S(2)}, u32[]{:S(2)}) collective-permute-start(f32[1,14,1024]{2,1,0:T(8,128)S(1)} %maximum_bitcast_fusion), channel_id=1, source_target_pairs={{0,2},{1,3},{2,0},{3,1},{4,6},{5,7},{6,4},{7,5},{8,10},{9,11},{10,... | collective-permute-start | bytes 172040 | tf_op jit(solution)/shard_map/ppermute | solution.py:272
  22.2 1.4 %collective-permute-start.4 = (f32[2,14,1024]{2,1,0:T(8,128)S(1)}, f32[2,14,1024]{2,1,0:T(8,128)S(1)}, u32[]{:S(2)}, u32[]{:S(2)}) collective-permute-start(f32[2,14,1024]{2,1,0:T(8,128)S(1)} %maximum_select_fusion.2), channel_id=1, source_target_pairs={{0,1},{1,0},{2,3},{3,2},{4,5},{5,4},{6,7},{7,6},{8,9},{9,8},{10,11... | collective-permute-start | bytes 344072 | tf_op jit(solution)/shard_map/ppermute | solution.py:272
  30.1 4.0 %collective-permute-start.5 = (f32[14,192]{1,0:T(8,128)}, f32[14,192]{1,0:T(8,128)S(1)}, u32[]{:S(2)}, u32[]{:S(2)}) collective-permute-start(f32[14,192]{1,0:T(8,128)} %get-tuple-element.16), channel_id=1, source_target_pairs={{0,16},{16,0},{1,17},{17,1},{2,18},{18,2},{3,19},{19,3},{4,20},{20... | collective-permute-start | bytes 32264 | tf_op jit(solution)/shard_map/ppermute | solution.py:279
  34.3 4.1 %collective-permute-start.6 = (f32[1,14,704]{2,0,1:T(1,128)S(1)}, f32[1,14,704]{2,0,1:T(1,128)S(1)}, u32[]{:S(2)}, u32[]{:S(2)}) collective-permute-start(f32[1,14,704]{2,0,1:T(1,128)S(1)} %broadcast_in_dim.18), channel_id=1, source_target_pairs={{0,4},{4,0},{8,12},{12,8},{1,5},{5,1},{9,13},{13,9},{2,6},{6,2},{1... | collective-permute-start | bytes 118280 | tf_op jit(solution)/shard_map/ppermute | solution.py:272
  38.5 5.8 %collective-permute-start.7 = (f32[2,14,704]{2,0,1:T(2,128)S(1)}, f32[2,14,704]{2,0,1:T(2,128)S(1)}, u32[]{:S(2)}, u32[]{:S(2)}) collective-permute-start(f32[2,14,704]{2,0,1:T(2,128)S(1)} %maximum_select_fusion.5), channel_id=1, source_target_pairs={{0,8},{4,12},{8,0},{12,4},{1,9},{5,13},{9,1},{13,5},{2,10},{6,14},... | collective-permute-start | bytes 236552 | tf_op jit(solution)/shard_map/ppermute | solution.py:272
  44.7 4.3 %collective-permute-start.8 = (f32[1,14,1024]{2,1,0:T(8,128)S(1)}, f32[1,14,1024]{2,1,0:T(8,128)S(1)}, u32[]{:S(2)}, u32[]{:S(2)}) collective-permute-start(f32[1,14,1024]{2,1,0:T(8,128)S(1)} %maximum_bitcast_fusion.1), channel_id=1, source_target_pairs={{0,2},{1,3},{2,0},{3,1},{4,6},{5,7},{6,4},{7,5},{8,10},{9,11},{10,... | collective-permute-start | bytes 172040 | tf_op jit(solution)/shard_map/ppermute | solution.py:272
  49.1 1.4 %collective-permute-start.9 = (f32[2,14,1024]{2,1,0:T(8,128)S(1)}, f32[2,14,1024]{2,1,0:T(8,128)S(1)}, u32[]{:S(2)}, u32[]{:S(2)}) collective-permute-start(f32[2,14,1024]{2,1,0:T(8,128)S(1)} %maximum_select_fusion.3), channel_id=1, source_target_pairs={{0,1},{1,0},{2,3},{3,2},{4,5},{5,4},{6,7},{7,6},{8,9},{9,8},{10,11... | collective-permute-start | bytes 344072 | tf_op jit(solution)/shard_map/ppermute | solution.py:272

commit v22 on v21

--- a/solution.py
+++ b/solution.py
@@ -232,6 +232,7 @@
     chunk = jnp.arange(half * lat_count * dons_each, dtype=jnp.int32)
 
     lon_bits = lon_count.bit_length() - 1
+    lat_bits = lat_count.bit_length() - 1
 
     def reverse(value, bits):
         return sum(((value >> i) & 1) << (bits - 1 - i) for i in range(bits))
@@ -239,7 +240,7 @@
     def pick_for(low_bit):
         block = chunk // (lat_count * dons_each)
         device = low_bit + reverse(block, lon_bits - 1) * 2
-        lat_of = chunk // dons_each % lat_count
+        lat_of = reverse(chunk // dons_each % lat_count, lat_bits)
         index = (lat_of * lon_count + device) * dons_each + chunk % dons_each
         return (index[:, None] == wanted[None, :]).astype(jnp.bfloat16)
 
@@ -280,7 +281,7 @@
         dons = given.shape[1]
         side_rows = jnp.concatenate([flat[:, :2, :], flat[:, rows - 2 :, :]], axis=1)
         lat_packet = jnp.concatenate([given, side_rows.reshape(comps * levels, -1)], axis=1)
-        lat_all = gather(lat_packet, "lat")[0]
+        lat_all = gather(lat_packet, "lat", far_first=True)[0]
         col_given = jnp.transpose(lat_all[:, :, :dons], (1, 0, 2)).reshape(comps * levels, -1)
         side_rows = lat_all[:, :, dons:].reshape(lat_count, comps, levels, 4, cols)
         side_cols = jnp.concatenate([flat[:, :, :2], flat[:, :, cols - 2 :]], axis=2)
@@ -291,8 +292,10 @@
         held_part = jnp.transpose(lon_held[:, :, :width], (1, 0, 2)).reshape(comps * levels, -1)
         new_part = jnp.transpose(lon_new[:, :, :width], (1, 0, 2)).reshape(comps * levels, -1)
         side_cols = lon_all[:, :, width:].reshape(lon_count, comps, levels, 4, rows)
-        up = lax.dynamic_index_in_dim(side_rows, jnp.maximum(lat_pos - 1, 0), keepdims=False)[:, :, 2:]
-        down = lax.dynamic_index_in_dim(side_rows, jnp.minimum(lat_pos + 1, lat_count - 1), keepdims=False)[:, :, :2]
+        up_at = reverse(jnp.maximum(lat_pos - 1, 0), lat_bits)
+        down_at = reverse(jnp.minimum(lat_pos + 1, lat_count - 1), lat_bits)
+        up = lax.dynamic_index_in_dim(side_rows, up_at, keepdims=False)[:, :, 2:]
+        down = lax.dynamic_index_in_dim(side_rows, down_at, keepdims=False)[:, :, :2]
         left_at = reverse(jnp.maximum(lon_pos - 1, 0), lon_bits)
         right_at = reverse(jnp.minimum(lon_pos + 1, lon_count - 1), lon_bits)
         left = lax.dynamic_index_in_dim(side_cols, left_at, keepdims=False)[:, :, 2:]

time: 56.1 us -> 55.8 us (level)
  no operation moved by 1% of the time
where the time goes in v22:
time: 55.8 us; the launch traced here: 55.5 us
  starting transfers between devices  18.7 us (34%)
  waiting for transfers between devices  16 us (29%)
  Pallas kernels  9.81 us (18%)
  local copies, waits for them, and re-layouts  5.64 us (10%)
  other arithmetic  2.44 us (4%)
  matrix products  2.34 us (4%)
  between operations  0.63 us (1%)
    ppermute x8, starting transfers between devices, gather(): other = lax.ppermute(held, axis, [(i, i ^ k) for i in range(size)])  13.8 us
    ppermute x8, waiting for transfers between devices, gather(): other = lax.ppermute(held, axis, [(i, i ^ k) for i in range(size)])  13.2 us
    pallas_call x2, Pallas kernels, advance(): pl.pallas_call(functools.partial(stencil_kernel, first=first), out_shape=...  7.18 us
    ppermute x2, starting transfers between devices, section(): given = lax.ppermute(donation, 'panel', [(0, 1), (1, 0)])  4.87 us
    ppermute x2, waiting for transfers between devices, section(): given = lax.ppermute(donation, 'panel', [(0, 1), (1, 0)])  2.77 us
    pallas_call x1, Pallas kernels, first_donation(): pl.pallas_call(donation_kernel, out_shape=(jax.ShapeDtypeStruct((planes,...  2.63 us
    dot_general x4, matrix products, select(): picked = jnp.dot(parts, pick, preferred_element_type=jnp.float32)  2.34 us
    slice x6, local copies, waits for them, and re-layouts, section(): side_cols = jnp.concatenate([flat[:, :, :2], flat[:, :, cols - 2:]], axis=2)  2.33 us
  transfers between devices with their start and end apart: 10, of which 10 were waited for; matrix products, arithmetic and copies ran while one was open for 8% of the time, Pallas kernels for 0%

profile of v22, /device:TPU:0, one launch (start us, length us, event | category | flops | bytes accessed | tf_op | source)
XLA Modules:
  0.0 55.5 jit_solution(8229677117812341964)
XLA Ops:
  0.0 2.6 %shard_map.55 = (f32[14,192]{1,0:T(8,128)}, f32[128,192]{1,0:T(8,128)}, f32[64,192]{1,0:T(8,128)}, f32[2,192]{1,0:T(2,128)}) custom-call(f32[14,64,128]{2,1,0:T(8,128)} %bitcast.78, s32[1,192]{1,0:T(1,128)} %bitcast.105, f32[2,192]{1,0:T(2,128)} %bitcast.104, f32[1,192]{1,0:T(1,128)} %bitcast.106), custom_call_target="tpu_custom_call" | custom-call | tf_op jit(solution)/shard_map/pallas_call | solution.py:178
  2.6 3.0 %collective-permute-start = (f32[14,192]{1,0:T(8,128)}, f32[14,192]{1,0:T(8,128)S(1)}, u32[]{:S(2)}, u32[]{:S(2)}) collective-permute-start(f32[14,192]{1,0:T(8,128)} %get-tuple-element.11), channel_id=1, source_target_pairs={{0,16},{16,0},{1,17},{17,1},{2,18},{18,2},{3,19},{19,3},{4,20},{20... | collective-permute-start | bytes 32264 | tf_op jit(solution)/shard_map/ppermute | solution.py:280
  6.8 0.7 %collective-permute-done = f32[14,192]{1,0:T(8,128)S(1)} collective-permute-done((f32[14,192]{1,0:T(8,128)}, f32[14,192]{1,0:T(8,128)S(1)}, u32[]{:S(2)}, u32[]{:S(2)}) %collective-permute-start) | collective-permute-done | bytes 10784 | tf_op jit(solution)/shard_map/ppermute | solution.py:280
  7.6 3.2 %collective-permute-start.1 = (f32[1,14,704]{2,0,1:T(1,128)S(1)}, f32[1,14,704]{2,0,1:T(1,128)S(1)}, u32[]{:S(2)}, u32[]{:S(2)}) collective-permute-start(f32[1,14,704]{2,0,1:T(1,128)S(1)} %broadcast_in_dim.16), channel_id=1, source_target_pairs={{0,8},{4,12},{8,0},{12,4},{1,9},{5,13},{9,1},{13,5},{2,10},{6,14},... | collective-permute-start | bytes 118280 | tf_op jit(solution)/shard_map/ppermute | solution.py:273
  11.0 1.8 %collective-permute-done.1 = f32[1,14,704]{2,0,1:T(1,128)S(1)} collective-permute-done((f32[1,14,704]{2,0,1:T(1,128)S(1)}, f32[1,14,704]{2,0,1:T(1,128)S(1)}, u32[]{:S(2)}, u32[]{:S(2)}) %collective-permute-start.1) | collective-permute-done | bytes 39456 | tf_op jit(solution)/shard_map/ppermute | solution.py:273
  12.9 2.0 %collective-permute-start.2 = (f32[2,14,704]{2,0,1:T(2,128)S(1)}, f32[2,14,704]{2,0,1:T(2,128)S(1)}, u32[]{:S(2)}, u32[]{:S(2)}) collective-permute-start(f32[2,14,704]{2,0,1:T(2,128)S(1)} %maximum_select_fusion.4), channel_id=1, source_target_pairs={{0,4},{4,0},{8,12},{12,8},{1,5},{5,1},{9,13},{13,9},{2,6},{6,2},{1... | collective-permute-start | bytes 236552 | tf_op jit(solution)/shard_map/ppermute | solution.py:273
  14.9 2.6 %collective-permute-done.2 = f32[2,14,704]{2,0,1:T(2,128)S(1)} collective-permute-done((f32[2,14,704]{2,0,1:T(2,128)S(1)}, f32[2,14,704]{2,0,1:T(2,128)S(1)}, u32[]{:S(2)}, u32[]{:S(2)}) %collective-permute-start.2) | collective-permute-done | bytes 78880 | tf_op jit(solution)/shard_map/ppermute | solution.py:273
  17.9 1.9 %collective-permute-start.3 = (f32[1,14,1024]{2,1,0:T(8,128)S(1)}, f32[1,14,1024]{2,1,0:T(8,128)S(1)}, u32[]{:S(2)}, u32[]{:S(2)}) collective-permute-start(f32[1,14,1024]{2,1,0:T(8,128)S(1)} %maximum_bitcast_fusion), channel_id=1, source_target_pairs={{0,2},{1,3},{2,0},{3,1},{4,6},{5,7},{6,4},{7,5},{8,10},{9,11},{10,... | collective-permute-start | bytes 172040 | tf_op jit(solution)/shard_map/ppermute | solution.py:273
  19.9 2.3 %collective-permute-done.3 = f32[1,14,1024]{2,1,0:T(8,128)S(1)} collective-permute-done((f32[1,14,1024]{2,1,0:T(8,128)S(1)}, f32[1,14,1024]{2,1,0:T(8,128)S(1)}, u32[]{:S(2)}, u32[]{:S(2)}) %collective-permute-start.3) | collective-permute-done | bytes 57376 | tf_op jit(solution)/shard_map/ppermute | solution.py:273
  22.5 0.6 %fusion.6 = f32[42,384]{1,0:T(8,128)S(1)} fusion(s32[384]{0:T(512)S(1)} %pad_add_fusion, s32[1536]{0:T(1024)S(1)} %fusion.61, bf16[14,1536]{1,0:T(8,128)(2,1)S(1)} %get-tuple-element.40, bf16[14,1536]{1,0:T(8,128)(2,1)S(1)} %get-tuple-element.41, bf16[14,1536]{1,0:T(8,128)(2,1)S(1)} %get-tuple-element.39), kind=kOutput, calls=%fused_computation.6 | convolution fusion | flops 50522112 | bytes 201216 | tf_op jit(solution)/shard_map/dot_general | solution.py:256
  24.9 0.6 %pad_maximum_fusion.4.refs_1_ = f32[14,8,128]{2,1,0:T(8,128)} fusion(f32[14,4,128]{2,1,0:T(4,128)S(1)} %select_maximum_fusion.1, f32[14,2,128]{2,1,0:T(2,128)S(1)} %bitcast.100, f32[14,2,128]{2,1,0:T(2,128)S(1)} %bitcast.99), kind=kLoop, calls=%fused_computation.76 | loop fusion | flops 28672 | bytes 114688 | tf_op jit(solution)/shard_map/concatenate | solution.py:311
  25.5 3.8 %shard_map.56 = (f32[14,64,128]{2,1,0:T(8,128)}, f32[14,192]{1,0:T(8,128)}) custom-call(f32[14,64,128]{2,1,0:T(8,128)} %bitcast.79, f32[14,8,128]{2,1,0:T(8,128)} %pad_maximum_fusion.4.refs_1_, f32[128,192]{1,0:T(8,128)} %get-tuple-element.12.refs_2_, f32[64,192]{1,0:T(8,128)} %get-tuple-element.13.refs_3_, f32[2,192]{1,0:T(2,128)} %get-tuple-element.14.refs_4_), custom_call_target="tpu_custom_call" | custom-call | tf_op jit(solution)/shard_map/pallas_call | solution.py:123
  29.3 0.9 %fusion.69 = (f32[14,2,128]{2,1,0:T(2,128)S(1)}, f32[14,2,128]{2,1,0:T(2,128)S(1)}) fusion(f32[14,64,128]{2,1,0:T(8,128)} %get-tuple-element.15.refs_0_), kind=kLoop, calls=%fused_computation.148 | loop fusion | bytes 57344 | tf_op jit(solution)/shard_map/slice | solution.py:282
  30.1 1.9 %collective-permute-start.5 = (f32[14,192]{1,0:T(8,128)}, f32[14,192]{1,0:T(8,128)S(1)}, u32[]{:S(2)}, u32[]{:S(2)}) collective-permute-start(f32[14,192]{1,0:T(8,128)} %get-tuple-element.16), channel_id=1, source_target_pairs={{0,16},{16,0},{1,17},{17,1},{2,18},{18,2},{3,19},{19,3},{4,20},{20... | collective-permute-start | bytes 32264 | tf_op jit(solution)/shard_map/ppermute | solution.py:280
  32.1 2.1 %collective-permute-done.5 = f32[14,192]{1,0:T(8,128)S(1)} collective-permute-done((f32[14,192]{1,0:T(8,128)}, f32[14,192]{1,0:T(8,128)S(1)}, u32[]{:S(2)}, u32[]{:S(2)}) %collective-permute-start.5) | collective-permute-done | bytes 10784 | tf_op jit(solution)/shard_map/ppermute | solution.py:280
  34.3 3.0 %collective-permute-start.6 = (f32[1,14,704]{2,0,1:T(1,128)S(1)}, f32[1,14,704]{2,0,1:T(1,128)S(1)}, u32[]{:S(2)}, u32[]{:S(2)}) collective-permute-start(f32[1,14,704]{2,0,1:T(1,128)S(1)} %broadcast_in_dim.18), channel_id=1, source_target_pairs={{0,8},{4,12},{8,0},{12,4},{1,9},{5,13},{9,1},{13,5},{2,10},{6,14},... | collective-permute-start | bytes 118280 | tf_op jit(solution)/shard_map/ppermute | solution.py:273
  37.3 1.3 %fusion.70 = (f32[14,64,2]{2,1,0:T(8,128)S(1)}, f32[14,64,2]{2,1,0:T(8,128)S(1)}) fusion(f32[14,64,128]{2,1,0:T(8,128)} %get-tuple-element.15.refs_0_), kind=kLoop, calls=%fused_computation.149 | loop fusion | bytes 28672 | tf_op jit(solution)/shard_map/slice | solution.py:287
  39.5 1.9 %collective-permute-start.7 = (f32[2,14,704]{2,0,1:T(2,128)S(1)}, f32[2,14,704]{2,0,1:T(2,128)S(1)}, u32[]{:S(2)}, u32[]{:S(2)}) collective-permute-start(f32[2,14,704]{2,0,1:T(2,128)S(1)} %maximum_select_fusion.5), channel_id=1, source_target_pairs={{0,4},{4,0},{8,12},{12,8},{1,5},{5,1},{9,13},{13,9},{2,6},{6,2},{1... | collective-permute-start | bytes 236552 | tf_op jit(solution)/shard_map/ppermute | solution.py:273
  41.5 2.6 %collective-permute-done.7 = f32[2,14,704]{2,0,1:T(2,128)S(1)} collective-permute-done((f32[2,14,704]{2,0,1:T(2,128)S(1)}, f32[2,14,704]{2,0,1:T(2,128)S(1)}, u32[]{:S(2)}, u32[]{:S(2)}) %collective-permute-start.7) | collective-permute-done | bytes 78880 | tf_op jit(solution)/shard_map/ppermute | solution.py:273
  44.5 1.8 %collective-permute-start.8 = (f32[1,14,1024]{2,1,0:T(8,128)S(1)}, f32[1,14,1024]{2,1,0:T(8,128)S(1)}, u32[]{:S(2)}, u32[]{:S(2)}) collective-permute-start(f32[1,14,1024]{2,1,0:T(8,128)S(1)} %maximum_bitcast_fusion.1), channel_id=1, source_target_pairs={{0,2},{1,3},{2,0},{3,1},{4,6},{5,7},{6,4},{7,5},{8,10},{9,11},{10,... | collective-permute-start | bytes 172040 | tf_op jit(solution)/shard_map/ppermute | solution.py:273
  46.3 2.5 %collective-permute-done.8 = f32[1,14,1024]{2,1,0:T(8,128)S(1)} collective-permute-done((f32[1,14,1024]{2,1,0:T(8,128)S(1)}, f32[1,14,1024]{2,1,0:T(8,128)S(1)}, u32[]{:S(2)}, u32[]{:S(2)}) %collective-permute-start.8) | collective-permute-done | bytes 57376 | tf_op jit(solution)/shard_map/ppermute | solution.py:273
  49.1 0.6 %fusion.4 = f32[42,384]{1,0:T(8,128)S(1)} fusion(s32[384]{0:T(512)S(1)} %pad_add_fusion, s32[1536]{0:T(1024)S(1)} %fusion.61, bf16[14,1536]{1,0:T(8,128)(2,1)S(1)} %get-tuple-element.34, bf16[14,1536]{1,0:T(8,128)(2,1)S(1)} %get-tuple-element.35, bf16[14,1536]{1,0:T(8,128)(2,1)S(1)} %get-tuple-element.33), kind=kOutput, calls=%fused_computation.4 | convolution fusion | flops 50522112 | bytes 201216 | tf_op jit(solution)/shard_map/dot_general | solution.py:256
  51.5 0.6 %pad_maximum_fusion.5.refs_1_ = f32[14,8,128]{2,1,0:T(8,128)} fusion(f32[14,4,128]{2,1,0:T(4,128)S(1)} %select_maximum_fusion, f32[14,2,128]{2,1,0:T(2,128)S(1)} %bitcast.96, f32[14,2,128]{2,1,0:T(2,128)S(1)} %bitcast.95), kind=kLoop, calls=%fused_computation.77 | loop fusion | flops 28672 | bytes 114688 | tf_op jit(solution)/shard_map/concatenate | solution.py:311
  52.1 3.4 %shard_map.57 = f32[14,64,128]{2,1,0:T(8,128)} custom-call(f32[14,64,128]{2,1,0:T(8,128)} %get-tuple-element.15.refs_0_, f32[14,8,128]{2,1,0:T(8,128)} %pad_maximum_fusion.5.refs_1_, f32[14,64,128]{2,1,0:T(8,128)} %bitcast.80), custom_call_target="tpu_custom_call" | custom-call | tf_op jit(solution)/shard_map/pallas_call | solution.py:123
  (100 shorter events, 7.4 us)
Async XLA Ops:
  0.0 5.6 %copy-start = (f32[1,7,2,64,128]{4,3,2,1,0:T(8,128)S(1)}, f32[1,7,2,64,128]{4,3,2,1,0:T(8,128)}, u32[]{:S(2)}) copy-start(f32[1,7,2,64,128]{4,3,2,1,0:T(8,128)} %param.5) | copy-start | bytes 1376260
  2.6 4.9 %collective-permute-start = (f32[14,192]{1,0:T(8,128)}, f32[14,192]{1,0:T(8,128)S(1)}, u32[]{:S(2)}, u32[]{:S(2)}) collective-permute-start(f32[14,192]{1,0:T(8,128)} %get-tuple-element.11), channel_id=1, source_target_pairs={{0,16},{16,0},{1,17},{17,1},{2,18},{18,2},{3,19},{19,3},{4,20},{20... | collective-permute-start | bytes 32264 | tf_op jit(solution)/shard_map/ppermute | solution.py:280
  5.6 0.7 %copy-start.1 = (s32[1,1,1,768]{3,2,1,0:T(1,128)S(1)}, s32[1,1,1,768]{3,2,1,0:T(1,128)}, u32[]{:S(2)}) copy-start(s32[1,1,1,768]{3,2,1,0:T(1,128)} %param.6) | copy-start | bytes 9220
  7.6 5.2 %collective-permute-start.1 = (f32[1,14,704]{2,0,1:T(1,128)S(1)}, f32[1,14,704]{2,0,1:T(1,128)S(1)}, u32[]{:S(2)}, u32[]{:S(2)}) collective-permute-start(f32[1,14,704]{2,0,1:T(1,128)S(1)} %broadcast_in_dim.16), channel_id=1, source_target_pairs={{0,8},{4,12},{8,0},{12,4},{1,9},{5,13},{9,1},{13,5},{2,10},{6,14},... | collective-permute-start | bytes 118280 | tf_op jit(solution)/shard_map/ppermute | solution.py:273
  12.9 4.6 %collective-permute-start.2 = (f32[2,14,704]{2,0,1:T(2,128)S(1)}, f32[2,14,704]{2,0,1:T(2,128)S(1)}, u32[]{:S(2)}, u32[]{:S(2)}) collective-permute-start(f32[2,14,704]{2,0,1:T(2,128)S(1)} %maximum_select_fusion.4), channel_id=1, source_target_pairs={{0,4},{4,0},{8,12},{12,8},{1,5},{5,1},{9,13},{13,9},{2,6},{6,2},{1... | collective-permute-start | bytes 236552 | tf_op jit(solution)/shard_map/ppermute | solution.py:273
  17.9 4.3 %collective-permute-start.3 = (f32[1,14,1024]{2,1,0:T(8,128)S(1)}, f32[1,14,1024]{2,1,0:T(8,128)S(1)}, u32[]{:S(2)}, u32[]{:S(2)}) collective-permute-start(f32[1,14,1024]{2,1,0:T(8,128)S(1)} %maximum_bitcast_fusion), channel_id=1, source_target_pairs={{0,2},{1,3},{2,0},{3,1},{4,6},{5,7},{6,4},{7,5},{8,10},{9,11},{10,... | collective-permute-start | bytes 172040 | tf_op jit(solution)/shard_map/ppermute | solution.py:273
  22.2 1.4 %collective-permute-start.4 = (f32[2,14,1024]{2,1,0:T(8,128)S(1)}, f32[2,14,1024]{2,1,0:T(8,128)S(1)}, u32[]{:S(2)}, u32[]{:S(2)}) collective-permute-start(f32[2,14,1024]{2,1,0:T(8,128)S(1)} %maximum_select_fusion.2), channel_id=1, source_target_pairs={{0,1},{1,0},{2,3},{3,2},{4,5},{5,4},{6,7},{7,6},{8,9},{9,8},{10,11... | collective-permute-start | bytes 344072 | tf_op jit(solution)/shard_map/ppermute | solution.py:273
  30.1 4.0 %collective-permute-start.5 = (f32[14,192]{1,0:T(8,128)}, f32[14,192]{1,0:T(8,128)S(1)}, u32[]{:S(2)}, u32[]{:S(2)}) collective-permute-start(f32[14,192]{1,0:T(8,128)} %get-tuple-element.16), channel_id=1, source_target_pairs={{0,16},{16,0},{1,17},{17,1},{2,18},{18,2},{3,19},{19,3},{4,20},{20... | collective-permute-start | bytes 32264 | tf_op jit(solution)/shard_map/ppermute | solution.py:280
  34.3 5.1 %collective-permute-start.6 = (f32[1,14,704]{2,0,1:T(1,128)S(1)}, f32[1,14,704]{2,0,1:T(1,128)S(1)}, u32[]{:S(2)}, u32[]{:S(2)}) collective-permute-start(f32[1,14,704]{2,0,1:T(1,128)S(1)} %broadcast_in_dim.18), channel_id=1, source_target_pairs={{0,8},{4,12},{8,0},{12,4},{1,9},{5,13},{9,1},{13,5},{2,10},{6,14},... | collective-permute-start | bytes 118280 | tf_op jit(solution)/shard_map/ppermute | solution.py:273
  39.5 4.6 %collective-permute-start.7 = (f32[2,14,704]{2,0,1:T(2,128)S(1)}, f32[2,14,704]{2,0,1:T(2,128)S(1)}, u32[]{:S(2)}, u32[]{:S(2)}) collective-permute-start(f32[2,14,704]{2,0,1:T(2,128)S(1)} %maximum_select_fusion.5), channel_id=1, source_target_pairs={{0,4},{4,0},{8,12},{12,8},{1,5},{5,1},{9,13},{13,9},{2,6},{6,2},{1... | collective-permute-start | bytes 236552 | tf_op jit(solution)/shard_map/ppermute | solution.py:273
  44.5 4.3 %collective-permute-start.8 = (f32[1,14,1024]{2,1,0:T(8,128)S(1)}, f32[1,14,1024]{2,1,0:T(8,128)S(1)}, u32[]{:S(2)}, u32[]{:S(2)}) collective-permute-start(f32[1,14,1024]{2,1,0:T(8,128)S(1)} %maximum_bitcast_fusion.1), channel_id=1, source_target_pairs={{0,2},{1,3},{2,0},{3,1},{4,6},{5,7},{6,4},{7,5},{8,10},{9,11},{10,... | collective-permute-start | bytes 172040 | tf_op jit(solution)/shard_map/ppermute | solution.py:273
  48.8 1.4 %collective-permute-start.9 = (f32[2,14,1024]{2,1,0:T(8,128)S(1)}, f32[2,14,1024]{2,1,0:T(8,128)S(1)}, u32[]{:S(2)}, u32[]{:S(2)}) collective-permute-start(f32[2,14,1024]{2,1,0:T(8,128)S(1)} %maximum_select_fusion.3), channel_id=1, source_target_pairs={{0,1},{1,0},{2,3},{3,2},{4,5},{5,4},{6,7},{7,6},{8,9},{9,8},{10,11... | collective-permute-start | bytes 344072 | tf_op jit(solution)/shard_map/ppermute | solution.py:273
